TPU v7x, 32 devices: a whole 2x2x4 slice. The times are simulated.
32 devices in a mesh: grp: 2 (over y), row: 4 (over z), col: 2 (over x), sub: 2 (over core).
Axes of the slice: x: 2, y: 2, z: 4, core: 2. Of those that a mesh axis runs over, the one named last changes fastest.
Arguments:
- a_blocks: bfloat16 [16, 2, 4, 2, 256, 256], P(('grp', 'row', 'sub'), 'col'), parts along dimension 0, may hold values from 20 to 2000
- block_list: int32 [16, 2, 4, 2], P(('grp', 'row', 'sub'), 'col'), parts along dimension 0, may hold values from 0 to 3, as said below
- block_count: int32 [16, 2, 4], P(('grp', 'row', 'sub'), 'col'), parts along dimension 0, may hold values from 1 to 2
- w_factor: bfloat16 [16, 1024, 256], P(('grp', 'row', 'sub')), parts along dimension 0, may hold values from 0.05 to 4
- h_factor: bfloat16 [256, 4096], P(None, ('grp', 'row', 'col')), parts along dimension 1, may hold values from 0.05 to 4
Outputs:
- w_new: float32 [16, 1024, 256], P(('grp', 'row', 'sub'), 'col'), parts along dimension 0
- h_new: float32 [256, 4096], P(None, ('grp', 'row', 'col')), parts along dimension 1
There are 2 independent parts, one for each index of `grp`. A program takes and returns all parts, laid end to end along the dimension named above; each array names one. Nothing has to cross between parts.
Inputs may be any that keep to these rules, and one draw needn't show every extreme that they name: `block_list`: within one block row and column group the 2 slots name different column blocks.
All inputs are finite; a program needn't handle non-finite values.
Results may differ from a plain program's by a relative error of at most 0.0003.
Values may be sent and summed in bfloat16 or wider, within the bound.
No kernel may reach another device: no remote copies, remote signals or barrier semaphores. Data moves between devices by JAX's collectives and lax.ppermute only.
A program may use at most 64 MiB of HBM per device.

v0:
```python
import jax
import jax.numpy as jnp
from jax import lax
from jax.sharding import PartitionSpec as P


def body(a_blocks, block_list, block_count, w_factor, h_factor):
    values = a_blocks[0, 0]
    lists = block_list[0, 0]
    counts = block_count[0, 0]
    w_tile = w_factor[0]
    row_blocks, stored, width = values.shape[0], values.shape[1], values.shape[2]
    rank = w_tile.shape[1]
    tile_rows = w_tile.shape[0]
    n_row = lax.axis_size("row")
    w_rows = w_tile.reshape(row_blocks, width, rank)

    h_all = lax.all_gather(h_factor, "row", axis=1, tiled=True)

    numer_h = jnp.zeros((rank, n_row * width), jnp.float32)
    parts_w = []
    for brow in range(row_blocks):
        part_w = jnp.zeros((width, rank), jnp.float32)
        for slot in range(stored):
            target = lists[brow, slot]
            live = slot < counts[brow]
            h_block = lax.dynamic_slice_in_dim(h_all, target * width, width, 1)
            product = jnp.dot(w_rows[brow], h_block, preferred_element_type=jnp.float32)
            ratios = (values[brow, slot].astype(jnp.float32) / product).astype(jnp.bfloat16)
            ratios = jnp.where(live, ratios, jnp.zeros_like(ratios))
            part_h = jnp.einsum(
                "ik,ij->kj", w_rows[brow], ratios, preferred_element_type=jnp.float32
            )
            part_w = part_w + jnp.einsum(
                "ij,kj->ik", ratios, h_block, preferred_element_type=jnp.float32
            )
            old = lax.dynamic_slice_in_dim(numer_h, target * width, width, 1)
            numer_h = lax.dynamic_update_slice_in_dim(numer_h, old + part_h, target * width, 1)
        parts_w.append(part_w)
    numer_w = jnp.stack(parts_w).reshape(tile_rows, rank)

    col_first = lax.axis_index("col") == 0
    sub_first = lax.axis_index("sub") == 0
    w_sum = jnp.sum(w_tile.astype(jnp.float32), axis=0)
    h_sum = jnp.sum(h_factor.astype(jnp.float32), axis=1)
    sums = jnp.concatenate(
        [jnp.where(col_first, w_sum, 0.0), jnp.where(sub_first, h_sum, 0.0)]
    )
    sums = lax.psum(sums, ("row", "col", "sub"))
    w_total = sums[:rank]
    h_total = sums[rank:]

    numer_h = lax.psum_scatter(numer_h, "row", scatter_dimension=1, tiled=True)
    numer_h = lax.psum(numer_h, "sub")
    h_new = h_factor.astype(jnp.float32) * numer_h / w_total[:, None]

    share = tile_rows // lax.axis_size("col")
    col_index = lax.axis_index("col")
    mine = lax.psum_scatter(numer_w, "col", scatter_dimension=0, tiled=True)
    w_part = lax.dynamic_slice_in_dim(w_tile, col_index * share, share, 0).astype(jnp.float32)
    w_new = (w_part * mine / h_total[None, :])[None]
    return (w_new, h_new)


def solution(mesh):
    placed = (
        P(("grp", "row", "sub"), "col", None, None, None, None),
        P(("grp", "row", "sub"), "col", None, None),
        P(("grp", "row", "sub"), "col", None),
        P(("grp", "row", "sub"), None, None),
        P(None, ("grp", "row", "col")),
    )
    return jax.shard_map(
        body,
        mesh=mesh,
        in_specs=placed,
        out_specs=(P(("grp", "row", "sub"), "col", None), P(None, ("grp", "row", "col"))),
        check_vma=False,
    )
```

profile of v0, /device:TPU:0, one launch (start us, length us, event | category | flops | bytes accessed | tf_op | source)
XLA Modules:
  0.0 123.7 jit_solution(1494217705936552093)
XLA Ops:
  7.2 1.5 %fusion.116 = (s32[1,1,1]{2,1,0:T(1,128)}, s32[1,1,1]{2,1,0:T(1,128)}, s32[1,1,1]{2,1,0:T(1,128)}, s32[1,1,1]{2,1,0:T(1,128)}) fusion(s32[1,1,4]{2,1,0:T(1,128)} %param.7), kind=kLoop, calls=%fused_computation.152 | loop fusion | bytes 32 | tf_op jit(solution)/shard_map/slice | solution.py:26
  13.8 0.7 copy-done.3
  14.5 0.7 fusion.115
  20.1 17.6 %all_gather.3 = bf16[256,1024]{1,0:T(8,128)(2,1)S(1)} all-gather(bf16[256,256]{1,0:T(8,128)(2,1)} %param.9), channel_id=1, replica_groups=mesh['grp'=2,'row'=4,'col'=2,'sub'=2] {'row'}, dimensions={1}, use_global_device_ids=true | all-gather | bytes 655360 | tf_op jit(solution)/shard_map/all_gather | solution.py:18
  37.7 1.5 %copy.7 = bf16[1,1,4,2,256,256]{4,5,3,2,1,0:T(8,128)(2,1)S(1)} copy(bf16[1,1,4,2,256,256]{5,4,3,2,1,0:T(8,128)(2,1)} %param.5) | data formatting | bytes 2097152 | tf_op args[0]
  39.3 0.2 fusion.35
  39.5 0.2 fusion.36
  39.8 0.2 fusion.37
  40.0 0.3 fusion.38
  40.3 0.2 fusion.39
  40.6 0.2 fusion.40
  40.8 0.2 fusion.41
  41.1 0.3 fusion.42
  43.0 1.0 copy-done
  44.3 0.2 fusion.3
  44.8 0.2 fusion.2
  46.0 1.1 pad_maximum_fusion
  47.1 0.8 copy-done.2
  48.3 30.9 %psum.14 = f32[512]{0:T(512)S(1)} all-reduce(f32[512]{0:T(512)S(1)} %pad_maximum_fusion.1), channel_id=1, replica_groups=mesh['grp'=2,'row'=4,'col'=2,'sub'=2] {'row','col','sub'}, use_global_device_ids=true, to_apply=%region_3.4 | all-reduce | flops 512 | bytes 4096 | tf_op jit(solution)/shard_map/psum | solution.py:49
  79.3 15.4 %reduce-scatter.3.cloned.1.call-done = f32[512,256]{1,0:T(8,128)} async-done(((f32[1024,256]{1,0:T(8,128)}), f32[512,256]{1,0:T(8,128)}) %reduce-scatter.3.cloned.1.call-update) | async-done | bytes 524304 | tf_op jit(solution)/shard_map/reduce_scatter | solution.py:59
  94.8 1.9 %fusion.44 = f32[1,512,256]{2,1,0:T(8,128)} fusion(f32[512,256]{1,0:T(8,128)} %reduce-scatter.3.cloned.1.call-done, f32[256]{0:T(256)S(1)} %get-tuple-element.5, bf16[1,1024,256]{2,1,0:T(8,128)(2,1)S(1)} %copy-done.1, s32[]{:T(128)S(6)} %select_n.106), kind=kLoop, calls=%fused_computation.67 | loop fusion | flops 393216 | bytes 1311748 | tf_op jit(solution)/shard_map/broadcast_in_dim | solution.py:61
  96.6 18.7 %all-reduce.2.cloned.1.call-done = f32[256,256]{0,1:T(8,128)} async-done(((f32[256,256]{0,1:T(8,128)}), f32[256,256]{0,1:T(8,128)}) %all-reduce.2.cloned.1.call-update) | async-done | bytes 262160 | tf_op jit(solution)/shard_map/psum | solution.py:54
  115.4 1.0 fusion.45
  116.4 0.8 copy.9
  (34 shorter events, 3.5 us)
Async XLA Ops:
  7.2 72.1 %reduce-scatter.5.cloned.1.call-start = ((), (), s32[]{:S(2)}) async-start(), calls=%async_computation.3 | async-start | bytes 1310720 | tf_op jit(solution)/shard_map/reduce_scatter | solution.py:53
  13.8 0.7 copy-start.3
  37.7 1.6 %copy-start.1 = (bf16[1,1024,256]{2,1,0:T(8,128)(2,1)S(1)}, bf16[1,1024,256]{2,1,0:T(8,128)(2,1)}, u32[]{:S(2)}) copy-start(bf16[1,1024,256]{2,1,0:T(8,128)(2,1)} %param.8) | copy-start | bytes 1572868
  43.0 1.0 copy-start
  44.0 50.7 %reduce-scatter.3.cloned.1.call-start = ((), (), s32[]{:S(2)}) async-start(), calls=%async_computation.2 | async-start | bytes 1572864 | tf_op jit(solution)/shard_map/reduce_scatter | solution.py:59
  47.0 0.9 copy-start.2
  47.1 68.3 %all-reduce.2.cloned.1.call-start = ((), (), s32[]{:S(2)}) async-start(), calls=%async_computation.4 | async-start | bytes 524288 | tf_op jit(solution)/shard_map/psum | solution.py:54
Sparse Core Ops, SparseCore 0:
  44.2 29.1 reduce-scatter.4
  75.7 18.9 reduce-scatter.2
  97.1 18.2 all-reduce.1
where the time goes:
time: 124 us
  blocking collectives  48.5 us (39%)
  waiting for transfers between devices  34.2 us (28%)
  between operations  24.2 us (20%)
  local copies, waits for them, and re-layouts  7.19 us (6%)
  matrix products  5.34 us (4%)
  other arithmetic  4.15 us (3%)
    psum x1, blocking collectives, body(): sums = lax.psum(sums, ('row', 'col', 'sub'))  30.9 us
    psum x1, waiting for transfers between devices, body(): numer_h = lax.psum(numer_h, 'sub')  18.7 us
    all_gather x1, blocking collectives, body(): h_all = lax.all_gather(h_factor, 'row', axis=1, tiled=True)  17.6 us
    reduce_scatter x1, waiting for transfers between devices, body(): mine = lax.psum_scatter(numer_w, 'col', scatter_dimension=0, tiled=True)  15.4 us
    unnamed x11, local copies, waits for them, and re-layouts  5 us
  transfers between devices with their start and end apart: 3, of which 2 were waited for; matrix products, arithmetic and copies ran while one was open for 4% of the time, Pallas kernels for 0%

commit v1 on v0

v1 whole, which is shorter than its diff:
```python
import jax
import jax.numpy as jnp
from jax import lax
from jax.sharding import PartitionSpec as P


def shifted(value, axis, by):
    length = lax.axis_size(axis)
    return lax.ppermute(value, axis, [(i, (i + by) % length) for i in range(length)])


def as_rows(vector, width):
    size = vector.shape[0]
    rows = -(-size // width)
    flat = jnp.pad(vector, (0, rows * width - size)).reshape(rows, width)
    return jnp.pad(flat, ((0, (-rows) % 8), (0, 0)))


def from_rows(rows, size):
    return rows.reshape(-1)[:size]


def body(a_blocks, block_list, block_count, w_factor, h_factor):
    values = a_blocks[0, 0]
    lists = block_list[0, 0]
    counts = block_count[0, 0]
    w_tile = w_factor[0]
    row_blocks, stored, width = values.shape[0], values.shape[1], values.shape[2]
    rank = w_tile.shape[1]
    tile_rows = w_tile.shape[0]
    n_row = lax.axis_size("row")
    n_col = lax.axis_size("col")
    n_sub = lax.axis_size("sub")
    row_index = lax.axis_index("row")
    col_index = lax.axis_index("col")
    w_rows = w_tile.reshape(row_blocks, width, rank)

    h_stack = jnp.stack([h_factor] + [shifted(h_factor, "row", d) for d in range(1, n_row)])
    h_sum = jnp.sum(h_stack.astype(jnp.float32), axis=(0, 2))
    w_sum = jnp.sum(w_tile.astype(jnp.float32), axis=0)

    numer_h_stack = jnp.zeros((n_row, rank, width), jnp.float32)
    parts_w = []
    for brow in range(row_blocks):
        part_w = jnp.zeros((width, rank), jnp.float32)
        for slot in range(stored):
            target = lists[brow, slot]
            live = slot < counts[brow]
            h_block = lax.dynamic_index_in_dim(
                h_stack, (row_index - target) % n_row, 0, keepdims=False
            )
            product = jnp.dot(w_rows[brow], h_block, preferred_element_type=jnp.float32)
            ratios = (values[brow, slot].astype(jnp.float32) / product).astype(jnp.bfloat16)
            ratios = jnp.where(live, ratios, jnp.zeros_like(ratios))
            part_h = jnp.einsum(
                "ik,ij->kj", w_rows[brow], ratios, preferred_element_type=jnp.float32
            )
            part_w = part_w + jnp.einsum(
                "ij,kj->ik", ratios, h_block, preferred_element_type=jnp.float32
            )
            offset = (target - row_index) % n_row
            old = lax.dynamic_index_in_dim(numer_h_stack, offset, 0, keepdims=True)
            numer_h_stack = lax.dynamic_update_index_in_dim(
                numer_h_stack, old + part_h[None], offset, 0
            )
        parts_w.append(part_w)
    numer_w = jnp.stack(parts_w).reshape(tile_rows, rank)

    share = tile_rows // n_col
    chunks = numer_w.reshape(n_col, share, rank)
    h_rows = as_rows(h_sum, rank)
    mine_w = lax.dynamic_index_in_dim(chunks, col_index, 0, keepdims=False)
    got_h = h_rows
    for d in range(1, n_col):
        chunk = lax.dynamic_index_in_dim(chunks, (col_index + d) % n_col, 0, keepdims=False)
        message = shifted(jnp.concatenate([chunk, h_rows]), "col", d)
        mine_w = mine_w + message[:share]
        got_h = got_h + message[share:]
    h_total = from_rows(got_h, rank)

    w_rows_sum = as_rows(w_sum, width)
    mine_h = numer_h_stack[0]
    got_w = w_rows_sum
    for d in range(1, n_row):
        message = shifted(jnp.concatenate([numer_h_stack[d], w_rows_sum]), "row", d)
        mine_h = mine_h + message[:rank]
        got_w = got_w + message[rank:]
    both = jnp.concatenate([mine_h, got_w])
    total = both
    for d in range(1, n_sub):
        total = total + shifted(both, "sub", d)
    numer_h = total[:rank]
    w_total = from_rows(total[rank:], rank)

    h_new = h_factor.astype(jnp.float32) * numer_h / w_total[:, None]
    w_part = lax.dynamic_slice_in_dim(w_tile, col_index * share, share, 0).astype(jnp.float32)
    w_new = (w_part * mine_w / h_total[None, :])[None]
    return (w_new, h_new)


def solution(mesh):
    placed = (
        P(("grp", "row", "sub"), "col", None, None, None, None),
        P(("grp", "row", "sub"), "col", None, None),
        P(("grp", "row", "sub"), "col", None),
        P(("grp", "row", "sub"), None, None),
        P(None, ("grp", "row", "col")),
    )
    return jax.shard_map(
        body,
        mesh=mesh,
        in_specs=placed,
        out_specs=(P(("grp", "row", "sub"), "col", None), P(None, ("grp", "row", "col"))),
        check_vma=False,
    )
```

time: 124 us -> 62.5 us (0.50)
  blocking collectives: 48.5 us -> 0 us
  waiting for transfers between devices: 34.2 us -> 19.1 us
  starting transfers between devices: 0.12 us -> 13.4 us
  between operations: 24.2 us -> 16.6 us
  local copies, waits for them, and re-layouts: 7.19 us -> 5.06 us
  other arithmetic: 4.15 us -> 2.33 us
    psum x1 -> x0, blocking collectives: 30.9 us -> none  [body(): sums = lax.psum(sums, ('row', 'col', 'sub'))]
    ppermute x0 -> x8, waiting for transfers between devices: none -> 19.1 us  [shifted(): lax.ppermute(value, axis, [(i, (i + by) % length) for i in range(length)])]
    psum x1 -> x0, waiting for transfers between devices: 18.7 us -> none  [body(): numer_h = lax.psum(numer_h, 'sub')]
    all_gather x1 -> x0, blocking collectives: 17.6 us -> none  [body(): h_all = lax.all_gather(h_factor, 'row', axis=1, tiled=True)]
    reduce_scatter x2 -> x0, waiting for transfers between devices: 15.5 us -> none  [the longest x1 15.4 us: body(): mine = lax.psum_scatter(numer_w, 'col', scatter_dimension=0, tiled=True)]
    ppermute x0 -> x8, starting transfers between devices: none -> 13.4 us  [shifted(): lax.ppermute(value, axis, [(i, (i + by) % length) for i in range(length)])]
    unnamed x11 -> x9, local copies, waits for them, and re-layouts: 5 us -> 3.57 us
  transfers between devices with their start and end apart: 3 -> 8, of which waited for: 2 -> 4; matrix products, arithmetic and copies ran while one was open for 4% -> 7% of each run, Pallas kernels for 0% -> 0%
where the time goes in v1:
time: 62.5 us; the launch traced here: 62.1 us
  waiting for transfers between devices  19.1 us (31%)
  between operations  16.6 us (27%)
  starting transfers between devices  13.4 us (21%)
  matrix products  5.6 us (9%)
  local copies, waits for them, and re-layouts  5.06 us (8%)
  other arithmetic  2.33 us (4%)
    ppermute x8, waiting for transfers between devices, shifted(): lax.ppermute(value, axis, [(i, (i + by) % length) for i in range(length)])  19.1 us
    ppermute x8, starting transfers between devices, shifted(): lax.ppermute(value, axis, [(i, (i + by) % length) for i in range(length)])  13.4 us
    unnamed x9, local copies, waits for them, and re-layouts  3.57 us
    dot_general x8, matrix products, body(): product = jnp.dot(w_rows[brow], h_block, preferred_element_type=jnp.float32)  1.94 us
    dot_general x8, matrix products, body(): jnp.einsum('ik,ij->kj', w_rows[brow], ratios, preferred_element_type=jnp....  1.85 us
    dot_general x8, matrix products, body(): jnp.einsum('ij,kj->ik', ratios, h_block, preferred_element_type=jnp.float32)  1.8 us
  transfers between devices with their start and end apart: 8, of which 4 were waited for; matrix products, arithmetic and copies ran while one was open for 7% of the time, Pallas kernels for 0%

profile of v1, /device:TPU:0, one launch (start us, length us, event | category | flops | bytes accessed | tf_op | source)
XLA Modules:
  0.0 62.1 jit_solution(13386405862268787143)
XLA Ops:
  0.6 4.1 %collective-permute-start.1 = (bf16[256,256]{1,0:T(8,128)(2,1)}, bf16[256,256]{1,0:T(8,128)(2,1)S(1)}, u32[]{:S(2)}, u32[]{:S(2)}) collective-permute-start(bf16[256,256]{1,0:T(8,128)(2,1)} %param.9), channel_id=1, source_target_pairs={{0,8},{4,12},{8,0},{12,4},{1,9},{5,13},{9,1},{13,5},{2,10},{6,14},... | collective-permute-start | bytes 393224 | tf_op jit(solution)/shard_map/ppermute | solution.py:9
  4.7 1.6 %collective-permute-start = (bf16[256,256]{1,0:T(8,128)(2,1)}, bf16[256,256]{1,0:T(8,128)(2,1)S(1)}, u32[]{:S(2)}, u32[]{:S(2)}) collective-permute-start(bf16[256,256]{1,0:T(8,128)(2,1)} %param.9), channel_id=1, source_target_pairs={{0,4},{4,8},{8,12},{12,0},{1,5},{5,9},{9,13},{13,1},{2,6},{6,10},{... | collective-permute-start | bytes 393224 | tf_op jit(solution)/shard_map/ppermute | solution.py:9
  6.3 2.2 %collective-permute-start.2 = (bf16[256,256]{1,0:T(8,128)(2,1)}, bf16[256,256]{1,0:T(8,128)(2,1)S(1)}, u32[]{:S(2)}, u32[]{:S(2)}) collective-permute-start(bf16[256,256]{1,0:T(8,128)(2,1)} %param.9), channel_id=1, source_target_pairs={{0,12},{4,0},{8,4},{12,8},{1,13},{5,1},{9,5},{13,9},{2,14},{6,2},{... | collective-permute-start | bytes 393224 | tf_op jit(solution)/shard_map/ppermute | solution.py:9
  8.6 0.7 %copy-done.3 = s32[1,1,4]{2,1,0:T(1,128)S(1)} copy-done((s32[1,1,4]{2,1,0:T(1,128)S(1)}, s32[1,1,4]{2,1,0:T(1,128)}, u32[]{:S(2)}) %copy-start.3) | copy-done | bytes 40
  9.2 0.6 %fusion.133 = (s32[1,1,1]{2,1,0:T(1,128)}, s32[1,1,1]{2,1,0:T(1,128)}, s32[1,1,1]{2,1,0:T(1,128)}, s32[1,1,1]{2,1,0:T(1,128)}) fusion(s32[1,1,4]{2,1,0:T(1,128)S(1)} %copy-done.3), kind=kLoop, calls=%fused_computation.184 | loop fusion | bytes 32 | tf_op jit(solution)/shard_map/slice | solution.py:48
  15.0 0.7 %copy-done.2 = s32[1,1,4,2]{2,3,1,0:T(2,128)S(1)} copy-done((s32[1,1,4,2]{2,3,1,0:T(2,128)S(1)}, s32[1,1,4,2]{2,3,1,0:T(2,128)}, u32[]{:S(2)}) %copy-start.2) | copy-done | bytes 56
  15.7 0.7 %fusion.132 = (s32[1,1]{0,1:T(1,128)}, s32[1,1]{0,1:T(1,128)}, s32[1,1]{0,1:T(1,128)}, s32[1,1]{0,1:T(1,128)}, s32[1,1]{0,1:T(1,128)}, /*index=5*/s32[1,1]{0,1:T(1,128)}, s32[1,1]{0,1:T(1,128)}, s32[1,1]{0,1:T(1,128)}) fusion(s32[4,2]{0,1:T(2,128)S(1)} %bitcast.326), kind=kLoop, calls=%fused_computation.183 | loop fusion | bytes 64 | tf_op jit(solution)/shard_map/slice | solution.py:47
  26.7 1.5 %copy.7 = bf16[1,1,4,2,256,256]{4,5,3,2,1,0:T(8,128)(2,1)S(1)} copy(bf16[1,1,4,2,256,256]{5,4,3,2,1,0:T(8,128)(2,1)} %param.5) | data formatting | bytes 2097152 | tf_op args[0]
  28.6 0.7 %copy-done.1 = bf16[256,256]{1,0:T(8,128)(2,1)S(1)} copy-done((bf16[256,256]{1,0:T(8,128)(2,1)S(1)}, bf16[256,256]{1,0:T(8,128)(2,1)}, u32[]{:S(2)}) %copy-start.1) | copy-done | bytes 131096
  29.4 0.2 fusion.42
  29.9 0.2 fusion.40
  30.4 0.2 fusion.38
  30.9 0.2 fusion.36
  31.6 0.2 fusion.37
  31.9 0.2 fusion.39
  32.1 0.2 fusion.41
  35.5 3.8 %collective-permute-start.6 = (f32[264,256]{1,0:T(8,128)S(1)}, f32[264,256]{1,0:T(8,128)S(1)}, u32[]{:S(2)}, u32[]{:S(2)}) collective-permute-start(f32[264,256]{1,0:T(8,128)S(1)} %get-tuple-element.8), channel_id=1, source_target_pairs={{0,12},{4,0},{8,4},{12,8},{1,13},{5,1},{9,5},{13,9},{2,14},{6,2},{... | collective-permute-start | bytes 811016 | tf_op jit(solution)/shard_map/ppermute | solution.py:9
  39.5 1.6 %collective-permute-start.3 = (f32[520,256]{1,0:T(8,128)S(1)}, f32[520,256]{1,0:T(8,128)S(1)}, u32[]{:S(2)}, u32[]{:S(2)}) collective-permute-start(f32[520,256]{1,0:T(8,128)S(1)} %pad_maximum_fusion.1), channel_id=1, source_target_pairs={{0,2},{2,0},{1,3},{3,1},{4,6},{6,4},{5,7},{7,5},{8,10},{10,8},{9,1... | collective-permute-start | bytes 1597448 | tf_op jit(solution)/shard_map/ppermute | solution.py:9
  41.1 5.6 %collective-permute-done.4 = f32[264,256]{1,0:T(8,128)S(1)} collective-permute-done((f32[264,256]{1,0:T(8,128)S(1)}, f32[264,256]{1,0:T(8,128)S(1)}, u32[]{:S(2)}, u32[]{:S(2)}) %collective-permute-start.4) | collective-permute-done | bytes 270368 | tf_op jit(solution)/shard_map/ppermute | solution.py:9
  46.7 3.8 %collective-permute-done.6 = f32[264,256]{1,0:T(8,128)S(1)} collective-permute-done((f32[264,256]{1,0:T(8,128)S(1)}, f32[264,256]{1,0:T(8,128)S(1)}, u32[]{:S(2)}, u32[]{:S(2)}) %collective-permute-start.6) | collective-permute-done | bytes 270368 | tf_op jit(solution)/shard_map/ppermute | solution.py:9
  50.5 9.0 %collective-permute-done.5 = f32[264,256]{1,0:T(8,128)S(1)} collective-permute-done((f32[264,256]{1,0:T(8,128)S(1)}, f32[264,256]{1,0:T(8,128)S(1)}, u32[]{:S(2)}, u32[]{:S(2)}) %collective-permute-start.5) | collective-permute-done | bytes 270368 | tf_op jit(solution)/shard_map/ppermute | solution.py:9
  59.8 0.9 %fusion.45 = f32[1,512,256]{2,1,0:T(8,128)} fusion(f32[520,256]{1,0:T(8,128)S(1)} %collective-permute-done.3, f32[2,512,256]{2,1,0:T(8,128)S(1)} %bitcast.313, s32[]{:T(128)S(6)} %select_n.223, f32[256]{0:T(256)S(1)} %bitcast.331, bf16[1,1024,256]{2,1,0:T(8,128)(2,1)S(1)} %copy-done, s32[]{:T(128)S(6)} %select_n.190), kind=kLoop, calls=%fused_computation.70 | loop fusion | flops 524288 | bytes 1836040 | tf_op jit(solution)/shard_map/broadcast_in_dim | solution.py:97
  60.6 0.6 collective-permute-done.7
  61.3 0.8 %fusion.46 = f32[256,256]{1,0:T(8,128)} fusion(f32[264,256]{1,0:T(8,128)S(1)} %fusion.131, bf16[256,256]{1,0:T(8,128)(2,1)S(1)} %copy-done.1, f32[256]{0:T(256)S(1)} %bitcast.332), kind=kLoop, calls=%fused_computation.78 | loop fusion | flops 196608 | bytes 656384 | tf_op jit(solution)/shard_map/div | solution.py:95
  (46 shorter events, 4.9 us)
Async XLA Ops:
  0.6 27.9 %collective-permute-start.1 = (bf16[256,256]{1,0:T(8,128)(2,1)}, bf16[256,256]{1,0:T(8,128)(2,1)S(1)}, u32[]{:S(2)}, u32[]{:S(2)}) collective-permute-start(bf16[256,256]{1,0:T(8,128)(2,1)} %param.9), channel_id=1, source_target_pairs={{0,8},{4,12},{8,0},{12,4},{1,9},{5,13},{9,1},{13,5},{2,10},{6,14},... | collective-permute-start | bytes 393224 | tf_op jit(solution)/shard_map/ppermute | solution.py:9
  4.7 23.8 %collective-permute-start = (bf16[256,256]{1,0:T(8,128)(2,1)}, bf16[256,256]{1,0:T(8,128)(2,1)S(1)}, u32[]{:S(2)}, u32[]{:S(2)}) collective-permute-start(bf16[256,256]{1,0:T(8,128)(2,1)} %param.9), channel_id=1, source_target_pairs={{0,4},{4,8},{8,12},{12,0},{1,5},{5,9},{9,13},{13,1},{2,6},{6,10},{... | collective-permute-start | bytes 393224 | tf_op jit(solution)/shard_map/ppermute | solution.py:9
  6.3 22.3 %collective-permute-start.2 = (bf16[256,256]{1,0:T(8,128)(2,1)}, bf16[256,256]{1,0:T(8,128)(2,1)S(1)}, u32[]{:S(2)}, u32[]{:S(2)}) collective-permute-start(bf16[256,256]{1,0:T(8,128)(2,1)} %param.9), channel_id=1, source_target_pairs={{0,12},{4,0},{8,4},{12,8},{1,13},{5,1},{9,5},{13,9},{2,14},{6,2},{... | collective-permute-start | bytes 393224 | tf_op jit(solution)/shard_map/ppermute | solution.py:9
  8.6 0.7 %copy-start.3 = (s32[1,1,4]{2,1,0:T(1,128)S(1)}, s32[1,1,4]{2,1,0:T(1,128)}, u32[]{:S(2)}) copy-start(s32[1,1,4]{2,1,0:T(1,128)} %param.7) | copy-start | bytes 52
  15.0 0.7 %copy-start.2 = (s32[1,1,4,2]{2,3,1,0:T(2,128)S(1)}, s32[1,1,4,2]{2,3,1,0:T(2,128)}, u32[]{:S(2)}) copy-start(s32[1,1,4,2]{2,3,1,0:T(2,128)} %param.6) | copy-start | bytes 100
  26.7 1.7 %copy-start = (bf16[1,1024,256]{2,1,0:T(8,128)(2,1)S(1)}, bf16[1,1024,256]{2,1,0:T(8,128)(2,1)}, u32[]{:S(2)}) copy-start(bf16[1,1024,256]{2,1,0:T(8,128)(2,1)} %param.8) | copy-start | bytes 1572868
  28.4 0.9 %copy-start.1 = (bf16[256,256]{1,0:T(8,128)(2,1)S(1)}, bf16[256,256]{1,0:T(8,128)(2,1)}, u32[]{:S(2)}) copy-start(bf16[256,256]{1,0:T(8,128)(2,1)} %param.9) | copy-start | bytes 393220
  35.4 11.3 %collective-permute-start.4 = (f32[264,256]{1,0:T(8,128)S(1)}, f32[264,256]{1,0:T(8,128)S(1)}, u32[]{:S(2)}, u32[]{:S(2)}) collective-permute-start(f32[264,256]{1,0:T(8,128)S(1)} %get-tuple-element.7), channel_id=1, source_target_pairs={{0,4},{4,8},{8,12},{12,0},{1,5},{5,9},{9,13},{13,1},{2,6},{6,10},{... | collective-permute-start | bytes 811016 | tf_op jit(solution)/shard_map/ppermute | solution.py:9
  35.5 15.0 %collective-permute-start.6 = (f32[264,256]{1,0:T(8,128)S(1)}, f32[264,256]{1,0:T(8,128)S(1)}, u32[]{:S(2)}, u32[]{:S(2)}) collective-permute-start(f32[264,256]{1,0:T(8,128)S(1)} %get-tuple-element.8), channel_id=1, source_target_pairs={{0,12},{4,0},{8,4},{12,8},{1,13},{5,1},{9,5},{13,9},{2,14},{6,2},{... | collective-permute-start | bytes 811016 | tf_op jit(solution)/shard_map/ppermute | solution.py:9
  39.3 20.2 %collective-permute-start.5 = (f32[264,256]{1,0:T(8,128)S(1)}, f32[264,256]{1,0:T(8,128)S(1)}, u32[]{:S(2)}, u32[]{:S(2)}) collective-permute-start(f32[264,256]{1,0:T(8,128)S(1)} %get-tuple-element.9), channel_id=1, source_target_pairs={{0,8},{4,12},{8,0},{12,4},{1,9},{5,13},{9,1},{13,5},{2,10},{6,14},... | collective-permute-start | bytes 811016 | tf_op jit(solution)/shard_map/ppermute | solution.py:9
  39.5 20.2 %collective-permute-start.3 = (f32[520,256]{1,0:T(8,128)S(1)}, f32[520,256]{1,0:T(8,128)S(1)}, u32[]{:S(2)}, u32[]{:S(2)}) collective-permute-start(f32[520,256]{1,0:T(8,128)S(1)} %pad_maximum_fusion.1), channel_id=1, source_target_pairs={{0,2},{2,0},{1,3},{3,1},{4,6},{6,4},{5,7},{7,5},{8,10},{10,8},{9,1... | collective-permute-start | bytes 1597448 | tf_op jit(solution)/shard_map/ppermute | solution.py:9
  59.6 1.6 %collective-permute-start.7 = (f32[264,256]{1,0:T(8,128)S(1)}, f32[264,256]{1,0:T(8,128)S(1)}, u32[]{:S(2)}, u32[]{:S(2)}) collective-permute-start(f32[264,256]{1,0:T(8,128)S(1)} %pad_maximum_fusion.6), channel_id=1, source_target_pairs={{0,1},{1,0},{2,3},{3,2},{4,5},{5,4},{6,7},{7,6},{8,9},{9,8},{10,11... | collective-permute-start | bytes 811016 | tf_op jit(solution)/shard_map/ppermute | solution.py:9

commit v2 on v1

--- a/solution.py
+++ b/solution.py
@@ -20,25 +20,35 @@
     return rows.reshape(-1)[:size]
 
 
-def body(a_blocks, block_list, block_count, w_factor, h_factor):
-    values = a_blocks[0, 0]
-    lists = block_list[0, 0]
-    counts = block_count[0, 0]
-    w_tile = w_factor[0]
+def dense_terms(values, lists, counts, w_tile, h_stack, row_index):
     row_blocks, stored, width = values.shape[0], values.shape[1], values.shape[2]
-    rank = w_tile.shape[1]
+    n_row, rank = h_stack.shape[0], h_stack.shape[1]
     tile_rows = w_tile.shape[0]
-    n_row = lax.axis_size("row")
-    n_col = lax.axis_size("col")
-    n_sub = lax.axis_size("sub")
-    row_index = lax.axis_index("row")
-    col_index = lax.axis_index("col")
+    h_all = jnp.concatenate([h_stack[d] for d in range(n_row)], axis=1)
+    block_of = (row_index - lax.iota(jnp.int32, n_row)) % n_row
+    live = lax.iota(jnp.int32, stored)[None, :] < counts[:, None]
+    mask = (lists[:, :, None] == block_of[None, None, :]) & live[:, :, None]
+    a_dense = jnp.zeros((row_blocks, width, n_row, width), values.dtype)
+    for slot in range(stored):
+        a_dense = jnp.where(
+            mask[:, slot, None, :, None], values[:, slot, :, None, :], a_dense
+        )
+    covered = jnp.any(mask, axis=1)[:, None, :, None]
+    product = jnp.dot(w_tile, h_all, preferred_element_type=jnp.float32)
+    product = product.reshape(row_blocks, width, n_row, width)
+    ratios = jnp.where(covered, a_dense.astype(jnp.float32) / product, 0.0).astype(jnp.bfloat16)
+    ratios = ratios.reshape(tile_rows, n_row * width)
+    numer_h_all = jnp.einsum("ik,ij->kj", w_tile, ratios, preferred_element_type=jnp.float32)
+    numer_w = jnp.einsum("ij,kj->ik", ratios, h_all, preferred_element_type=jnp.float32)
+    numer_h_chunks = numer_h_all.reshape(rank, n_row, width)
+    return [numer_h_chunks[:, (-e) % n_row] for e in range(n_row)], numer_w
+
+
+def slot_terms(values, lists, counts, w_tile, h_stack, row_index):
+    row_blocks, stored, width = values.shape[0], values.shape[1], values.shape[2]
+    n_row, rank = h_stack.shape[0], h_stack.shape[1]
+    tile_rows = w_tile.shape[0]
     w_rows = w_tile.reshape(row_blocks, width, rank)
-
-    h_stack = jnp.stack([h_factor] + [shifted(h_factor, "row", d) for d in range(1, n_row)])
-    h_sum = jnp.sum(h_stack.astype(jnp.float32), axis=(0, 2))
-    w_sum = jnp.sum(w_tile.astype(jnp.float32), axis=0)
-
     numer_h_stack = jnp.zeros((n_row, rank, width), jnp.float32)
     parts_w = []
     for brow in range(row_blocks):
@@ -65,6 +75,31 @@
             )
         parts_w.append(part_w)
     numer_w = jnp.stack(parts_w).reshape(tile_rows, rank)
+    return [numer_h_stack[e] for e in range(n_row)], numer_w
+
+
+def body(a_blocks, block_list, block_count, w_factor, h_factor):
+    values = a_blocks[0, 0]
+    lists = block_list[0, 0]
+    counts = block_count[0, 0]
+    w_tile = w_factor[0]
+    row_blocks, stored, width = values.shape[0], values.shape[1], values.shape[2]
+    rank = w_tile.shape[1]
+    tile_rows = w_tile.shape[0]
+    n_row = lax.axis_size("row")
+    n_col = lax.axis_size("col")
+    n_sub = lax.axis_size("sub")
+    row_index = lax.axis_index("row")
+    col_index = lax.axis_index("col")
+
+    h_stack = jnp.stack([h_factor] + [shifted(h_factor, "row", d) for d in range(1, n_row)])
+    h_sum = jnp.sum(h_stack.astype(jnp.float32), axis=(0, 2))
+    w_sum = jnp.sum(w_tile.astype(jnp.float32), axis=0)
+
+    if tile_rows * n_row * width * 4 <= (8 << 20):
+        numer_h_stack, numer_w = dense_terms(values, lists, counts, w_tile, h_stack, row_index)
+    else:
+        numer_h_stack, numer_w = slot_terms(values, lists, counts, w_tile, h_stack, row_index)
 
     share = tile_rows // n_col
     chunks = numer_w.reshape(n_col, share, rank)

time: 62.5 us -> 56.1 us (0.90)
  the two profiles are of different devices: /device:TPU:0 before, /device:TPU:11 now
where the time goes in v2:
time: 56.1 us; the launch traced here: 55.8 us
  waiting for transfers between devices  21.3 us (38%)
  local copies, waits for them, and re-layouts  9.9 us (18%)
  other arithmetic  9.24 us (16%)
  starting transfers between devices  8.43 us (15%)
  matrix products  5.97 us (11%)
  between operations  0.93 us (2%)
    ppermute x8, waiting for transfers between devices, shifted(): lax.ppermute(value, axis, [(i, (i + by) % length) for i in range(length)])  21.3 us
    ppermute x8, starting transfers between devices, shifted(): lax.ppermute(value, axis, [(i, (i + by) % length) for i in range(length)])  8.43 us
    unnamed x29, local copies, waits for them, and re-layouts  7.87 us
    dot_general x1, matrix products, dense_terms(): product = jnp.dot(w_tile, h_all, preferred_element_type=jnp.float32)  3.45 us
    convert_element_type x1, other arithmetic, dense_terms(): a_dense.astype(jnp.float32) / product  2.88 us
    dot_general x1, matrix products, dense_terms(): jnp.einsum('ij,kj->ik', ratios, h_all, preferred_element_type=jnp.float32)  1.78 us
    broadcast_in_dim x2, local copies, waits for them, and re-layouts, dense_terms(): jnp.where(mask[:, slot, None, :, None], values[:, slot, :, None, :], a_de...  1.28 us
    add x1, other arithmetic, body(): mine_h = mine_h + message[:rank]  1.17 us
  transfers between devices with their start and end apart: 8, of which 4 were waited for; matrix products, arithmetic and copies ran while one was open for 32% of the time, Pallas kernels for 0%

profile of v2, /device:TPU:11, one launch (start us, length us, event | category | flops | bytes accessed | tf_op | source)
XLA Modules:
  0.0 55.8 jit_solution(8571899264193049006)
XLA Ops:
  0.6 1.3 %collective-permute-start = (bf16[256,256]{1,0:T(8,128)(2,1)}, bf16[256,256]{1,0:T(8,128)(2,1)S(1)}, u32[]{:S(2)}, u32[]{:S(2)}) collective-permute-start(bf16[256,256]{1,0:T(8,128)(2,1)} %param.9), channel_id=1, source_target_pairs={{0,4},{4,8},{8,12},{12,0},{1,5},{5,9},{9,13},{13,1},{2,6},{6,10},{... | collective-permute-start | bytes 393224 | tf_op jit(solution)/shard_map/ppermute | solution.py:9
  2.0 1.1 %collective-permute-start.1 = (bf16[256,256]{1,0:T(8,128)(2,1)}, bf16[256,256]{1,0:T(8,128)(2,1)S(1)}, u32[]{:S(2)}, u32[]{:S(2)}) collective-permute-start(bf16[256,256]{1,0:T(8,128)(2,1)} %param.9), channel_id=1, source_target_pairs={{0,8},{4,12},{8,0},{12,4},{1,9},{5,13},{9,1},{13,5},{2,10},{6,14},... | collective-permute-start | bytes 393224 | tf_op jit(solution)/shard_map/ppermute | solution.py:9
  3.1 1.4 %collective-permute-start.2 = (bf16[256,256]{1,0:T(8,128)(2,1)}, bf16[256,256]{1,0:T(8,128)(2,1)S(1)}, u32[]{:S(2)}, u32[]{:S(2)}) collective-permute-start(bf16[256,256]{1,0:T(8,128)(2,1)} %param.9), channel_id=1, source_target_pairs={{0,12},{4,0},{8,4},{12,8},{1,13},{5,1},{9,5},{13,9},{2,14},{6,2},{... | collective-permute-start | bytes 393224 | tf_op jit(solution)/shard_map/ppermute | solution.py:9
  4.5 0.7 %iota_compare_fusion = pred[4,2]{0,1:T(4,128)(4,1)S(1)} fusion(s32[4]{0:T(128)} %bitcast.82), kind=kLoop, calls=%fused_computation.42 | loop fusion | flops 8 | bytes 24 | tf_op jit(solution)/shard_map/lt | solution.py:29
  5.1 0.8 %fusion.13 = (pred[4,4]{1,0:T(4,128)(4,1)S(1)}, pred[4,2,4]{2,0,1:T(4,128)(4,1)S(1)}) fusion(pred[4,2]{0,1:T(4,128)(4,1)S(1)} %iota_compare_fusion, s32[4]{0:T(128)S(1)} %and_select_fusion, s32[4,2]{0,1:T(2,128)} %bitcast.81), kind=kLoop, calls=%fused_computation.45 | loop fusion | flops 80 | bytes 104 | tf_op jit(solution)/shard_map/reduce_or | solution.py:36
  5.9 1.3 %slice_bitcast_fusion.1 = (bf16[4,256,256]{2,1,0:T(8,128)(2,1)S(1)}, bf16[4,256,256]{2,1,0:T(8,128)(2,1)S(1)}) fusion(bf16[4,2,256,256]{3,2,1,0:T(8,128)(2,1)} %bitcast.69), kind=kLoop, calls=%fused_computation.12 | loop fusion | bytes 2097152 | tf_op jit(solution)/shard_map/jit(_where)/broadcast_in_dim | solution.py:33
  7.2 2.9 %select_convert_fusion = f32[4,256,4,256]{3,2,1,0:T(4,128)} fusion(pred[4,4]{1,0:T(4,128)(4,1)S(1)} %get-tuple-element.14, pred[4,4]{1,0:T(4,128)(4,1)S(1)} %get-tuple-element.13, bf16[4,256,256]{2,1,0:T(8,128)(2,1)S(1)} %get-tuple-element.9, bf16[4,256,256]{2,1,0:T(8,128)(2,1)S(1)} %get-tuple-element.8), kind=kLoop, calls=%fused_computation.3 | loop fusion | flops 3145728 | bytes 5242912 | tf_op jit(solution)/shard_map/convert_element_type | solution.py:39
  10.3 5.1 %copy.16 = f32[128,8,4,256]{3,1,2,0:T(8,128)} copy(f32[128,8,4,256]{3,2,1,0:T(4,128)} %bitcast.61) | data formatting | bytes 8388608
  15.4 0.6 %broadcast_in_dim.60 = pred[4,256,4,256]{3,2,1,0:T(4,128)(4,1)S(1)} broadcast(pred[4,4]{1,0:T(4,128)(4,1)S(1)} %get-tuple-element.2), dimensions={0,2} | broadcast | bytes 1048592 | tf_op jit(solution)/shard_map/jit(_where)/broadcast_in_dim | solution.py:39
  16.0 1.5 %copy.15 = pred[128,8,4,256]{3,1,2,0:T(8,128)(4,1)} copy(pred[128,8,4,256]{3,2,1,0:T(4,128)(4,1)S(1)} %bitcast.63) | data formatting | bytes 2097152
  17.7 0.6 %copy-done.8 = bf16[256,256]{1,0:T(8,128)(2,1)} copy-done((bf16[256,256]{1,0:T(8,128)(2,1)}, bf16[256,256]{1,0:T(8,128)(2,1)S(1)}, u32[]{:S(2)}) %copy-start.8) | copy-done | bytes 131096
  18.3 3.5 %fusion.1 = bf16[1024,1024]{1,0:T(8,128)(2,1)S(1)} fusion(pred[1024,1024]{1,0:T(8,128)(4,1)} %bitcast.70, f32[1024,1024]{1,0:T(8,128)} %bitcast.62, bf16[256,1024]{1,0:T(8,128)(2,1)S(1)} %constant_dynamic-update-slice_fusion, bf16[1,1024,256]{2,1,0:T(8,128)(2,1)S(1)} %copy-done.1), kind=kOutput, calls=%fused_computation.2 | convolution fusion | flops 540016640 | bytes 8388608 | tf_op jit(solution)/shard_map/dot_general | solution.py:37
  21.8 0.7 %fusion.7 = f32[1024,256]{1,0:T(8,128)S(1)} fusion(bf16[1024,1024]{1,0:T(8,128)(2,1)S(1)} %fusion.1, bf16[1,1024,256]{2,1,0:T(8,128)(2,1)S(1)} %copy-done.1), kind=kOutput, calls=%fused_computation.15 | convolution fusion | flops 536870912 | bytes 3670016 | tf_op jit(solution)/shard_map/ik,ij->kj/dot_general | solution.py:41
  23.0 0.9 %pad_maximum_fusion.3 = (f32[264,256]{1,0:T(8,128)}, f32[264,256]{1,0:T(8,128)}, f32[264,256]{1,0:T(8,128)}) fusion(f32[8,256]{1,0:T(8,128)S(1)} %pad.8, f32[256,256]{1,0:T(8,128)S(1)} %bitcast.66, f32[256,256]{1,0:T(8,128)S(1)} %bitcast.68, f32[256,256]{1,0:T(8,128)S(1)} %bitcast.67), kind=kLoop, calls=%fused_computation.21 | loop fusion | flops 202752 | bytes 1605632 | tf_op jit(solution)/shard_map/concatenate | solution.py:120
  24.0 3.1 %collective-permute-start.5 = (f32[264,256]{1,0:T(8,128)}, f32[264,256]{1,0:T(8,128)}, u32[]{:S(2)}, u32[]{:S(2)}) collective-permute-start(f32[264,256]{1,0:T(8,128)} %get-tuple-element.12), channel_id=1, source_target_pairs={{0,8},{4,12},{8,0},{12,4},{1,9},{5,13},{9,1},{13,5},{2,10},{6,14},... | collective-permute-start | bytes 811016 | tf_op jit(solution)/shard_map/ppermute | solution.py:9
  27.1 1.8 %fusion.5 = f32[2,512,256]{2,1,0:T(8,128)S(1)} fusion(bf16[2,512,1024]{2,1,0:T(8,128)(2,1)S(1)} %bitcast.64, bf16[256,1024]{1,0:T(8,128)(2,1)} %copy-done.3), kind=kOutput, calls=%fused_computation.13 | convolution fusion | flops 536870912 | bytes 3670016 | tf_op jit(solution)/shard_map/ij,kj->ik/dot_general | solution.py:42
  29.6 1.1 %collective-permute-done.4 = f32[264,256]{1,0:T(8,128)} collective-permute-done((f32[264,256]{1,0:T(8,128)}, f32[264,256]{1,0:T(8,128)}, u32[]{:S(2)}, u32[]{:S(2)}) %collective-permute-start.4) | collective-permute-done | bytes 270368 | tf_op jit(solution)/shard_map/ppermute | solution.py:9
  30.7 15.4 %collective-permute-done.5 = f32[264,256]{1,0:T(8,128)} collective-permute-done((f32[264,256]{1,0:T(8,128)}, f32[264,256]{1,0:T(8,128)}, u32[]{:S(2)}, u32[]{:S(2)}) %collective-permute-start.5) | collective-permute-done | bytes 270368 | tf_op jit(solution)/shard_map/ppermute | solution.py:9
  46.1 4.6 %collective-permute-done.6 = f32[264,256]{1,0:T(8,128)} collective-permute-done((f32[264,256]{1,0:T(8,128)}, f32[264,256]{1,0:T(8,128)}, u32[]{:S(2)}, u32[]{:S(2)}) %collective-permute-start.6) | collective-permute-done | bytes 270368 | tf_op jit(solution)/shard_map/ppermute | solution.py:9
  50.7 0.7 %slice_add_fusion.4 = f32[8,256]{1,0:T(8,128)S(1)} fusion(f32[264,256]{1,0:T(8,128)} %collective-permute-done.6, f32[264,256]{1,0:T(8,128)} %collective-permute-done.5, f32[264,256]{1,0:T(8,128)} %collective-permute-done.4, f32[1,256]{1,0:T(1,128)S(1)} %bitcast.76), kind=kLoop, calls=%fused_computation.32 | loop fusion | flops 6144 | bytes 33792 | tf_op jit(solution)/shard_map/add | solution.py:122
  51.4 1.2 %slice_add_fusion.1 = f32[256,256]{1,0:T(8,128)S(1)} fusion(f32[264,256]{1,0:T(8,128)} %collective-permute-done.6, f32[264,256]{1,0:T(8,128)} %collective-permute-done.5, f32[264,256]{1,0:T(8,128)} %collective-permute-done.4, f32[256,1,256]{2,0,1:T(8,128)S(1)} %copy.11), kind=kLoop, calls=%fused_computation.25 | loop fusion | flops 196608 | bytes 1310720 | tf_op jit(solution)/shard_map/add | solution.py:121
  52.6 1.1 %collective-permute-start.7 = (f32[264,256]{1,0:T(8,128)S(1)}, f32[264,256]{1,0:T(8,128)S(1)}, u32[]{:S(2)}, u32[]{:S(2)}) collective-permute-start(f32[264,256]{1,0:T(8,128)S(1)} %pad_maximum_fusion.4), channel_id=1, source_target_pairs={{0,1},{1,0},{2,3},{3,2},{4,5},{5,4},{6,7},{7,6},{8,9},{9,8},{10,11... | collective-permute-start | bytes 811016 | tf_op jit(solution)/shard_map/ppermute | solution.py:9
  53.8 0.9 %fusion.4 = f32[1,512,256]{2,1,0:T(8,128)} fusion(f32[520,256]{1,0:T(8,128)S(1)} %collective-permute-done.3, f32[2,512,256]{2,1,0:T(8,128)S(1)} %fusion.5, s32[]{:T(128)S(6)} %select_n.48, f32[256]{0:T(256)S(1)} %bitcast.79, bf16[1,1024,256]{2,1,0:T(8,128)(2,1)S(1)} %copy-done.2, s32[]{:T(128)S(6)} %select_n.43), kind=kLoop, calls=%fused_computation.10 | loop fusion | flops 524288 | bytes 1836040 | tf_op jit(solution)/shard_map/broadcast_in_dim | solution.py:132
  55.0 0.8 %fusion.10 = f32[256,256]{1,0:T(8,128)} fusion(f32[264,256]{1,0:T(8,128)S(1)} %fusion.12, bf16[256,256]{1,0:T(8,128)(2,1)S(1)} %copy-done, f32[256]{0:T(256)S(1)} %bitcast.80), kind=kLoop, calls=%fused_computation.24 | loop fusion | flops 196608 | bytes 656384 | tf_op jit(solution)/shard_map/div | solution.py:130
  (49 shorter events, 1.8 us)
Async XLA Ops:
  0.6 16.9 %collective-permute-start = (bf16[256,256]{1,0:T(8,128)(2,1)}, bf16[256,256]{1,0:T(8,128)(2,1)S(1)}, u32[]{:S(2)}, u32[]{:S(2)}) collective-permute-start(bf16[256,256]{1,0:T(8,128)(2,1)} %param.9), channel_id=1, source_target_pairs={{0,4},{4,8},{8,12},{12,0},{1,5},{5,9},{9,13},{13,1},{2,6},{6,10},{... | collective-permute-start | bytes 393224 | tf_op jit(solution)/shard_map/ppermute | solution.py:9
  2.0 15.6 %collective-permute-start.1 = (bf16[256,256]{1,0:T(8,128)(2,1)}, bf16[256,256]{1,0:T(8,128)(2,1)S(1)}, u32[]{:S(2)}, u32[]{:S(2)}) collective-permute-start(bf16[256,256]{1,0:T(8,128)(2,1)} %param.9), channel_id=1, source_target_pairs={{0,8},{4,12},{8,0},{12,4},{1,9},{5,13},{9,1},{13,5},{2,10},{6,14},... | collective-permute-start | bytes 393224 | tf_op jit(solution)/shard_map/ppermute | solution.py:9
  3.1 14.5 %collective-permute-start.2 = (bf16[256,256]{1,0:T(8,128)(2,1)}, bf16[256,256]{1,0:T(8,128)(2,1)S(1)}, u32[]{:S(2)}, u32[]{:S(2)}) collective-permute-start(bf16[256,256]{1,0:T(8,128)(2,1)} %param.9), channel_id=1, source_target_pairs={{0,12},{4,0},{8,4},{12,8},{1,13},{5,1},{9,5},{13,9},{2,14},{6,2},{... | collective-permute-start | bytes 393224 | tf_op jit(solution)/shard_map/ppermute | solution.py:9
  7.2 2.9 %copy-start.1 = (bf16[1,1024,256]{2,1,0:T(8,128)(2,1)S(1)}, bf16[1,1024,256]{2,1,0:T(8,128)(2,1)}, u32[]{:S(2)}) copy-start(bf16[1,1024,256]{2,1,0:T(8,128)(2,1)} %param.8) | copy-start | bytes 1572868
  7.2 3.1 %copy-start = (bf16[256,256]{1,0:T(8,128)(2,1)S(1)}, bf16[256,256]{1,0:T(8,128)(2,1)}, u32[]{:S(2)}) copy-start(bf16[256,256]{1,0:T(8,128)(2,1)} %param.9) | copy-start | bytes 393220
  17.5 4.2 %copy-start.4 = (bf16[256,256]{1,0:T(8,128)(2,1)}, bf16[256,256]{1,0:T(8,128)(2,1)S(1)}, u32[]{:S(2)}) copy-start(bf16[256,256]{1,0:T(8,128)(2,1)S(1)} %collective-permute-done) | copy-start | bytes 393220
  17.6 4.2 %copy-start.6 = (bf16[256,256]{1,0:T(8,128)(2,1)}, bf16[256,256]{1,0:T(8,128)(2,1)S(1)}, u32[]{:S(2)}) copy-start(bf16[256,256]{1,0:T(8,128)(2,1)S(1)} %collective-permute-done.1) | copy-start | bytes 393220
  17.6 0.7 %copy-start.8 = (bf16[256,256]{1,0:T(8,128)(2,1)}, bf16[256,256]{1,0:T(8,128)(2,1)S(1)}, u32[]{:S(2)}) copy-start(bf16[256,256]{1,0:T(8,128)(2,1)S(1)} %collective-permute-done.2) | copy-start | bytes 393220
  17.7 4.1 %copy-start.3 = (bf16[256,1024]{1,0:T(8,128)(2,1)}, bf16[256,1024]{1,0:T(8,128)(2,1)S(1)}, u32[]{:S(2)}) copy-start(bf16[256,1024]{1,0:T(8,128)(2,1)S(1)} %constant_dynamic-update-slice_fusion) | copy-start | bytes 1572868
  23.9 5.0 %copy-start.5 = (bf16[256,256]{1,0:T(8,128)(2,1)S(1)}, bf16[256,256]{1,0:T(8,128)(2,1)}, u32[]{:S(2)}) copy-start(bf16[256,256]{1,0:T(8,128)(2,1)} %copy-done.4) | copy-start | bytes 393220
  23.9 5.0 %copy-start.7 = (bf16[256,256]{1,0:T(8,128)(2,1)S(1)}, bf16[256,256]{1,0:T(8,128)(2,1)}, u32[]{:S(2)}) copy-start(bf16[256,256]{1,0:T(8,128)(2,1)} %copy-done.6) | copy-start | bytes 393220
  23.9 5.0 %copy-start.9 = (bf16[256,256]{1,0:T(8,128)(2,1)S(1)}, bf16[256,256]{1,0:T(8,128)(2,1)}, u32[]{:S(2)}) copy-start(bf16[256,256]{1,0:T(8,128)(2,1)} %copy-done.8) | copy-start | bytes 393220
  23.9 6.8 %collective-permute-start.4 = (f32[264,256]{1,0:T(8,128)}, f32[264,256]{1,0:T(8,128)}, u32[]{:S(2)}, u32[]{:S(2)}) collective-permute-start(f32[264,256]{1,0:T(8,128)} %get-tuple-element.10), channel_id=1, source_target_pairs={{0,4},{4,8},{8,12},{12,0},{1,5},{5,9},{9,13},{13,1},{2,6},{6,10},{... | collective-permute-start | bytes 811016 | tf_op jit(solution)/shard_map/ppermute | solution.py:9
  24.0 22.1 %collective-permute-start.5 = (f32[264,256]{1,0:T(8,128)}, f32[264,256]{1,0:T(8,128)}, u32[]{:S(2)}, u32[]{:S(2)}) collective-permute-start(f32[264,256]{1,0:T(8,128)} %get-tuple-element.12), channel_id=1, source_target_pairs={{0,8},{4,12},{8,0},{12,4},{1,9},{5,13},{9,1},{13,5},{2,10},{6,14},... | collective-permute-start | bytes 811016 | tf_op jit(solution)/shard_map/ppermute | solution.py:9
  27.1 23.6 %collective-permute-start.6 = (f32[264,256]{1,0:T(8,128)}, f32[264,256]{1,0:T(8,128)}, u32[]{:S(2)}, u32[]{:S(2)}) collective-permute-start(f32[264,256]{1,0:T(8,128)} %get-tuple-element.11), channel_id=1, source_target_pairs={{0,12},{4,0},{8,4},{12,8},{1,13},{5,1},{9,5},{13,9},{2,14},{6,2},{... | collective-permute-start | bytes 811016 | tf_op jit(solution)/shard_map/ppermute | solution.py:9
  29.2 24.6 %copy-start.2 = (bf16[1,1024,256]{2,1,0:T(8,128)(2,1)S(1)}, bf16[1,1024,256]{2,1,0:T(8,128)(2,1)}, u32[]{:S(2)}) copy-start(bf16[1,1024,256]{2,1,0:T(8,128)(2,1)} %param.8) | copy-start | bytes 1572868
  29.3 24.4 %collective-permute-start.3 = (f32[520,256]{1,0:T(8,128)S(1)}, f32[520,256]{1,0:T(8,128)S(1)}, u32[]{:S(2)}, u32[]{:S(2)}) collective-permute-start(f32[520,256]{1,0:T(8,128)S(1)} %pad_maximum_fusion), channel_id=1, source_target_pairs={{0,2},{2,0},{1,3},{3,1},{4,6},{6,4},{5,7},{7,5},{8,10},{10,8},{9,1... | collective-permute-start | bytes 1597448 | tf_op jit(solution)/shard_map/ppermute | solution.py:9
  52.6 2.3 %collective-permute-start.7 = (f32[264,256]{1,0:T(8,128)S(1)}, f32[264,256]{1,0:T(8,128)S(1)}, u32[]{:S(2)}, u32[]{:S(2)}) collective-permute-start(f32[264,256]{1,0:T(8,128)S(1)} %pad_maximum_fusion.4), channel_id=1, source_target_pairs={{0,1},{1,0},{2,3},{3,2},{4,5},{5,4},{6,7},{7,6},{8,9},{9,8},{10,11... | collective-permute-start | bytes 811016 | tf_op jit(solution)/shard_map/ppermute | solution.py:9

commit v3 on v2

--- a/solution.py
+++ b/solution.py
@@ -25,23 +25,24 @@
     n_row, rank = h_stack.shape[0], h_stack.shape[1]
     tile_rows = w_tile.shape[0]
     h_all = jnp.concatenate([h_stack[d] for d in range(n_row)], axis=1)
-    block_of = (row_index - lax.iota(jnp.int32, n_row)) % n_row
-    live = lax.iota(jnp.int32, stored)[None, :] < counts[:, None]
-    mask = (lists[:, :, None] == block_of[None, None, :]) & live[:, :, None]
-    a_dense = jnp.zeros((row_blocks, width, n_row, width), values.dtype)
-    for slot in range(stored):
-        a_dense = jnp.where(
-            mask[:, slot, None, :, None], values[:, slot, :, None, :], a_dense
-        )
-    covered = jnp.any(mask, axis=1)[:, None, :, None]
     product = jnp.dot(w_tile, h_all, preferred_element_type=jnp.float32)
-    product = product.reshape(row_blocks, width, n_row, width)
-    ratios = jnp.where(covered, a_dense.astype(jnp.float32) / product, 0.0).astype(jnp.bfloat16)
-    ratios = ratios.reshape(tile_rows, n_row * width)
+    chunks = []
+    for d in range(n_row):
+        block = (row_index - d) % n_row
+        a_d = jnp.zeros((row_blocks, width, width), values.dtype)
+        covered = jnp.zeros((row_blocks,), jnp.bool_)
+        for slot in range(stored):
+            match = (lists[:, slot] == block) & (slot < counts)
+            a_d = jnp.where(match[:, None, None], values[:, slot], a_d)
+            covered = covered | match
+        p_d = product[:, d * width:(d + 1) * width].reshape(row_blocks, width, width)
+        r_d = jnp.where(covered[:, None, None], a_d.astype(jnp.float32) / p_d, 0.0)
+        chunks.append(r_d.astype(jnp.bfloat16).reshape(tile_rows, width))
+    ratios = jnp.concatenate(chunks, axis=1)
     numer_h_all = jnp.einsum("ik,ij->kj", w_tile, ratios, preferred_element_type=jnp.float32)
     numer_w = jnp.einsum("ij,kj->ik", ratios, h_all, preferred_element_type=jnp.float32)
-    numer_h_chunks = numer_h_all.reshape(rank, n_row, width)
-    return [numer_h_chunks[:, (-e) % n_row] for e in range(n_row)], numer_w
+    starts = [((-e) % n_row) * width for e in range(n_row)]
+    return [numer_h_all[:, s:s + width] for s in starts], numer_w
 
 
 def slot_terms(values, lists, counts, w_tile, h_stack, row_index):

time: 56.1 us -> 49.4 us (0.88)
  the two profiles are of different devices: /device:TPU:11 before, /device:TPU:0 now
where the time goes in v3:
time: 49.4 us; the launch traced here: 49.2 us
  waiting for transfers between devices  24.7 us (50%)
  starting transfers between devices  12.5 us (25%)
  other arithmetic  5.03 us (10%)
  local copies, waits for them, and re-layouts  3.81 us (8%)
  matrix products  2.29 us (5%)
  between operations  0.88 us (2%)
    ppermute x8, waiting for transfers between devices, shifted(): lax.ppermute(value, axis, [(i, (i + by) % length) for i in range(length)])  24.7 us
    ppermute x8, starting transfers between devices, shifted(): lax.ppermute(value, axis, [(i, (i + by) % length) for i in range(length)])  12.5 us
    slice x1, local copies, waits for them, and re-layouts, dense_terms(): a_d = jnp.where(match[:, None, None], values[:, slot], a_d)  1.27 us
    reduce_sum x1, other arithmetic, body(): w_sum = jnp.sum(w_tile.astype(jnp.float32), axis=0)  1.19 us
  transfers between devices with their start and end apart: 8, of which 5 were waited for; matrix products, arithmetic and copies ran while one was open for 14% of the time, Pallas kernels for 0%

profile of v3, /device:TPU:0, one launch (start us, length us, event | category | flops | bytes accessed | tf_op | source)
XLA Modules:
  0.0 49.2 jit_solution(10733242746581440732)
XLA Ops:
  0.6 5.1 %collective-permute-start.2 = (bf16[256,256]{1,0:T(8,128)(2,1)}, bf16[256,256]{1,0:T(8,128)(2,1)S(1)}, u32[]{:S(2)}, u32[]{:S(2)}) collective-permute-start(bf16[256,256]{1,0:T(8,128)(2,1)} %param.9), channel_id=1, source_target_pairs={{0,12},{4,0},{8,4},{12,8},{1,13},{5,1},{9,5},{13,9},{2,14},{6,2},{... | collective-permute-start | bytes 393224 | tf_op jit(solution)/shard_map/ppermute | solution.py:9
  5.7 1.0 %collective-permute-start = (bf16[256,256]{1,0:T(8,128)(2,1)}, bf16[256,256]{1,0:T(8,128)(2,1)S(1)}, u32[]{:S(2)}, u32[]{:S(2)}) collective-permute-start(bf16[256,256]{1,0:T(8,128)(2,1)} %param.9), channel_id=1, source_target_pairs={{0,4},{4,8},{8,12},{12,0},{1,5},{5,9},{9,13},{13,1},{2,6},{6,10},{... | collective-permute-start | bytes 393224 | tf_op jit(solution)/shard_map/ppermute | solution.py:9
  6.8 1.3 %fusion.23 = (bf16[4,1,256,256]{3,2,1,0:T(8,128)(2,1)S(1)}, bf16[4,1,256,256]{3,2,1,0:T(8,128)(2,1)S(1)}) fusion(bf16[4,2,256,256]{3,2,1,0:T(8,128)(2,1)} %bitcast.79), kind=kLoop, calls=%fused_computation.61 | loop fusion | bytes 2097152 | tf_op jit(solution)/shard_map/slice | solution.py:36
  8.1 0.8 %fusion.18 = (pred[4]{0:T(512)(128)(4,1)S(1)}, pred[4]{0:T(512)(128)(4,1)S(1)}, pred[4]{0:T(512)(128)(4,1)S(1)}, pred[4]{0:T(512)(128)(4,1)S(1)}, pred[4]{0:T(51...) fusion(s32[1,1,4]{2,1,0:T(1,128)} %param.7, ...), kind=kLoop, calls=%fused_computation.56 | loop fusion | flops 88 | bytes 112 | tf_op jit(solution)/shard_map/or | solution.py:37
  8.8 1.2 %convert_reduce_fusion = f32[256]{0:T(256)S(1)} fusion(bf16[1,1024,256]{2,1,0:T(8,128)(2,1)} %param.8), kind=kLoop, calls=%fused_computation.15 | loop fusion | flops 524032 | bytes 525312 | tf_op jit(solution)/shard_map/reduce_sum | solution.py:98
  10.0 0.9 %constant_dynamic-update-slice_fusion.3 = bf16[256,1024]{1,0:T(8,128)(2,1)S(1)} fusion(bf16[256,256]{1,0:T(8,128)(2,1)} %param.9), kind=kLoop, calls=%fused_computation.38 | loop fusion | bytes 262144
  11.0 0.2 copy.9
  11.2 0.2 copy.10
  12.5 2.9 %collective-permute-done = bf16[256,256]{1,0:T(8,128)(2,1)S(1)} collective-permute-done((bf16[256,256]{1,0:T(8,128)(2,1)}, bf16[256,256]{1,0:T(8,128)(2,1)S(1)}, u32[]{:S(2)}, u32[]{:S(2)}) %collective-permute-start) | collective-permute-done | bytes 131104 | tf_op jit(solution)/shard_map/ppermute | solution.py:9
  15.3 1.8 %collective-permute-done.1 = bf16[256,256]{1,0:T(8,128)(2,1)S(1)} collective-permute-done((bf16[256,256]{1,0:T(8,128)(2,1)}, bf16[256,256]{1,0:T(8,128)(2,1)S(1)}, u32[]{:S(2)}, u32[]{:S(2)}) %collective-permute-start.1) | collective-permute-done | bytes 131104 | tf_op jit(solution)/shard_map/ppermute | solution.py:9
  17.2 0.8 %convolution_bitcast_fusion = f32[1024,1024]{0,1:T(8,128)S(1)} fusion(bf16[256,1024]{1,0:T(8,128)(2,1)S(1)} %constant_dynamic-update-slice_fusion, bf16[1,1024,256]{2,1,0:T(8,128)(2,1)S(1)} %copy-done), kind=kOutput, calls=%fused_computation | convolution fusion | flops 536870912 | bytes 5242880 | tf_op jit(solution)/shard_map/dot_general | solution.py:28
  18.0 0.9 %fusion.7 = (bf16[1024,256]{0,1:T(8,128)(2,1)S(1)}, bf16[1024,256]{0,1:T(8,128)(2,1)S(1)}, bf16[1024,256]{0,1:T(8,128)(2,1)S(1)}, bf16[1024,256]{0,1:T(8,128)(2,1)S(1)}) fusion(f32[1024,1024]{0,1:T(8,128)S(1)} %convolution_bitcast_fusion, bf16[1024,256]{0,1:T(8,128)(2,1)S(1)} %copy.9, bf16[1024,256]{0,1:T(8,128)(2,1)S(1)} %copy.10, ...), kind=kLoop, calls=%fused_computation.14 | loop fusion | flops 6291456 | bytes 7352320 | tf_op jit(solution)/shard_map/convert_element_type | solution.py:40
  18.9 0.8 %fusion.13 = f32[1024,256]{1,0:T(8,128)S(1)} fusion(bf16[256,1024]{1,0:T(8,128)(2,1)S(1)} %constant_dynamic-update-slice_fusion, bf16[1024,256]{0,1:T(8,128)(2,1)S(1)} %get-tuple-element.15, bf16[1024,256]{0,1:T(8,128)(2,1)S(1)} %get-tuple-element.16, bf16[1024,256]{0,1:T(8,128)(2,1)S(1)} %get-tuple-element.17, bf16[1024,256]{0,1:T(8,128)(2,1)S(1)} %get-tuple-element.14), kind=kOutput, calls=%fused_computation.28 | convolution fusion | flops 545259520 | bytes 3670016 | tf_op jit(solution)/shard_map/ij,kj->ik/dot_general | solution.py:43
  19.7 0.8 %convolution_bitcast_fusion.1 = f32[256,1024]{1,0:T(8,128)S(1)} fusion(bf16[1,1024,256]{2,1,0:T(8,128)(2,1)S(1)} %copy-done, bf16[1024,256]{0,1:T(8,128)(2,1)S(1)} %get-tuple-element.15, bf16[1024,256]{0,1:T(8,128)(2,1)S(1)} %get-tuple-element.16, bf16[1024,256]{0,1:T(8,128)(2,1)S(1)} %get-tuple-element.17, bf16[1024,256]{0,1:T(8,128)(2,1)S(1)} %get-tuple-element.14), kind=kOutput, calls=%fused_computation.2 | convolution fusion | flops 545259520 | bytes 3670016 | tf_op jit(solution)/shard_map/ik,ij->kj/dot_general | solution.py:42
  20.6 1.6 %collective-permute-start.6 = (f32[264,256]{1,0:T(8,128)S(1)}, f32[264,256]{1,0:T(8,128)S(1)}, u32[]{:S(2)}, u32[]{:S(2)}) collective-permute-start(f32[264,256]{1,0:T(8,128)S(1)} %get-tuple-element.24), channel_id=1, source_target_pairs={{0,12},{4,0},{8,4},{12,8},{1,13},{5,1},{9,5},{13,9},{2,14},{6,2},{... | collective-permute-start | bytes 811016 | tf_op jit(solution)/shard_map/ppermute | solution.py:9
  22.2 1.1 %collective-permute-start.5 = (f32[264,256]{1,0:T(8,128)S(1)}, f32[264,256]{1,0:T(8,128)S(1)}, u32[]{:S(2)}, u32[]{:S(2)}) collective-permute-start(f32[264,256]{1,0:T(8,128)S(1)} %get-tuple-element.25), channel_id=1, source_target_pairs={{0,8},{4,12},{8,0},{12,4},{1,9},{5,13},{9,1},{13,5},{2,10},{6,14},... | collective-permute-start | bytes 811016 | tf_op jit(solution)/shard_map/ppermute | solution.py:9
  23.4 1.9 %collective-permute-start.4 = (f32[264,256]{1,0:T(8,128)S(1)}, f32[264,256]{1,0:T(8,128)S(1)}, u32[]{:S(2)}, u32[]{:S(2)}) collective-permute-start(f32[264,256]{1,0:T(8,128)S(1)} %get-tuple-element.23), channel_id=1, source_target_pairs={{0,4},{4,8},{8,12},{12,0},{1,5},{5,9},{9,13},{13,1},{2,6},{6,10},{... | collective-permute-start | bytes 811016 | tf_op jit(solution)/shard_map/ppermute | solution.py:9
  25.3 0.1 convert_reduce_fusion.1
  25.6 1.6 %collective-permute-start.3 = (f32[520,256]{1,0:T(8,128)S(1)}, f32[520,256]{1,0:T(8,128)S(1)}, u32[]{:S(2)}, u32[]{:S(2)}) collective-permute-start(f32[520,256]{1,0:T(8,128)S(1)} %pad_maximum_fusion.1), channel_id=1, source_target_pairs={{0,2},{2,0},{1,3},{3,1},{4,6},{6,4},{5,7},{7,5},{8,10},{10,8},{9,1... | collective-permute-start | bytes 1597448 | tf_op jit(solution)/shard_map/ppermute | solution.py:9
  27.1 2.1 %collective-permute-done.6 = f32[264,256]{1,0:T(8,128)S(1)} collective-permute-done((f32[264,256]{1,0:T(8,128)S(1)}, f32[264,256]{1,0:T(8,128)S(1)}, u32[]{:S(2)}, u32[]{:S(2)}) %collective-permute-start.6) | collective-permute-done | bytes 270368 | tf_op jit(solution)/shard_map/ppermute | solution.py:9
  29.2 17.3 %collective-permute-done.5 = f32[264,256]{1,0:T(8,128)S(1)} collective-permute-done((f32[264,256]{1,0:T(8,128)S(1)}, f32[264,256]{1,0:T(8,128)S(1)}, u32[]{:S(2)}, u32[]{:S(2)}) %collective-permute-start.5) | collective-permute-done | bytes 270368 | tf_op jit(solution)/shard_map/ppermute | solution.py:9
  46.8 0.9 %fusion.10 = f32[1,512,256]{2,1,0:T(8,128)} fusion(f32[520,256]{1,0:T(8,128)S(1)} %collective-permute-done.3, f32[2,512,256]{2,1,0:T(8,128)S(1)} %bitcast.81, s32[]{:T(128)S(6)} %select_n.100, f32[256]{0:T(256)S(1)} %bitcast.89, bf16[1,1024,256]{2,1,0:T(8,128)(2,1)S(1)} %copy-done, s32[]{:T(128)S(6)} %select_n.83), kind=kLoop, calls=%fused_computation.21 | loop fusion | flops 524288 | bytes 1836040 | tf_op jit(solution)/shard_map/broadcast_in_dim | solution.py:133
  47.7 0.6 %collective-permute-done.7 = f32[264,256]{1,0:T(8,128)S(1)} collective-permute-done((f32[264,256]{1,0:T(8,128)S(1)}, f32[264,256]{1,0:T(8,128)S(1)}, u32[]{:S(2)}, u32[]{:S(2)}) %collective-permute-start.7) | collective-permute-done | bytes 270368 | tf_op jit(solution)/shard_map/ppermute | solution.py:9
  48.4 0.8 %fusion.14 = f32[256,256]{1,0:T(8,128)} fusion(f32[264,256]{1,0:T(8,128)S(1)} %fusion.17, bf16[256,256]{1,0:T(8,128)(2,1)S(1)} %copy-done.1, f32[256]{0:T(256)S(1)} %bitcast.90), kind=kLoop, calls=%fused_computation.31 | loop fusion | flops 196608 | bytes 656384 | tf_op jit(solution)/shard_map/div | solution.py:131
  (49 shorter events, 1.6 us)
Async XLA Ops:
  0.6 16.6 %copy-start = (bf16[1,1024,256]{2,1,0:T(8,128)(2,1)S(1)}, bf16[1,1024,256]{2,1,0:T(8,128)(2,1)}, u32[]{:S(2)}) copy-start(bf16[1,1024,256]{2,1,0:T(8,128)(2,1)} %param.8) | copy-start | bytes 1572868
  0.6 16.5 %collective-permute-start.2 = (bf16[256,256]{1,0:T(8,128)(2,1)}, bf16[256,256]{1,0:T(8,128)(2,1)S(1)}, u32[]{:S(2)}, u32[]{:S(2)}) collective-permute-start(bf16[256,256]{1,0:T(8,128)(2,1)} %param.9), channel_id=1, source_target_pairs={{0,12},{4,0},{8,4},{12,8},{1,13},{5,1},{9,5},{13,9},{2,14},{6,2},{... | collective-permute-start | bytes 393224 | tf_op jit(solution)/shard_map/ppermute | solution.py:9
  5.7 11.4 %collective-permute-start.1 = (bf16[256,256]{1,0:T(8,128)(2,1)}, bf16[256,256]{1,0:T(8,128)(2,1)S(1)}, u32[]{:S(2)}, u32[]{:S(2)}) collective-permute-start(bf16[256,256]{1,0:T(8,128)(2,1)} %param.9), channel_id=1, source_target_pairs={{0,8},{4,12},{8,0},{12,4},{1,9},{5,13},{9,1},{13,5},{2,10},{6,14},... | collective-permute-start | bytes 393224 | tf_op jit(solution)/shard_map/ppermute | solution.py:9
  5.7 9.6 %collective-permute-start = (bf16[256,256]{1,0:T(8,128)(2,1)}, bf16[256,256]{1,0:T(8,128)(2,1)S(1)}, u32[]{:S(2)}, u32[]{:S(2)}) collective-permute-start(bf16[256,256]{1,0:T(8,128)(2,1)} %param.9), channel_id=1, source_target_pairs={{0,4},{4,8},{8,12},{12,0},{1,5},{5,9},{9,13},{13,1},{2,6},{6,10},{... | collective-permute-start | bytes 393224 | tf_op jit(solution)/shard_map/ppermute | solution.py:9
  19.7 5.7 %copy-start.1 = (bf16[256,256]{1,0:T(8,128)(2,1)S(1)}, bf16[256,256]{1,0:T(8,128)(2,1)}, u32[]{:S(2)}) copy-start(bf16[256,256]{1,0:T(8,128)(2,1)} %param.9) | copy-start | bytes 393220
  20.6 8.7 %collective-permute-start.6 = (f32[264,256]{1,0:T(8,128)S(1)}, f32[264,256]{1,0:T(8,128)S(1)}, u32[]{:S(2)}, u32[]{:S(2)}) collective-permute-start(f32[264,256]{1,0:T(8,128)S(1)} %get-tuple-element.24), channel_id=1, source_target_pairs={{0,12},{4,0},{8,4},{12,8},{1,13},{5,1},{9,5},{13,9},{2,14},{6,2},{... | collective-permute-start | bytes 811016 | tf_op jit(solution)/shard_map/ppermute | solution.py:9
  22.2 24.3 %collective-permute-start.5 = (f32[264,256]{1,0:T(8,128)S(1)}, f32[264,256]{1,0:T(8,128)S(1)}, u32[]{:S(2)}, u32[]{:S(2)}) collective-permute-start(f32[264,256]{1,0:T(8,128)S(1)} %get-tuple-element.25), channel_id=1, source_target_pairs={{0,8},{4,12},{8,0},{12,4},{1,9},{5,13},{9,1},{13,5},{2,10},{6,14},... | collective-permute-start | bytes 811016 | tf_op jit(solution)/shard_map/ppermute | solution.py:9
  23.4 23.2 %collective-permute-start.4 = (f32[264,256]{1,0:T(8,128)S(1)}, f32[264,256]{1,0:T(8,128)S(1)}, u32[]{:S(2)}, u32[]{:S(2)}) collective-permute-start(f32[264,256]{1,0:T(8,128)S(1)} %get-tuple-element.23), channel_id=1, source_target_pairs={{0,4},{4,8},{8,12},{12,0},{1,5},{5,9},{9,13},{13,1},{2,6},{6,10},{... | collective-permute-start | bytes 811016 | tf_op jit(solution)/shard_map/ppermute | solution.py:9
  25.6 21.2 %collective-permute-start.3 = (f32[520,256]{1,0:T(8,128)S(1)}, f32[520,256]{1,0:T(8,128)S(1)}, u32[]{:S(2)}, u32[]{:S(2)}) collective-permute-start(f32[520,256]{1,0:T(8,128)S(1)} %pad_maximum_fusion.1), channel_id=1, source_target_pairs={{0,2},{2,0},{1,3},{3,1},{4,6},{6,4},{5,7},{7,5},{8,10},{10,8},{9,1... | collective-permute-start | bytes 1597448 | tf_op jit(solution)/shard_map/ppermute | solution.py:9
  46.7 1.6 %collective-permute-start.7 = (f32[264,256]{1,0:T(8,128)S(1)}, f32[264,256]{1,0:T(8,128)S(1)}, u32[]{:S(2)}, u32[]{:S(2)}) collective-permute-start(f32[264,256]{1,0:T(8,128)S(1)} %pad_maximum_fusion.7), channel_id=1, source_target_pairs={{0,1},{1,0},{2,3},{3,2},{4,5},{5,4},{6,7},{7,6},{8,9},{9,8},{10,11... | collective-permute-start | bytes 811016 | tf_op jit(solution)/shard_map/ppermute | solution.py:9

commit v4 on v3

--- a/solution.py
+++ b/solution.py
@@ -18,6 +18,17 @@
 
 def from_rows(rows, size):
     return rows.reshape(-1)[:size]
+
+
+def assemble(pieces, index, count, axis):
+    out = []
+    for j in range(count):
+        want = (index - j) % count
+        chosen = pieces[0]
+        for k in range(1, count):
+            chosen = jnp.where(want == k, pieces[k], chosen)
+        out.append(chosen)
+    return jnp.concatenate(out, axis=axis)
 
 
 def dense_terms(values, lists, counts, w_tile, h_stack, row_index):
@@ -93,7 +104,13 @@
     row_index = lax.axis_index("row")
     col_index = lax.axis_index("col")
 
-    h_stack = jnp.stack([h_factor] + [shifted(h_factor, "row", d) for d in range(1, n_row)])
+    sub_index = lax.axis_index("sub")
+    half = width // n_sub
+    own_piece = lax.dynamic_slice_in_dim(h_factor, sub_index * half, half, 1)
+    fetched = jnp.stack([shifted(own_piece, "row", d) for d in range(1, n_row)])
+    swapped = [fetched] + [shifted(fetched, "sub", k) for k in range(1, n_sub)]
+    others = assemble(swapped, sub_index, n_sub, 2)
+    h_stack = jnp.concatenate([h_factor[None], others])
     h_sum = jnp.sum(h_stack.astype(jnp.float32), axis=(0, 2))
     w_sum = jnp.sum(w_tile.astype(jnp.float32), axis=0)
 
@@ -115,16 +132,22 @@
     h_total = from_rows(got_h, rank)
 
     w_rows_sum = as_rows(w_sum, width)
-    mine_h = numer_h_stack[0]
-    got_w = w_rows_sum
+    def piece_message(p):
+        return jnp.concatenate(
+            [lax.dynamic_slice_in_dim(x, p * half, half, 1) for x in numer_h_stack + [w_rows_sum]]
+        )
+    reduced = piece_message(sub_index)
+    for k in range(1, n_sub):
+        reduced = reduced + shifted(piece_message((sub_index + k) % n_sub), "sub", k)
+    extra = reduced[n_row * rank:]
+    mine_h = reduced[:rank]
+    got_w = extra
     for d in range(1, n_row):
-        message = shifted(jnp.concatenate([numer_h_stack[d], w_rows_sum]), "row", d)
+        message = shifted(jnp.concatenate([reduced[d * rank:(d + 1) * rank], extra]), "row", d)
         mine_h = mine_h + message[:rank]
         got_w = got_w + message[rank:]
-    both = jnp.concatenate([mine_h, got_w])
-    total = both
-    for d in range(1, n_sub):
-        total = total + shifted(both, "sub", d)
+    final = jnp.concatenate([mine_h, got_w])
+    total = assemble([final] + [shifted(final, "sub", k) for k in range(1, n_sub)], sub_index, n_sub, 1)
     numer_h = total[:rank]
     w_total = from_rows(total[rank:], rank)
 

time: 49.4 us -> 43.1 us (0.87)
  waiting for transfers between devices: 24.7 us -> 13.5 us
  local copies, waits for them, and re-layouts: 3.81 us -> 7.8 us
  other arithmetic: 5.03 us -> 6.07 us
    ppermute x8 -> x10, waiting for transfers between devices: 24.7 us -> 13.5 us  [shifted(): lax.ppermute(value, axis, [(i, (i + by) % length) for i in range(length)])]
    unnamed x7 -> x8, local copies, waits for them, and re-layouts: 0.95 us -> 2.7 us
    add x1, other arithmetic: 0.04 us -> 1.1 us  [body(): reduced + shifted(piece_message((sub_index + k) % n_sub), 'sub', k)]
    reduce_sum x1, other arithmetic: 1.19 us -> 0.15 us  [body(): w_sum = jnp.sum(w_tile.astype(jnp.float32), axis=0)]
    broadcast_in_dim x1, other arithmetic: 0.92 us -> 1.93 us  [body(): w_new = (w_part * mine_w / h_total[None, :])[None]]
    dynamic_slice x0 -> x1, local copies, waits for them, and re-layouts: none -> 0.91 us  [body(): own_piece = lax.dynamic_slice_in_dim(h_factor, sub_index * half, half, 1)]
    slice x1, local copies, waits for them, and re-layouts: 0.01 us -> 0.7 us  [body(): got_h = got_h + message[share:]]
    concatenate x1 -> x2, local copies, waits for them, and re-layouts: 0.01 us -> 0.61 us  [the longest x1 0.6 us: piece_message(): jnp.concatenate([lax.dynamic_slice_in_dim(x, p * half, half, 1) for x in...]
  transfers between devices with their start and end apart: 8 -> 10, of which waited for: 5 -> 4; matrix products, arithmetic and copies ran while one was open for 14% -> 20% of each run, Pallas kernels for 0% -> 0%
where the time goes in v4:
time: 43.1 us; the launch traced here: 42.7 us
  waiting for transfers between devices  13.5 us (31%)
  starting transfers between devices  12.1 us (28%)
  local copies, waits for them, and re-layouts  7.8 us (18%)
  other arithmetic  6.07 us (14%)
  matrix products  2.27 us (5%)
  between operations  0.98 us (2%)
    ppermute x10, waiting for transfers between devices, shifted(): lax.ppermute(value, axis, [(i, (i + by) % length) for i in range(length)])  13.5 us
    ppermute x10, starting transfers between devices, shifted(): lax.ppermute(value, axis, [(i, (i + by) % length) for i in range(length)])  12.1 us
    unnamed x8, local copies, waits for them, and re-layouts  2.7 us
    broadcast_in_dim x1, other arithmetic, body(): w_new = (w_part * mine_w / h_total[None, :])[None]  1.93 us
    slice x1, local copies, waits for them, and re-layouts, dense_terms(): a_d = jnp.where(match[:, None, None], values[:, slot], a_d)  1.27 us
    add x1, other arithmetic, body(): reduced + shifted(piece_message((sub_index + k) % n_sub), 'sub', k)  1.1 us
    dynamic_slice x1, local copies, waits for them, and re-layouts, body(): own_piece = lax.dynamic_slice_in_dim(h_factor, sub_index * half, half, 1)  0.91 us
    convert_element_type x1, other arithmetic, dense_terms(): chunks.append(r_d.astype(jnp.bfloat16).reshape(tile_rows, width))  0.91 us
  transfers between devices with their start and end apart: 10, of which 4 were waited for; matrix products, arithmetic and copies ran while one was open for 20% of the time, Pallas kernels for 0%

profile of v4, /device:TPU:0, one launch (start us, length us, event | category | flops | bytes accessed | tf_op | source)
XLA Modules:
  0.0 42.7 jit_solution(8585303221323914440)
XLA Ops:
  0.7 0.9 %constant_dynamic-slice_fusion = bf16[256,128]{1,0:T(8,128)(2,1)S(1)} fusion(bf16[256,256]{1,0:T(8,128)(2,1)} %param.9, s32[]{:T(128)S(6)} %select_n.148), kind=kLoop, calls=%fused_computation.68 | loop fusion | bytes 131076 | tf_op jit(solution)/shard_map/dynamic_slice | solution.py:109
  1.6 5.0 %collective-permute-start.2 = (bf16[256,128]{1,0:T(8,128)(2,1)S(1)}, bf16[256,128]{1,0:T(8,128)(2,1)S(1)}, u32[]{:S(2)}, u32[]{:S(2)}) collective-permute-start(bf16[256,128]{1,0:T(8,128)(2,1)S(1)} %constant_dynamic-slice_fusion), channel_id=1, source_target_pairs={{0,12},{4,0},{8,4},{12,8},{1,13},{5,1},{9,5},{13,9},{2,14},{6,2},{... | collective-permute-start | bytes 196616 | tf_op jit(solution)/shard_map/ppermute | solution.py:9
  6.6 1.0 %collective-permute-start = (bf16[256,128]{1,0:T(8,128)(2,1)S(1)}, bf16[256,128]{1,0:T(8,128)(2,1)S(1)}, u32[]{:S(2)}, u32[]{:S(2)}) collective-permute-start(bf16[256,128]{1,0:T(8,128)(2,1)S(1)} %constant_dynamic-slice_fusion), channel_id=1, source_target_pairs={{0,4},{4,8},{8,12},{12,0},{1,5},{5,9},{9,13},{13,1},{2,6},{6,10},{... | collective-permute-start | bytes 196616 | tf_op jit(solution)/shard_map/ppermute | solution.py:9
  7.6 1.3 %fusion.30 = (bf16[4,1,256,256]{3,2,1,0:T(8,128)(2,1)S(1)}, bf16[4,1,256,256]{3,2,1,0:T(8,128)(2,1)S(1)}) fusion(bf16[4,2,256,256]{3,2,1,0:T(8,128)(2,1)} %bitcast.83), kind=kLoop, calls=%fused_computation.89 | loop fusion | bytes 2097152 | tf_op jit(solution)/shard_map/slice | solution.py:47
  9.1 4.0 %collective-permute-done.1 = bf16[256,128]{1,0:T(8,128)(2,1)S(1)} collective-permute-done((bf16[256,128]{1,0:T(8,128)(2,1)S(1)}, bf16[256,128]{1,0:T(8,128)(2,1)S(1)}, u32[]{:S(2)}, u32[]{:S(2)}) %collective-permute-start.1) | collective-permute-done | bytes 65568 | tf_op jit(solution)/shard_map/ppermute | solution.py:9
  13.2 0.8 %fusion.25 = (pred[4]{0:T(512)(128)(4,1)S(1)}, pred[4]{0:T(512)(128)(4,1)S(1)}, pred[4]{0:T(512)(128)(4,1)S(1)}, pred[4]{0:T(512)(128)(4,1)S(1)}, pred[4]{0:T(51...) fusion(s32[1,1,4]{2,1,0:T(1,128)} %param.7, ...), kind=kLoop, calls=%fused_computation.84 | loop fusion | flops 88 | bytes 112 | tf_op jit(solution)/shard_map/or | solution.py:48
  15.8 0.8 %convolution_bitcast_fusion = f32[1024,1024]{0,1:T(8,128)S(1)} fusion(bf16[1,1024,256]{2,1,0:T(8,128)(2,1)S(1)} %copy-done, bf16[256,256]{1,0:T(8,128)(2,1)S(1)} %get-tuple-element.27, bf16[256,256]{1,0:T(8,128)(2,1)S(1)} %get-tuple-element.28, bf16[256,256]{1,0:T(8,128)(2,1)S(1)} %get-tuple-element.26, bf16[256,256]{1,0:T(8,128)(2,1)S(1)} %copy-done.1), kind=kOutput, calls=%fused_computation | convolution fusion | flops 538968064 | bytes 5242880 | tf_op jit(solution)/shard_map/dot_general | solution.py:39
  16.5 0.9 %fusion.7 = (bf16[1024,256]{0,1:T(8,128)(2,1)S(1)}, bf16[1024,256]{0,1:T(8,128)(2,1)S(1)}, bf16[1024,256]{0,1:T(8,128)(2,1)S(1)}, bf16[1024,256]{0,1:T(8,128)(2,1)S(1)}) fusion(f32[1024,1024]{0,1:T(8,128)S(1)} %convolution_bitcast_fusion, bf16[1024,256]{0,1:T(8,128)(2,1)S(1)} %copy.9, bf16[1024,256]{0,1:T(8,128)(2,1)S(1)} %copy.10, ...), kind=kLoop, calls=%fused_computation.14 | loop fusion | flops 6291456 | bytes 7352320 | tf_op jit(solution)/shard_map/convert_element_type | solution.py:51
  17.5 0.8 %convolution_bitcast_fusion.1 = f32[256,1024]{1,0:T(8,128)S(1)} fusion(bf16[1,1024,256]{2,1,0:T(8,128)(2,1)S(1)} %copy-done, bf16[1024,256]{0,1:T(8,128)(2,1)S(1)} %get-tuple-element.15, bf16[1024,256]{0,1:T(8,128)(2,1)S(1)} %get-tuple-element.16, bf16[1024,256]{0,1:T(8,128)(2,1)S(1)} %get-tuple-element.17, bf16[1024,256]{0,1:T(8,128)(2,1)S(1)} %get-tuple-element.14), kind=kOutput, calls=%fused_computation.2 | convolution fusion | flops 545259520 | bytes 3670016 | tf_op jit(solution)/shard_map/ik,ij->kj/dot_general | solution.py:53
  18.3 0.7 %dynamic-slice_dynamic-update-slice_fusion.3 = (f32[1032,128]{1,0:T(8,128)}, f32[1032,128]{1,0:T(8,128)S(1)}) fusion(f32[256,256]{1,0:T(8,128)S(1)} %get-tuple-element.21, s32[]{:T(128)S(6)} %select_n.171, s32[]{:T(128)S(6)} %select_n.148), kind=kLoop, calls=%fused_computation.54 | loop fusion | bytes 524296
  19.0 0.7 %dynamic-slice_dynamic-update-slice_fusion.2 = (f32[1032,128]{1,0:T(8,128)}, f32[1032,128]{1,0:T(8,128)S(1)}) fusion(f32[1032,128]{1,0:T(8,128)} %get-tuple-element.39, f32[256,256]{1,0:T(8,128)S(1)} %get-tuple-element.20, s32[]{:T(128)S(6)} %select_n.171, f32[1032,128]{1,0:T(8,128)S(1)} %get-tuple-element.40, s32[]{:T(128)S(6)} %select_n.148), kind=kLoop, calls=%fused_computation.53 | loop fusion | bytes 524296
  19.7 0.7 %dynamic-slice_dynamic-update-slice_fusion.1 = (f32[1032,128]{1,0:T(8,128)}, f32[1032,128]{1,0:T(8,128)S(1)}) fusion(f32[1032,128]{1,0:T(8,128)} %get-tuple-element.37, f32[256,256]{1,0:T(8,128)S(1)} %get-tuple-element.19, s32[]{:T(128)S(6)} %select_n.171, f32[1032,128]{1,0:T(8,128)S(1)} %get-tuple-element.38, s32[]{:T(128)S(6)} %select_n.148), kind=kLoop, calls=%fused_computation.52 | loop fusion | bytes 524296
  20.4 0.7 %dynamic-slice_dynamic-update-slice_fusion = (f32[1032,128]{1,0:T(8,128)}, f32[1032,128]{1,0:T(8,128)S(1)}) fusion(f32[1032,128]{1,0:T(8,128)} %get-tuple-element.35, f32[256,256]{1,0:T(8,128)S(1)} %get-tuple-element.18, s32[]{:T(128)S(6)} %select_n.171, f32[1032,128]{1,0:T(8,128)S(1)} %get-tuple-element.36, s32[]{:T(128)S(6)} %select_n.148), kind=kLoop, calls=%fused_computation.51 | loop fusion | bytes 524296
  21.0 0.6 %constant_dynamic-update-slice_fusion.1 = (f32[1032,128]{1,0:T(8,128)}, f32[1032,128]{1,0:T(8,128)S(1)}) fusion(f32[1032,128]{1,0:T(8,128)} %get-tuple-element.33, s32[]{:T(128)S(6)} %select_n.171, f32[1,256]{1,0:T(1,128)S(1)} %bitcast.95, f32[1032,128]{1,0:T(8,128)S(1)} %get-tuple-element.34, s32[]{:T(128)S(6)} %select_n.148), kind=kLoop, calls=%fused_computation.62 | loop fusion | bytes 9224 | tf_op jit(solution)/shard_map/concatenate | solution.py:136
  22.1 0.8 %fusion.13 = f32[1024,256]{1,0:T(8,128)S(1)} fusion(bf16[1024,256]{0,1:T(8,128)(2,1)S(1)} %get-tuple-element.15, bf16[1024,256]{0,1:T(8,128)(2,1)S(1)} %get-tuple-element.16, bf16[1024,256]{0,1:T(8,128)(2,1)S(1)} %get-tuple-element.17, bf16[1024,256]{0,1:T(8,128)(2,1)S(1)} %get-tuple-element.14, bf16[256,256]{1,0:T(8,128)(2,1)S(1)} %get-tuple-element.27, ...), kind=kOutput, calls=%fused_computation.30 | convolution fusion | flops 547356672 | bytes 3670016 | tf_op jit(solution)/shard_map/ij,kj->ik/dot_general | solution.py:54
  23.1 1.6 %collective-permute-start.4 = (f32[520,256]{1,0:T(8,128)S(1)}, f32[520,256]{1,0:T(8,128)}, u32[]{:S(2)}, u32[]{:S(2)}) collective-permute-start(f32[520,256]{1,0:T(8,128)S(1)} %pad_maximum_fusion.1), channel_id=1, source_target_pairs={{0,2},{2,0},{1,3},{3,1},{4,6},{6,4},{5,7},{7,5},{8,10},{10,8},{9,1... | collective-permute-start | bytes 1597448 | tf_op jit(solution)/shard_map/ppermute | solution.py:9
  24.7 1.1 %add.110 = f32[1032,128]{1,0:T(8,128)S(1)} add(f32[1032,128]{1,0:T(8,128)S(1)} %get-tuple-element.53, f32[1032,128]{1,0:T(8,128)} %collective-permute-done.5) | non-fusion elementwise | flops 132096 | bytes 1585152 | tf_op jit(solution)/shard_map/add | solution.py:141
  25.8 1.9 %collective-permute-start.8 = (f32[264,128]{1,0:T(8,128)S(1)}, f32[264,128]{1,0:T(8,128)S(1)}, u32[]{:S(2)}, u32[]{:S(2)}) collective-permute-start(f32[264,128]{1,0:T(8,128)S(1)} %concatenate.48), channel_id=1, source_target_pairs={{0,12},{4,0},{8,4},{12,8},{1,13},{5,1},{9,5},{13,9},{2,14},{6,2},{... | collective-permute-start | bytes 405512 | tf_op jit(solution)/shard_map/ppermute | solution.py:9
  27.9 1.9 %collective-permute-start.6 = (f32[264,128]{1,0:T(8,128)S(1)}, f32[264,128]{1,0:T(8,128)S(1)}, u32[]{:S(2)}, u32[]{:S(2)}) collective-permute-start(f32[264,128]{1,0:T(8,128)S(1)} %get-tuple-element.41), channel_id=1, source_target_pairs={{0,4},{4,8},{8,12},{12,0},{1,5},{5,9},{9,13},{13,1},{2,6},{6,10},{... | collective-permute-start | bytes 405512 | tf_op jit(solution)/shard_map/ppermute | solution.py:9
  29.8 7.5 %collective-permute-done.4 = f32[520,256]{1,0:T(8,128)} collective-permute-done((f32[520,256]{1,0:T(8,128)S(1)}, f32[520,256]{1,0:T(8,128)}, u32[]{:S(2)}, u32[]{:S(2)}) %collective-permute-start.4) | collective-permute-done | bytes 532512 | tf_op jit(solution)/shard_map/ppermute | solution.py:9
  37.3 0.7 %slice.149 = f32[8,256]{1,0:T(8,128)S(1)} slice(f32[520,256]{1,0:T(8,128)} %collective-permute-done.4), slice={[512:520], [0:256]} | slice | bytes 16384 | tf_op jit(solution)/shard_map/slice | solution.py:131
  38.0 1.8 %collective-permute-done.7 = f32[264,128]{1,0:T(8,128)S(1)} collective-permute-done((f32[264,128]{1,0:T(8,128)S(1)}, f32[264,128]{1,0:T(8,128)S(1)}, u32[]{:S(2)}, u32[]{:S(2)}) %collective-permute-start.7) | collective-permute-done | bytes 135200 | tf_op jit(solution)/shard_map/ppermute | solution.py:9
  39.9 1.9 %fusion.10 = f32[1,512,256]{2,1,0:T(8,128)} fusion(f32[520,256]{1,0:T(8,128)} %collective-permute-done.4, f32[2,512,256]{2,1,0:T(8,128)S(1)} %bitcast.85, s32[]{:T(128)S(6)} %select_n.166, f32[256]{0:T(256)S(1)} %bitcast.96, bf16[1,1024,256]{2,1,0:T(8,128)(2,1)S(1)} %copy-done, s32[]{:T(128)S(6)} %select_n.142), kind=kLoop, calls=%fused_computation.21 | loop fusion | flops 524288 | bytes 1836040 | tf_op jit(solution)/shard_map/broadcast_in_dim | solution.py:156
  41.9 0.8 %fusion.16 = f32[256,256]{1,0:T(8,128)} fusion(f32[264,128]{1,0:T(8,128)S(1)} %get-tuple-element.32, f32[264,128]{1,0:T(8,128)S(1)} %get-tuple-element.31, bf16[256,256]{1,0:T(8,128)(2,1)S(1)} %copy-done.1, f32[256]{0:T(256)S(1)} %bitcast.94), kind=kLoop, calls=%fused_computation.35 | loop fusion | flops 262144 | bytes 664576 | tf_op jit(solution)/shard_map/div | solution.py:154
  (61 shorter events, 3.1 us)
Async XLA Ops:
  0.6 15.2 %copy-start.1 = (bf16[256,256]{1,0:T(8,128)(2,1)S(1)}, bf16[256,256]{1,0:T(8,128)(2,1)}, u32[]{:S(2)}) copy-start(bf16[256,256]{1,0:T(8,128)(2,1)} %param.9) | copy-start | bytes 393220
  0.6 14.9 %copy-start = (bf16[1,1024,256]{2,1,0:T(8,128)(2,1)S(1)}, bf16[1,1024,256]{2,1,0:T(8,128)(2,1)}, u32[]{:S(2)}) copy-start(bf16[1,1024,256]{2,1,0:T(8,128)(2,1)} %param.8) | copy-start | bytes 1572868
  1.6 7.5 %collective-permute-start.2 = (bf16[256,128]{1,0:T(8,128)(2,1)S(1)}, bf16[256,128]{1,0:T(8,128)(2,1)S(1)}, u32[]{:S(2)}, u32[]{:S(2)}) collective-permute-start(bf16[256,128]{1,0:T(8,128)(2,1)S(1)} %constant_dynamic-slice_fusion), channel_id=1, source_target_pairs={{0,12},{4,0},{8,4},{12,8},{1,13},{5,1},{9,5},{13,9},{2,14},{6,2},{... | collective-permute-start | bytes 196616 | tf_op jit(solution)/shard_map/ppermute | solution.py:9
  6.6 6.5 %collective-permute-start.1 = (bf16[256,128]{1,0:T(8,128)(2,1)S(1)}, bf16[256,128]{1,0:T(8,128)(2,1)S(1)}, u32[]{:S(2)}, u32[]{:S(2)}) collective-permute-start(bf16[256,128]{1,0:T(8,128)(2,1)S(1)} %constant_dynamic-slice_fusion), channel_id=1, source_target_pairs={{0,8},{4,12},{8,0},{12,4},{1,9},{5,13},{9,1},{13,5},{2,10},{6,14},... | collective-permute-start | bytes 196616 | tf_op jit(solution)/shard_map/ppermute | solution.py:9
  6.6 6.5 %collective-permute-start = (bf16[256,128]{1,0:T(8,128)(2,1)S(1)}, bf16[256,128]{1,0:T(8,128)(2,1)S(1)}, u32[]{:S(2)}, u32[]{:S(2)}) collective-permute-start(bf16[256,128]{1,0:T(8,128)(2,1)S(1)} %constant_dynamic-slice_fusion), channel_id=1, source_target_pairs={{0,4},{4,8},{8,12},{12,0},{1,5},{5,9},{9,13},{13,1},{2,6},{6,10},{... | collective-permute-start | bytes 196616 | tf_op jit(solution)/shard_map/ppermute | solution.py:9
  13.1 2.5 %collective-permute-start.3 = (bf16[3,256,128]{2,1,0:T(8,128)(2,1)S(1)}, bf16[3,256,128]{2,1,0:T(8,128)(2,1)S(1)}, u32[]{:S(2)}, u32[]{:S(2)}) collective-permute-start(bf16[3,256,128]{2,1,0:T(8,128)(2,1)S(1)} %pad_maximum_fusion.5), channel_id=1, source_target_pairs={{0,1},{1,0},{2,3},{3,2},{4,5},{5,4},{6,7},{7,6},{8,9},{9,8},{10,11... | collective-permute-start | bytes 589832 | tf_op jit(solution)/shard_map/ppermute | solution.py:9
  21.6 3.1 %collective-permute-start.5 = (f32[1032,128]{1,0:T(8,128)}, f32[1032,128]{1,0:T(8,128)}, u32[]{:S(2)}, u32[]{:S(2)}) collective-permute-start(f32[1032,128]{1,0:T(8,128)} %get-tuple-element.52), channel_id=1, source_target_pairs={{0,1},{1,0},{2,3},{3,2},{4,5},{5,4},{6,7},{7,6},{8,9},{9,8},{10,11... | collective-permute-start | bytes 1585160 | tf_op jit(solution)/shard_map/ppermute | solution.py:9
  23.1 14.2 %collective-permute-start.4 = (f32[520,256]{1,0:T(8,128)S(1)}, f32[520,256]{1,0:T(8,128)}, u32[]{:S(2)}, u32[]{:S(2)}) collective-permute-start(f32[520,256]{1,0:T(8,128)S(1)} %pad_maximum_fusion.1), channel_id=1, source_target_pairs={{0,2},{2,0},{1,3},{3,1},{4,6},{6,4},{5,7},{7,5},{8,10},{10,8},{9,1... | collective-permute-start | bytes 1597448 | tf_op jit(solution)/shard_map/ppermute | solution.py:9
  25.8 12.2 %collective-permute-start.8 = (f32[264,128]{1,0:T(8,128)S(1)}, f32[264,128]{1,0:T(8,128)S(1)}, u32[]{:S(2)}, u32[]{:S(2)}) collective-permute-start(f32[264,128]{1,0:T(8,128)S(1)} %concatenate.48), channel_id=1, source_target_pairs={{0,12},{4,0},{8,4},{12,8},{1,13},{5,1},{9,5},{13,9},{2,14},{6,2},{... | collective-permute-start | bytes 405512 | tf_op jit(solution)/shard_map/ppermute | solution.py:9
  27.8 12.0 %collective-permute-start.7 = (f32[264,128]{1,0:T(8,128)S(1)}, f32[264,128]{1,0:T(8,128)S(1)}, u32[]{:S(2)}, u32[]{:S(2)}) collective-permute-start(f32[264,128]{1,0:T(8,128)S(1)} %get-tuple-element.42), channel_id=1, source_target_pairs={{0,8},{4,12},{8,0},{12,4},{1,9},{5,13},{9,1},{13,5},{2,10},{6,14},... | collective-permute-start | bytes 405512 | tf_op jit(solution)/shard_map/ppermute | solution.py:9
  27.9 11.9 %collective-permute-start.6 = (f32[264,128]{1,0:T(8,128)S(1)}, f32[264,128]{1,0:T(8,128)S(1)}, u32[]{:S(2)}, u32[]{:S(2)}) collective-permute-start(f32[264,128]{1,0:T(8,128)S(1)} %get-tuple-element.41), channel_id=1, source_target_pairs={{0,4},{4,8},{8,12},{12,0},{1,5},{5,9},{9,13},{13,1},{2,6},{6,10},{... | collective-permute-start | bytes 405512 | tf_op jit(solution)/shard_map/ppermute | solution.py:9
  39.9 2.0 %collective-permute-start.9 = (f32[264,128]{1,0:T(8,128)S(1)}, f32[264,128]{1,0:T(8,128)S(1)}, u32[]{:S(2)}, u32[]{:S(2)}) collective-permute-start(f32[264,128]{1,0:T(8,128)S(1)} %pad_maximum_fusion.8), channel_id=1, source_target_pairs={{0,1},{1,0},{2,3},{3,2},{4,5},{5,4},{6,7},{7,6},{8,9},{9,8},{10,11... | collective-permute-start | bytes 405512 | tf_op jit(solution)/shard_map/ppermute | solution.py:9

commit v5 on v4

--- a/solution.py
+++ b/solution.py
@@ -132,13 +132,19 @@
     h_total = from_rows(got_h, rank)
 
     w_rows_sum = as_rows(w_sum, width)
-    def piece_message(p):
-        return jnp.concatenate(
-            [lax.dynamic_slice_in_dim(x, p * half, half, 1) for x in numer_h_stack + [w_rows_sum]]
-        )
-    reduced = piece_message(sub_index)
+    messages = [
+        jnp.concatenate([x[:, p * half:(p + 1) * half] for x in numer_h_stack + [w_rows_sum]])
+        for p in range(n_sub)
+    ]
+    def piece_message(k):
+        want = (sub_index + k) % n_sub
+        chosen = messages[0]
+        for p in range(1, n_sub):
+            chosen = jnp.where(want == p, messages[p], chosen)
+        return chosen
+    reduced = piece_message(0)
     for k in range(1, n_sub):
-        reduced = reduced + shifted(piece_message((sub_index + k) % n_sub), "sub", k)
+        reduced = reduced + shifted(piece_message(k), "sub", k)
     extra = reduced[n_row * rank:]
     mine_h = reduced[:rank]
     got_w = extra

time: 43.1 us -> 38.2 us (0.89)
  local copies, waits for them, and re-layouts: 7.8 us -> 3.81 us
  other arithmetic: 6.07 us -> 4.1 us
  waiting for transfers between devices: 13.5 us -> 14.6 us
    unnamed x8, local copies, waits for them, and re-layouts: 2.7 us -> 0.09 us
    ppermute x10, waiting for transfers between devices: 13.5 us -> 14.6 us  [shifted(): lax.ppermute(value, axis, [(i, (i + by) % length) for i in range(length)])]
    broadcast_in_dim x1, other arithmetic: 1.93 us -> 0.89 us  [body(): w_new = (w_part * mine_w / h_total[None, :])[None]]
    add x1, other arithmetic: 1.1 us -> 0.09 us  [body(): reduced = reduced + shifted(piece_message(k), 'sub', k)]
    slice x1, local copies, waits for them, and re-layouts: 0.7 us -> 0.01 us  [body(): got_h = got_h + message[share:]]
    concatenate x1, local copies, waits for them, and re-layouts: 0.6 us -> 0.01 us  [body(): jnp.concatenate([x[:, p * half:(p + 1) * half] for x in numer_h_stack + [...]
  transfers between devices with their start and end apart: 10 -> 10, of which waited for: 4 -> 5; matrix products, arithmetic and copies ran while one was open for 20% -> 15% of each run, Pallas kernels for 0% -> 0%
where the time goes in v5:
time: 38.2 us; the launch traced here: 38 us
  waiting for transfers between devices  14.6 us (38%)
  starting transfers between devices  12.2 us (32%)
  other arithmetic  4.1 us (11%)
  local copies, waits for them, and re-layouts  3.81 us (10%)
  matrix products  2.27 us (6%)
  between operations  1 us (3%)
    ppermute x10, waiting for transfers between devices, shifted(): lax.ppermute(value, axis, [(i, (i + by) % length) for i in range(length)])  14.6 us
    ppermute x10, starting transfers between devices, shifted(): lax.ppermute(value, axis, [(i, (i + by) % length) for i in range(length)])  12.2 us
    slice x1, local copies, waits for them, and re-layouts, dense_terms(): a_d = jnp.where(match[:, None, None], values[:, slot], a_d)  1.27 us
    dynamic_slice x1, local copies, waits for them, and re-layouts, body(): own_piece = lax.dynamic_slice_in_dim(h_factor, sub_index * half, half, 1)  0.91 us
    convert_element_type x1, other arithmetic, dense_terms(): chunks.append(r_d.astype(jnp.bfloat16).reshape(tile_rows, width))  0.91 us
    broadcast_in_dim x1, other arithmetic, body(): w_new = (w_part * mine_w / h_total[None, :])[None]  0.89 us
    div x1, other arithmetic, body(): h_new = h_factor.astype(jnp.float32) * numer_h / w_total[:, None]  0.82 us
    or x1, other arithmetic, dense_terms(): covered = covered | match  0.77 us
  transfers between devices with their start and end apart: 10, of which 5 were waited for; matrix products, arithmetic and copies ran while one was open for 15% of the time, Pallas kernels for 0%

profile of v5, /device:TPU:0, one launch (start us, length us, event | category | flops | bytes accessed | tf_op | source)
XLA Modules:
  0.0 38.0 jit_solution(18424174664431829940)
XLA Ops:
  0.7 0.9 %constant_dynamic-slice_fusion = bf16[256,128]{1,0:T(8,128)(2,1)S(1)} fusion(bf16[256,256]{1,0:T(8,128)(2,1)} %param.9, s32[]{:T(128)S(6)} %select_n.152), kind=kLoop, calls=%fused_computation.80 | loop fusion | bytes 131076 | tf_op jit(solution)/shard_map/dynamic_slice | solution.py:109
  1.6 5.0 %collective-permute-start.2 = (bf16[256,128]{1,0:T(8,128)(2,1)S(1)}, bf16[256,128]{1,0:T(8,128)(2,1)S(1)}, u32[]{:S(2)}, u32[]{:S(2)}) collective-permute-start(bf16[256,128]{1,0:T(8,128)(2,1)S(1)} %constant_dynamic-slice_fusion), channel_id=1, source_target_pairs={{0,12},{4,0},{8,4},{12,8},{1,13},{5,1},{9,5},{13,9},{2,14},{6,2},{... | collective-permute-start | bytes 196616 | tf_op jit(solution)/shard_map/ppermute | solution.py:9
  6.6 1.0 %collective-permute-start = (bf16[256,128]{1,0:T(8,128)(2,1)S(1)}, bf16[256,128]{1,0:T(8,128)(2,1)S(1)}, u32[]{:S(2)}, u32[]{:S(2)}) collective-permute-start(bf16[256,128]{1,0:T(8,128)(2,1)S(1)} %constant_dynamic-slice_fusion), channel_id=1, source_target_pairs={{0,4},{4,8},{8,12},{12,0},{1,5},{5,9},{9,13},{13,1},{2,6},{6,10},{... | collective-permute-start | bytes 196616 | tf_op jit(solution)/shard_map/ppermute | solution.py:9
  7.6 1.3 %fusion.29 = (bf16[4,1,256,256]{3,2,1,0:T(8,128)(2,1)S(1)}, bf16[4,1,256,256]{3,2,1,0:T(8,128)(2,1)S(1)}) fusion(bf16[4,2,256,256]{3,2,1,0:T(8,128)(2,1)} %bitcast.83), kind=kLoop, calls=%fused_computation.90 | loop fusion | bytes 2097152 | tf_op jit(solution)/shard_map/slice | solution.py:47
  9.0 0.2 collective-permute-done.2
  9.1 4.0 %collective-permute-done.1 = bf16[256,128]{1,0:T(8,128)(2,1)S(1)} collective-permute-done((bf16[256,128]{1,0:T(8,128)(2,1)S(1)}, bf16[256,128]{1,0:T(8,128)(2,1)S(1)}, u32[]{:S(2)}, u32[]{:S(2)}) %collective-permute-start.1) | collective-permute-done | bytes 65568 | tf_op jit(solution)/shard_map/ppermute | solution.py:9
  13.2 0.8 %fusion.25 = (pred[4]{0:T(512)(128)(4,1)S(1)}, pred[4]{0:T(512)(128)(4,1)S(1)}, pred[4]{0:T(512)(128)(4,1)S(1)}, pred[4]{0:T(512)(128)(4,1)S(1)}, pred[4]{0:T(51...) fusion(s32[1,1,4]{2,1,0:T(1,128)} %param.7, ...), kind=kLoop, calls=%fused_computation.86 | loop fusion | flops 88 | bytes 112 | tf_op jit(solution)/shard_map/or | solution.py:48
  14.0 0.2 copy.9
  14.2 0.2 copy.10
  15.5 0.2 convert_reduce_fusion
  15.8 0.8 %convolution_bitcast_fusion = f32[1024,1024]{0,1:T(8,128)S(1)} fusion(bf16[1,1024,256]{2,1,0:T(8,128)(2,1)S(1)} %copy-done, bf16[256,256]{1,0:T(8,128)(2,1)S(1)} %get-tuple-element.31, bf16[256,256]{1,0:T(8,128)(2,1)S(1)} %get-tuple-element.32, bf16[256,256]{1,0:T(8,128)(2,1)S(1)} %get-tuple-element.30, bf16[256,256]{1,0:T(8,128)(2,1)S(1)} %copy-done.1), kind=kOutput, calls=%fused_computation | convolution fusion | flops 538968064 | bytes 5242880 | tf_op jit(solution)/shard_map/dot_general | solution.py:39
  16.5 0.9 %fusion.7 = (bf16[1024,256]{0,1:T(8,128)(2,1)S(1)}, bf16[1024,256]{0,1:T(8,128)(2,1)S(1)}, bf16[1024,256]{0,1:T(8,128)(2,1)S(1)}, bf16[1024,256]{0,1:T(8,128)(2,1)S(1)}) fusion(f32[1024,1024]{0,1:T(8,128)S(1)} %convolution_bitcast_fusion, bf16[1024,256]{0,1:T(8,128)(2,1)S(1)} %copy.9, bf16[1024,256]{0,1:T(8,128)(2,1)S(1)} %copy.10, ...), kind=kLoop, calls=%fused_computation.14 | loop fusion | flops 6291456 | bytes 7352320 | tf_op jit(solution)/shard_map/convert_element_type | solution.py:51
  17.5 0.8 %convolution_bitcast_fusion.1 = f32[256,1024]{1,0:T(8,128)S(1)} fusion(bf16[1,1024,256]{2,1,0:T(8,128)(2,1)S(1)} %copy-done, bf16[1024,256]{0,1:T(8,128)(2,1)S(1)} %get-tuple-element.15, bf16[1024,256]{0,1:T(8,128)(2,1)S(1)} %get-tuple-element.16, bf16[1024,256]{0,1:T(8,128)(2,1)S(1)} %get-tuple-element.17, bf16[1024,256]{0,1:T(8,128)(2,1)S(1)} %get-tuple-element.14), kind=kOutput, calls=%fused_computation.2 | convolution fusion | flops 545259520 | bytes 3670016 | tf_op jit(solution)/shard_map/ik,ij->kj/dot_general | solution.py:53
  18.4 0.6 %collective-permute-start.5 = (f32[1032,128]{1,0:T(8,128)S(1)}, f32[1032,128]{1,0:T(8,128)S(1)}, u32[]{:S(2)}, u32[]{:S(2)}) collective-permute-start(f32[1032,128]{1,0:T(8,128)S(1)} %broadcast_select_fusion), channel_id=1, source_target_pairs={{0,1},{1,0},{2,3},{3,2},{4,5},{5,4},{6,7},{7,6},{8,9},{9,8},{10,11... | collective-permute-start | bytes 1585160 | tf_op jit(solution)/shard_map/ppermute | solution.py:9
  19.0 0.1 convert_reduce_fusion.1
  19.1 0.8 %fusion.13 = f32[1024,256]{1,0:T(8,128)S(1)} fusion(bf16[1024,256]{0,1:T(8,128)(2,1)S(1)} %get-tuple-element.15, bf16[1024,256]{0,1:T(8,128)(2,1)S(1)} %get-tuple-element.16, bf16[1024,256]{0,1:T(8,128)(2,1)S(1)} %get-tuple-element.17, bf16[1024,256]{0,1:T(8,128)(2,1)S(1)} %get-tuple-element.14, bf16[256,256]{1,0:T(8,128)(2,1)S(1)} %get-tuple-element.31, ...), kind=kOutput, calls=%fused_computation.31 | convolution fusion | flops 547356672 | bytes 3670016 | tf_op jit(solution)/shard_map/ij,kj->ik/dot_general | solution.py:54
  20.0 1.6 %collective-permute-start.4 = (f32[520,256]{1,0:T(8,128)S(1)}, f32[520,256]{1,0:T(8,128)S(1)}, u32[]{:S(2)}, u32[]{:S(2)}) collective-permute-start(f32[520,256]{1,0:T(8,128)S(1)} %pad_maximum_fusion.1), channel_id=1, source_target_pairs={{0,2},{2,0},{1,3},{3,1},{4,6},{6,4},{5,7},{7,5},{8,10},{10,8},{9,1... | collective-permute-start | bytes 1597448 | tf_op jit(solution)/shard_map/ppermute | solution.py:9
  21.7 1.9 %collective-permute-start.8 = (f32[264,128]{1,0:T(8,128)S(1)}, f32[264,128]{1,0:T(8,128)S(1)}, u32[]{:S(2)}, u32[]{:S(2)}) collective-permute-start(f32[264,128]{1,0:T(8,128)S(1)} %concatenate.48), channel_id=1, source_target_pairs={{0,12},{4,0},{8,4},{12,8},{1,13},{5,1},{9,5},{13,9},{2,14},{6,2},{... | collective-permute-start | bytes 405512 | tf_op jit(solution)/shard_map/ppermute | solution.py:9
  23.7 1.9 %collective-permute-start.6 = (f32[264,128]{1,0:T(8,128)S(1)}, f32[264,128]{1,0:T(8,128)S(1)}, u32[]{:S(2)}, u32[]{:S(2)}) collective-permute-start(f32[264,128]{1,0:T(8,128)S(1)} %get-tuple-element.37), channel_id=1, source_target_pairs={{0,4},{4,8},{8,12},{12,0},{1,5},{5,9},{9,13},{13,1},{2,6},{6,10},{... | collective-permute-start | bytes 405512 | tf_op jit(solution)/shard_map/ppermute | solution.py:9
  25.6 8.4 %collective-permute-done.4 = f32[520,256]{1,0:T(8,128)S(1)} collective-permute-done((f32[520,256]{1,0:T(8,128)S(1)}, f32[520,256]{1,0:T(8,128)S(1)}, u32[]{:S(2)}, u32[]{:S(2)}) %collective-permute-start.4) | collective-permute-done | bytes 532512 | tf_op jit(solution)/shard_map/ppermute | solution.py:9
  34.1 1.6 %collective-permute-done.7 = f32[264,128]{1,0:T(8,128)S(1)} collective-permute-done((f32[264,128]{1,0:T(8,128)S(1)}, f32[264,128]{1,0:T(8,128)S(1)}, u32[]{:S(2)}, u32[]{:S(2)}) %collective-permute-start.7) | collective-permute-done | bytes 135200 | tf_op jit(solution)/shard_map/ppermute | solution.py:9
  35.8 0.9 %fusion.10 = f32[1,512,256]{2,1,0:T(8,128)} fusion(f32[520,256]{1,0:T(8,128)S(1)} %collective-permute-done.4, f32[2,512,256]{2,1,0:T(8,128)S(1)} %bitcast.85, s32[]{:T(128)S(6)} %select_n.170, f32[256]{0:T(256)S(1)} %bitcast.96, bf16[1,1024,256]{2,1,0:T(8,128)(2,1)S(1)} %copy-done, s32[]{:T(128)S(6)} %select_n.146), kind=kLoop, calls=%fused_computation.22 | loop fusion | flops 524288 | bytes 1836040 | tf_op jit(solution)/shard_map/broadcast_in_dim | solution.py:162
  36.7 0.4 %collective-permute-done.9 = f32[264,128]{1,0:T(8,128)S(1)} collective-permute-done((f32[264,128]{1,0:T(8,128)S(1)}, f32[264,128]{1,0:T(8,128)S(1)}, u32[]{:S(2)}, u32[]{:S(2)}) %collective-permute-start.9) | collective-permute-done | bytes 135200 | tf_op jit(solution)/shard_map/ppermute | solution.py:9
  37.2 0.8 %fusion.16 = f32[256,256]{1,0:T(8,128)} fusion(f32[264,128]{1,0:T(8,128)S(1)} %get-tuple-element.36, f32[264,128]{1,0:T(8,128)S(1)} %get-tuple-element.35, bf16[256,256]{1,0:T(8,128)(2,1)S(1)} %copy-done.1, f32[256]{0:T(256)S(1)} %bitcast.94), kind=kLoop, calls=%fused_computation.37 | loop fusion | flops 262144 | bytes 664576 | tf_op jit(solution)/shard_map/div | solution.py:160
  (61 shorter events, 1.9 us)
Async XLA Ops:
  0.6 15.1 %copy-start.1 = (bf16[256,256]{1,0:T(8,128)(2,1)S(1)}, bf16[256,256]{1,0:T(8,128)(2,1)}, u32[]{:S(2)}) copy-start(bf16[256,256]{1,0:T(8,128)(2,1)} %param.9) | copy-start | bytes 393220
  0.6 14.9 %copy-start = (bf16[1,1024,256]{2,1,0:T(8,128)(2,1)S(1)}, bf16[1,1024,256]{2,1,0:T(8,128)(2,1)}, u32[]{:S(2)}) copy-start(bf16[1,1024,256]{2,1,0:T(8,128)(2,1)} %param.8) | copy-start | bytes 1572868
  1.6 7.5 %collective-permute-start.2 = (bf16[256,128]{1,0:T(8,128)(2,1)S(1)}, bf16[256,128]{1,0:T(8,128)(2,1)S(1)}, u32[]{:S(2)}, u32[]{:S(2)}) collective-permute-start(bf16[256,128]{1,0:T(8,128)(2,1)S(1)} %constant_dynamic-slice_fusion), channel_id=1, source_target_pairs={{0,12},{4,0},{8,4},{12,8},{1,13},{5,1},{9,5},{13,9},{2,14},{6,2},{... | collective-permute-start | bytes 196616 | tf_op jit(solution)/shard_map/ppermute | solution.py:9
  6.6 6.5 %collective-permute-start.1 = (bf16[256,128]{1,0:T(8,128)(2,1)S(1)}, bf16[256,128]{1,0:T(8,128)(2,1)S(1)}, u32[]{:S(2)}, u32[]{:S(2)}) collective-permute-start(bf16[256,128]{1,0:T(8,128)(2,1)S(1)} %constant_dynamic-slice_fusion), channel_id=1, source_target_pairs={{0,8},{4,12},{8,0},{12,4},{1,9},{5,13},{9,1},{13,5},{2,10},{6,14},... | collective-permute-start | bytes 196616 | tf_op jit(solution)/shard_map/ppermute | solution.py:9
  6.6 6.5 %collective-permute-start = (bf16[256,128]{1,0:T(8,128)(2,1)S(1)}, bf16[256,128]{1,0:T(8,128)(2,1)S(1)}, u32[]{:S(2)}, u32[]{:S(2)}) collective-permute-start(bf16[256,128]{1,0:T(8,128)(2,1)S(1)} %constant_dynamic-slice_fusion), channel_id=1, source_target_pairs={{0,4},{4,8},{8,12},{12,0},{1,5},{5,9},{9,13},{13,1},{2,6},{6,10},{... | collective-permute-start | bytes 196616 | tf_op jit(solution)/shard_map/ppermute | solution.py:9
  13.1 2.5 %collective-permute-start.3 = (bf16[3,256,128]{2,1,0:T(8,128)(2,1)S(1)}, bf16[3,256,128]{2,1,0:T(8,128)(2,1)S(1)}, u32[]{:S(2)}, u32[]{:S(2)}) collective-permute-start(bf16[3,256,128]{2,1,0:T(8,128)(2,1)S(1)} %pad_maximum_fusion.5), channel_id=1, source_target_pairs={{0,1},{1,0},{2,3},{3,2},{4,5},{5,4},{6,7},{7,6},{8,9},{9,8},{10,11... | collective-permute-start | bytes 589832 | tf_op jit(solution)/shard_map/ppermute | solution.py:9
  18.4 3.1 %collective-permute-start.5 = (f32[1032,128]{1,0:T(8,128)S(1)}, f32[1032,128]{1,0:T(8,128)S(1)}, u32[]{:S(2)}, u32[]{:S(2)}) collective-permute-start(f32[1032,128]{1,0:T(8,128)S(1)} %broadcast_select_fusion), channel_id=1, source_target_pairs={{0,1},{1,0},{2,3},{3,2},{4,5},{5,4},{6,7},{7,6},{8,9},{9,8},{10,11... | collective-permute-start | bytes 1585160 | tf_op jit(solution)/shard_map/ppermute | solution.py:9
  20.0 14.1 %collective-permute-start.4 = (f32[520,256]{1,0:T(8,128)S(1)}, f32[520,256]{1,0:T(8,128)S(1)}, u32[]{:S(2)}, u32[]{:S(2)}) collective-permute-start(f32[520,256]{1,0:T(8,128)S(1)} %pad_maximum_fusion.1), channel_id=1, source_target_pairs={{0,2},{2,0},{1,3},{3,1},{4,6},{6,4},{5,7},{7,5},{8,10},{10,8},{9,1... | collective-permute-start | bytes 1597448 | tf_op jit(solution)/shard_map/ppermute | solution.py:9
  21.7 12.4 %collective-permute-start.8 = (f32[264,128]{1,0:T(8,128)S(1)}, f32[264,128]{1,0:T(8,128)S(1)}, u32[]{:S(2)}, u32[]{:S(2)}) collective-permute-start(f32[264,128]{1,0:T(8,128)S(1)} %concatenate.48), channel_id=1, source_target_pairs={{0,12},{4,0},{8,4},{12,8},{1,13},{5,1},{9,5},{13,9},{2,14},{6,2},{... | collective-permute-start | bytes 405512 | tf_op jit(solution)/shard_map/ppermute | solution.py:9
  23.7 12.0 %collective-permute-start.7 = (f32[264,128]{1,0:T(8,128)S(1)}, f32[264,128]{1,0:T(8,128)S(1)}, u32[]{:S(2)}, u32[]{:S(2)}) collective-permute-start(f32[264,128]{1,0:T(8,128)S(1)} %get-tuple-element.38), channel_id=1, source_target_pairs={{0,8},{4,12},{8,0},{12,4},{1,9},{5,13},{9,1},{13,5},{2,10},{6,14},... | collective-permute-start | bytes 405512 | tf_op jit(solution)/shard_map/ppermute | solution.py:9
  23.7 11.9 %collective-permute-start.6 = (f32[264,128]{1,0:T(8,128)S(1)}, f32[264,128]{1,0:T(8,128)S(1)}, u32[]{:S(2)}, u32[]{:S(2)}) collective-permute-start(f32[264,128]{1,0:T(8,128)S(1)} %get-tuple-element.37), channel_id=1, source_target_pairs={{0,4},{4,8},{8,12},{12,0},{1,5},{5,9},{9,13},{13,1},{2,6},{6,10},{... | collective-permute-start | bytes 405512 | tf_op jit(solution)/shard_map/ppermute | solution.py:9
  35.7 1.4 %collective-permute-start.9 = (f32[264,128]{1,0:T(8,128)S(1)}, f32[264,128]{1,0:T(8,128)S(1)}, u32[]{:S(2)}, u32[]{:S(2)}) collective-permute-start(f32[264,128]{1,0:T(8,128)S(1)} %pad_maximum_fusion.8), channel_id=1, source_target_pairs={{0,1},{1,0},{2,3},{3,2},{4,5},{5,4},{6,7},{7,6},{8,9},{9,8},{10,11... | collective-permute-start | bytes 405512 | tf_op jit(solution)/shard_map/ppermute | solution.py:9

commit v6 on v5

--- a/solution.py
+++ b/solution.py
@@ -126,9 +126,11 @@
     got_h = h_rows
     for d in range(1, n_col):
         chunk = lax.dynamic_index_in_dim(chunks, (col_index + d) % n_col, 0, keepdims=False)
-        message = shifted(jnp.concatenate([chunk, h_rows]), "col", d)
-        mine_w = mine_w + message[:share]
-        got_h = got_h + message[share:]
+        cut = share // 2
+        first = shifted(chunk[:cut], "col", d)
+        second = shifted(jnp.concatenate([chunk[cut:], h_rows]), "col", d)
+        mine_w = mine_w + jnp.concatenate([first, second[:share - cut]])
+        got_h = got_h + second[share - cut:]
     h_total = from_rows(got_h, rank)
 
     w_rows_sum = as_rows(w_sum, width)

time: 38.2 us -> 48.1 us (1.26)
  waiting for transfers between devices: 14.6 us -> 21.4 us
  other arithmetic: 4.1 us -> 5.91 us
  local copies, waits for them, and re-layouts: 3.81 us -> 4.52 us
  starting transfers between devices: 12.2 us -> 12.7 us
    ppermute x10 -> x11, waiting for transfers between devices: 14.6 us -> 21.4 us  [shifted(): lax.ppermute(value, axis, [(i, (i + by) % length) for i in range(length)])]
    add x1, other arithmetic: 0.09 us -> 1.12 us  [body(): reduced = reduced + shifted(piece_message(k), 'sub', k)]
    broadcast_in_dim x1 -> x0, other arithmetic: 0.89 us -> none  [body(): w_new = (w_part * mine_w / h_total[None, :])[None]]
    div x0 -> x1, other arithmetic: none -> 0.89 us  [body(): w_new = (w_part * mine_w / h_total[None, :])[None]]
    select_n x1, other arithmetic: 0.06 us -> 0.87 us  [piece_message(): chosen = jnp.where(want == p, messages[p], chosen)]
    slice x1 -> x2, local copies, waits for them, and re-layouts: 0.01 us -> 0.74 us  [the longest x1 0.74 us: body(): first = shifted(chunk[:cut], 'col', d)]
    ppermute x10 -> x11, starting transfers between devices: 12.2 us -> 12.7 us  [shifted(): lax.ppermute(value, axis, [(i, (i + by) % length) for i in range(length)])]
  transfers between devices with their start and end apart: 10 -> 11, of which waited for: 5 -> 6; matrix products, arithmetic and copies ran while one was open for 15% -> 14% of each run, Pallas kernels for 0% -> 0%
where the time goes in v6:
time: 48.1 us; the launch traced here: 47.9 us
  waiting for transfers between devices  21.4 us (44%)
  starting transfers between devices  12.7 us (26%)
  other arithmetic  5.91 us (12%)
  local copies, waits for them, and re-layouts  4.52 us (9%)
  matrix products  2.27 us (5%)
  between operations  1.01 us (2%)
    ppermute x11, waiting for transfers between devices, shifted(): lax.ppermute(value, axis, [(i, (i + by) % length) for i in range(length)])  21.4 us
    ppermute x11, starting transfers between devices, shifted(): lax.ppermute(value, axis, [(i, (i + by) % length) for i in range(length)])  12.7 us
    slice x1, local copies, waits for them, and re-layouts, dense_terms(): a_d = jnp.where(match[:, None, None], values[:, slot], a_d)  1.27 us
    add x1, other arithmetic, body(): reduced = reduced + shifted(piece_message(k), 'sub', k)  1.12 us
  transfers between devices with their start and end apart: 11, of which 6 were waited for; matrix products, arithmetic and copies ran while one was open for 14% of the time, Pallas kernels for 0%

profile of v6, /device:TPU:0, one launch (start us, length us, event | category | flops | bytes accessed | tf_op | source)
XLA Modules:
  0.0 47.9 jit_solution(15446389343368851205)
XLA Ops:
  0.7 0.9 %constant_dynamic-slice_fusion = bf16[256,128]{1,0:T(8,128)(2,1)S(1)} fusion(bf16[256,256]{1,0:T(8,128)(2,1)} %param.9, s32[]{:T(128)S(6)} %select_n.152), kind=kLoop, calls=%fused_computation.79 | loop fusion | bytes 131076 | tf_op jit(solution)/shard_map/dynamic_slice | solution.py:109
  1.6 5.0 %collective-permute-start.2 = (bf16[256,128]{1,0:T(8,128)(2,1)S(1)}, bf16[256,128]{1,0:T(8,128)(2,1)S(1)}, u32[]{:S(2)}, u32[]{:S(2)}) collective-permute-start(bf16[256,128]{1,0:T(8,128)(2,1)S(1)} %constant_dynamic-slice_fusion), channel_id=1, source_target_pairs={{0,12},{4,0},{8,4},{12,8},{1,13},{5,1},{9,5},{13,9},{2,14},{6,2},{... | collective-permute-start | bytes 196616 | tf_op jit(solution)/shard_map/ppermute | solution.py:9
  6.6 1.0 %collective-permute-start = (bf16[256,128]{1,0:T(8,128)(2,1)S(1)}, bf16[256,128]{1,0:T(8,128)(2,1)S(1)}, u32[]{:S(2)}, u32[]{:S(2)}) collective-permute-start(bf16[256,128]{1,0:T(8,128)(2,1)S(1)} %constant_dynamic-slice_fusion), channel_id=1, source_target_pairs={{0,4},{4,8},{8,12},{12,0},{1,5},{5,9},{9,13},{13,1},{2,6},{6,10},{... | collective-permute-start | bytes 196616 | tf_op jit(solution)/shard_map/ppermute | solution.py:9
  7.6 1.3 %fusion.28 = (bf16[4,1,256,256]{3,2,1,0:T(8,128)(2,1)S(1)}, bf16[4,1,256,256]{3,2,1,0:T(8,128)(2,1)S(1)}) fusion(bf16[4,2,256,256]{3,2,1,0:T(8,128)(2,1)} %bitcast.81), kind=kLoop, calls=%fused_computation.91 | loop fusion | bytes 2097152 | tf_op jit(solution)/shard_map/slice | solution.py:47
  9.1 4.0 %collective-permute-done.1 = bf16[256,128]{1,0:T(8,128)(2,1)S(1)} collective-permute-done((bf16[256,128]{1,0:T(8,128)(2,1)S(1)}, bf16[256,128]{1,0:T(8,128)(2,1)S(1)}, u32[]{:S(2)}, u32[]{:S(2)}) %collective-permute-start.1) | collective-permute-done | bytes 65568 | tf_op jit(solution)/shard_map/ppermute | solution.py:9
  13.2 0.8 %fusion.24 = (pred[4]{0:T(512)(128)(4,1)S(1)}, pred[4]{0:T(512)(128)(4,1)S(1)}, pred[4]{0:T(512)(128)(4,1)S(1)}, pred[4]{0:T(512)(128)(4,1)S(1)}, pred[4]{0:T(51...) fusion(s32[1,1,4]{2,1,0:T(1,128)} %param.7, ...), kind=kLoop, calls=%fused_computation.87 | loop fusion | flops 88 | bytes 112 | tf_op jit(solution)/shard_map/or | solution.py:48
  15.8 0.8 %convolution_bitcast_fusion = f32[1024,1024]{0,1:T(8,128)S(1)} fusion(bf16[1,1024,256]{2,1,0:T(8,128)(2,1)S(1)} %copy-done, bf16[256,256]{1,0:T(8,128)(2,1)S(1)} %get-tuple-element.33, bf16[256,256]{1,0:T(8,128)(2,1)S(1)} %get-tuple-element.34, bf16[256,256]{1,0:T(8,128)(2,1)S(1)} %get-tuple-element.32, bf16[256,256]{1,0:T(8,128)(2,1)S(1)} %copy-done.1), kind=kOutput, calls=%fused_computation | convolution fusion | flops 538968064 | bytes 5242880 | tf_op jit(solution)/shard_map/dot_general | solution.py:39
  16.5 0.9 %fusion.7 = (bf16[1024,256]{0,1:T(8,128)(2,1)S(1)}, bf16[1024,256]{0,1:T(8,128)(2,1)S(1)}, bf16[1024,256]{0,1:T(8,128)(2,1)S(1)}, bf16[1024,256]{0,1:T(8,128)(2,1)S(1)}) fusion(f32[1024,1024]{0,1:T(8,128)S(1)} %convolution_bitcast_fusion, bf16[1024,256]{0,1:T(8,128)(2,1)S(1)} %copy.9, bf16[1024,256]{0,1:T(8,128)(2,1)S(1)} %copy.10, ...), kind=kLoop, calls=%fused_computation.14 | loop fusion | flops 6291456 | bytes 7352320 | tf_op jit(solution)/shard_map/convert_element_type | solution.py:51
  17.5 0.8 %fusion.12 = f32[1024,256]{1,0:T(8,128)S(1)} fusion(bf16[1024,256]{0,1:T(8,128)(2,1)S(1)} %get-tuple-element.15, bf16[1024,256]{0,1:T(8,128)(2,1)S(1)} %get-tuple-element.16, bf16[1024,256]{0,1:T(8,128)(2,1)S(1)} %get-tuple-element.17, bf16[1024,256]{0,1:T(8,128)(2,1)S(1)} %get-tuple-element.14, bf16[256,256]{1,0:T(8,128)(2,1)S(1)} %get-tuple-element.33, ...), kind=kOutput, calls=%fused_computation.28 | convolution fusion | flops 547356672 | bytes 3670016 | tf_op jit(solution)/shard_map/ij,kj->ik/dot_general | solution.py:54
  18.2 0.8 %convolution_bitcast_fusion.1 = f32[256,1024]{1,0:T(8,128)S(1)} fusion(bf16[1,1024,256]{2,1,0:T(8,128)(2,1)S(1)} %copy-done, bf16[1024,256]{0,1:T(8,128)(2,1)S(1)} %get-tuple-element.15, bf16[1024,256]{0,1:T(8,128)(2,1)S(1)} %get-tuple-element.16, bf16[1024,256]{0,1:T(8,128)(2,1)S(1)} %get-tuple-element.17, bf16[1024,256]{0,1:T(8,128)(2,1)S(1)} %get-tuple-element.14), kind=kOutput, calls=%fused_computation.2 | convolution fusion | flops 545259520 | bytes 3670016 | tf_op jit(solution)/shard_map/ik,ij->kj/dot_general | solution.py:53
  19.2 0.9 %broadcast_select_fusion = f32[1032,128]{1,0:T(8,128)} fusion(f32[1032,128]{1,0:T(8,128)S(1)} %get-tuple-element.51, f32[1032,128]{1,0:T(8,128)S(1)} %get-tuple-element.50, pred[]{:T(512)S(6)} %eq.166), kind=kLoop, calls=%fused_computation.32 | loop fusion | flops 132096 | bytes 1585153 | tf_op jit(solution)/shard_map/jit(_where)/select_n | solution.py:145
  20.1 0.5 %collective-permute-start.6 = (f32[1032,128]{1,0:T(8,128)}, f32[1032,128]{1,0:T(8,128)}, u32[]{:S(2)}, u32[]{:S(2)}) collective-permute-start(f32[1032,128]{1,0:T(8,128)} %broadcast_select_fusion), channel_id=1, source_target_pairs={{0,1},{1,0},{2,3},{3,2},{4,5},{5,4},{6,7},{7,6},{8,9},{9,8},{10,11... | collective-permute-start | bytes 1585160 | tf_op jit(solution)/shard_map/ppermute | solution.py:9
  20.6 0.7 %dynamic-slice_bitcast_fusion.1 = (f32[256,256]{1,0:T(8,128)}, f32[256,256]{1,0:T(8,128)S(1)}) fusion(f32[2,512,256]{2,1,0:T(8,128)S(1)} %bitcast.82, s32[]{:T(128)S(6)} %select_n.172, s32[]{:T(128)S(6)} %add.106), kind=kLoop, calls=%fused_computation.38 | loop fusion | bytes 1048584 | tf_op jit(solution)/shard_map/slice | solution.py:130
  21.4 1.6 %collective-permute-start.5 = (f32[264,256]{1,0:T(8,128)S(1)}, f32[264,256]{1,0:T(8,128)S(1)}, u32[]{:S(2)}, u32[]{:S(2)}) collective-permute-start(f32[264,256]{1,0:T(8,128)S(1)} %pad_maximum_fusion.4), channel_id=1, source_target_pairs={{0,2},{2,0},{1,3},{3,1},{4,6},{6,4},{5,7},{7,5},{8,10},{10,8},{9,1... | collective-permute-start | bytes 811016 | tf_op jit(solution)/shard_map/ppermute | solution.py:9
  22.9 0.5 %collective-permute-start.4 = (f32[256,256]{1,0:T(8,128)}, f32[256,256]{1,0:T(8,128)S(1)}, u32[]{:S(2)}, u32[]{:S(2)}) collective-permute-start(f32[256,256]{1,0:T(8,128)} %get-tuple-element.26), channel_id=1, source_target_pairs={{0,2},{2,0},{1,3},{3,1},{4,6},{6,4},{5,7},{7,5},{8,10},{10,8},{9,1... | collective-permute-start | bytes 786440 | tf_op jit(solution)/shard_map/ppermute | solution.py:9
  23.5 7.3 %collective-permute-done.5 = f32[264,256]{1,0:T(8,128)S(1)} collective-permute-done((f32[264,256]{1,0:T(8,128)S(1)}, f32[264,256]{1,0:T(8,128)S(1)}, u32[]{:S(2)}, u32[]{:S(2)}) %collective-permute-start.5) | collective-permute-done | bytes 270368 | tf_op jit(solution)/shard_map/ppermute | solution.py:9
  30.8 1.1 %select_add_fusion = f32[1032,128]{1,0:T(8,128)S(1)} fusion(f32[1032,128]{1,0:T(8,128)} %collective-permute-done.6, f32[1032,128]{1,0:T(8,128)S(1)} %get-tuple-element.51, f32[1032,128]{1,0:T(8,128)S(1)} %get-tuple-element.50, pred[]{:T(512)S(6)} %eq.149), kind=kLoop, calls=%fused_computation.17 | loop fusion | flops 264192 | bytes 2113537 | tf_op jit(solution)/shard_map/add | solution.py:149
  32.0 1.9 %collective-permute-start.9 = (f32[264,128]{1,0:T(8,128)S(1)}, f32[264,128]{1,0:T(8,128)S(1)}, u32[]{:S(2)}, u32[]{:S(2)}) collective-permute-start(f32[264,128]{1,0:T(8,128)S(1)} %concatenate.59), channel_id=1, source_target_pairs={{0,12},{4,0},{8,4},{12,8},{1,13},{5,1},{9,5},{13,9},{2,14},{6,2},{... | collective-permute-start | bytes 405512 | tf_op jit(solution)/shard_map/ppermute | solution.py:9
  34.0 1.9 %collective-permute-start.7 = (f32[264,128]{1,0:T(8,128)S(1)}, f32[264,128]{1,0:T(8,128)S(1)}, u32[]{:S(2)}, u32[]{:S(2)}) collective-permute-start(f32[264,128]{1,0:T(8,128)S(1)} %get-tuple-element.39), channel_id=1, source_target_pairs={{0,4},{4,8},{8,12},{12,0},{1,5},{5,9},{9,13},{13,1},{2,6},{6,10},{... | collective-permute-start | bytes 405512 | tf_op jit(solution)/shard_map/ppermute | solution.py:9
  35.9 2.0 %collective-permute-done.9 = f32[264,128]{1,0:T(8,128)S(1)} collective-permute-done((f32[264,128]{1,0:T(8,128)S(1)}, f32[264,128]{1,0:T(8,128)S(1)}, u32[]{:S(2)}, u32[]{:S(2)}) %collective-permute-start.9) | collective-permute-done | bytes 135200 | tf_op jit(solution)/shard_map/ppermute | solution.py:9
  38.0 7.5 %collective-permute-done.8 = f32[264,128]{1,0:T(8,128)S(1)} collective-permute-done((f32[264,128]{1,0:T(8,128)S(1)}, f32[264,128]{1,0:T(8,128)S(1)}, u32[]{:S(2)}, u32[]{:S(2)}) %collective-permute-start.8) | collective-permute-done | bytes 135200 | tf_op jit(solution)/shard_map/ppermute | solution.py:9
  45.7 0.9 %fusion.9 = f32[1,512,256]{2,1,0:T(8,128)} fusion(f32[1,256,256]{2,1,0:T(8,128)S(1)} %slice_bitcast_fusion, f32[1,256,256]{2,1,0:T(8,128)S(1)} %bitcast.90, f32[2,512,256]{2,1,0:T(8,128)S(1)} %bitcast.83, s32[]{:T(128)S(6)} %select_n.170, f32[256]{0:T(256)S(1)} %bitcast.95, bf16[1,1024,256]{2,1,0:T(8,128)(2,1)S(1)} %copy-done, s32[]{:T(128)S(6)} %select_n.146), kind=kLoop, calls=%fused_computation.21 | loop fusion | flops 655360 | bytes 1836040 | tf_op jit(solution)/shard_map/div | solution.py:164
  46.6 0.4 collective-permute-done.10
  47.0 0.8 %fusion.15 = f32[256,256]{1,0:T(8,128)} fusion(f32[264,128]{1,0:T(8,128)S(1)} %get-tuple-element.38, f32[264,128]{1,0:T(8,128)S(1)} %get-tuple-element.37, bf16[256,256]{1,0:T(8,128)(2,1)S(1)} %copy-done.1, f32[256]{0:T(256)S(1)} %bitcast.93), kind=kLoop, calls=%fused_computation.35 | loop fusion | flops 262144 | bytes 664576 | tf_op jit(solution)/shard_map/div | solution.py:162
  (64 shorter events, 2.5 us)
Async XLA Ops:
  0.6 15.1 %copy-start.1 = (bf16[256,256]{1,0:T(8,128)(2,1)S(1)}, bf16[256,256]{1,0:T(8,128)(2,1)}, u32[]{:S(2)}) copy-start(bf16[256,256]{1,0:T(8,128)(2,1)} %param.9) | copy-start | bytes 393220
  0.6 14.9 %copy-start = (bf16[1,1024,256]{2,1,0:T(8,128)(2,1)S(1)}, bf16[1,1024,256]{2,1,0:T(8,128)(2,1)}, u32[]{:S(2)}) copy-start(bf16[1,1024,256]{2,1,0:T(8,128)(2,1)} %param.8) | copy-start | bytes 1572868
  1.6 7.5 %collective-permute-start.2 = (bf16[256,128]{1,0:T(8,128)(2,1)S(1)}, bf16[256,128]{1,0:T(8,128)(2,1)S(1)}, u32[]{:S(2)}, u32[]{:S(2)}) collective-permute-start(bf16[256,128]{1,0:T(8,128)(2,1)S(1)} %constant_dynamic-slice_fusion), channel_id=1, source_target_pairs={{0,12},{4,0},{8,4},{12,8},{1,13},{5,1},{9,5},{13,9},{2,14},{6,2},{... | collective-permute-start | bytes 196616 | tf_op jit(solution)/shard_map/ppermute | solution.py:9
  6.6 6.5 %collective-permute-start.1 = (bf16[256,128]{1,0:T(8,128)(2,1)S(1)}, bf16[256,128]{1,0:T(8,128)(2,1)S(1)}, u32[]{:S(2)}, u32[]{:S(2)}) collective-permute-start(bf16[256,128]{1,0:T(8,128)(2,1)S(1)} %constant_dynamic-slice_fusion), channel_id=1, source_target_pairs={{0,8},{4,12},{8,0},{12,4},{1,9},{5,13},{9,1},{13,5},{2,10},{6,14},... | collective-permute-start | bytes 196616 | tf_op jit(solution)/shard_map/ppermute | solution.py:9
  6.6 6.5 %collective-permute-start = (bf16[256,128]{1,0:T(8,128)(2,1)S(1)}, bf16[256,128]{1,0:T(8,128)(2,1)S(1)}, u32[]{:S(2)}, u32[]{:S(2)}) collective-permute-start(bf16[256,128]{1,0:T(8,128)(2,1)S(1)} %constant_dynamic-slice_fusion), channel_id=1, source_target_pairs={{0,4},{4,8},{8,12},{12,0},{1,5},{5,9},{9,13},{13,1},{2,6},{6,10},{... | collective-permute-start | bytes 196616 | tf_op jit(solution)/shard_map/ppermute | solution.py:9
  13.1 2.5 %collective-permute-start.3 = (bf16[3,256,128]{2,1,0:T(8,128)(2,1)S(1)}, bf16[3,256,128]{2,1,0:T(8,128)(2,1)S(1)}, u32[]{:S(2)}, u32[]{:S(2)}) collective-permute-start(bf16[3,256,128]{2,1,0:T(8,128)(2,1)S(1)} %pad_maximum_fusion.5), channel_id=1, source_target_pairs={{0,1},{1,0},{2,3},{3,2},{4,5},{5,4},{6,7},{7,6},{8,9},{9,8},{10,11... | collective-permute-start | bytes 589832 | tf_op jit(solution)/shard_map/ppermute | solution.py:9
  20.1 10.7 %collective-permute-start.6 = (f32[1032,128]{1,0:T(8,128)}, f32[1032,128]{1,0:T(8,128)}, u32[]{:S(2)}, u32[]{:S(2)}) collective-permute-start(f32[1032,128]{1,0:T(8,128)} %broadcast_select_fusion), channel_id=1, source_target_pairs={{0,1},{1,0},{2,3},{3,2},{4,5},{5,4},{6,7},{7,6},{8,9},{9,8},{10,11... | collective-permute-start | bytes 1585160 | tf_op jit(solution)/shard_map/ppermute | solution.py:9
  21.4 9.4 %collective-permute-start.5 = (f32[264,256]{1,0:T(8,128)S(1)}, f32[264,256]{1,0:T(8,128)S(1)}, u32[]{:S(2)}, u32[]{:S(2)}) collective-permute-start(f32[264,256]{1,0:T(8,128)S(1)} %pad_maximum_fusion.4), channel_id=1, source_target_pairs={{0,2},{2,0},{1,3},{3,1},{4,6},{6,4},{5,7},{7,5},{8,10},{10,8},{9,1... | collective-permute-start | bytes 811016 | tf_op jit(solution)/shard_map/ppermute | solution.py:9
  22.9 22.7 %collective-permute-start.4 = (f32[256,256]{1,0:T(8,128)}, f32[256,256]{1,0:T(8,128)S(1)}, u32[]{:S(2)}, u32[]{:S(2)}) collective-permute-start(f32[256,256]{1,0:T(8,128)} %get-tuple-element.26), channel_id=1, source_target_pairs={{0,2},{2,0},{1,3},{3,1},{4,6},{6,4},{5,7},{7,5},{8,10},{10,8},{9,1... | collective-permute-start | bytes 786440 | tf_op jit(solution)/shard_map/ppermute | solution.py:9
  32.0 6.0 %collective-permute-start.9 = (f32[264,128]{1,0:T(8,128)S(1)}, f32[264,128]{1,0:T(8,128)S(1)}, u32[]{:S(2)}, u32[]{:S(2)}) collective-permute-start(f32[264,128]{1,0:T(8,128)S(1)} %concatenate.59), channel_id=1, source_target_pairs={{0,12},{4,0},{8,4},{12,8},{1,13},{5,1},{9,5},{13,9},{2,14},{6,2},{... | collective-permute-start | bytes 405512 | tf_op jit(solution)/shard_map/ppermute | solution.py:9
  34.0 11.5 %collective-permute-start.8 = (f32[264,128]{1,0:T(8,128)S(1)}, f32[264,128]{1,0:T(8,128)S(1)}, u32[]{:S(2)}, u32[]{:S(2)}) collective-permute-start(f32[264,128]{1,0:T(8,128)S(1)} %get-tuple-element.40), channel_id=1, source_target_pairs={{0,8},{4,12},{8,0},{12,4},{1,9},{5,13},{9,1},{13,5},{2,10},{6,14},... | collective-permute-start | bytes 405512 | tf_op jit(solution)/shard_map/ppermute | solution.py:9
  34.0 11.5 %collective-permute-start.7 = (f32[264,128]{1,0:T(8,128)S(1)}, f32[264,128]{1,0:T(8,128)S(1)}, u32[]{:S(2)}, u32[]{:S(2)}) collective-permute-start(f32[264,128]{1,0:T(8,128)S(1)} %get-tuple-element.39), channel_id=1, source_target_pairs={{0,4},{4,8},{8,12},{12,0},{1,5},{5,9},{9,13},{13,1},{2,6},{6,10},{... | collective-permute-start | bytes 405512 | tf_op jit(solution)/shard_map/ppermute | solution.py:9
  45.6 1.4 %collective-permute-start.10 = (f32[264,128]{1,0:T(8,128)S(1)}, f32[264,128]{1,0:T(8,128)S(1)}, u32[]{:S(2)}, u32[]{:S(2)}) collective-permute-start(f32[264,128]{1,0:T(8,128)S(1)} %pad_maximum_fusion.8), channel_id=1, source_target_pairs={{0,1},{1,0},{2,3},{3,2},{4,5},{5,4},{6,7},{7,6},{8,9},{9,8},{10,11... | collective-permute-start | bytes 405512 | tf_op jit(solution)/shard_map/ppermute | solution.py:9

commit v7 on v5

--- a/solution.py
+++ b/solution.py
@@ -146,13 +146,13 @@
     for k in range(1, n_sub):
         reduced = reduced + shifted(piece_message(k), "sub", k)
     extra = reduced[n_row * rank:]
-    mine_h = reduced[:rank]
-    got_w = extra
-    for d in range(1, n_row):
-        message = shifted(jnp.concatenate([reduced[d * rank:(d + 1) * rank], extra]), "row", d)
-        mine_h = mine_h + message[:rank]
-        got_w = got_w + message[rank:]
-    final = jnp.concatenate([mine_h, got_w])
+    outgoing = jnp.stack(
+        [jnp.concatenate([reduced[e * rank:(e + 1) * rank], extra]) for e in range(n_row)]
+    )
+    doubled = jnp.concatenate([outgoing, outgoing])
+    outgoing = lax.dynamic_slice_in_dim(doubled, n_row - row_index, n_row, 0)
+    incoming = lax.all_to_all(outgoing, "row", 0, 0, tiled=True)
+    final = jnp.sum(incoming, axis=0)
     total = assemble([final] + [shifted(final, "sub", k) for k in range(1, n_sub)], sub_index, n_sub, 1)
     numer_h = total[:rank]
     w_total = from_rows(total[rank:], rank)

time: 38.2 us -> 45.8 us (1.20)
  waiting for transfers between devices: 14.6 us -> 17.7 us
  local copies, waits for them, and re-layouts: 3.81 us -> 6.06 us
  matrix products: 2.27 us -> 3.65 us
  other arithmetic: 4.1 us -> 5.18 us
  starting transfers between devices: 12.2 us -> 11.7 us
    ppermute x10 -> x7, starting transfers between devices: 12.2 us -> 8.23 us  [shifted(): lax.ppermute(value, axis, [(i, (i + by) % length) for i in range(length)])]
    all_to_all x0 -> x1, starting transfers between devices: none -> 3.47 us  [body(): incoming = lax.all_to_all(outgoing, 'row', 0, 0, tiled=True)]
    ppermute x10 -> x7, waiting for transfers between devices: 14.6 us -> 16.6 us  [shifted(): lax.ppermute(value, axis, [(i, (i + by) % length) for i in range(length)])]
    dot_general x1, matrix products: 0.76 us -> 2.12 us  [dense_terms(): jnp.einsum('ij,kj->ik', ratios, h_all, preferred_element_type=jnp.float32)]
    all_to_all x0 -> x1, waiting for transfers between devices: none -> 1.12 us  [body(): incoming = lax.all_to_all(outgoing, 'row', 0, 0, tiled=True)]
    broadcast_in_dim x1, other arithmetic: 0.89 us -> 1.93 us  [body(): w_new = (w_part * mine_w / h_total[None, :])[None]]
    dynamic_slice x0 -> x1, local copies, waits for them, and re-layouts: none -> 0.84 us  [body(): outgoing = lax.dynamic_slice_in_dim(doubled, n_row - row_index, n_row, 0)]
    select_n x1, other arithmetic: 0.06 us -> 0.86 us  [piece_message(): chosen = jnp.where(want == p, messages[p], chosen)]
  transfers between devices with their start and end apart: 10 -> 8, of which waited for: 5 -> 4; matrix products, arithmetic and copies ran while one was open for 15% -> 17% of each run, Pallas kernels for 0% -> 0%
where the time goes in v7:
time: 45.8 us; the launch traced here: 45.4 us
  waiting for transfers between devices  17.7 us (39%)
  starting transfers between devices  11.7 us (26%)
  local copies, waits for them, and re-layouts  6.06 us (13%)
  other arithmetic  5.18 us (11%)
  matrix products  3.65 us (8%)
  between operations  1.11 us (2%)
    ppermute x7, waiting for transfers between devices, shifted(): lax.ppermute(value, axis, [(i, (i + by) % length) for i in range(length)])  16.6 us
    ppermute x7, starting transfers between devices, shifted(): lax.ppermute(value, axis, [(i, (i + by) % length) for i in range(length)])  8.23 us
    all_to_all x1, starting transfers between devices, body(): incoming = lax.all_to_all(outgoing, 'row', 0, 0, tiled=True)  3.47 us
    dot_general x1, matrix products, dense_terms(): jnp.einsum('ij,kj->ik', ratios, h_all, preferred_element_type=jnp.float32)  2.12 us
    broadcast_in_dim x1, other arithmetic, body(): w_new = (w_part * mine_w / h_total[None, :])[None]  1.93 us
    slice x1, local copies, waits for them, and re-layouts, dense_terms(): a_d = jnp.where(match[:, None, None], values[:, slot], a_d)  1.33 us
    all_to_all x1, waiting for transfers between devices, body(): incoming = lax.all_to_all(outgoing, 'row', 0, 0, tiled=True)  1.12 us
  transfers between devices with their start and end apart: 8, of which 4 were waited for; matrix products, arithmetic and copies ran while one was open for 17% of the time, Pallas kernels for 0%

profile of v7, /device:TPU:0, one launch (start us, length us, event | category | flops | bytes accessed | tf_op | source)
XLA Modules:
  0.0 45.4 jit_solution(16135801465978130298)
XLA Ops:
  0.7 0.9 %constant_dynamic-slice_fusion = bf16[256,128]{1,0:T(8,128)(2,1)S(1)} fusion(bf16[256,256]{1,0:T(8,128)(2,1)} %param.9, s32[]{:T(128)S(6)} %select_n.155), kind=kLoop, calls=%fused_computation.84 | loop fusion | bytes 131076 | tf_op jit(solution)/shard_map/dynamic_slice | solution.py:109
  1.5 5.0 %collective-permute-start.2 = (bf16[256,128]{1,0:T(8,128)(2,1)S(1)}, bf16[256,128]{1,0:T(8,128)(2,1)S(1)}, u32[]{:S(2)}, u32[]{:S(2)}) collective-permute-start(bf16[256,128]{1,0:T(8,128)(2,1)S(1)} %constant_dynamic-slice_fusion), channel_id=1, source_target_pairs={{0,12},{4,0},{8,4},{12,8},{1,13},{5,1},{9,5},{13,9},{2,14},{6,2},{... | collective-permute-start | bytes 196616 | tf_op jit(solution)/shard_map/ppermute | solution.py:9
  6.6 1.0 %collective-permute-start = (bf16[256,128]{1,0:T(8,128)(2,1)S(1)}, bf16[256,128]{1,0:T(8,128)(2,1)S(1)}, u32[]{:S(2)}, u32[]{:S(2)}) collective-permute-start(bf16[256,128]{1,0:T(8,128)(2,1)S(1)} %constant_dynamic-slice_fusion), channel_id=1, source_target_pairs={{0,4},{4,8},{8,12},{12,0},{1,5},{5,9},{9,13},{13,1},{2,6},{6,10},{... | collective-permute-start | bytes 196616 | tf_op jit(solution)/shard_map/ppermute | solution.py:9
  7.6 1.3 %fusion.40 = (bf16[4,1,256,256]{3,2,1,0:T(8,128)(2,1)S(1)}, bf16[4,1,256,256]{3,2,1,0:T(8,128)(2,1)S(1)}) fusion(bf16[4,2,256,256]{3,2,1,0:T(8,128)(2,1)} %bitcast.107), kind=kLoop, calls=%fused_computation.97 | loop fusion | bytes 2097152 | tf_op jit(solution)/shard_map/slice | solution.py:47
  9.1 4.0 %collective-permute-done.1 = bf16[256,128]{1,0:T(8,128)(2,1)S(1)} collective-permute-done((bf16[256,128]{1,0:T(8,128)(2,1)S(1)}, bf16[256,128]{1,0:T(8,128)(2,1)S(1)}, u32[]{:S(2)}, u32[]{:S(2)}) %collective-permute-start.1) | collective-permute-done | bytes 65568 | tf_op jit(solution)/shard_map/ppermute | solution.py:9
  13.2 0.2 copy.9
  13.4 0.2 copy.10
  14.7 0.2 convert_reduce_fusion
  15.0 0.8 %convolution_bitcast_fusion = f32[1024,1024]{0,1:T(8,128)S(1)} fusion(bf16[1,1024,256]{2,1,0:T(8,128)(2,1)S(1)} %copy-done, bf16[256,256]{1,0:T(8,128)(2,1)S(1)} %get-tuple-element.32, bf16[256,256]{1,0:T(8,128)(2,1)S(1)} %get-tuple-element.33, bf16[256,256]{1,0:T(8,128)(2,1)S(1)} %get-tuple-element.31, bf16[256,256]{1,0:T(8,128)(2,1)S(1)} %copy-done.1), kind=kOutput, calls=%fused_computation | convolution fusion | flops 538968064 | bytes 5242880 | tf_op jit(solution)/shard_map/dot_general | solution.py:39
  15.7 0.9 %fusion.7 = (bf16[1024,256]{0,1:T(8,128)(2,1)S(1)}, bf16[1024,256]{0,1:T(8,128)(2,1)S(1)}, bf16[1024,256]{0,1:T(8,128)(2,1)S(1)}, bf16[1024,256]{0,1:T(8,128)(2,1)S(1)}) fusion(f32[1024,1024]{0,1:T(8,128)S(1)} %convolution_bitcast_fusion, bf16[1024,256]{0,1:T(8,128)(2,1)S(1)} %copy.9, bf16[1024,256]{0,1:T(8,128)(2,1)S(1)} %copy.10, ...), kind=kLoop, calls=%fused_computation.14 | loop fusion | flops 6291456 | bytes 7352320 | tf_op jit(solution)/shard_map/convert_element_type | solution.py:51
  16.7 0.8 %convolution_bitcast_fusion.1 = f32[256,1024]{1,0:T(8,128)S(1)} fusion(bf16[1,1024,256]{2,1,0:T(8,128)(2,1)S(1)} %copy-done, bf16[1024,256]{0,1:T(8,128)(2,1)S(1)} %get-tuple-element.15, bf16[1024,256]{0,1:T(8,128)(2,1)S(1)} %get-tuple-element.16, bf16[1024,256]{0,1:T(8,128)(2,1)S(1)} %get-tuple-element.17, bf16[1024,256]{0,1:T(8,128)(2,1)S(1)} %get-tuple-element.14), kind=kOutput, calls=%fused_computation.2 | convolution fusion | flops 545259520 | bytes 3670016 | tf_op jit(solution)/shard_map/ik,ij->kj/dot_general | solution.py:53
  17.6 0.9 %broadcast_select_fusion = f32[1032,128]{1,0:T(8,128)} fusion(f32[1032,128]{1,0:T(8,128)S(1)} %get-tuple-element.48, f32[1032,128]{1,0:T(8,128)S(1)} %get-tuple-element.47, pred[]{:T(512)S(6)} %eq.166), kind=kLoop, calls=%fused_computation.34 | loop fusion | flops 132096 | bytes 1585153 | tf_op jit(solution)/shard_map/jit(_where)/select_n | solution.py:143
  18.5 0.5 %collective-permute-start.5 = (f32[1032,128]{1,0:T(8,128)}, f32[1032,128]{1,0:T(8,128)S(1)}, u32[]{:S(2)}, u32[]{:S(2)}) collective-permute-start(f32[1032,128]{1,0:T(8,128)} %broadcast_select_fusion), channel_id=1, source_target_pairs={{0,1},{1,0},{2,3},{3,2},{4,5},{5,4},{6,7},{7,6},{8,9},{9,8},{10,11... | collective-permute-start | bytes 1585160 | tf_op jit(solution)/shard_map/ppermute | solution.py:9
  18.9 0.1 convert_reduce_fusion.1
  19.1 0.6 %pad.7 = f32[8,256]{1,0:T(8,128)} pad(f32[1,256]{1,0:T(1,128)S(1)} %bitcast.116, f32[]{:T(128)} %constant.95.clone.1), padding=0_7x0_0 | pad | bytes 9220 | tf_op jit(solution)/shard_map/jit(_pad)/pad | solution.py:16
  19.7 2.1 %fusion.13 = f32[1024,256]{1,0:T(8,128)S(1)} fusion(bf16[1024,256]{0,1:T(8,128)(2,1)} %copy-done.3, bf16[1024,256]{0,1:T(8,128)(2,1)} %copy-done.4, bf16[1024,256]{0,1:T(8,128)(2,1)} %copy-done.5, bf16[1024,256]{0,1:T(8,128)(2,1)S(1)} %get-tuple-element.14, bf16[256,256]{1,0:T(8,128)(2,1)S(1)} %get-tuple-element.32, ...), kind=kOutput, calls=%fused_computation.31 | convolution fusion | flops 547356672 | bytes 3670016 | tf_op jit(solution)/shard_map/ij,kj->ik/dot_general | solution.py:54
  22.0 0.8 %copy-done.2 = f32[1024,256]{1,0:T(8,128)} copy-done((f32[1024,256]{1,0:T(8,128)}, f32[1024,256]{1,0:T(8,128)S(1)}, u32[]{:S(2)}) %copy-start.2) | copy-done | bytes 1048600
  22.9 0.8 %constant_dynamic-slice_fusion.1 = f32[4,264,128]{2,1,0:T(8,128)} fusion(f32[8,264,128]{2,1,0:T(8,128)S(1)} %fusion.26, s32[]{:T(128)S(6)} %select_n.182), kind=kLoop, calls=%fused_computation.85 | loop fusion | bytes 1081348 | tf_op jit(solution)/shard_map/dynamic_slice | solution.py:153
  23.8 3.5 %all-to-all-start = ((f32[4,264,128]{2,1,0:T(8,128)}), f32[4,264,128]{2,1,0:T(8,128)S(1)}, u32[]{:S(2)}, u32[]{:S(2)}) async-start(f32[4,264,128]{2,1,0:T(8,128)} %constant_dynamic-slice_fusion.1), calls=%async_computation | async-start | bytes 1081344 | tf_op jit(solution)/shard_map/all_to_all | solution.py:154
  27.3 1.6 %collective-permute-start.4 = (f32[520,256]{1,0:T(8,128)S(1)}, f32[520,256]{1,0:T(8,128)S(1)}, u32[]{:S(2)}, u32[]{:S(2)}) collective-permute-start(f32[520,256]{1,0:T(8,128)S(1)} %pad_maximum_fusion.1), channel_id=1, source_target_pairs={{0,2},{2,0},{1,3},{3,1},{4,6},{6,4},{5,7},{7,5},{8,10},{10,8},{9,1... | collective-permute-start | bytes 1597448 | tf_op jit(solution)/shard_map/ppermute | solution.py:9
  28.9 12.6 %collective-permute-done.4 = f32[520,256]{1,0:T(8,128)S(1)} collective-permute-done((f32[520,256]{1,0:T(8,128)S(1)}, f32[520,256]{1,0:T(8,128)S(1)}, u32[]{:S(2)}, u32[]{:S(2)}) %collective-permute-start.4) | collective-permute-done | bytes 532512 | tf_op jit(solution)/shard_map/ppermute | solution.py:9
  41.4 1.1 %all-to-all-done = f32[4,264,128]{2,1,0:T(8,128)S(1)} async-done(((f32[4,264,128]{2,1,0:T(8,128)}), f32[4,264,128]{2,1,0:T(8,128)S(1)}, u32[]{:S(2)}, u32[]{:S(2)}) %all-to-all-start) | async-done | bytes 540704 | tf_op jit(solution)/shard_map/all_to_all | solution.py:154
  42.7 1.9 %fusion.10 = f32[1,512,256]{2,1,0:T(8,128)} fusion(f32[520,256]{1,0:T(8,128)S(1)} %collective-permute-done.4, f32[2,512,256]{2,1,0:T(8,128)} %bitcast.109, s32[]{:T(128)S(6)} %select_n.173, f32[256]{0:T(256)S(1)} %bitcast.120, bf16[1,1024,256]{2,1,0:T(8,128)(2,1)S(1)} %copy-done, s32[]{:T(128)S(6)} %select_n.149), kind=kLoop, calls=%fused_computation.22 | loop fusion | flops 524288 | bytes 1836040 | tf_op jit(solution)/shard_map/broadcast_in_dim | solution.py:162
  44.6 0.8 %fusion.16 = f32[256,256]{1,0:T(8,128)} fusion(f32[264,128]{1,0:T(8,128)S(1)} %get-tuple-element.37, f32[264,128]{1,0:T(8,128)S(1)} %get-tuple-element.36, bf16[256,256]{1,0:T(8,128)(2,1)S(1)} %copy-done.1, f32[256]{0:T(256)S(1)} %bitcast.118), kind=kLoop, calls=%fused_computation.37 | loop fusion | flops 262144 | bytes 664576 | tf_op jit(solution)/shard_map/div | solution.py:160
  (76 shorter events, 1.9 us)
Async XLA Ops:
  0.6 12.5 %copy-start.8 = (s32[1,1,4]{2,1,0:T(1,128)S(1)}, s32[1,1,4]{2,1,0:T(1,128)}, u32[]{:S(2)}) copy-start(s32[1,1,4]{2,1,0:T(1,128)} %param.7) | copy-start | bytes 52
  0.6 12.5 %copy-start.7 = (s32[1,1,4,2]{2,3,1,0:T(2,128)S(1)}, s32[1,1,4,2]{2,3,1,0:T(2,128)}, u32[]{:S(2)}) copy-start(s32[1,1,4,2]{2,3,1,0:T(2,128)} %param.6) | copy-start | bytes 100
  1.5 7.5 %collective-permute-start.2 = (bf16[256,128]{1,0:T(8,128)(2,1)S(1)}, bf16[256,128]{1,0:T(8,128)(2,1)S(1)}, u32[]{:S(2)}, u32[]{:S(2)}) collective-permute-start(bf16[256,128]{1,0:T(8,128)(2,1)S(1)} %constant_dynamic-slice_fusion), channel_id=1, source_target_pairs={{0,12},{4,0},{8,4},{12,8},{1,13},{5,1},{9,5},{13,9},{2,14},{6,2},{... | collective-permute-start | bytes 196616 | tf_op jit(solution)/shard_map/ppermute | solution.py:9
  6.6 6.5 %collective-permute-start.1 = (bf16[256,128]{1,0:T(8,128)(2,1)S(1)}, bf16[256,128]{1,0:T(8,128)(2,1)S(1)}, u32[]{:S(2)}, u32[]{:S(2)}) collective-permute-start(bf16[256,128]{1,0:T(8,128)(2,1)S(1)} %constant_dynamic-slice_fusion), channel_id=1, source_target_pairs={{0,8},{4,12},{8,0},{12,4},{1,9},{5,13},{9,1},{13,5},{2,10},{6,14},... | collective-permute-start | bytes 196616 | tf_op jit(solution)/shard_map/ppermute | solution.py:9
  6.6 6.5 %collective-permute-start = (bf16[256,128]{1,0:T(8,128)(2,1)S(1)}, bf16[256,128]{1,0:T(8,128)(2,1)S(1)}, u32[]{:S(2)}, u32[]{:S(2)}) collective-permute-start(bf16[256,128]{1,0:T(8,128)(2,1)S(1)} %constant_dynamic-slice_fusion), channel_id=1, source_target_pairs={{0,4},{4,8},{8,12},{12,0},{1,5},{5,9},{9,13},{13,1},{2,6},{6,10},{... | collective-permute-start | bytes 196616 | tf_op jit(solution)/shard_map/ppermute | solution.py:9
  7.6 7.1 %copy-start = (bf16[1,1024,256]{2,1,0:T(8,128)(2,1)S(1)}, bf16[1,1024,256]{2,1,0:T(8,128)(2,1)}, u32[]{:S(2)}) copy-start(bf16[1,1024,256]{2,1,0:T(8,128)(2,1)} %param.8) | copy-start | bytes 1572868
  13.1 1.8 %collective-permute-start.3 = (bf16[3,256,128]{2,1,0:T(8,128)(2,1)S(1)}, bf16[3,256,128]{2,1,0:T(8,128)(2,1)S(1)}, u32[]{:S(2)}, u32[]{:S(2)}) collective-permute-start(bf16[3,256,128]{2,1,0:T(8,128)(2,1)S(1)} %pad_maximum_fusion.8), channel_id=1, source_target_pairs={{0,1},{1,0},{2,3},{3,2},{4,5},{5,4},{6,7},{7,6},{8,9},{9,8},{10,11... | collective-permute-start | bytes 589832 | tf_op jit(solution)/shard_map/ppermute | solution.py:9
  13.2 1.8 %copy-start.1 = (bf16[256,256]{1,0:T(8,128)(2,1)S(1)}, bf16[256,256]{1,0:T(8,128)(2,1)}, u32[]{:S(2)}) copy-start(bf16[256,256]{1,0:T(8,128)(2,1)} %param.9) | copy-start | bytes 393220
  16.6 0.8 %copy-start.5 = (bf16[1024,256]{0,1:T(8,128)(2,1)}, bf16[1024,256]{0,1:T(8,128)(2,1)S(1)}, u32[]{:S(2)}) copy-start(bf16[1024,256]{0,1:T(8,128)(2,1)S(1)} %get-tuple-element.17) | copy-start | bytes 1572868
  16.7 1.8 %copy-start.3 = (bf16[1024,256]{0,1:T(8,128)(2,1)}, bf16[1024,256]{0,1:T(8,128)(2,1)S(1)}, u32[]{:S(2)}) copy-start(bf16[1024,256]{0,1:T(8,128)(2,1)S(1)} %get-tuple-element.15) | copy-start | bytes 1572868
  16.7 1.8 %copy-start.4 = (bf16[1024,256]{0,1:T(8,128)(2,1)}, bf16[1024,256]{0,1:T(8,128)(2,1)S(1)}, u32[]{:S(2)}) copy-start(bf16[1024,256]{0,1:T(8,128)(2,1)S(1)} %get-tuple-element.16) | copy-start | bytes 1572868
  18.5 3.4 %collective-permute-start.5 = (f32[1032,128]{1,0:T(8,128)}, f32[1032,128]{1,0:T(8,128)S(1)}, u32[]{:S(2)}, u32[]{:S(2)}) collective-permute-start(f32[1032,128]{1,0:T(8,128)} %broadcast_select_fusion), channel_id=1, source_target_pairs={{0,1},{1,0},{2,3},{3,2},{4,5},{5,4},{6,7},{7,6},{8,9},{9,8},{10,11... | collective-permute-start | bytes 1585160 | tf_op jit(solution)/shard_map/ppermute | solution.py:9
  21.8 1.0 %copy-start.2 = (f32[1024,256]{1,0:T(8,128)}, f32[1024,256]{1,0:T(8,128)S(1)}, u32[]{:S(2)}) copy-start(f32[1024,256]{1,0:T(8,128)S(1)} %fusion.13) | copy-start | bytes 3145732
  22.8 4.5 %copy-start.6 = (f32[8,256]{1,0:T(8,128)S(1)}, f32[8,256]{1,0:T(8,128)}, u32[]{:S(2)}) copy-start(f32[8,256]{1,0:T(8,128)} %pad.7) | copy-start | bytes 24580
  23.8 18.8 %all-to-all-start = ((f32[4,264,128]{2,1,0:T(8,128)}), f32[4,264,128]{2,1,0:T(8,128)S(1)}, u32[]{:S(2)}, u32[]{:S(2)}) async-start(f32[4,264,128]{2,1,0:T(8,128)} %constant_dynamic-slice_fusion.1), calls=%async_computation | async-start | bytes 1081344 | tf_op jit(solution)/shard_map/all_to_all | solution.py:154
  27.3 14.1 %collective-permute-start.4 = (f32[520,256]{1,0:T(8,128)S(1)}, f32[520,256]{1,0:T(8,128)S(1)}, u32[]{:S(2)}, u32[]{:S(2)}) collective-permute-start(f32[520,256]{1,0:T(8,128)S(1)} %pad_maximum_fusion.1), channel_id=1, source_target_pairs={{0,2},{2,0},{1,3},{3,1},{4,6},{6,4},{5,7},{7,5},{8,10},{10,8},{9,1... | collective-permute-start | bytes 1597448 | tf_op jit(solution)/shard_map/ppermute | solution.py:9
  42.6 2.0 %collective-permute-start.6 = (f32[264,128]{1,0:T(8,128)S(1)}, f32[264,128]{1,0:T(8,128)S(1)}, u32[]{:S(2)}, u32[]{:S(2)}) collective-permute-start(f32[264,128]{1,0:T(8,128)S(1)} %reduce_sum.29), channel_id=1, source_target_pairs={{0,1},{1,0},{2,3},{3,2},{4,5},{5,4},{6,7},{7,6},{8,9},{9,8},{10,11... | collective-permute-start | bytes 405512 | tf_op jit(solution)/shard_map/ppermute | solution.py:9

commit v8 on v5

--- a/solution.py
+++ b/solution.py
@@ -107,7 +107,8 @@
     sub_index = lax.axis_index("sub")
     half = width // n_sub
     own_piece = lax.dynamic_slice_in_dim(h_factor, sub_index * half, half, 1)
-    fetched = jnp.stack([shifted(own_piece, "row", d) for d in range(1, n_row)])
+    arrived = {d: shifted(own_piece, "row", d) for d in reversed(range(1, n_row))}
+    fetched = jnp.stack([arrived[d] for d in range(1, n_row)])
     swapped = [fetched] + [shifted(fetched, "sub", k) for k in range(1, n_sub)]
     others = assemble(swapped, sub_index, n_sub, 2)
     h_stack = jnp.concatenate([h_factor[None], others])
@@ -148,7 +149,7 @@
     extra = reduced[n_row * rank:]
     mine_h = reduced[:rank]
     got_w = extra
-    for d in range(1, n_row):
+    for d in reversed(range(1, n_row)):
         message = shifted(jnp.concatenate([reduced[d * rank:(d + 1) * rank], extra]), "row", d)
         mine_h = mine_h + message[:rank]
         got_w = got_w + message[rank:]

time: 38.2 us -> 37.3 us (0.976)
  waiting for transfers between devices: 14.6 us -> 12.8 us
  starting transfers between devices: 12.2 us -> 13.1 us
    ppermute x10, waiting for transfers between devices: 14.6 us -> 12.8 us  [shifted(): lax.ppermute(value, axis, [(i, (i + by) % length) for i in range(length)])]
    ppermute x10, starting transfers between devices: 12.2 us -> 13.1 us  [shifted(): lax.ppermute(value, axis, [(i, (i + by) % length) for i in range(length)])]
where the time goes in v8:
time: 37.3 us; the launch traced here: 37.1 us
  starting transfers between devices  13.1 us (35%)
  waiting for transfers between devices  12.8 us (34%)
  other arithmetic  4.1 us (11%)
  local copies, waits for them, and re-layouts  3.81 us (10%)
  matrix products  2.27 us (6%)
  between operations  0.99 us (3%)
    ppermute x10, starting transfers between devices, shifted(): lax.ppermute(value, axis, [(i, (i + by) % length) for i in range(length)])  13.1 us
    ppermute x10, waiting for transfers between devices, shifted(): lax.ppermute(value, axis, [(i, (i + by) % length) for i in range(length)])  12.8 us
    slice x1, local copies, waits for them, and re-layouts, dense_terms(): a_d = jnp.where(match[:, None, None], values[:, slot], a_d)  1.27 us
    dynamic_slice x1, local copies, waits for them, and re-layouts, body(): own_piece = lax.dynamic_slice_in_dim(h_factor, sub_index * half, half, 1)  0.91 us
    convert_element_type x1, other arithmetic, dense_terms(): chunks.append(r_d.astype(jnp.bfloat16).reshape(tile_rows, width))  0.91 us
    broadcast_in_dim x1, other arithmetic, body(): w_new = (w_part * mine_w / h_total[None, :])[None]  0.89 us
    div x1, other arithmetic, body(): h_new = h_factor.astype(jnp.float32) * numer_h / w_total[:, None]  0.82 us
    or x1, other arithmetic, dense_terms(): covered = covered | match  0.77 us
  transfers between devices with their start and end apart: 10, of which 5 were waited for; matrix products, arithmetic and copies ran while one was open for 15% of the time, Pallas kernels for 0%

profile of v8, /device:TPU:0, one launch (start us, length us, event | category | flops | bytes accessed | tf_op | source)
XLA Modules:
  0.0 37.1 jit_solution(16232308688637334164)
XLA Ops:
  0.7 0.9 %constant_dynamic-slice_fusion = bf16[256,128]{1,0:T(8,128)(2,1)S(1)} fusion(bf16[256,256]{1,0:T(8,128)(2,1)} %param.9, s32[]{:T(128)S(6)} %select_n.152), kind=kLoop, calls=%fused_computation.80 | loop fusion | bytes 131076 | tf_op jit(solution)/shard_map/dynamic_slice | solution.py:109
  1.6 5.0 %collective-permute-start.2 = (bf16[256,128]{1,0:T(8,128)(2,1)S(1)}, bf16[256,128]{1,0:T(8,128)(2,1)S(1)}, u32[]{:S(2)}, u32[]{:S(2)}) collective-permute-start(bf16[256,128]{1,0:T(8,128)(2,1)S(1)} %constant_dynamic-slice_fusion), channel_id=1, source_target_pairs={{0,12},{4,0},{8,4},{12,8},{1,13},{5,1},{9,5},{13,9},{2,14},{6,2},{... | collective-permute-start | bytes 196616 | tf_op jit(solution)/shard_map/ppermute | solution.py:9
  6.6 1.0 %collective-permute-start = (bf16[256,128]{1,0:T(8,128)(2,1)S(1)}, bf16[256,128]{1,0:T(8,128)(2,1)S(1)}, u32[]{:S(2)}, u32[]{:S(2)}) collective-permute-start(bf16[256,128]{1,0:T(8,128)(2,1)S(1)} %constant_dynamic-slice_fusion), channel_id=1, source_target_pairs={{0,4},{4,8},{8,12},{12,0},{1,5},{5,9},{9,13},{13,1},{2,6},{6,10},{... | collective-permute-start | bytes 196616 | tf_op jit(solution)/shard_map/ppermute | solution.py:9
  7.6 1.3 %fusion.29 = (bf16[4,1,256,256]{3,2,1,0:T(8,128)(2,1)S(1)}, bf16[4,1,256,256]{3,2,1,0:T(8,128)(2,1)S(1)}) fusion(bf16[4,2,256,256]{3,2,1,0:T(8,128)(2,1)} %bitcast.83), kind=kLoop, calls=%fused_computation.90 | loop fusion | bytes 2097152 | tf_op jit(solution)/shard_map/slice | solution.py:47
  9.0 0.2 collective-permute-done.2
  9.1 4.0 %collective-permute-done.1 = bf16[256,128]{1,0:T(8,128)(2,1)S(1)} collective-permute-done((bf16[256,128]{1,0:T(8,128)(2,1)S(1)}, bf16[256,128]{1,0:T(8,128)(2,1)S(1)}, u32[]{:S(2)}, u32[]{:S(2)}) %collective-permute-start.1) | collective-permute-done | bytes 65568 | tf_op jit(solution)/shard_map/ppermute | solution.py:9
  13.2 0.8 %fusion.25 = (pred[4]{0:T(512)(128)(4,1)S(1)}, pred[4]{0:T(512)(128)(4,1)S(1)}, pred[4]{0:T(512)(128)(4,1)S(1)}, pred[4]{0:T(512)(128)(4,1)S(1)}, pred[4]{0:T(51...) fusion(s32[1,1,4]{2,1,0:T(1,128)} %param.7, ...), kind=kLoop, calls=%fused_computation.86 | loop fusion | flops 88 | bytes 112 | tf_op jit(solution)/shard_map/or | solution.py:48
  14.0 0.2 copy.9
  14.2 0.2 copy.10
  15.5 0.2 convert_reduce_fusion
  15.8 0.8 %convolution_bitcast_fusion = f32[1024,1024]{0,1:T(8,128)S(1)} fusion(bf16[1,1024,256]{2,1,0:T(8,128)(2,1)S(1)} %copy-done, bf16[256,256]{1,0:T(8,128)(2,1)S(1)} %get-tuple-element.31, bf16[256,256]{1,0:T(8,128)(2,1)S(1)} %get-tuple-element.32, bf16[256,256]{1,0:T(8,128)(2,1)S(1)} %get-tuple-element.30, bf16[256,256]{1,0:T(8,128)(2,1)S(1)} %copy-done.1), kind=kOutput, calls=%fused_computation | convolution fusion | flops 538968064 | bytes 5242880 | tf_op jit(solution)/shard_map/dot_general | solution.py:39
  16.5 0.9 %fusion.7 = (bf16[1024,256]{0,1:T(8,128)(2,1)S(1)}, bf16[1024,256]{0,1:T(8,128)(2,1)S(1)}, bf16[1024,256]{0,1:T(8,128)(2,1)S(1)}, bf16[1024,256]{0,1:T(8,128)(2,1)S(1)}) fusion(f32[1024,1024]{0,1:T(8,128)S(1)} %convolution_bitcast_fusion, bf16[1024,256]{0,1:T(8,128)(2,1)S(1)} %copy.9, bf16[1024,256]{0,1:T(8,128)(2,1)S(1)} %copy.10, ...), kind=kLoop, calls=%fused_computation.14 | loop fusion | flops 6291456 | bytes 7352320 | tf_op jit(solution)/shard_map/convert_element_type | solution.py:51
  17.5 0.8 %convolution_bitcast_fusion.1 = f32[256,1024]{1,0:T(8,128)S(1)} fusion(bf16[1,1024,256]{2,1,0:T(8,128)(2,1)S(1)} %copy-done, bf16[1024,256]{0,1:T(8,128)(2,1)S(1)} %get-tuple-element.15, bf16[1024,256]{0,1:T(8,128)(2,1)S(1)} %get-tuple-element.16, bf16[1024,256]{0,1:T(8,128)(2,1)S(1)} %get-tuple-element.17, bf16[1024,256]{0,1:T(8,128)(2,1)S(1)} %get-tuple-element.14), kind=kOutput, calls=%fused_computation.2 | convolution fusion | flops 545259520 | bytes 3670016 | tf_op jit(solution)/shard_map/ik,ij->kj/dot_general | solution.py:53
  18.4 0.6 %collective-permute-start.5 = (f32[1032,128]{1,0:T(8,128)S(1)}, f32[1032,128]{1,0:T(8,128)S(1)}, u32[]{:S(2)}, u32[]{:S(2)}) collective-permute-start(f32[1032,128]{1,0:T(8,128)S(1)} %broadcast_select_fusion), channel_id=1, source_target_pairs={{0,1},{1,0},{2,3},{3,2},{4,5},{5,4},{6,7},{7,6},{8,9},{9,8},{10,11... | collective-permute-start | bytes 1585160 | tf_op jit(solution)/shard_map/ppermute | solution.py:9
  19.1 0.8 %fusion.13 = f32[1024,256]{1,0:T(8,128)S(1)} fusion(bf16[1024,256]{0,1:T(8,128)(2,1)S(1)} %get-tuple-element.15, bf16[1024,256]{0,1:T(8,128)(2,1)S(1)} %get-tuple-element.16, bf16[1024,256]{0,1:T(8,128)(2,1)S(1)} %get-tuple-element.17, bf16[1024,256]{0,1:T(8,128)(2,1)S(1)} %get-tuple-element.14, bf16[256,256]{1,0:T(8,128)(2,1)S(1)} %get-tuple-element.31, ...), kind=kOutput, calls=%fused_computation.31 | convolution fusion | flops 547356672 | bytes 3670016 | tf_op jit(solution)/shard_map/ij,kj->ik/dot_general | solution.py:54
  20.0 1.6 %collective-permute-start.4 = (f32[520,256]{1,0:T(8,128)S(1)}, f32[520,256]{1,0:T(8,128)S(1)}, u32[]{:S(2)}, u32[]{:S(2)}) collective-permute-start(f32[520,256]{1,0:T(8,128)S(1)} %pad_maximum_fusion.1), channel_id=1, source_target_pairs={{0,2},{2,0},{1,3},{3,1},{4,6},{6,4},{5,7},{7,5},{8,10},{10,8},{9,1... | collective-permute-start | bytes 1597448 | tf_op jit(solution)/shard_map/ppermute | solution.py:9
  21.7 0.2 collective-permute-start.8
  21.9 2.3 %collective-permute-start.7 = (f32[264,128]{1,0:T(8,128)S(1)}, f32[264,128]{1,0:T(8,128)S(1)}, u32[]{:S(2)}, u32[]{:S(2)}) collective-permute-start(f32[264,128]{1,0:T(8,128)S(1)} %get-tuple-element.37), channel_id=1, source_target_pairs={{0,8},{4,12},{8,0},{12,4},{1,9},{5,13},{9,1},{13,5},{2,10},{6,14},... | collective-permute-start | bytes 405512 | tf_op jit(solution)/shard_map/ppermute | solution.py:9
  24.2 2.2 %collective-permute-start.6 = (f32[264,128]{1,0:T(8,128)S(1)}, f32[264,128]{1,0:T(8,128)S(1)}, u32[]{:S(2)}, u32[]{:S(2)}) collective-permute-start(f32[264,128]{1,0:T(8,128)S(1)} %concatenate.48), channel_id=1, source_target_pairs={{0,12},{4,0},{8,4},{12,8},{1,13},{5,1},{9,5},{13,9},{2,14},{6,2},{... | collective-permute-start | bytes 405512 | tf_op jit(solution)/shard_map/ppermute | solution.py:9
  26.5 7.6 %collective-permute-done.4 = f32[520,256]{1,0:T(8,128)S(1)} collective-permute-done((f32[520,256]{1,0:T(8,128)S(1)}, f32[520,256]{1,0:T(8,128)S(1)}, u32[]{:S(2)}, u32[]{:S(2)}) %collective-permute-start.4) | collective-permute-done | bytes 532512 | tf_op jit(solution)/shard_map/ppermute | solution.py:9
  34.1 0.6 %collective-permute-done.7 = f32[264,128]{1,0:T(8,128)S(1)} collective-permute-done((f32[264,128]{1,0:T(8,128)S(1)}, f32[264,128]{1,0:T(8,128)S(1)}, u32[]{:S(2)}, u32[]{:S(2)}) %collective-permute-start.7) | collective-permute-done | bytes 135200 | tf_op jit(solution)/shard_map/ppermute | solution.py:9
  34.9 0.9 %fusion.10 = f32[1,512,256]{2,1,0:T(8,128)} fusion(f32[520,256]{1,0:T(8,128)S(1)} %collective-permute-done.4, f32[2,512,256]{2,1,0:T(8,128)S(1)} %bitcast.85, s32[]{:T(128)S(6)} %select_n.170, f32[256]{0:T(256)S(1)} %bitcast.96, bf16[1,1024,256]{2,1,0:T(8,128)(2,1)S(1)} %copy-done, s32[]{:T(128)S(6)} %select_n.146), kind=kLoop, calls=%fused_computation.22 | loop fusion | flops 524288 | bytes 1836040 | tf_op jit(solution)/shard_map/broadcast_in_dim | solution.py:163
  35.8 0.4 %collective-permute-done.9 = f32[264,128]{1,0:T(8,128)S(1)} collective-permute-done((f32[264,128]{1,0:T(8,128)S(1)}, f32[264,128]{1,0:T(8,128)S(1)}, u32[]{:S(2)}, u32[]{:S(2)}) %collective-permute-start.9) | collective-permute-done | bytes 135200 | tf_op jit(solution)/shard_map/ppermute | solution.py:9
  36.3 0.8 %fusion.16 = f32[256,256]{1,0:T(8,128)} fusion(f32[264,128]{1,0:T(8,128)S(1)} %get-tuple-element.36, f32[264,128]{1,0:T(8,128)S(1)} %get-tuple-element.35, bf16[256,256]{1,0:T(8,128)(2,1)S(1)} %copy-done.1, f32[256]{0:T(256)S(1)} %bitcast.94), kind=kLoop, calls=%fused_computation.37 | loop fusion | flops 262144 | bytes 664576 | tf_op jit(solution)/shard_map/div | solution.py:161
  (61 shorter events, 1.9 us)
Async XLA Ops:
  0.6 15.1 %copy-start.1 = (bf16[256,256]{1,0:T(8,128)(2,1)S(1)}, bf16[256,256]{1,0:T(8,128)(2,1)}, u32[]{:S(2)}) copy-start(bf16[256,256]{1,0:T(8,128)(2,1)} %param.9) | copy-start | bytes 393220
  0.6 14.9 %copy-start = (bf16[1,1024,256]{2,1,0:T(8,128)(2,1)S(1)}, bf16[1,1024,256]{2,1,0:T(8,128)(2,1)}, u32[]{:S(2)}) copy-start(bf16[1,1024,256]{2,1,0:T(8,128)(2,1)} %param.8) | copy-start | bytes 1572868
  1.6 7.5 %collective-permute-start.2 = (bf16[256,128]{1,0:T(8,128)(2,1)S(1)}, bf16[256,128]{1,0:T(8,128)(2,1)S(1)}, u32[]{:S(2)}, u32[]{:S(2)}) collective-permute-start(bf16[256,128]{1,0:T(8,128)(2,1)S(1)} %constant_dynamic-slice_fusion), channel_id=1, source_target_pairs={{0,12},{4,0},{8,4},{12,8},{1,13},{5,1},{9,5},{13,9},{2,14},{6,2},{... | collective-permute-start | bytes 196616 | tf_op jit(solution)/shard_map/ppermute | solution.py:9
  6.6 6.5 %collective-permute-start.1 = (bf16[256,128]{1,0:T(8,128)(2,1)S(1)}, bf16[256,128]{1,0:T(8,128)(2,1)S(1)}, u32[]{:S(2)}, u32[]{:S(2)}) collective-permute-start(bf16[256,128]{1,0:T(8,128)(2,1)S(1)} %constant_dynamic-slice_fusion), channel_id=1, source_target_pairs={{0,8},{4,12},{8,0},{12,4},{1,9},{5,13},{9,1},{13,5},{2,10},{6,14},... | collective-permute-start | bytes 196616 | tf_op jit(solution)/shard_map/ppermute | solution.py:9
  6.6 6.5 %collective-permute-start = (bf16[256,128]{1,0:T(8,128)(2,1)S(1)}, bf16[256,128]{1,0:T(8,128)(2,1)S(1)}, u32[]{:S(2)}, u32[]{:S(2)}) collective-permute-start(bf16[256,128]{1,0:T(8,128)(2,1)S(1)} %constant_dynamic-slice_fusion), channel_id=1, source_target_pairs={{0,4},{4,8},{8,12},{12,0},{1,5},{5,9},{9,13},{13,1},{2,6},{6,10},{... | collective-permute-start | bytes 196616 | tf_op jit(solution)/shard_map/ppermute | solution.py:9
  13.1 2.5 %collective-permute-start.3 = (bf16[3,256,128]{2,1,0:T(8,128)(2,1)S(1)}, bf16[3,256,128]{2,1,0:T(8,128)(2,1)S(1)}, u32[]{:S(2)}, u32[]{:S(2)}) collective-permute-start(bf16[3,256,128]{2,1,0:T(8,128)(2,1)S(1)} %pad_maximum_fusion.5), channel_id=1, source_target_pairs={{0,1},{1,0},{2,3},{3,2},{4,5},{5,4},{6,7},{7,6},{8,9},{9,8},{10,11... | collective-permute-start | bytes 589832 | tf_op jit(solution)/shard_map/ppermute | solution.py:9
  18.4 3.1 %collective-permute-start.5 = (f32[1032,128]{1,0:T(8,128)S(1)}, f32[1032,128]{1,0:T(8,128)S(1)}, u32[]{:S(2)}, u32[]{:S(2)}) collective-permute-start(f32[1032,128]{1,0:T(8,128)S(1)} %broadcast_select_fusion), channel_id=1, source_target_pairs={{0,1},{1,0},{2,3},{3,2},{4,5},{5,4},{6,7},{7,6},{8,9},{9,8},{10,11... | collective-permute-start | bytes 1585160 | tf_op jit(solution)/shard_map/ppermute | solution.py:9
  20.0 14.1 %collective-permute-start.4 = (f32[520,256]{1,0:T(8,128)S(1)}, f32[520,256]{1,0:T(8,128)S(1)}, u32[]{:S(2)}, u32[]{:S(2)}) collective-permute-start(f32[520,256]{1,0:T(8,128)S(1)} %pad_maximum_fusion.1), channel_id=1, source_target_pairs={{0,2},{2,0},{1,3},{3,1},{4,6},{6,4},{5,7},{7,5},{8,10},{10,8},{9,1... | collective-permute-start | bytes 1597448 | tf_op jit(solution)/shard_map/ppermute | solution.py:9
  21.7 12.4 %collective-permute-start.8 = (f32[264,128]{1,0:T(8,128)S(1)}, f32[264,128]{1,0:T(8,128)S(1)}, u32[]{:S(2)}, u32[]{:S(2)}) collective-permute-start(f32[264,128]{1,0:T(8,128)S(1)} %get-tuple-element.38), channel_id=1, source_target_pairs={{0,4},{4,8},{8,12},{12,0},{1,5},{5,9},{9,13},{13,1},{2,6},{6,10},{... | collective-permute-start | bytes 405512 | tf_op jit(solution)/shard_map/ppermute | solution.py:9
  21.9 12.8 %collective-permute-start.7 = (f32[264,128]{1,0:T(8,128)S(1)}, f32[264,128]{1,0:T(8,128)S(1)}, u32[]{:S(2)}, u32[]{:S(2)}) collective-permute-start(f32[264,128]{1,0:T(8,128)S(1)} %get-tuple-element.37), channel_id=1, source_target_pairs={{0,8},{4,12},{8,0},{12,4},{1,9},{5,13},{9,1},{13,5},{2,10},{6,14},... | collective-permute-start | bytes 405512 | tf_op jit(solution)/shard_map/ppermute | solution.py:9
  24.2 10.5 %collective-permute-start.6 = (f32[264,128]{1,0:T(8,128)S(1)}, f32[264,128]{1,0:T(8,128)S(1)}, u32[]{:S(2)}, u32[]{:S(2)}) collective-permute-start(f32[264,128]{1,0:T(8,128)S(1)} %concatenate.48), channel_id=1, source_target_pairs={{0,12},{4,0},{8,4},{12,8},{1,13},{5,1},{9,5},{13,9},{2,14},{6,2},{... | collective-permute-start | bytes 405512 | tf_op jit(solution)/shard_map/ppermute | solution.py:9
  34.8 1.4 %collective-permute-start.9 = (f32[264,128]{1,0:T(8,128)S(1)}, f32[264,128]{1,0:T(8,128)S(1)}, u32[]{:S(2)}, u32[]{:S(2)}) collective-permute-start(f32[264,128]{1,0:T(8,128)S(1)} %pad_maximum_fusion.8), channel_id=1, source_target_pairs={{0,1},{1,0},{2,3},{3,2},{4,5},{5,4},{6,7},{7,6},{8,9},{9,8},{10,11... | collective-permute-start | bytes 405512 | tf_op jit(solution)/shard_map/ppermute | solution.py:9

commit v9 on v8

--- a/solution.py
+++ b/solution.py
@@ -107,13 +107,17 @@
     sub_index = lax.axis_index("sub")
     half = width // n_sub
     own_piece = lax.dynamic_slice_in_dim(h_factor, sub_index * half, half, 1)
-    arrived = {d: shifted(own_piece, "row", d) for d in reversed(range(1, n_row))}
+    w_sum = jnp.sum(w_tile.astype(jnp.float32), axis=0)
+    middle = n_row // 2
+    later, _ = lax.optimization_barrier((own_piece, w_sum))
+    arrived = {
+        d: shifted(own_piece if d == middle else later, "row", d) for d in range(1, n_row)
+    }
     fetched = jnp.stack([arrived[d] for d in range(1, n_row)])
     swapped = [fetched] + [shifted(fetched, "sub", k) for k in range(1, n_sub)]
     others = assemble(swapped, sub_index, n_sub, 2)
     h_stack = jnp.concatenate([h_factor[None], others])
     h_sum = jnp.sum(h_stack.astype(jnp.float32), axis=(0, 2))
-    w_sum = jnp.sum(w_tile.astype(jnp.float32), axis=0)
 
     if tile_rows * n_row * width * 4 <= (8 << 20):
         numer_h_stack, numer_w = dense_terms(values, lists, counts, w_tile, h_stack, row_index)

time: 37.3 us -> 37.4 us (level)
  starting transfers between devices: 13.1 us -> 11.9 us
  waiting for transfers between devices: 12.8 us -> 13.7 us
    ppermute x10, starting transfers between devices: 13.1 us -> 11.9 us  [shifted(): lax.ppermute(value, axis, [(i, (i + by) % length) for i in range(length)])]
    reduce_sum x1, other arithmetic: 0.15 us -> 1.19 us  [body(): w_sum = jnp.sum(w_tile.astype(jnp.float32), axis=0)]
    ppermute x10, waiting for transfers between devices: 12.8 us -> 13.7 us  [shifted(): lax.ppermute(value, axis, [(i, (i + by) % length) for i in range(length)])]
    or x1, other arithmetic: 0.77 us -> 0.02 us  [dense_terms(): covered = covered | match]
  transfers between devices with their start and end apart: 10 -> 10, of which waited for: 5 -> 6; matrix products, arithmetic and copies ran while one was open for 15% -> 16% of each run, Pallas kernels for 0% -> 0%
where the time goes in v9:
time: 37.4 us; the launch traced here: 37.2 us
  waiting for transfers between devices  13.7 us (37%)
  starting transfers between devices  11.9 us (32%)
  other arithmetic  4.39 us (12%)
  local copies, waits for them, and re-layouts  3.84 us (10%)
  matrix products  2.27 us (6%)
  between operations  1.06 us (3%)
    ppermute x10, waiting for transfers between devices, shifted(): lax.ppermute(value, axis, [(i, (i + by) % length) for i in range(length)])  13.7 us
    ppermute x10, starting transfers between devices, shifted(): lax.ppermute(value, axis, [(i, (i + by) % length) for i in range(length)])  11.9 us
    slice x1, local copies, waits for them, and re-layouts, dense_terms(): a_d = jnp.where(match[:, None, None], values[:, slot], a_d)  1.27 us
    reduce_sum x1, other arithmetic, body(): w_sum = jnp.sum(w_tile.astype(jnp.float32), axis=0)  1.19 us
    dynamic_slice x1, local copies, waits for them, and re-layouts, body(): own_piece = lax.dynamic_slice_in_dim(h_factor, sub_index * half, half, 1)  0.93 us
    convert_element_type x1, other arithmetic, dense_terms(): chunks.append(r_d.astype(jnp.bfloat16).reshape(tile_rows, width))  0.91 us
    broadcast_in_dim x1, other arithmetic, body(): w_new = (w_part * mine_w / h_total[None, :])[None]  0.89 us
    div x1, other arithmetic, body(): h_new = h_factor.astype(jnp.float32) * numer_h / w_total[:, None]  0.82 us
  transfers between devices with their start and end apart: 10, of which 6 were waited for; matrix products, arithmetic and copies ran while one was open for 16% of the time, Pallas kernels for 0%

profile of v9, /device:TPU:0, one launch (start us, length us, event | category | flops | bytes accessed | tf_op | source)
XLA Modules:
  0.0 37.2 jit_solution(8110637820185680768)
XLA Ops:
  0.7 0.9 %constant_dynamic-slice_fusion = bf16[256,128]{1,0:T(8,128)(2,1)S(1)} fusion(bf16[256,256]{1,0:T(8,128)(2,1)} %param.9, s32[]{:T(128)S(6)} %select_n.152), kind=kLoop, calls=%fused_computation.80 | loop fusion | bytes 131076 | tf_op jit(solution)/shard_map/dynamic_slice | solution.py:109
  1.6 4.0 %collective-permute-start.1 = (bf16[256,128]{1,0:T(8,128)(2,1)S(1)}, bf16[256,128]{1,0:T(8,128)(2,1)S(1)}, u32[]{:S(2)}, u32[]{:S(2)}) collective-permute-start(bf16[256,128]{1,0:T(8,128)(2,1)S(1)} %constant_dynamic-slice_fusion), channel_id=1, source_target_pairs={{0,8},{4,12},{8,0},{12,4},{1,9},{5,13},{9,1},{13,5},{2,10},{6,14},... | collective-permute-start | bytes 196616 | tf_op jit(solution)/shard_map/ppermute | solution.py:9
  5.6 1.2 %convert_reduce_fusion.1 = f32[256]{0:T(256)S(1)} fusion(bf16[1,1024,256]{2,1,0:T(8,128)(2,1)} %param.8), kind=kLoop, calls=%fused_computation.16 | loop fusion | flops 524032 | bytes 525312 | tf_op jit(solution)/shard_map/reduce_sum | solution.py:110
  6.8 1.4 %collective-permute-start.2 = (bf16[256,128]{1,0:T(8,128)(2,1)S(1)}, bf16[256,128]{1,0:T(8,128)(2,1)S(1)}, u32[]{:S(2)}, u32[]{:S(2)}) collective-permute-start(bf16[256,128]{1,0:T(8,128)(2,1)S(1)} %constant_dynamic-slice_fusion), channel_id=1, source_target_pairs={{0,12},{4,0},{8,4},{12,8},{1,13},{5,1},{9,5},{13,9},{2,14},{6,2},{... | collective-permute-start | bytes 196616 | tf_op jit(solution)/shard_map/ppermute | solution.py:9
  8.2 0.7 %collective-permute-start = (bf16[256,128]{1,0:T(8,128)(2,1)S(1)}, bf16[256,128]{1,0:T(8,128)(2,1)S(1)}, u32[]{:S(2)}, u32[]{:S(2)}) collective-permute-start(bf16[256,128]{1,0:T(8,128)(2,1)S(1)} %constant_dynamic-slice_fusion), channel_id=1, source_target_pairs={{0,4},{4,8},{8,12},{12,0},{1,5},{5,9},{9,13},{13,1},{2,6},{6,10},{... | collective-permute-start | bytes 196616 | tf_op jit(solution)/shard_map/ppermute | solution.py:9
  8.9 1.3 %fusion.29 = (bf16[4,1,256,256]{3,2,1,0:T(8,128)(2,1)S(1)}, bf16[4,1,256,256]{3,2,1,0:T(8,128)(2,1)S(1)}) fusion(bf16[4,2,256,256]{3,2,1,0:T(8,128)(2,1)} %bitcast.83), kind=kLoop, calls=%fused_computation.90 | loop fusion | bytes 2097152 | tf_op jit(solution)/shard_map/slice | solution.py:47
  10.3 0.2 copy.9
  10.5 0.2 copy.10
  10.7 0.4 %collective-permute-done.2 = bf16[256,128]{1,0:T(8,128)(2,1)S(1)} collective-permute-done((bf16[256,128]{1,0:T(8,128)(2,1)S(1)}, bf16[256,128]{1,0:T(8,128)(2,1)S(1)}, u32[]{:S(2)}, u32[]{:S(2)}) %collective-permute-start.2) | collective-permute-done | bytes 65568 | tf_op jit(solution)/shard_map/ppermute | solution.py:9
  11.2 3.1 %collective-permute-done = bf16[256,128]{1,0:T(8,128)(2,1)S(1)} collective-permute-done((bf16[256,128]{1,0:T(8,128)(2,1)S(1)}, bf16[256,128]{1,0:T(8,128)(2,1)S(1)}, u32[]{:S(2)}, u32[]{:S(2)}) %collective-permute-start) | collective-permute-done | bytes 65568 | tf_op jit(solution)/shard_map/ppermute | solution.py:9
  15.5 0.3 collective-permute-done.3
  16.0 0.8 %convolution_bitcast_fusion = f32[1024,1024]{0,1:T(8,128)S(1)} fusion(bf16[1,1024,256]{2,1,0:T(8,128)(2,1)S(1)} %copy-done, bf16[256,256]{1,0:T(8,128)(2,1)S(1)} %get-tuple-element.33, bf16[256,256]{1,0:T(8,128)(2,1)S(1)} %get-tuple-element.34, bf16[256,256]{1,0:T(8,128)(2,1)S(1)} %get-tuple-element.32, bf16[256,256]{1,0:T(8,128)(2,1)S(1)} %copy-done.1), kind=kOutput, calls=%fused_computation | convolution fusion | flops 538968064 | bytes 5242880 | tf_op jit(solution)/shard_map/dot_general | solution.py:39
  16.7 0.9 %fusion.7 = (bf16[1024,256]{0,1:T(8,128)(2,1)S(1)}, bf16[1024,256]{0,1:T(8,128)(2,1)S(1)}, bf16[1024,256]{0,1:T(8,128)(2,1)S(1)}, bf16[1024,256]{0,1:T(8,128)(2,1)S(1)}) fusion(f32[1024,1024]{0,1:T(8,128)S(1)} %convolution_bitcast_fusion, bf16[1024,256]{0,1:T(8,128)(2,1)S(1)} %copy.9, bf16[1024,256]{0,1:T(8,128)(2,1)S(1)} %copy.10, ...), kind=kLoop, calls=%fused_computation.14 | loop fusion | flops 6291456 | bytes 7352320 | tf_op jit(solution)/shard_map/convert_element_type | solution.py:51
  17.6 0.8 %convolution_bitcast_fusion.1 = f32[256,1024]{1,0:T(8,128)S(1)} fusion(bf16[1,1024,256]{2,1,0:T(8,128)(2,1)S(1)} %copy-done, bf16[1024,256]{0,1:T(8,128)(2,1)S(1)} %get-tuple-element.17, bf16[1024,256]{0,1:T(8,128)(2,1)S(1)} %get-tuple-element.18, bf16[1024,256]{0,1:T(8,128)(2,1)S(1)} %get-tuple-element.19, bf16[1024,256]{0,1:T(8,128)(2,1)S(1)} %get-tuple-element.16), kind=kOutput, calls=%fused_computation.2 | convolution fusion | flops 545259520 | bytes 3670016 | tf_op jit(solution)/shard_map/ik,ij->kj/dot_general | solution.py:53
  18.6 0.2 collective-permute-start.5
  18.9 0.8 %fusion.13 = f32[1024,256]{1,0:T(8,128)S(1)} fusion(bf16[1024,256]{0,1:T(8,128)(2,1)S(1)} %get-tuple-element.17, bf16[1024,256]{0,1:T(8,128)(2,1)S(1)} %get-tuple-element.18, bf16[1024,256]{0,1:T(8,128)(2,1)S(1)} %get-tuple-element.19, bf16[1024,256]{0,1:T(8,128)(2,1)S(1)} %get-tuple-element.16, bf16[256,256]{1,0:T(8,128)(2,1)S(1)} %get-tuple-element.33, ...), kind=kOutput, calls=%fused_computation.31 | convolution fusion | flops 547356672 | bytes 3670016 | tf_op jit(solution)/shard_map/ij,kj->ik/dot_general | solution.py:54
  19.8 1.6 %collective-permute-start.4 = (f32[520,256]{1,0:T(8,128)S(1)}, f32[520,256]{1,0:T(8,128)S(1)}, u32[]{:S(2)}, u32[]{:S(2)}) collective-permute-start(f32[520,256]{1,0:T(8,128)S(1)} %pad_maximum_fusion.1), channel_id=1, source_target_pairs={{0,2},{2,0},{1,3},{3,1},{4,6},{6,4},{5,7},{7,5},{8,10},{10,8},{9,1... | collective-permute-start | bytes 1597448 | tf_op jit(solution)/shard_map/ppermute | solution.py:9
  21.6 1.5 %collective-permute-start.7 = (f32[264,128]{1,0:T(8,128)S(1)}, f32[264,128]{1,0:T(8,128)S(1)}, u32[]{:S(2)}, u32[]{:S(2)}) collective-permute-start(f32[264,128]{1,0:T(8,128)S(1)} %get-tuple-element.39), channel_id=1, source_target_pairs={{0,8},{4,12},{8,0},{12,4},{1,9},{5,13},{9,1},{13,5},{2,10},{6,14},... | collective-permute-start | bytes 405512 | tf_op jit(solution)/shard_map/ppermute | solution.py:9
  23.2 2.3 %collective-permute-start.6 = (f32[264,128]{1,0:T(8,128)S(1)}, f32[264,128]{1,0:T(8,128)S(1)}, u32[]{:S(2)}, u32[]{:S(2)}) collective-permute-start(f32[264,128]{1,0:T(8,128)S(1)} %concatenate.48), channel_id=1, source_target_pairs={{0,12},{4,0},{8,4},{12,8},{1,13},{5,1},{9,5},{13,9},{2,14},{6,2},{... | collective-permute-start | bytes 405512 | tf_op jit(solution)/shard_map/ppermute | solution.py:9
  25.4 8.8 %collective-permute-done.4 = f32[520,256]{1,0:T(8,128)S(1)} collective-permute-done((f32[520,256]{1,0:T(8,128)S(1)}, f32[520,256]{1,0:T(8,128)S(1)}, u32[]{:S(2)}, u32[]{:S(2)}) %collective-permute-start.4) | collective-permute-done | bytes 532512 | tf_op jit(solution)/shard_map/ppermute | solution.py:9
  34.3 0.6 %collective-permute-done.7 = f32[264,128]{1,0:T(8,128)S(1)} collective-permute-done((f32[264,128]{1,0:T(8,128)S(1)}, f32[264,128]{1,0:T(8,128)S(1)}, u32[]{:S(2)}, u32[]{:S(2)}) %collective-permute-start.7) | collective-permute-done | bytes 135200 | tf_op jit(solution)/shard_map/ppermute | solution.py:9
  35.0 0.9 %fusion.10 = f32[1,512,256]{2,1,0:T(8,128)} fusion(f32[520,256]{1,0:T(8,128)S(1)} %collective-permute-done.4, f32[2,512,256]{2,1,0:T(8,128)S(1)} %bitcast.85, s32[]{:T(128)S(6)} %select_n.170, f32[256]{0:T(256)S(1)} %bitcast.96, bf16[1,1024,256]{2,1,0:T(8,128)(2,1)S(1)} %copy-done, s32[]{:T(128)S(6)} %select_n.146), kind=kLoop, calls=%fused_computation.22 | loop fusion | flops 524288 | bytes 1836040 | tf_op jit(solution)/shard_map/broadcast_in_dim | solution.py:167
  35.9 0.4 %collective-permute-done.9 = f32[264,128]{1,0:T(8,128)S(1)} collective-permute-done((f32[264,128]{1,0:T(8,128)S(1)}, f32[264,128]{1,0:T(8,128)S(1)}, u32[]{:S(2)}, u32[]{:S(2)}) %collective-permute-start.9) | collective-permute-done | bytes 135200 | tf_op jit(solution)/shard_map/ppermute | solution.py:9
  36.4 0.8 %fusion.16 = f32[256,256]{1,0:T(8,128)} fusion(f32[264,128]{1,0:T(8,128)S(1)} %get-tuple-element.38, f32[264,128]{1,0:T(8,128)S(1)} %get-tuple-element.37, bf16[256,256]{1,0:T(8,128)(2,1)S(1)} %copy-done.1, f32[256]{0:T(256)S(1)} %bitcast.94), kind=kLoop, calls=%fused_computation.37 | loop fusion | flops 262144 | bytes 664576 | tf_op jit(solution)/shard_map/div | solution.py:165
  (65 shorter events, 2.0 us)
Async XLA Ops:
  0.6 15.3 %copy-start.1 = (bf16[256,256]{1,0:T(8,128)(2,1)S(1)}, bf16[256,256]{1,0:T(8,128)(2,1)}, u32[]{:S(2)}) copy-start(bf16[256,256]{1,0:T(8,128)(2,1)} %param.9) | copy-start | bytes 393220
  0.6 15.3 %copy-start = (bf16[1,1024,256]{2,1,0:T(8,128)(2,1)S(1)}, bf16[1,1024,256]{2,1,0:T(8,128)(2,1)}, u32[]{:S(2)}) copy-start(bf16[1,1024,256]{2,1,0:T(8,128)(2,1)} %param.8) | copy-start | bytes 1572868
  0.7 13.8 %copy-start.3 = (s32[1,1,4]{2,1,0:T(1,128)S(1)}, s32[1,1,4]{2,1,0:T(1,128)}, u32[]{:S(2)}) copy-start(s32[1,1,4]{2,1,0:T(1,128)} %param.7) | copy-start | bytes 52
  0.7 13.8 %copy-start.2 = (s32[1,1,4,2]{2,3,1,0:T(2,128)S(1)}, s32[1,1,4,2]{2,3,1,0:T(2,128)}, u32[]{:S(2)}) copy-start(s32[1,1,4,2]{2,3,1,0:T(2,128)} %param.6) | copy-start | bytes 100
  1.6 9.5 %collective-permute-start.1 = (bf16[256,128]{1,0:T(8,128)(2,1)S(1)}, bf16[256,128]{1,0:T(8,128)(2,1)S(1)}, u32[]{:S(2)}, u32[]{:S(2)}) collective-permute-start(bf16[256,128]{1,0:T(8,128)(2,1)S(1)} %constant_dynamic-slice_fusion), channel_id=1, source_target_pairs={{0,8},{4,12},{8,0},{12,4},{1,9},{5,13},{9,1},{13,5},{2,10},{6,14},... | collective-permute-start | bytes 196616 | tf_op jit(solution)/shard_map/ppermute | solution.py:9
  6.8 4.3 %collective-permute-start.2 = (bf16[256,128]{1,0:T(8,128)(2,1)S(1)}, bf16[256,128]{1,0:T(8,128)(2,1)S(1)}, u32[]{:S(2)}, u32[]{:S(2)}) collective-permute-start(bf16[256,128]{1,0:T(8,128)(2,1)S(1)} %constant_dynamic-slice_fusion), channel_id=1, source_target_pairs={{0,12},{4,0},{8,4},{12,8},{1,13},{5,1},{9,5},{13,9},{2,14},{6,2},{... | collective-permute-start | bytes 196616 | tf_op jit(solution)/shard_map/ppermute | solution.py:9
  8.2 6.1 %collective-permute-start = (bf16[256,128]{1,0:T(8,128)(2,1)S(1)}, bf16[256,128]{1,0:T(8,128)(2,1)S(1)}, u32[]{:S(2)}, u32[]{:S(2)}) collective-permute-start(bf16[256,128]{1,0:T(8,128)(2,1)S(1)} %constant_dynamic-slice_fusion), channel_id=1, source_target_pairs={{0,4},{4,8},{8,12},{12,0},{1,5},{5,9},{9,13},{13,1},{2,6},{6,10},{... | collective-permute-start | bytes 196616 | tf_op jit(solution)/shard_map/ppermute | solution.py:9
  14.3 1.5 %collective-permute-start.3 = (bf16[3,256,128]{2,1,0:T(8,128)(2,1)S(1)}, bf16[3,256,128]{2,1,0:T(8,128)(2,1)S(1)}, u32[]{:S(2)}, u32[]{:S(2)}) collective-permute-start(bf16[3,256,128]{2,1,0:T(8,128)(2,1)S(1)} %pad_maximum_fusion.5), channel_id=1, source_target_pairs={{0,1},{1,0},{2,3},{3,2},{4,5},{5,4},{6,7},{7,6},{8,9},{9,8},{10,11... | collective-permute-start | bytes 589832 | tf_op jit(solution)/shard_map/ppermute | solution.py:9
  18.6 2.8 %collective-permute-start.5 = (f32[1032,128]{1,0:T(8,128)S(1)}, f32[1032,128]{1,0:T(8,128)S(1)}, u32[]{:S(2)}, u32[]{:S(2)}) collective-permute-start(f32[1032,128]{1,0:T(8,128)S(1)} %broadcast_select_fusion), channel_id=1, source_target_pairs={{0,1},{1,0},{2,3},{3,2},{4,5},{5,4},{6,7},{7,6},{8,9},{9,8},{10,11... | collective-permute-start | bytes 1585160 | tf_op jit(solution)/shard_map/ppermute | solution.py:9
  19.8 14.4 %collective-permute-start.4 = (f32[520,256]{1,0:T(8,128)S(1)}, f32[520,256]{1,0:T(8,128)S(1)}, u32[]{:S(2)}, u32[]{:S(2)}) collective-permute-start(f32[520,256]{1,0:T(8,128)S(1)} %pad_maximum_fusion.1), channel_id=1, source_target_pairs={{0,2},{2,0},{1,3},{3,1},{4,6},{6,4},{5,7},{7,5},{8,10},{10,8},{9,1... | collective-permute-start | bytes 1597448 | tf_op jit(solution)/shard_map/ppermute | solution.py:9
  21.6 12.7 %collective-permute-start.8 = (f32[264,128]{1,0:T(8,128)S(1)}, f32[264,128]{1,0:T(8,128)S(1)}, u32[]{:S(2)}, u32[]{:S(2)}) collective-permute-start(f32[264,128]{1,0:T(8,128)S(1)} %get-tuple-element.40), channel_id=1, source_target_pairs={{0,4},{4,8},{8,12},{12,0},{1,5},{5,9},{9,13},{13,1},{2,6},{6,10},{... | collective-permute-start | bytes 405512 | tf_op jit(solution)/shard_map/ppermute | solution.py:9
  21.6 13.2 %collective-permute-start.7 = (f32[264,128]{1,0:T(8,128)S(1)}, f32[264,128]{1,0:T(8,128)S(1)}, u32[]{:S(2)}, u32[]{:S(2)}) collective-permute-start(f32[264,128]{1,0:T(8,128)S(1)} %get-tuple-element.39), channel_id=1, source_target_pairs={{0,8},{4,12},{8,0},{12,4},{1,9},{5,13},{9,1},{13,5},{2,10},{6,14},... | collective-permute-start | bytes 405512 | tf_op jit(solution)/shard_map/ppermute | solution.py:9
  23.2 11.7 %collective-permute-start.6 = (f32[264,128]{1,0:T(8,128)S(1)}, f32[264,128]{1,0:T(8,128)S(1)}, u32[]{:S(2)}, u32[]{:S(2)}) collective-permute-start(f32[264,128]{1,0:T(8,128)S(1)} %concatenate.48), channel_id=1, source_target_pairs={{0,12},{4,0},{8,4},{12,8},{1,13},{5,1},{9,5},{13,9},{2,14},{6,2},{... | collective-permute-start | bytes 405512 | tf_op jit(solution)/shard_map/ppermute | solution.py:9
  34.9 1.4 %collective-permute-start.9 = (f32[264,128]{1,0:T(8,128)S(1)}, f32[264,128]{1,0:T(8,128)S(1)}, u32[]{:S(2)}, u32[]{:S(2)}) collective-permute-start(f32[264,128]{1,0:T(8,128)S(1)} %pad_maximum_fusion.8), channel_id=1, source_target_pairs={{0,1},{1,0},{2,3},{3,2},{4,5},{5,4},{6,7},{7,6},{8,9},{9,8},{10,11... | collective-permute-start | bytes 405512 | tf_op jit(solution)/shard_map/ppermute | solution.py:9

commit v10 on v8

--- a/solution.py
+++ b/solution.py
@@ -131,6 +131,8 @@
         mine_w = mine_w + message[:share]
         got_h = got_h + message[share:]
     h_total = from_rows(got_h, rank)
+    w_part = lax.dynamic_slice_in_dim(w_tile, col_index * share, share, 0)
+    w_new = (w_part.astype(jnp.float32) * mine_w / h_total[None, :])[None]
 
     w_rows_sum = as_rows(w_sum, width)
     messages = [
@@ -151,6 +153,8 @@
     got_w = extra
     for d in reversed(range(1, n_row)):
         message = shifted(jnp.concatenate([reduced[d * rank:(d + 1) * rank], extra]), "row", d)
+        if d == 1:
+            message, w_new = lax.optimization_barrier((message, w_new))
         mine_h = mine_h + message[:rank]
         got_w = got_w + message[rank:]
     final = jnp.concatenate([mine_h, got_w])
@@ -159,8 +163,6 @@
     w_total = from_rows(total[rank:], rank)
 
     h_new = h_factor.astype(jnp.float32) * numer_h / w_total[:, None]
-    w_part = lax.dynamic_slice_in_dim(w_tile, col_index * share, share, 0).astype(jnp.float32)
-    w_new = (w_part * mine_w / h_total[None, :])[None]
     return (w_new, h_new)
 
 

time: 37.3 us -> 38.2 us (1.024)
  waiting for transfers between devices: 12.8 us -> 14.6 us
  starting transfers between devices: 13.1 us -> 12.2 us
    ppermute x10, waiting for transfers between devices: 12.8 us -> 14.6 us  [shifted(): lax.ppermute(value, axis, [(i, (i + by) % length) for i in range(length)])]
    ppermute x10, starting transfers between devices: 13.1 us -> 12.2 us  [shifted(): lax.ppermute(value, axis, [(i, (i + by) % length) for i in range(length)])]
where the time goes in v10:
time: 38.2 us; the launch traced here: 38 us
  waiting for transfers between devices  14.6 us (38%)
  starting transfers between devices  12.2 us (32%)
  other arithmetic  4.09 us (11%)
  local copies, waits for them, and re-layouts  3.81 us (10%)
  matrix products  2.27 us (6%)
  between operations  1.02 us (3%)
    ppermute x10, waiting for transfers between devices, shifted(): lax.ppermute(value, axis, [(i, (i + by) % length) for i in range(length)])  14.6 us
    ppermute x10, starting transfers between devices, shifted(): lax.ppermute(value, axis, [(i, (i + by) % length) for i in range(length)])  12.2 us
    slice x1, local copies, waits for them, and re-layouts, dense_terms(): a_d = jnp.where(match[:, None, None], values[:, slot], a_d)  1.27 us
    dynamic_slice x1, local copies, waits for them, and re-layouts, body(): own_piece = lax.dynamic_slice_in_dim(h_factor, sub_index * half, half, 1)  0.91 us
    convert_element_type x1, other arithmetic, dense_terms(): chunks.append(r_d.astype(jnp.bfloat16).reshape(tile_rows, width))  0.91 us
    broadcast_in_dim x1, other arithmetic, body(): w_new = (w_part.astype(jnp.float32) * mine_w / h_total[None, :])[None]  0.89 us
    div x1, other arithmetic, body(): h_new = h_factor.astype(jnp.float32) * numer_h / w_total[:, None]  0.82 us
    or x1, other arithmetic, dense_terms(): covered = covered | match  0.77 us
  transfers between devices with their start and end apart: 10, of which 5 were waited for; matrix products, arithmetic and copies ran while one was open for 15% of the time, Pallas kernels for 0%

profile of v10, /device:TPU:0, one launch (start us, length us, event | category | flops | bytes accessed | tf_op | source)
XLA Modules:
  0.0 38.0 jit_solution(6093917866962252577)
XLA Ops:
  0.7 0.9 %constant_dynamic-slice_fusion = bf16[256,128]{1,0:T(8,128)(2,1)S(1)} fusion(bf16[256,256]{1,0:T(8,128)(2,1)} %param.9, s32[]{:T(128)S(6)} %select_n.152), kind=kLoop, calls=%fused_computation.80 | loop fusion | bytes 131076 | tf_op jit(solution)/shard_map/dynamic_slice | solution.py:109
  1.6 5.0 %collective-permute-start.2 = (bf16[256,128]{1,0:T(8,128)(2,1)S(1)}, bf16[256,128]{1,0:T(8,128)(2,1)S(1)}, u32[]{:S(2)}, u32[]{:S(2)}) collective-permute-start(bf16[256,128]{1,0:T(8,128)(2,1)S(1)} %constant_dynamic-slice_fusion), channel_id=1, source_target_pairs={{0,12},{4,0},{8,4},{12,8},{1,13},{5,1},{9,5},{13,9},{2,14},{6,2},{... | collective-permute-start | bytes 196616 | tf_op jit(solution)/shard_map/ppermute | solution.py:9
  6.6 1.0 %collective-permute-start = (bf16[256,128]{1,0:T(8,128)(2,1)S(1)}, bf16[256,128]{1,0:T(8,128)(2,1)S(1)}, u32[]{:S(2)}, u32[]{:S(2)}) collective-permute-start(bf16[256,128]{1,0:T(8,128)(2,1)S(1)} %constant_dynamic-slice_fusion), channel_id=1, source_target_pairs={{0,4},{4,8},{8,12},{12,0},{1,5},{5,9},{9,13},{13,1},{2,6},{6,10},{... | collective-permute-start | bytes 196616 | tf_op jit(solution)/shard_map/ppermute | solution.py:9
  7.6 1.3 %fusion.31 = (bf16[4,1,256,256]{3,2,1,0:T(8,128)(2,1)S(1)}, bf16[4,1,256,256]{3,2,1,0:T(8,128)(2,1)S(1)}) fusion(bf16[4,2,256,256]{3,2,1,0:T(8,128)(2,1)} %bitcast.83), kind=kLoop, calls=%fused_computation.90 | loop fusion | bytes 2097152 | tf_op jit(solution)/shard_map/slice | solution.py:47
  9.0 0.2 collective-permute-done.2
  9.1 4.0 %collective-permute-done.1 = bf16[256,128]{1,0:T(8,128)(2,1)S(1)} collective-permute-done((bf16[256,128]{1,0:T(8,128)(2,1)S(1)}, bf16[256,128]{1,0:T(8,128)(2,1)S(1)}, u32[]{:S(2)}, u32[]{:S(2)}) %collective-permute-start.1) | collective-permute-done | bytes 65568 | tf_op jit(solution)/shard_map/ppermute | solution.py:9
  13.2 0.8 %fusion.27 = (pred[4]{0:T(512)(128)(4,1)S(1)}, pred[4]{0:T(512)(128)(4,1)S(1)}, pred[4]{0:T(512)(128)(4,1)S(1)}, pred[4]{0:T(512)(128)(4,1)S(1)}, pred[4]{0:T(51...) fusion(s32[1,1,4]{2,1,0:T(1,128)} %param.7, ...), kind=kLoop, calls=%fused_computation.86 | loop fusion | flops 88 | bytes 112 | tf_op jit(solution)/shard_map/or | solution.py:48
  15.1 0.2 copy.10
  15.3 0.2 copy.9
  15.5 0.2 convert_reduce_fusion.1
  15.8 0.8 %convolution_bitcast_fusion = f32[1024,1024]{0,1:T(8,128)S(1)} fusion(bf16[1,1024,256]{2,1,0:T(8,128)(2,1)S(1)} %copy-done, bf16[256,256]{1,0:T(8,128)(2,1)S(1)} %get-tuple-element.35, bf16[256,256]{1,0:T(8,128)(2,1)S(1)} %get-tuple-element.36, bf16[256,256]{1,0:T(8,128)(2,1)S(1)} %get-tuple-element.34, bf16[256,256]{1,0:T(8,128)(2,1)S(1)} %copy-done.1), kind=kOutput, calls=%fused_computation | convolution fusion | flops 538968064 | bytes 5242880 | tf_op jit(solution)/shard_map/dot_general | solution.py:39
  16.6 0.9 %fusion.7 = (bf16[1024,256]{0,1:T(8,128)(2,1)S(1)}, bf16[1024,256]{0,1:T(8,128)(2,1)S(1)}, bf16[1024,256]{0,1:T(8,128)(2,1)S(1)}, bf16[1024,256]{0,1:T(8,128)(2,1)S(1)}) fusion(f32[1024,1024]{0,1:T(8,128)S(1)} %convolution_bitcast_fusion, bf16[1024,256]{0,1:T(8,128)(2,1)S(1)} %copy.9, bf16[1024,256]{0,1:T(8,128)(2,1)S(1)} %copy.10, ...), kind=kLoop, calls=%fused_computation.14 | loop fusion | flops 6291456 | bytes 7352320 | tf_op jit(solution)/shard_map/convert_element_type | solution.py:51
  17.5 0.8 %convolution_bitcast_fusion.1 = f32[256,1024]{1,0:T(8,128)S(1)} fusion(bf16[1,1024,256]{2,1,0:T(8,128)(2,1)S(1)} %copy-done, bf16[1024,256]{0,1:T(8,128)(2,1)S(1)} %get-tuple-element.19, bf16[1024,256]{0,1:T(8,128)(2,1)S(1)} %get-tuple-element.20, bf16[1024,256]{0,1:T(8,128)(2,1)S(1)} %get-tuple-element.21, bf16[1024,256]{0,1:T(8,128)(2,1)S(1)} %get-tuple-element.18), kind=kOutput, calls=%fused_computation.2 | convolution fusion | flops 545259520 | bytes 3670016 | tf_op jit(solution)/shard_map/ik,ij->kj/dot_general | solution.py:53
  18.4 0.6 %collective-permute-start.4 = (f32[1032,128]{1,0:T(8,128)S(1)}, f32[1032,128]{1,0:T(8,128)S(1)}, u32[]{:S(2)}, u32[]{:S(2)}) collective-permute-start(f32[1032,128]{1,0:T(8,128)S(1)} %broadcast_select_fusion), channel_id=1, source_target_pairs={{0,1},{1,0},{2,3},{3,2},{4,5},{5,4},{6,7},{7,6},{8,9},{9,8},{10,11... | collective-permute-start | bytes 1585160 | tf_op jit(solution)/shard_map/ppermute | solution.py:9
  19.0 0.1 convert_reduce_fusion
  19.1 0.8 %fusion.13 = f32[1024,256]{1,0:T(8,128)S(1)} fusion(bf16[1024,256]{0,1:T(8,128)(2,1)S(1)} %get-tuple-element.19, bf16[1024,256]{0,1:T(8,128)(2,1)S(1)} %get-tuple-element.20, bf16[1024,256]{0,1:T(8,128)(2,1)S(1)} %get-tuple-element.21, bf16[1024,256]{0,1:T(8,128)(2,1)S(1)} %get-tuple-element.18, bf16[256,256]{1,0:T(8,128)(2,1)S(1)} %get-tuple-element.35, ...), kind=kOutput, calls=%fused_computation.31 | convolution fusion | flops 547356672 | bytes 3670016 | tf_op jit(solution)/shard_map/ij,kj->ik/dot_general | solution.py:54
  20.0 1.6 %collective-permute-start.6 = (f32[520,256]{1,0:T(8,128)S(1)}, f32[520,256]{1,0:T(8,128)S(1)}, u32[]{:S(2)}, u32[]{:S(2)}) collective-permute-start(f32[520,256]{1,0:T(8,128)S(1)} %pad_maximum_fusion.1), channel_id=1, source_target_pairs={{0,2},{2,0},{1,3},{3,1},{4,6},{6,4},{5,7},{7,5},{8,10},{10,8},{9,1... | collective-permute-start | bytes 1597448 | tf_op jit(solution)/shard_map/ppermute | solution.py:9
  21.7 1.9 %collective-permute-start.7 = (f32[264,128]{1,0:T(8,128)S(1)}, f32[264,128]{1,0:T(8,128)S(1)}, u32[]{:S(2)}, u32[]{:S(2)}) collective-permute-start(f32[264,128]{1,0:T(8,128)S(1)} %concatenate.48), channel_id=1, source_target_pairs={{0,12},{4,0},{8,4},{12,8},{1,13},{5,1},{9,5},{13,9},{2,14},{6,2},{... | collective-permute-start | bytes 405512 | tf_op jit(solution)/shard_map/ppermute | solution.py:9
  23.7 1.9 %collective-permute-start.5 = (f32[264,128]{1,0:T(8,128)S(1)}, f32[264,128]{1,0:T(8,128)S(1)}, u32[]{:S(2)}, u32[]{:S(2)}) collective-permute-start(f32[264,128]{1,0:T(8,128)S(1)} %get-tuple-element.42), channel_id=1, source_target_pairs={{0,4},{4,8},{8,12},{12,0},{1,5},{5,9},{9,13},{13,1},{2,6},{6,10},{... | collective-permute-start | bytes 405512 | tf_op jit(solution)/shard_map/ppermute | solution.py:9
  25.7 8.4 %collective-permute-done.6 = f32[520,256]{1,0:T(8,128)S(1)} collective-permute-done((f32[520,256]{1,0:T(8,128)S(1)}, f32[520,256]{1,0:T(8,128)S(1)}, u32[]{:S(2)}, u32[]{:S(2)}) %collective-permute-start.6) | collective-permute-done | bytes 532512 | tf_op jit(solution)/shard_map/ppermute | solution.py:9
  34.1 0.9 %fusion.10 = f32[1,512,256]{2,1,0:T(8,128)} fusion(f32[520,256]{1,0:T(8,128)S(1)} %collective-permute-done.6, f32[2,512,256]{2,1,0:T(8,128)S(1)} %bitcast.85, s32[]{:T(128)S(6)} %select_n.175, f32[256]{0:T(256)S(1)} %bitcast.96, bf16[1,1024,256]{2,1,0:T(8,128)(2,1)S(1)} %copy-done, s32[]{:T(128)S(6)} %select_n.174), kind=kLoop, calls=%fused_computation.22 | loop fusion | flops 524288 | bytes 1836040 | tf_op jit(solution)/shard_map/broadcast_in_dim | solution.py:135
  35.0 0.7 %collective-permute-done.8 = f32[264,128]{1,0:T(8,128)S(1)} collective-permute-done((f32[264,128]{1,0:T(8,128)S(1)}, f32[264,128]{1,0:T(8,128)S(1)}, u32[]{:S(2)}, u32[]{:S(2)}) %collective-permute-start.8) | collective-permute-done | bytes 135200 | tf_op jit(solution)/shard_map/ppermute | solution.py:9
  35.8 1.3 %collective-permute-done.9 = f32[264,128]{1,0:T(8,128)S(1)} collective-permute-done((f32[264,128]{1,0:T(8,128)S(1)}, f32[264,128]{1,0:T(8,128)S(1)}, u32[]{:S(2)}, u32[]{:S(2)}) %collective-permute-start.9) | collective-permute-done | bytes 135200 | tf_op jit(solution)/shard_map/ppermute | solution.py:9
  37.2 0.8 %fusion.16 = f32[256,256]{1,0:T(8,128)} fusion(f32[264,128]{1,0:T(8,128)S(1)} %get-tuple-element.40, f32[264,128]{1,0:T(8,128)S(1)} %get-tuple-element.39, bf16[256,256]{1,0:T(8,128)(2,1)S(1)} %copy-done.1, f32[256]{0:T(256)S(1)} %bitcast.94), kind=kLoop, calls=%fused_computation.37 | loop fusion | flops 262144 | bytes 664576 | tf_op jit(solution)/shard_map/div | solution.py:165
  (61 shorter events, 1.9 us)
Async XLA Ops:
  0.6 15.2 %copy-start.1 = (bf16[256,256]{1,0:T(8,128)(2,1)S(1)}, bf16[256,256]{1,0:T(8,128)(2,1)}, u32[]{:S(2)}) copy-start(bf16[256,256]{1,0:T(8,128)(2,1)} %param.9) | copy-start | bytes 393220
  0.6 14.9 %copy-start = (bf16[1,1024,256]{2,1,0:T(8,128)(2,1)S(1)}, bf16[1,1024,256]{2,1,0:T(8,128)(2,1)}, u32[]{:S(2)}) copy-start(bf16[1,1024,256]{2,1,0:T(8,128)(2,1)} %param.8) | copy-start | bytes 1572868
  1.6 7.5 %collective-permute-start.2 = (bf16[256,128]{1,0:T(8,128)(2,1)S(1)}, bf16[256,128]{1,0:T(8,128)(2,1)S(1)}, u32[]{:S(2)}, u32[]{:S(2)}) collective-permute-start(bf16[256,128]{1,0:T(8,128)(2,1)S(1)} %constant_dynamic-slice_fusion), channel_id=1, source_target_pairs={{0,12},{4,0},{8,4},{12,8},{1,13},{5,1},{9,5},{13,9},{2,14},{6,2},{... | collective-permute-start | bytes 196616 | tf_op jit(solution)/shard_map/ppermute | solution.py:9
  6.6 6.5 %collective-permute-start.1 = (bf16[256,128]{1,0:T(8,128)(2,1)S(1)}, bf16[256,128]{1,0:T(8,128)(2,1)S(1)}, u32[]{:S(2)}, u32[]{:S(2)}) collective-permute-start(bf16[256,128]{1,0:T(8,128)(2,1)S(1)} %constant_dynamic-slice_fusion), channel_id=1, source_target_pairs={{0,8},{4,12},{8,0},{12,4},{1,9},{5,13},{9,1},{13,5},{2,10},{6,14},... | collective-permute-start | bytes 196616 | tf_op jit(solution)/shard_map/ppermute | solution.py:9
  6.6 6.5 %collective-permute-start = (bf16[256,128]{1,0:T(8,128)(2,1)S(1)}, bf16[256,128]{1,0:T(8,128)(2,1)S(1)}, u32[]{:S(2)}, u32[]{:S(2)}) collective-permute-start(bf16[256,128]{1,0:T(8,128)(2,1)S(1)} %constant_dynamic-slice_fusion), channel_id=1, source_target_pairs={{0,4},{4,8},{8,12},{12,0},{1,5},{5,9},{9,13},{13,1},{2,6},{6,10},{... | collective-permute-start | bytes 196616 | tf_op jit(solution)/shard_map/ppermute | solution.py:9
  13.1 2.6 %collective-permute-start.3 = (bf16[3,256,128]{2,1,0:T(8,128)(2,1)S(1)}, bf16[3,256,128]{2,1,0:T(8,128)(2,1)S(1)}, u32[]{:S(2)}, u32[]{:S(2)}) collective-permute-start(bf16[3,256,128]{2,1,0:T(8,128)(2,1)S(1)} %pad_maximum_fusion.5), channel_id=1, source_target_pairs={{0,1},{1,0},{2,3},{3,2},{4,5},{5,4},{6,7},{7,6},{8,9},{9,8},{10,11... | collective-permute-start | bytes 589832 | tf_op jit(solution)/shard_map/ppermute | solution.py:9
  18.4 3.1 %collective-permute-start.4 = (f32[1032,128]{1,0:T(8,128)S(1)}, f32[1032,128]{1,0:T(8,128)S(1)}, u32[]{:S(2)}, u32[]{:S(2)}) collective-permute-start(f32[1032,128]{1,0:T(8,128)S(1)} %broadcast_select_fusion), channel_id=1, source_target_pairs={{0,1},{1,0},{2,3},{3,2},{4,5},{5,4},{6,7},{7,6},{8,9},{9,8},{10,11... | collective-permute-start | bytes 1585160 | tf_op jit(solution)/shard_map/ppermute | solution.py:9
  20.0 14.1 %collective-permute-start.6 = (f32[520,256]{1,0:T(8,128)S(1)}, f32[520,256]{1,0:T(8,128)S(1)}, u32[]{:S(2)}, u32[]{:S(2)}) collective-permute-start(f32[520,256]{1,0:T(8,128)S(1)} %pad_maximum_fusion.1), channel_id=1, source_target_pairs={{0,2},{2,0},{1,3},{3,1},{4,6},{6,4},{5,7},{7,5},{8,10},{10,8},{9,1... | collective-permute-start | bytes 1597448 | tf_op jit(solution)/shard_map/ppermute | solution.py:9
  21.7 13.3 %collective-permute-start.7 = (f32[264,128]{1,0:T(8,128)S(1)}, f32[264,128]{1,0:T(8,128)S(1)}, u32[]{:S(2)}, u32[]{:S(2)}) collective-permute-start(f32[264,128]{1,0:T(8,128)S(1)} %concatenate.48), channel_id=1, source_target_pairs={{0,12},{4,0},{8,4},{12,8},{1,13},{5,1},{9,5},{13,9},{2,14},{6,2},{... | collective-permute-start | bytes 405512 | tf_op jit(solution)/shard_map/ppermute | solution.py:9
  23.7 12.0 %collective-permute-start.8 = (f32[264,128]{1,0:T(8,128)S(1)}, f32[264,128]{1,0:T(8,128)S(1)}, u32[]{:S(2)}, u32[]{:S(2)}) collective-permute-start(f32[264,128]{1,0:T(8,128)S(1)} %get-tuple-element.41), channel_id=1, source_target_pairs={{0,8},{4,12},{8,0},{12,4},{1,9},{5,13},{9,1},{13,5},{2,10},{6,14},... | collective-permute-start | bytes 405512 | tf_op jit(solution)/shard_map/ppermute | solution.py:9
  23.7 11.2 %collective-permute-start.5 = (f32[264,128]{1,0:T(8,128)S(1)}, f32[264,128]{1,0:T(8,128)S(1)}, u32[]{:S(2)}, u32[]{:S(2)}) collective-permute-start(f32[264,128]{1,0:T(8,128)S(1)} %get-tuple-element.42), channel_id=1, source_target_pairs={{0,4},{4,8},{8,12},{12,0},{1,5},{5,9},{9,13},{13,1},{2,6},{6,10},{... | collective-permute-start | bytes 405512 | tf_op jit(solution)/shard_map/ppermute | solution.py:9
  35.7 1.4 %collective-permute-start.9 = (f32[264,128]{1,0:T(8,128)S(1)}, f32[264,128]{1,0:T(8,128)S(1)}, u32[]{:S(2)}, u32[]{:S(2)}) collective-permute-start(f32[264,128]{1,0:T(8,128)S(1)} %pad_maximum_fusion.8), channel_id=1, source_target_pairs={{0,1},{1,0},{2,3},{3,2},{4,5},{5,4},{6,7},{7,6},{8,9},{9,8},{10,11... | collective-permute-start | bytes 405512 | tf_op jit(solution)/shard_map/ppermute | solution.py:9

commit v11 on v8

--- a/solution.py
+++ b/solution.py
@@ -35,8 +35,14 @@
     row_blocks, stored, width = values.shape[0], values.shape[1], values.shape[2]
     n_row, rank = h_stack.shape[0], h_stack.shape[1]
     tile_rows = w_tile.shape[0]
-    h_all = jnp.concatenate([h_stack[d] for d in range(n_row)], axis=1)
-    product = jnp.dot(w_tile, h_all, preferred_element_type=jnp.float32)
+    h_rest = jnp.concatenate([h_stack[d] for d in range(1, n_row)], axis=1)
+    product = jnp.concatenate(
+        [
+            jnp.dot(w_tile, h_stack[0], preferred_element_type=jnp.float32),
+            jnp.dot(w_tile, h_rest, preferred_element_type=jnp.float32),
+        ],
+        axis=1,
+    )
     chunks = []
     for d in range(n_row):
         block = (row_index - d) % n_row
@@ -49,9 +55,17 @@
         p_d = product[:, d * width:(d + 1) * width].reshape(row_blocks, width, width)
         r_d = jnp.where(covered[:, None, None], a_d.astype(jnp.float32) / p_d, 0.0)
         chunks.append(r_d.astype(jnp.bfloat16).reshape(tile_rows, width))
-    ratios = jnp.concatenate(chunks, axis=1)
-    numer_h_all = jnp.einsum("ik,ij->kj", w_tile, ratios, preferred_element_type=jnp.float32)
-    numer_w = jnp.einsum("ij,kj->ik", ratios, h_all, preferred_element_type=jnp.float32)
+    ratios_rest = jnp.concatenate(chunks[1:], axis=1)
+    numer_h_all = jnp.concatenate(
+        [
+            jnp.einsum("ik,ij->kj", w_tile, chunks[0], preferred_element_type=jnp.float32),
+            jnp.einsum("ik,ij->kj", w_tile, ratios_rest, preferred_element_type=jnp.float32),
+        ],
+        axis=1,
+    )
+    numer_w = jnp.einsum(
+        "ij,kj->ik", chunks[0], h_stack[0], preferred_element_type=jnp.float32
+    ) + jnp.einsum("ij,kj->ik", ratios_rest, h_rest, preferred_element_type=jnp.float32)
     starts = [((-e) % n_row) * width for e in range(n_row)]
     return [numer_h_all[:, s:s + width] for s in starts], numer_w
 

time: 37.3 us -> 36.4 us (0.976)
  waiting for transfers between devices: 12.8 us -> 10.1 us
  matrix products: 2.27 us -> 4 us
  other arithmetic: 4.1 us -> 3.18 us
  local copies, waits for them, and re-layouts: 3.81 us -> 4.36 us
    ppermute x10, waiting for transfers between devices: 12.8 us -> 10.1 us  [shifted(): lax.ppermute(value, axis, [(i, (i + by) % length) for i in range(length)])]
    unnamed x8 -> x15, local copies, waits for them, and re-layouts: 0.09 us -> 2.08 us
    dot_general x3 -> x6, matrix products: 2.27 us -> 4 us  [the longest x1 1.33 us: dense_terms(): jnp.einsum('ij,kj->ik', chunks[0], h_stack[0], preferred_element_type=jnp...]
    slice x1, local copies, waits for them, and re-layouts: 1.27 us -> 0.07 us  [dense_terms(): a_d = jnp.where(match[:, None, None], values[:, slot], a_d)]
    or x1, other arithmetic: 0.77 us -> 0.02 us  [dense_terms(): covered = covered | match]
  transfers between devices with their start and end apart: 10 -> 10, of which waited for: 5 -> 3; matrix products, arithmetic and copies ran while one was open for 15% -> 19% of each run, Pallas kernels for 0% -> 0%
where the time goes in v11:
time: 36.4 us; the launch traced here: 35.8 us
  starting transfers between devices  13.1 us (36%)
  waiting for transfers between devices  10.1 us (28%)
  local copies, waits for them, and re-layouts  4.36 us (12%)
  matrix products  4 us (11%)
  other arithmetic  3.18 us (9%)
  between operations  1.08 us (3%)
    ppermute x10, starting transfers between devices, shifted(): lax.ppermute(value, axis, [(i, (i + by) % length) for i in range(length)])  13.1 us
    ppermute x10, waiting for transfers between devices, shifted(): lax.ppermute(value, axis, [(i, (i + by) % length) for i in range(length)])  10.1 us
    unnamed x15, local copies, waits for them, and re-layouts  2.08 us
    dot_general x1, matrix products, dense_terms(): jnp.einsum('ij,kj->ik', chunks[0], h_stack[0], preferred_element_type=jnp...  1.33 us
    dynamic_slice x1, local copies, waits for them, and re-layouts, body(): own_piece = lax.dynamic_slice_in_dim(h_factor, sub_index * half, half, 1)  0.92 us
    broadcast_in_dim x1, other arithmetic, body(): w_new = (w_part * mine_w / h_total[None, :])[None]  0.9 us
    div x1, other arithmetic, body(): h_new = h_factor.astype(jnp.float32) * numer_h / w_total[:, None]  0.82 us
    convert_element_type x1, other arithmetic, dense_terms(): chunks.append(r_d.astype(jnp.bfloat16).reshape(tile_rows, width))  0.74 us
  transfers between devices with their start and end apart: 10, of which 3 were waited for; matrix products, arithmetic and copies ran while one was open for 19% of the time, Pallas kernels for 0%

profile of v11, /device:TPU:0, one launch (start us, length us, event | category | flops | bytes accessed | tf_op | source)
XLA Modules:
  0.0 35.8 jit_solution(9521110909828253681)
XLA Ops:
  0.7 0.9 %constant_dynamic-slice_fusion = bf16[256,128]{1,0:T(8,128)(2,1)S(1)} fusion(bf16[256,256]{1,0:T(8,128)(2,1)} %param.9, s32[]{:T(128)S(6)} %select_n.153), kind=kLoop, calls=%fused_computation.86 | loop fusion | bytes 131076 | tf_op jit(solution)/shard_map/dynamic_slice | solution.py:123
  1.6 3.0 %collective-permute-start = (bf16[256,128]{1,0:T(8,128)(2,1)S(1)}, bf16[256,128]{1,0:T(8,128)(2,1)S(1)}, u32[]{:S(2)}, u32[]{:S(2)}) collective-permute-start(bf16[256,128]{1,0:T(8,128)(2,1)S(1)} %constant_dynamic-slice_fusion), channel_id=1, source_target_pairs={{0,4},{4,8},{8,12},{12,0},{1,5},{5,9},{9,13},{13,1},{2,6},{6,10},{... | collective-permute-start | bytes 196616 | tf_op jit(solution)/shard_map/ppermute | solution.py:9
  4.6 2.6 %collective-permute-start.1 = (bf16[256,128]{1,0:T(8,128)(2,1)S(1)}, bf16[256,128]{1,0:T(8,128)(2,1)S(1)}, u32[]{:S(2)}, u32[]{:S(2)}) collective-permute-start(bf16[256,128]{1,0:T(8,128)(2,1)S(1)} %constant_dynamic-slice_fusion), channel_id=1, source_target_pairs={{0,8},{4,12},{8,0},{12,4},{1,9},{5,13},{9,1},{13,5},{2,10},{6,14},... | collective-permute-start | bytes 196616 | tf_op jit(solution)/shard_map/ppermute | solution.py:9
  7.2 1.3 %collective-permute-start.2 = (bf16[256,128]{1,0:T(8,128)(2,1)S(1)}, bf16[256,128]{1,0:T(8,128)(2,1)S(1)}, u32[]{:S(2)}, u32[]{:S(2)}) collective-permute-start(bf16[256,128]{1,0:T(8,128)(2,1)S(1)} %constant_dynamic-slice_fusion), channel_id=1, source_target_pairs={{0,12},{4,0},{8,4},{12,8},{1,13},{5,1},{9,5},{13,9},{2,14},{6,2},{... | collective-permute-start | bytes 196616 | tf_op jit(solution)/shard_map/ppermute | solution.py:9
  8.6 1.3 %copy.15 = bf16[1,1,4,2,256,256]{5,4,2,3,1,0:T(8,128)(2,1)S(1)} copy(bf16[1,1,4,2,256,256]{5,4,3,2,1,0:T(8,128)(2,1)} %param.5) | data formatting | bytes 2097152 | tf_op args[0]
  10.0 0.4 %fusion.1 = bf16[4,256,256]{2,1,0:T(8,128)(2,1)S(1)} fusion(bf16[4,256,256]{2,1,0:T(8,128)(2,1)S(1)} %bitcast.103, pred[4]{0:T(512)(128)(4,1)S(1)} %get-tuple-element.46, pred[4]{0:T(512)(128)(4,1)S(1)} %get-tuple-element.45, pred[4]{0:T(512)(128)(4,1)S(1)} %get-tuple-element.44, bf16[256,256]{1,0:T(8,128)(2,1)S(1)} %copy-done.1, ...), kind=kOutput, calls=%fused_computation.5 | convolution fusion | flops 135790592 | bytes 2228236 | tf_op jit(solution)/shard_map/dot_general | solution.py:41
  10.4 0.4 convolution_bitcast_fusion.2
  10.8 1.3 %fusion.33 = f32[1024,256]{1,0:T(8,128)} fusion(bf16[1024,256]{1,0:T(8,128)(2,1)S(1)} %bitcast.107, bf16[256,256]{1,0:T(8,128)(2,1)S(1)} %copy-done.1), kind=kOutput, calls=%fused_computation.98 | convolution fusion | flops 134217728 | bytes 1703936 | tf_op jit(solution)/shard_map/ij,kj->ik/dot_general | solution.py:66
  13.1 0.2 copy.8
  13.3 0.2 copy.9
  13.7 1.4 %collective-permute-done.3 = bf16[3,256,128]{2,1,0:T(8,128)(2,1)S(1)} collective-permute-done((bf16[3,256,128]{2,1,0:T(8,128)(2,1)S(1)}, bf16[3,256,128]{2,1,0:T(8,128)(2,1)S(1)}, u32[]{:S(2)}, u32[]{:S(2)}) %collective-permute-start.3) | collective-permute-done | bytes 196640 | tf_op jit(solution)/shard_map/ppermute | solution.py:9
  15.2 0.6 %convolution_bitcast_fusion = f32[1024,768]{0,1:T(8,128)S(1)} fusion(bf16[1,1024,256]{2,1,0:T(8,128)(2,1)S(1)} %copy-done, bf16[256,256]{1,0:T(8,128)(2,1)S(1)} %get-tuple-element.28, bf16[256,256]{1,0:T(8,128)(2,1)S(1)} %get-tuple-element.29, bf16[256,256]{1,0:T(8,128)(2,1)S(1)} %get-tuple-element.27), kind=kOutput, calls=%fused_computation | convolution fusion | flops 403832832 | bytes 4063232 | tf_op jit(solution)/shard_map/dot_general | solution.py:42
  15.9 0.7 %fusion.7 = (bf16[1024,256]{0,1:T(8,128)(2,1)S(1)}, bf16[1024,256]{0,1:T(8,128)(2,1)S(1)}, bf16[1024,256]{0,1:T(8,128)(2,1)S(1)}) fusion(f32[1024,768]{0,1:T(8,128)S(1)} %convolution_bitcast_fusion, bf16[1024,256]{0,1:T(8,128)(2,1)S(1)} %copy.9, bf16[1024,256]{0,1:T(8,128)(2,1)S(1)} %copy.8, pred[1024]{0:T(1024)(128)(4,1)S(1)} %broadcast_in_dim.142, ...), kind=kLoop, calls=%fused_computation.16 | loop fusion | flops 4718592 | bytes 5776384 | tf_op jit(solution)/shard_map/convert_element_type | solution.py:57
  16.6 0.7 %convolution_bitcast_fusion.1 = f32[256,768]{1,0:T(8,128)S(1)} fusion(bf16[1024,256]{0,1:T(8,128)(2,1)S(1)} %get-tuple-element.15, bf16[1024,256]{0,1:T(8,128)(2,1)S(1)} %get-tuple-element.16, bf16[1024,256]{0,1:T(8,128)(2,1)S(1)} %get-tuple-element.14, bf16[1,1024,256]{2,1,0:T(8,128)(2,1)S(1)} %copy-done), kind=kOutput, calls=%fused_computation.6 | convolution fusion | flops 407371776 | bytes 2883584 | tf_op jit(solution)/shard_map/ik,ij->kj/dot_general | solution.py:62
  17.8 0.7 %copy-done.2 = f32[1024,256]{1,0:T(8,128)S(1)} copy-done((f32[1024,256]{1,0:T(8,128)S(1)}, f32[1024,256]{1,0:T(8,128)}, u32[]{:S(2)}) %copy-start.2) | copy-done | bytes 1048600
  18.5 0.6 %convolution_add_fusion = f32[1024,256]{1,0:T(8,128)S(1)} fusion(f32[1024,256]{1,0:T(8,128)S(1)} %copy-done.2, bf16[1024,256]{0,1:T(8,128)(2,1)S(1)} %get-tuple-element.15, bf16[1024,256]{0,1:T(8,128)(2,1)S(1)} %get-tuple-element.16, bf16[1024,256]{0,1:T(8,128)(2,1)S(1)} %get-tuple-element.14, bf16[256,256]{1,0:T(8,128)(2,1)S(1)} %get-tuple-element.28, ...), kind=kOutput, calls=%fused_computation.2 | convolution fusion | flops 408813568 | bytes 4063232 | tf_op jit(solution)/shard_map/ij,kj->ik/dot_general | solution.py:68
  19.2 1.6 %collective-permute-start.4 = (f32[520,256]{1,0:T(8,128)S(1)}, f32[520,256]{1,0:T(8,128)S(1)}, u32[]{:S(2)}, u32[]{:S(2)}) collective-permute-start(f32[520,256]{1,0:T(8,128)S(1)} %pad_maximum_fusion.3), channel_id=1, source_target_pairs={{0,2},{2,0},{1,3},{3,1},{4,6},{6,4},{5,7},{7,5},{8,10},{10,8},{9,1... | collective-permute-start | bytes 1597448 | tf_op jit(solution)/shard_map/ppermute | solution.py:9
  21.0 0.4 %collective-permute-start.7 = (f32[264,128]{1,0:T(8,128)S(1)}, f32[264,128]{1,0:T(8,128)S(1)}, u32[]{:S(2)}, u32[]{:S(2)}) collective-permute-start(f32[264,128]{1,0:T(8,128)S(1)} %get-tuple-element.36), channel_id=1, source_target_pairs={{0,8},{4,12},{8,0},{12,4},{1,9},{5,13},{9,1},{13,5},{2,10},{6,14},... | collective-permute-start | bytes 405512 | tf_op jit(solution)/shard_map/ppermute | solution.py:9
  21.4 1.6 %collective-permute-start.8 = (f32[264,128]{1,0:T(8,128)S(1)}, f32[264,128]{1,0:T(8,128)S(1)}, u32[]{:S(2)}, u32[]{:S(2)}) collective-permute-start(f32[264,128]{1,0:T(8,128)S(1)} %get-tuple-element.37), channel_id=1, source_target_pairs={{0,4},{4,8},{8,12},{12,0},{1,5},{5,9},{9,13},{13,1},{2,6},{6,10},{... | collective-permute-start | bytes 405512 | tf_op jit(solution)/shard_map/ppermute | solution.py:9
  22.9 2.3 %collective-permute-start.6 = (f32[264,128]{1,0:T(8,128)S(1)}, f32[264,128]{1,0:T(8,128)S(1)}, u32[]{:S(2)}, u32[]{:S(2)}) collective-permute-start(f32[264,128]{1,0:T(8,128)S(1)} %concatenate.48), channel_id=1, source_target_pairs={{0,12},{4,0},{8,4},{12,8},{1,13},{5,1},{9,5},{13,9},{2,14},{6,2},{... | collective-permute-start | bytes 405512 | tf_op jit(solution)/shard_map/ppermute | solution.py:9
  25.2 8.3 %collective-permute-done.4 = f32[520,256]{1,0:T(8,128)S(1)} collective-permute-done((f32[520,256]{1,0:T(8,128)S(1)}, f32[520,256]{1,0:T(8,128)S(1)}, u32[]{:S(2)}, u32[]{:S(2)}) %collective-permute-start.4) | collective-permute-done | bytes 532512 | tf_op jit(solution)/shard_map/ppermute | solution.py:9
  33.6 0.9 %fusion.10 = f32[1,512,256]{2,1,0:T(8,128)} fusion(f32[520,256]{1,0:T(8,128)S(1)} %collective-permute-done.4, f32[2,512,256]{2,1,0:T(8,128)S(1)} %bitcast.112, s32[]{:T(128)S(6)} %select_n.167, f32[256]{0:T(256)S(1)} %bitcast.123, bf16[1,1024,256]{2,1,0:T(8,128)(2,1)S(1)} %copy-done, s32[]{:T(128)S(6)} %select_n.143), kind=kLoop, calls=%fused_computation.25 | loop fusion | flops 524288 | bytes 1836040 | tf_op jit(solution)/shard_map/broadcast_in_dim | solution.py:177
  34.5 0.4 %collective-permute-done.9 = f32[264,128]{1,0:T(8,128)S(1)} collective-permute-done((f32[264,128]{1,0:T(8,128)S(1)}, f32[264,128]{1,0:T(8,128)S(1)}, u32[]{:S(2)}, u32[]{:S(2)}) %collective-permute-start.9) | collective-permute-done | bytes 135200 | tf_op jit(solution)/shard_map/ppermute | solution.py:9
  35.0 0.8 %fusion.17 = f32[256,256]{1,0:T(8,128)} fusion(f32[264,128]{1,0:T(8,128)S(1)} %get-tuple-element.33, f32[264,128]{1,0:T(8,128)S(1)} %get-tuple-element.32, bf16[256,256]{1,0:T(8,128)(2,1)S(1)} %copy-done.1, f32[256]{0:T(256)S(1)} %bitcast.121), kind=kLoop, calls=%fused_computation.42 | loop fusion | flops 262144 | bytes 664576 | tf_op jit(solution)/shard_map/div | solution.py:175
  (65 shorter events, 2.2 us)
Async XLA Ops:
  0.6 9.4 %copy-start.1 = (bf16[256,256]{1,0:T(8,128)(2,1)S(1)}, bf16[256,256]{1,0:T(8,128)(2,1)}, u32[]{:S(2)}) copy-start(bf16[256,256]{1,0:T(8,128)(2,1)} %param.9) | copy-start | bytes 393220
  0.6 9.3 %copy-start.3 = (s32[1,1,4,2]{2,3,1,0:T(2,128)S(1)}, s32[1,1,4,2]{2,3,1,0:T(2,128)}, u32[]{:S(2)}) copy-start(s32[1,1,4,2]{2,3,1,0:T(2,128)} %param.6) | copy-start | bytes 100
  0.7 9.3 %copy-start.4 = (s32[1,1,4]{2,1,0:T(1,128)S(1)}, s32[1,1,4]{2,1,0:T(1,128)}, u32[]{:S(2)}) copy-start(s32[1,1,4]{2,1,0:T(1,128)} %param.7) | copy-start | bytes 52
  0.7 9.4 %copy-start = (bf16[1,1024,256]{2,1,0:T(8,128)(2,1)S(1)}, bf16[1,1024,256]{2,1,0:T(8,128)(2,1)}, u32[]{:S(2)}) copy-start(bf16[1,1024,256]{2,1,0:T(8,128)(2,1)} %param.8) | copy-start | bytes 1572868
  1.6 12.0 %collective-permute-start = (bf16[256,128]{1,0:T(8,128)(2,1)S(1)}, bf16[256,128]{1,0:T(8,128)(2,1)S(1)}, u32[]{:S(2)}, u32[]{:S(2)}) collective-permute-start(bf16[256,128]{1,0:T(8,128)(2,1)S(1)} %constant_dynamic-slice_fusion), channel_id=1, source_target_pairs={{0,4},{4,8},{8,12},{12,0},{1,5},{5,9},{9,13},{13,1},{2,6},{6,10},{... | collective-permute-start | bytes 196616 | tf_op jit(solution)/shard_map/ppermute | solution.py:9
  4.6 8.9 %collective-permute-start.1 = (bf16[256,128]{1,0:T(8,128)(2,1)S(1)}, bf16[256,128]{1,0:T(8,128)(2,1)S(1)}, u32[]{:S(2)}, u32[]{:S(2)}) collective-permute-start(bf16[256,128]{1,0:T(8,128)(2,1)S(1)} %constant_dynamic-slice_fusion), channel_id=1, source_target_pairs={{0,8},{4,12},{8,0},{12,4},{1,9},{5,13},{9,1},{13,5},{2,10},{6,14},... | collective-permute-start | bytes 196616 | tf_op jit(solution)/shard_map/ppermute | solution.py:9
  7.2 6.4 %collective-permute-start.2 = (bf16[256,128]{1,0:T(8,128)(2,1)S(1)}, bf16[256,128]{1,0:T(8,128)(2,1)S(1)}, u32[]{:S(2)}, u32[]{:S(2)}) collective-permute-start(bf16[256,128]{1,0:T(8,128)(2,1)S(1)} %constant_dynamic-slice_fusion), channel_id=1, source_target_pairs={{0,12},{4,0},{8,4},{12,8},{1,13},{5,1},{9,5},{13,9},{2,14},{6,2},{... | collective-permute-start | bytes 196616 | tf_op jit(solution)/shard_map/ppermute | solution.py:9
  13.6 1.5 %collective-permute-start.3 = (bf16[3,256,128]{2,1,0:T(8,128)(2,1)S(1)}, bf16[3,256,128]{2,1,0:T(8,128)(2,1)S(1)}, u32[]{:S(2)}, u32[]{:S(2)}) collective-permute-start(bf16[3,256,128]{2,1,0:T(8,128)(2,1)S(1)} %pad_maximum_fusion.5), channel_id=1, source_target_pairs={{0,1},{1,0},{2,3},{3,2},{4,5},{5,4},{6,7},{7,6},{8,9},{9,8},{10,11... | collective-permute-start | bytes 589832 | tf_op jit(solution)/shard_map/ppermute | solution.py:9
  17.3 1.2 %copy-start.2 = (f32[1024,256]{1,0:T(8,128)S(1)}, f32[1024,256]{1,0:T(8,128)}, u32[]{:S(2)}) copy-start(f32[1024,256]{1,0:T(8,128)} %fusion.33) | copy-start | bytes 3145732
  17.4 3.4 %collective-permute-start.5 = (f32[1032,128]{1,0:T(8,128)S(1)}, f32[1032,128]{1,0:T(8,128)S(1)}, u32[]{:S(2)}, u32[]{:S(2)}) collective-permute-start(f32[1032,128]{1,0:T(8,128)S(1)} %broadcast_select_fusion), channel_id=1, source_target_pairs={{0,1},{1,0},{2,3},{3,2},{4,5},{5,4},{6,7},{7,6},{8,9},{9,8},{10,11... | collective-permute-start | bytes 1585160 | tf_op jit(solution)/shard_map/ppermute | solution.py:9
  19.2 14.2 %collective-permute-start.4 = (f32[520,256]{1,0:T(8,128)S(1)}, f32[520,256]{1,0:T(8,128)S(1)}, u32[]{:S(2)}, u32[]{:S(2)}) collective-permute-start(f32[520,256]{1,0:T(8,128)S(1)} %pad_maximum_fusion.3), channel_id=1, source_target_pairs={{0,2},{2,0},{1,3},{3,1},{4,6},{6,4},{5,7},{7,5},{8,10},{10,8},{9,1... | collective-permute-start | bytes 1597448 | tf_op jit(solution)/shard_map/ppermute | solution.py:9
  21.0 12.5 %collective-permute-start.7 = (f32[264,128]{1,0:T(8,128)S(1)}, f32[264,128]{1,0:T(8,128)S(1)}, u32[]{:S(2)}, u32[]{:S(2)}) collective-permute-start(f32[264,128]{1,0:T(8,128)S(1)} %get-tuple-element.36), channel_id=1, source_target_pairs={{0,8},{4,12},{8,0},{12,4},{1,9},{5,13},{9,1},{13,5},{2,10},{6,14},... | collective-permute-start | bytes 405512 | tf_op jit(solution)/shard_map/ppermute | solution.py:9
  21.4 12.1 %collective-permute-start.8 = (f32[264,128]{1,0:T(8,128)S(1)}, f32[264,128]{1,0:T(8,128)S(1)}, u32[]{:S(2)}, u32[]{:S(2)}) collective-permute-start(f32[264,128]{1,0:T(8,128)S(1)} %get-tuple-element.37), channel_id=1, source_target_pairs={{0,4},{4,8},{8,12},{12,0},{1,5},{5,9},{9,13},{13,1},{2,6},{6,10},{... | collective-permute-start | bytes 405512 | tf_op jit(solution)/shard_map/ppermute | solution.py:9
  22.9 10.6 %collective-permute-start.6 = (f32[264,128]{1,0:T(8,128)S(1)}, f32[264,128]{1,0:T(8,128)S(1)}, u32[]{:S(2)}, u32[]{:S(2)}) collective-permute-start(f32[264,128]{1,0:T(8,128)S(1)} %concatenate.48), channel_id=1, source_target_pairs={{0,12},{4,0},{8,4},{12,8},{1,13},{5,1},{9,5},{13,9},{2,14},{6,2},{... | collective-permute-start | bytes 405512 | tf_op jit(solution)/shard_map/ppermute | solution.py:9
  33.6 1.4 %collective-permute-start.9 = (f32[264,128]{1,0:T(8,128)S(1)}, f32[264,128]{1,0:T(8,128)S(1)}, u32[]{:S(2)}, u32[]{:S(2)}) collective-permute-start(f32[264,128]{1,0:T(8,128)S(1)} %pad_maximum_fusion.10), channel_id=1, source_target_pairs={{0,1},{1,0},{2,3},{3,2},{4,5},{5,4},{6,7},{7,6},{8,9},{9,8},{10,11... | collective-permute-start | bytes 405512 | tf_op jit(solution)/shard_map/ppermute | solution.py:9

commit v12 on v11

--- a/solution.py
+++ b/solution.py
@@ -145,6 +145,8 @@
         mine_w = mine_w + message[:share]
         got_h = got_h + message[share:]
     h_total = from_rows(got_h, rank)
+    w_part = lax.dynamic_slice_in_dim(w_tile, col_index * share, share, 0)
+    w_new = (w_part.astype(jnp.float32) * mine_w / h_total[None, :])[None]
 
     w_rows_sum = as_rows(w_sum, width)
     messages = [
@@ -165,6 +167,8 @@
     got_w = extra
     for d in reversed(range(1, n_row)):
         message = shifted(jnp.concatenate([reduced[d * rank:(d + 1) * rank], extra]), "row", d)
+        if d == 1:
+            message, w_new = lax.optimization_barrier((message, w_new))
         mine_h = mine_h + message[:rank]
         got_w = got_w + message[rank:]
     final = jnp.concatenate([mine_h, got_w])
@@ -173,8 +177,6 @@
     w_total = from_rows(total[rank:], rank)
 
     h_new = h_factor.astype(jnp.float32) * numer_h / w_total[:, None]
-    w_part = lax.dynamic_slice_in_dim(w_tile, col_index * share, share, 0).astype(jnp.float32)
-    w_new = (w_part * mine_w / h_total[None, :])[None]
     return (w_new, h_new)
 
 

time: 36.4 us -> 36.5 us (level)
  waiting for transfers between devices: 10.1 us -> 11.4 us
  local copies, waits for them, and re-layouts: 4.36 us -> 3.84 us
  starting transfers between devices: 13.1 us -> 12.7 us
    ppermute x10, waiting for transfers between devices: 10.1 us -> 11.4 us  [shifted(): lax.ppermute(value, axis, [(i, (i + by) % length) for i in range(length)])]
    unnamed x15, local copies, waits for them, and re-layouts: 2.08 us -> 1.57 us
  transfers between devices with their start and end apart: 10 -> 10, of which waited for: 3 -> 3; matrix products, arithmetic and copies ran while one was open for 19% -> 18% of each run, Pallas kernels for 0% -> 0%
where the time goes in v12:
time: 36.5 us; the launch traced here: 36.3 us
  starting transfers between devices  12.7 us (35%)
  waiting for transfers between devices  11.4 us (31%)
  matrix products  4.01 us (11%)
  local copies, waits for them, and re-layouts  3.84 us (11%)
  other arithmetic  3.18 us (9%)
  between operations  1.08 us (3%)
    ppermute x10, starting transfers between devices, shifted(): lax.ppermute(value, axis, [(i, (i + by) % length) for i in range(length)])  12.7 us
    ppermute x10, waiting for transfers between devices, shifted(): lax.ppermute(value, axis, [(i, (i + by) % length) for i in range(length)])  11.4 us
    unnamed x15, local copies, waits for them, and re-layouts  1.57 us
    dot_general x1, matrix products, dense_terms(): jnp.einsum('ij,kj->ik', chunks[0], h_stack[0], preferred_element_type=jnp...  1.33 us
    dynamic_slice x1, local copies, waits for them, and re-layouts, body(): own_piece = lax.dynamic_slice_in_dim(h_factor, sub_index * half, half, 1)  0.92 us
    broadcast_in_dim x1, other arithmetic, body(): w_new = (w_part.astype(jnp.float32) * mine_w / h_total[None, :])[None]  0.89 us
    div x1, other arithmetic, body(): h_new = h_factor.astype(jnp.float32) * numer_h / w_total[:, None]  0.82 us
    convert_element_type x1, other arithmetic, dense_terms(): chunks.append(r_d.astype(jnp.bfloat16).reshape(tile_rows, width))  0.74 us
  transfers between devices with their start and end apart: 10, of which 3 were waited for; matrix products, arithmetic and copies ran while one was open for 18% of the time, Pallas kernels for 0%

profile of v12, /device:TPU:0, one launch (start us, length us, event | category | flops | bytes accessed | tf_op | source)
XLA Modules:
  0.0 36.3 jit_solution(12154898707266408303)
XLA Ops:
  0.7 0.9 %constant_dynamic-slice_fusion = bf16[256,128]{1,0:T(8,128)(2,1)S(1)} fusion(bf16[256,256]{1,0:T(8,128)(2,1)} %param.9, s32[]{:T(128)S(6)} %select_n.153), kind=kLoop, calls=%fused_computation.86 | loop fusion | bytes 131076 | tf_op jit(solution)/shard_map/dynamic_slice | solution.py:123
  1.6 3.0 %collective-permute-start = (bf16[256,128]{1,0:T(8,128)(2,1)S(1)}, bf16[256,128]{1,0:T(8,128)(2,1)S(1)}, u32[]{:S(2)}, u32[]{:S(2)}) collective-permute-start(bf16[256,128]{1,0:T(8,128)(2,1)S(1)} %constant_dynamic-slice_fusion), channel_id=1, source_target_pairs={{0,4},{4,8},{8,12},{12,0},{1,5},{5,9},{9,13},{13,1},{2,6},{6,10},{... | collective-permute-start | bytes 196616 | tf_op jit(solution)/shard_map/ppermute | solution.py:9
  4.6 2.6 %collective-permute-start.1 = (bf16[256,128]{1,0:T(8,128)(2,1)S(1)}, bf16[256,128]{1,0:T(8,128)(2,1)S(1)}, u32[]{:S(2)}, u32[]{:S(2)}) collective-permute-start(bf16[256,128]{1,0:T(8,128)(2,1)S(1)} %constant_dynamic-slice_fusion), channel_id=1, source_target_pairs={{0,8},{4,12},{8,0},{12,4},{1,9},{5,13},{9,1},{13,5},{2,10},{6,14},... | collective-permute-start | bytes 196616 | tf_op jit(solution)/shard_map/ppermute | solution.py:9
  7.2 1.3 %collective-permute-start.2 = (bf16[256,128]{1,0:T(8,128)(2,1)S(1)}, bf16[256,128]{1,0:T(8,128)(2,1)S(1)}, u32[]{:S(2)}, u32[]{:S(2)}) collective-permute-start(bf16[256,128]{1,0:T(8,128)(2,1)S(1)} %constant_dynamic-slice_fusion), channel_id=1, source_target_pairs={{0,12},{4,0},{8,4},{12,8},{1,13},{5,1},{9,5},{13,9},{2,14},{6,2},{... | collective-permute-start | bytes 196616 | tf_op jit(solution)/shard_map/ppermute | solution.py:9
  8.6 1.3 %copy.15 = bf16[1,1,4,2,256,256]{5,4,2,3,1,0:T(8,128)(2,1)S(1)} copy(bf16[1,1,4,2,256,256]{5,4,3,2,1,0:T(8,128)(2,1)} %param.5) | data formatting | bytes 2097152 | tf_op args[0]
  10.0 0.4 %fusion.1 = bf16[4,256,256]{2,1,0:T(8,128)(2,1)S(1)} fusion(bf16[4,256,256]{2,1,0:T(8,128)(2,1)S(1)} %bitcast.103, pred[4]{0:T(512)(128)(4,1)S(1)} %get-tuple-element.50, pred[4]{0:T(512)(128)(4,1)S(1)} %get-tuple-element.49, pred[4]{0:T(512)(128)(4,1)S(1)} %get-tuple-element.48, bf16[256,256]{1,0:T(8,128)(2,1)S(1)} %copy-done.1, ...), kind=kOutput, calls=%fused_computation.5 | convolution fusion | flops 135790592 | bytes 2228236 | tf_op jit(solution)/shard_map/dot_general | solution.py:41
  10.4 1.3 %fusion.35 = f32[1024,256]{1,0:T(8,128)} fusion(bf16[1024,256]{1,0:T(8,128)(2,1)S(1)} %bitcast.106, bf16[256,256]{1,0:T(8,128)(2,1)S(1)} %copy-done.1), kind=kOutput, calls=%fused_computation.98 | convolution fusion | flops 134217728 | bytes 1703936 | tf_op jit(solution)/shard_map/ij,kj->ik/dot_general | solution.py:66
  11.8 0.3 convolution_bitcast_fusion.2
  13.1 0.2 copy.8
  13.3 0.2 copy.9
  13.7 1.4 %collective-permute-done.3 = bf16[3,256,128]{2,1,0:T(8,128)(2,1)S(1)} collective-permute-done((bf16[3,256,128]{2,1,0:T(8,128)(2,1)S(1)}, bf16[3,256,128]{2,1,0:T(8,128)(2,1)S(1)}, u32[]{:S(2)}, u32[]{:S(2)}) %collective-permute-start.3) | collective-permute-done | bytes 196640 | tf_op jit(solution)/shard_map/ppermute | solution.py:9
  15.4 0.6 %convolution_bitcast_fusion = f32[1024,768]{0,1:T(8,128)S(1)} fusion(bf16[1,1024,256]{2,1,0:T(8,128)(2,1)S(1)} %copy-done, bf16[256,256]{1,0:T(8,128)(2,1)S(1)} %get-tuple-element.32, bf16[256,256]{1,0:T(8,128)(2,1)S(1)} %get-tuple-element.33, bf16[256,256]{1,0:T(8,128)(2,1)S(1)} %get-tuple-element.31), kind=kOutput, calls=%fused_computation | convolution fusion | flops 403832832 | bytes 4063232 | tf_op jit(solution)/shard_map/dot_general | solution.py:42
  16.0 0.7 %fusion.7 = (bf16[1024,256]{0,1:T(8,128)(2,1)S(1)}, bf16[1024,256]{0,1:T(8,128)(2,1)S(1)}, bf16[1024,256]{0,1:T(8,128)(2,1)S(1)}) fusion(f32[1024,768]{0,1:T(8,128)S(1)} %convolution_bitcast_fusion, bf16[1024,256]{0,1:T(8,128)(2,1)S(1)} %copy.9, bf16[1024,256]{0,1:T(8,128)(2,1)S(1)} %copy.8, pred[1024]{0:T(1024)(128)(4,1)S(1)} %broadcast_in_dim.142, ...), kind=kLoop, calls=%fused_computation.16 | loop fusion | flops 4718592 | bytes 5776384 | tf_op jit(solution)/shard_map/convert_element_type | solution.py:57
  16.8 0.7 %convolution_bitcast_fusion.1 = f32[256,768]{1,0:T(8,128)S(1)} fusion(bf16[1024,256]{0,1:T(8,128)(2,1)S(1)} %get-tuple-element.19, bf16[1024,256]{0,1:T(8,128)(2,1)S(1)} %get-tuple-element.20, bf16[1024,256]{0,1:T(8,128)(2,1)S(1)} %get-tuple-element.18, bf16[1,1024,256]{2,1,0:T(8,128)(2,1)S(1)} %copy-done), kind=kOutput, calls=%fused_computation.6 | convolution fusion | flops 407371776 | bytes 2883584 | tf_op jit(solution)/shard_map/ik,ij->kj/dot_general | solution.py:62
  17.6 0.2 collective-permute-start.4
  18.0 0.6 %convolution_add_fusion = f32[1024,256]{1,0:T(8,128)S(1)} fusion(f32[1024,256]{1,0:T(8,128)S(1)} %copy-done.2, bf16[1024,256]{0,1:T(8,128)(2,1)S(1)} %get-tuple-element.19, bf16[1024,256]{0,1:T(8,128)(2,1)S(1)} %get-tuple-element.20, bf16[1024,256]{0,1:T(8,128)(2,1)S(1)} %get-tuple-element.18, bf16[256,256]{1,0:T(8,128)(2,1)S(1)} %get-tuple-element.32, ...), kind=kOutput, calls=%fused_computation.2 | convolution fusion | flops 408813568 | bytes 4063232 | tf_op jit(solution)/shard_map/ij,kj->ik/dot_general | solution.py:68
  18.7 1.6 %collective-permute-start.6 = (f32[520,256]{1,0:T(8,128)S(1)}, f32[520,256]{1,0:T(8,128)S(1)}, u32[]{:S(2)}, u32[]{:S(2)}) collective-permute-start(f32[520,256]{1,0:T(8,128)S(1)} %pad_maximum_fusion.3), channel_id=1, source_target_pairs={{0,2},{2,0},{1,3},{3,1},{4,6},{6,4},{5,7},{7,5},{8,10},{10,8},{9,1... | collective-permute-start | bytes 1597448 | tf_op jit(solution)/shard_map/ppermute | solution.py:9
  20.5 0.7 %collective-permute-start.5 = (f32[264,128]{1,0:T(8,128)S(1)}, f32[264,128]{1,0:T(8,128)S(1)}, u32[]{:S(2)}, u32[]{:S(2)}) collective-permute-start(f32[264,128]{1,0:T(8,128)S(1)} %get-tuple-element.41), channel_id=1, source_target_pairs={{0,4},{4,8},{8,12},{12,0},{1,5},{5,9},{9,13},{13,1},{2,6},{6,10},{... | collective-permute-start | bytes 405512 | tf_op jit(solution)/shard_map/ppermute | solution.py:9
  21.2 1.2 %collective-permute-start.8 = (f32[264,128]{1,0:T(8,128)S(1)}, f32[264,128]{1,0:T(8,128)S(1)}, u32[]{:S(2)}, u32[]{:S(2)}) collective-permute-start(f32[264,128]{1,0:T(8,128)S(1)} %get-tuple-element.40), channel_id=1, source_target_pairs={{0,8},{4,12},{8,0},{12,4},{1,9},{5,13},{9,1},{13,5},{2,10},{6,14},... | collective-permute-start | bytes 405512 | tf_op jit(solution)/shard_map/ppermute | solution.py:9
  22.4 2.0 %collective-permute-start.7 = (f32[264,128]{1,0:T(8,128)S(1)}, f32[264,128]{1,0:T(8,128)S(1)}, u32[]{:S(2)}, u32[]{:S(2)}) collective-permute-start(f32[264,128]{1,0:T(8,128)S(1)} %concatenate.48), channel_id=1, source_target_pairs={{0,12},{4,0},{8,4},{12,8},{1,13},{5,1},{9,5},{13,9},{2,14},{6,2},{... | collective-permute-start | bytes 405512 | tf_op jit(solution)/shard_map/ppermute | solution.py:9
  24.3 8.7 %collective-permute-done.6 = f32[520,256]{1,0:T(8,128)S(1)} collective-permute-done((f32[520,256]{1,0:T(8,128)S(1)}, f32[520,256]{1,0:T(8,128)S(1)}, u32[]{:S(2)}, u32[]{:S(2)}) %collective-permute-start.6) | collective-permute-done | bytes 532512 | tf_op jit(solution)/shard_map/ppermute | solution.py:9
  33.0 0.9 %fusion.10 = f32[1,512,256]{2,1,0:T(8,128)} fusion(f32[520,256]{1,0:T(8,128)S(1)} %collective-permute-done.6, f32[2,512,256]{2,1,0:T(8,128)S(1)} %bitcast.112, s32[]{:T(128)S(6)} %select_n.172, f32[256]{0:T(256)S(1)} %bitcast.123, bf16[1,1024,256]{2,1,0:T(8,128)(2,1)S(1)} %copy-done, s32[]{:T(128)S(6)} %select_n.171), kind=kLoop, calls=%fused_computation.25 | loop fusion | flops 524288 | bytes 1836040 | tf_op jit(solution)/shard_map/broadcast_in_dim | solution.py:149
  34.1 1.3 %collective-permute-done.9 = f32[264,128]{1,0:T(8,128)S(1)} collective-permute-done((f32[264,128]{1,0:T(8,128)S(1)}, f32[264,128]{1,0:T(8,128)S(1)}, u32[]{:S(2)}, u32[]{:S(2)}) %collective-permute-start.9) | collective-permute-done | bytes 135200 | tf_op jit(solution)/shard_map/ppermute | solution.py:9
  35.4 0.8 %fusion.17 = f32[256,256]{1,0:T(8,128)} fusion(f32[264,128]{1,0:T(8,128)S(1)} %get-tuple-element.37, f32[264,128]{1,0:T(8,128)S(1)} %get-tuple-element.36, bf16[256,256]{1,0:T(8,128)(2,1)S(1)} %copy-done.1, f32[256]{0:T(256)S(1)} %bitcast.121), kind=kLoop, calls=%fused_computation.42 | loop fusion | flops 262144 | bytes 664576 | tf_op jit(solution)/shard_map/div | solution.py:179
  (65 shorter events, 2.1 us)
Async XLA Ops:
  0.6 9.4 %copy-start.1 = (bf16[256,256]{1,0:T(8,128)(2,1)S(1)}, bf16[256,256]{1,0:T(8,128)(2,1)}, u32[]{:S(2)}) copy-start(bf16[256,256]{1,0:T(8,128)(2,1)} %param.9) | copy-start | bytes 393220
  0.6 9.3 %copy-start.3 = (s32[1,1,4,2]{2,3,1,0:T(2,128)S(1)}, s32[1,1,4,2]{2,3,1,0:T(2,128)}, u32[]{:S(2)}) copy-start(s32[1,1,4,2]{2,3,1,0:T(2,128)} %param.6) | copy-start | bytes 100
  0.7 9.3 %copy-start.4 = (s32[1,1,4]{2,1,0:T(1,128)S(1)}, s32[1,1,4]{2,1,0:T(1,128)}, u32[]{:S(2)}) copy-start(s32[1,1,4]{2,1,0:T(1,128)} %param.7) | copy-start | bytes 52
  0.7 9.4 %copy-start = (bf16[1,1024,256]{2,1,0:T(8,128)(2,1)S(1)}, bf16[1,1024,256]{2,1,0:T(8,128)(2,1)}, u32[]{:S(2)}) copy-start(bf16[1,1024,256]{2,1,0:T(8,128)(2,1)} %param.8) | copy-start | bytes 1572868
  1.6 12.0 %collective-permute-start = (bf16[256,128]{1,0:T(8,128)(2,1)S(1)}, bf16[256,128]{1,0:T(8,128)(2,1)S(1)}, u32[]{:S(2)}, u32[]{:S(2)}) collective-permute-start(bf16[256,128]{1,0:T(8,128)(2,1)S(1)} %constant_dynamic-slice_fusion), channel_id=1, source_target_pairs={{0,4},{4,8},{8,12},{12,0},{1,5},{5,9},{9,13},{13,1},{2,6},{6,10},{... | collective-permute-start | bytes 196616 | tf_op jit(solution)/shard_map/ppermute | solution.py:9
  4.6 8.9 %collective-permute-start.1 = (bf16[256,128]{1,0:T(8,128)(2,1)S(1)}, bf16[256,128]{1,0:T(8,128)(2,1)S(1)}, u32[]{:S(2)}, u32[]{:S(2)}) collective-permute-start(bf16[256,128]{1,0:T(8,128)(2,1)S(1)} %constant_dynamic-slice_fusion), channel_id=1, source_target_pairs={{0,8},{4,12},{8,0},{12,4},{1,9},{5,13},{9,1},{13,5},{2,10},{6,14},... | collective-permute-start | bytes 196616 | tf_op jit(solution)/shard_map/ppermute | solution.py:9
  7.2 6.4 %collective-permute-start.2 = (bf16[256,128]{1,0:T(8,128)(2,1)S(1)}, bf16[256,128]{1,0:T(8,128)(2,1)S(1)}, u32[]{:S(2)}, u32[]{:S(2)}) collective-permute-start(bf16[256,128]{1,0:T(8,128)(2,1)S(1)} %constant_dynamic-slice_fusion), channel_id=1, source_target_pairs={{0,12},{4,0},{8,4},{12,8},{1,13},{5,1},{9,5},{13,9},{2,14},{6,2},{... | collective-permute-start | bytes 196616 | tf_op jit(solution)/shard_map/ppermute | solution.py:9
  13.6 1.5 %collective-permute-start.3 = (bf16[3,256,128]{2,1,0:T(8,128)(2,1)S(1)}, bf16[3,256,128]{2,1,0:T(8,128)(2,1)S(1)}, u32[]{:S(2)}, u32[]{:S(2)}) collective-permute-start(bf16[3,256,128]{2,1,0:T(8,128)(2,1)S(1)} %pad_maximum_fusion.5), channel_id=1, source_target_pairs={{0,1},{1,0},{2,3},{3,2},{4,5},{5,4},{6,7},{7,6},{8,9},{9,8},{10,11... | collective-permute-start | bytes 589832 | tf_op jit(solution)/shard_map/ppermute | solution.py:9
  16.8 1.2 %copy-start.2 = (f32[1024,256]{1,0:T(8,128)S(1)}, f32[1024,256]{1,0:T(8,128)}, u32[]{:S(2)}) copy-start(f32[1024,256]{1,0:T(8,128)} %fusion.35) | copy-start | bytes 3145732
  17.6 2.7 %collective-permute-start.4 = (f32[1032,128]{1,0:T(8,128)S(1)}, f32[1032,128]{1,0:T(8,128)S(1)}, u32[]{:S(2)}, u32[]{:S(2)}) collective-permute-start(f32[1032,128]{1,0:T(8,128)S(1)} %broadcast_select_fusion), channel_id=1, source_target_pairs={{0,1},{1,0},{2,3},{3,2},{4,5},{5,4},{6,7},{7,6},{8,9},{9,8},{10,11... | collective-permute-start | bytes 1585160 | tf_op jit(solution)/shard_map/ppermute | solution.py:9
  18.7 14.3 %collective-permute-start.6 = (f32[520,256]{1,0:T(8,128)S(1)}, f32[520,256]{1,0:T(8,128)S(1)}, u32[]{:S(2)}, u32[]{:S(2)}) collective-permute-start(f32[520,256]{1,0:T(8,128)S(1)} %pad_maximum_fusion.3), channel_id=1, source_target_pairs={{0,2},{2,0},{1,3},{3,1},{4,6},{6,4},{5,7},{7,5},{8,10},{10,8},{9,1... | collective-permute-start | bytes 1597448 | tf_op jit(solution)/shard_map/ppermute | solution.py:9
  20.5 13.4 %collective-permute-start.5 = (f32[264,128]{1,0:T(8,128)S(1)}, f32[264,128]{1,0:T(8,128)S(1)}, u32[]{:S(2)}, u32[]{:S(2)}) collective-permute-start(f32[264,128]{1,0:T(8,128)S(1)} %get-tuple-element.41), channel_id=1, source_target_pairs={{0,4},{4,8},{8,12},{12,0},{1,5},{5,9},{9,13},{13,1},{2,6},{6,10},{... | collective-permute-start | bytes 405512 | tf_op jit(solution)/shard_map/ppermute | solution.py:9
  21.2 12.7 %collective-permute-start.8 = (f32[264,128]{1,0:T(8,128)S(1)}, f32[264,128]{1,0:T(8,128)S(1)}, u32[]{:S(2)}, u32[]{:S(2)}) collective-permute-start(f32[264,128]{1,0:T(8,128)S(1)} %get-tuple-element.40), channel_id=1, source_target_pairs={{0,8},{4,12},{8,0},{12,4},{1,9},{5,13},{9,1},{13,5},{2,10},{6,14},... | collective-permute-start | bytes 405512 | tf_op jit(solution)/shard_map/ppermute | solution.py:9
  22.4 11.5 %collective-permute-start.7 = (f32[264,128]{1,0:T(8,128)S(1)}, f32[264,128]{1,0:T(8,128)S(1)}, u32[]{:S(2)}, u32[]{:S(2)}) collective-permute-start(f32[264,128]{1,0:T(8,128)S(1)} %concatenate.48), channel_id=1, source_target_pairs={{0,12},{4,0},{8,4},{12,8},{1,13},{5,1},{9,5},{13,9},{2,14},{6,2},{... | collective-permute-start | bytes 405512 | tf_op jit(solution)/shard_map/ppermute | solution.py:9
  34.0 1.4 %collective-permute-start.9 = (f32[264,128]{1,0:T(8,128)S(1)}, f32[264,128]{1,0:T(8,128)S(1)}, u32[]{:S(2)}, u32[]{:S(2)}) collective-permute-start(f32[264,128]{1,0:T(8,128)S(1)} %pad_maximum_fusion.10), channel_id=1, source_target_pairs={{0,1},{1,0},{2,3},{3,2},{4,5},{5,4},{6,7},{7,6},{8,9},{9,8},{10,11... | collective-permute-start | bytes 405512 | tf_op jit(solution)/shard_map/ppermute | solution.py:9

commit v13 on v11

--- a/solution.py
+++ b/solution.py
@@ -104,6 +104,90 @@
     return [numer_h_stack[e] for e in range(n_row)], numer_w
 
 
+def piece_body(values, lists, counts, w_tile, h_factor):
+    row_blocks, stored, width = values.shape[0], values.shape[1], values.shape[2]
+    rank = w_tile.shape[1]
+    tile_rows = w_tile.shape[0]
+    n_row = lax.axis_size("row")
+    n_col = lax.axis_size("col")
+    n_sub = lax.axis_size("sub")
+    row_index = lax.axis_index("row")
+    col_index = lax.axis_index("col")
+    sub_index = lax.axis_index("sub")
+    half = width // n_sub
+
+    own_piece = lax.dynamic_slice_in_dim(h_factor, sub_index * half, half, 1)
+    h_pieces = [own_piece] + [shifted(own_piece, "row", d) for d in range(1, n_row)]
+    h_cols = jnp.concatenate(h_pieces, axis=1)
+
+    tiles = [(w_tile, lax.dynamic_slice_in_dim(values, sub_index * half, half, 3), lists, counts)]
+    for k in range(1, n_sub):
+        piece = lax.dynamic_slice_in_dim(values, ((sub_index + k) % n_sub) * half, half, 3)
+        tiles.append(tuple(shifted(x, "sub", k) for x in (w_tile, piece, lists, counts)))
+
+    numer_h_piece = None
+    partials_w = []
+    w_chip = None
+    for w_k, values_k, lists_k, counts_k in tiles:
+        product = jnp.dot(w_k, h_cols, preferred_element_type=jnp.float32)
+        columns = []
+        for d in range(n_row):
+            block = (row_index - d) % n_row
+            a_d = jnp.zeros((row_blocks, width, half), values_k.dtype)
+            covered = jnp.zeros((row_blocks,), jnp.bool_)
+            for slot in range(stored):
+                match = (lists_k[:, slot] == block) & (slot < counts_k)
+                a_d = jnp.where(match[:, None, None], values_k[:, slot], a_d)
+                covered = covered | match
+            p_d = product[:, d * half:(d + 1) * half].reshape(row_blocks, width, half)
+            r_d = jnp.where(covered[:, None, None], a_d.astype(jnp.float32) / p_d, 0.0)
+            columns.append(r_d.astype(jnp.bfloat16).reshape(tile_rows, half))
+        ratios = jnp.concatenate(columns, axis=1)
+        part_h = jnp.einsum("ik,ij->kj", w_k, ratios, preferred_element_type=jnp.float32)
+        numer_h_piece = part_h if numer_h_piece is None else numer_h_piece + part_h
+        partials_w.append(jnp.einsum("ij,kj->ik", ratios, h_cols, preferred_element_type=jnp.float32))
+        w_k_sum = jnp.sum(w_k.astype(jnp.float32), axis=0)
+        w_chip = w_k_sum if w_chip is None else w_chip + w_k_sum
+
+    h_part = as_rows(jnp.sum(h_cols.astype(jnp.float32), axis=1), rank)
+    numer_w = partials_w[0]
+    h_group = h_part
+    for k in range(1, n_sub):
+        back = shifted(jnp.concatenate([partials_w[k], h_part]), "sub", n_sub - k)
+        numer_w = numer_w + back[:tile_rows]
+        h_group = h_group + back[tile_rows:]
+
+    share = tile_rows // n_col
+    chunks = numer_w.reshape(n_col, share, rank)
+    mine_w = lax.dynamic_index_in_dim(chunks, col_index, 0, keepdims=False)
+    got_h = h_group
+    for d in range(1, n_col):
+        chunk = lax.dynamic_index_in_dim(chunks, (col_index + d) % n_col, 0, keepdims=False)
+        message = shifted(jnp.concatenate([chunk, h_group]), "col", d)
+        mine_w = mine_w + message[:share]
+        got_h = got_h + message[share:]
+    h_total = from_rows(got_h, rank)
+
+    w_rows_sum = lax.dynamic_slice_in_dim(as_rows(w_chip, width), sub_index * half, half, 1)
+    mine_h = numer_h_piece[:, :half]
+    got_w = w_rows_sum
+    for e in reversed(range(1, n_row)):
+        d = (-e) % n_row
+        message = jnp.concatenate([numer_h_piece[:, d * half:(d + 1) * half], w_rows_sum])
+        message = shifted(message, "row", e)
+        mine_h = mine_h + message[:rank]
+        got_w = got_w + message[rank:]
+    final = jnp.concatenate([mine_h, got_w])
+    total = assemble([final] + [shifted(final, "sub", k) for k in range(1, n_sub)], sub_index, n_sub, 1)
+    numer_h = total[:rank]
+    w_total = from_rows(total[rank:], rank)
+
+    h_new = h_factor.astype(jnp.float32) * numer_h / w_total[:, None]
+    w_part = lax.dynamic_slice_in_dim(w_tile, col_index * share, share, 0).astype(jnp.float32)
+    w_new = (w_part * mine_w / h_total[None, :])[None]
+    return (w_new, h_new)
+
+
 def body(a_blocks, block_list, block_count, w_factor, h_factor):
     values = a_blocks[0, 0]
     lists = block_list[0, 0]
@@ -118,6 +202,8 @@
     row_index = lax.axis_index("row")
     col_index = lax.axis_index("col")
 
+    if tile_rows * n_row * width * 4 <= (8 << 20):
+        return piece_body(values, lists, counts, w_tile, h_factor)
     sub_index = lax.axis_index("sub")
     half = width // n_sub
     own_piece = lax.dynamic_slice_in_dim(h_factor, sub_index * half, half, 1)

time: 36.4 us -> 52.6 us (1.45)
  waiting for transfers between devices: 10.1 us -> 20.9 us
  other arithmetic: 3.18 us -> 5.48 us
  local copies, waits for them, and re-layouts: 4.36 us -> 5.83 us
  matrix products: 4 us -> 5.16 us
  starting transfers between devices: 13.1 us -> 13.8 us
    ppermute x10 -> x13, waiting for transfers between devices: 10.1 us -> 20.9 us  [shifted(): lax.ppermute(value, axis, [(i, (i + by) % length) for i in range(length)])]
    add x4 -> x5, other arithmetic: 0.14 us -> 1.47 us  [the longest x1 0.74 us: piece_body(): h_group = h_group + back[tile_rows:]]
    broadcast_in_dim x18 -> x48, local copies, waits for them, and re-layouts: 0.78 us -> 2.09 us  [the longest x32 1.39 us: piece_body(): a_d = jnp.where(match[:, None, None], values_k[:, slot], a_d)]
    dynamic_slice x1 -> x3, local copies, waits for them, and re-layouts: 0.92 us -> 2.19 us  [the longest x1 1.33 us: piece_body(): lax.dynamic_slice_in_dim(values, sub_index * half, half, 3)]
    unnamed x15 -> x16, local copies, waits for them, and re-layouts: 2.08 us -> 0.83 us
    dot_general x6, matrix products: 4 us -> 5.16 us  [the longest x2 2.38 us: piece_body(): jnp.einsum('ij,kj->ik', ratios, h_cols, preferred_element_type=jnp.float32)]
    concatenate x3 -> x4, other arithmetic: 0.07 us -> 0.86 us  [the longest x1 0.74 us: piece_body(): jnp.concatenate([numer_h_piece[:, d * half:(d + 1) * half], w_rows_sum])]
    ppermute x10 -> x13, starting transfers between devices: 13.1 us -> 13.8 us  [shifted(): lax.ppermute(value, axis, [(i, (i + by) % length) for i in range(length)])]
  transfers between devices with their start and end apart: 10 -> 13, of which waited for: 3 -> 2; matrix products, arithmetic and copies ran while one was open for 19% -> 23% of each run, Pallas kernels for 0% -> 0%
where the time goes in v13:
time: 52.6 us; the launch traced here: 52.1 us
  waiting for transfers between devices  20.9 us (40%)
  starting transfers between devices  13.8 us (26%)
  local copies, waits for them, and re-layouts  5.83 us (11%)
  other arithmetic  5.48 us (10%)
  matrix products  5.16 us (10%)
  between operations  1.01 us (2%)
    ppermute x13, waiting for transfers between devices, shifted(): lax.ppermute(value, axis, [(i, (i + by) % length) for i in range(length)])  20.9 us
    ppermute x13, starting transfers between devices, shifted(): lax.ppermute(value, axis, [(i, (i + by) % length) for i in range(length)])  13.8 us
    dot_general x2, matrix products, piece_body(): jnp.einsum('ij,kj->ik', ratios, h_cols, preferred_element_type=jnp.float32)  2.38 us
    dot_general x2, matrix products, piece_body(): jnp.einsum('ik,ij->kj', w_k, ratios, preferred_element_type=jnp.float32)  1.79 us
    broadcast_in_dim x32, local copies, waits for them, and re-layouts, piece_body(): a_d = jnp.where(match[:, None, None], values_k[:, slot], a_d)  1.39 us
    dynamic_slice x1, local copies, waits for them, and re-layouts, piece_body(): lax.dynamic_slice_in_dim(values, sub_index * half, half, 3)  1.33 us
  transfers between devices with their start and end apart: 13, of which 2 were waited for; matrix products, arithmetic and copies ran while one was open for 23% of the time, Pallas kernels for 0%

profile of v13, /device:TPU:0, one launch (start us, length us, event | category | flops | bytes accessed | tf_op | source)
XLA Modules:
  0.0 52.1 jit_solution(727119952129829787)
XLA Ops:
  0.6 0.8 %constant_dynamic-slice_fusion = bf16[256,128]{1,0:T(8,128)(2,1)S(1)} fusion(bf16[256,256]{1,0:T(8,128)(2,1)} %param.9, s32[]{:T(128)S(6)} %select_n.175), kind=kLoop, calls=%fused_computation.81 | loop fusion | bytes 131076 | tf_op jit(solution)/shard_map/dynamic_slice | solution.py:119
  1.5 3.0 %collective-permute-start = (bf16[256,128]{1,0:T(8,128)(2,1)S(1)}, bf16[256,128]{1,0:T(8,128)(2,1)S(1)}, u32[]{:S(2)}, u32[]{:S(2)}) collective-permute-start(bf16[256,128]{1,0:T(8,128)(2,1)S(1)} %constant_dynamic-slice_fusion), channel_id=1, source_target_pairs={{0,4},{4,8},{8,12},{12,0},{1,5},{5,9},{9,13},{13,1},{2,6},{6,10},{... | collective-permute-start | bytes 196616 | tf_op jit(solution)/shard_map/ppermute | solution.py:9
  4.5 2.6 %collective-permute-start.1 = (bf16[256,128]{1,0:T(8,128)(2,1)S(1)}, bf16[256,128]{1,0:T(8,128)(2,1)S(1)}, u32[]{:S(2)}, u32[]{:S(2)}) collective-permute-start(bf16[256,128]{1,0:T(8,128)(2,1)S(1)} %constant_dynamic-slice_fusion), channel_id=1, source_target_pairs={{0,8},{4,12},{8,0},{12,4},{1,9},{5,13},{9,1},{13,5},{2,10},{6,14},... | collective-permute-start | bytes 196616 | tf_op jit(solution)/shard_map/ppermute | solution.py:9
  7.1 1.3 %collective-permute-start.2 = (bf16[256,128]{1,0:T(8,128)(2,1)S(1)}, bf16[256,128]{1,0:T(8,128)(2,1)S(1)}, u32[]{:S(2)}, u32[]{:S(2)}) collective-permute-start(bf16[256,128]{1,0:T(8,128)(2,1)S(1)} %constant_dynamic-slice_fusion), channel_id=1, source_target_pairs={{0,12},{4,0},{8,4},{12,8},{1,13},{5,1},{9,5},{13,9},{2,14},{6,2},{... | collective-permute-start | bytes 196616 | tf_op jit(solution)/shard_map/ppermute | solution.py:9
  8.5 0.5 collective-permute-start.4
  9.0 1.3 %dynamic-slice_bitcast_fusion.2 = (bf16[4,2,256,128]{3,2,1,0:T(8,128)(2,1)S(1)}, bf16[4,2,256,128]{3,2,1,0:T(8,128)(2,1)S(1)}) fusion(bf16[1,1,4,2,256,256]{5,4,3,2,1,0:T(8,128)(2,1)} %param.5, s32[]{:T(128)S(6)} %select_n.175, s32[]{:T(128)S(6)} %select_n.192), kind=kLoop, calls=%fused_computation.42 | loop fusion | bytes 2097160 | tf_op jit(solution)/shard_map/dynamic_slice | solution.py:123
  12.0 0.5 collective-permute-start.6
  13.6 0.5 convolution_bitcast_fusion.1
  14.8 1.3 %fusion.24 = f32[512,256]{0,1:T(8,128)} fusion(bf16[1024,128]{0,1:T(8,128)(2,1)S(1)} %get-tuple-element.27, bf16[1024,128]{0,1:T(8,128)(2,1)S(1)} %get-tuple-element.28, bf16[1024,128]{0,1:T(8,128)(2,1)S(1)} %get-tuple-element.29, bf16[1024,128]{0,1:T(8,128)(2,1)S(1)} %get-tuple-element.26, bf16[1,1024,256]{2,1,0:T(8,128)(2,1)S(1)} %copy-done), kind=kOutput, calls=%fused_computation.53 | convolution fusion | flops 272629760 | bytes 2097152 | tf_op jit(solution)/shard_map/ik,ij->kj/dot_general | solution.py:146
  16.6 0.5 convolution_bitcast_fusion
  17.6 0.5 fusion.23
  18.4 0.8 %copy-done.7 = f32[512,256]{0,1:T(8,128)S(1)} copy-done((f32[512,256]{0,1:T(8,128)S(1)}, f32[512,256]{0,1:T(8,128)}, u32[]{:S(2)}) %copy-start.7) | copy-done | bytes 524312
  19.2 0.5 fusion
  19.7 0.7 %pad_maximum_fusion.7 = (f32[264,128]{1,0:T(8,128)S(1)}, f32[264,128]{1,0:T(8,128)}, f32[264,128]{1,0:T(8,128)}) fusion(f32[8,128]{1,0:T(8,128)S(1)} %pad_dynamic-slice_fusion, f32[256,128]{1,0:T(8,128)S(1)} %get-tuple-element.36, f32[256,128]{1,0:T(8,128)S(1)} %get-tuple-element.38, f32[256,128]{1,0:T(8,128)S(1)} %get-tuple-element.37), kind=kLoop, calls=%fused_computation.51 | loop fusion | flops 101376 | bytes 802816 | tf_op jit(solution)/shard_map/concatenate | solution.py:176
  20.5 1.6 %collective-permute-start.11 = (f32[264,128]{1,0:T(8,128)}, f32[264,128]{1,0:T(8,128)S(1)}, u32[]{:S(2)}, u32[]{:S(2)}) collective-permute-start(f32[264,128]{1,0:T(8,128)} %get-tuple-element.47), channel_id=1, source_target_pairs={{0,4},{4,8},{8,12},{12,0},{1,5},{5,9},{9,13},{13,1},{2,6},{6,10},{... | collective-permute-start | bytes 405512 | tf_op jit(solution)/shard_map/ppermute | solution.py:9
  22.1 2.2 %collective-permute-start.9 = (f32[264,128]{1,0:T(8,128)S(1)}, f32[264,128]{1,0:T(8,128)S(1)}, u32[]{:S(2)}, u32[]{:S(2)}) collective-permute-start(f32[264,128]{1,0:T(8,128)S(1)} %get-tuple-element.45), channel_id=1, source_target_pairs={{0,12},{4,0},{8,4},{12,8},{1,13},{5,1},{9,5},{13,9},{2,14},{6,2},{... | collective-permute-start | bytes 405512 | tf_op jit(solution)/shard_map/ppermute | solution.py:9
  24.4 8.7 %collective-permute-done.10 = f32[264,128]{1,0:T(8,128)S(1)} collective-permute-done((f32[264,128]{1,0:T(8,128)}, f32[264,128]{1,0:T(8,128)S(1)}, u32[]{:S(2)}, u32[]{:S(2)}) %collective-permute-start.10) | collective-permute-done | bytes 135200 | tf_op jit(solution)/shard_map/ppermute | solution.py:9
  33.1 0.7 %slice_add_fusion.5 = f32[8,128]{1,0:T(8,128)S(1)} fusion(f32[264,128]{1,0:T(8,128)S(1)} %collective-permute-done.11, f32[264,128]{1,0:T(8,128)S(1)} %collective-permute-done.10, f32[264,128]{1,0:T(8,128)S(1)} %collective-permute-done.9, s32[]{:T(128)S(6)} %select_n.175, f32[1,256]{1,0:T(1,128)} %bitcast.122), kind=kLoop, calls=%fused_computation.62 | loop fusion | flops 3072 | bytes 17412 | tf_op jit(solution)/shard_map/add | solution.py:179
  33.9 1.9 %convolution_add_fusion = f32[1024,256]{1,0:T(8,128)S(1)} fusion(f32[1032,256]{1,0:T(8,128)} %collective-permute-done.7, bf16[1024,128]{0,1:T(8,128)(2,1)S(1)} %get-tuple-element.27, bf16[1024,128]{0,1:T(8,128)(2,1)} %copy-done.2, bf16[1024,128]{0,1:T(8,128)(2,1)} %copy-done.3, bf16[1024,128]{0,1:T(8,128)(2,1)S(1)} %get-tuple-element.26, ...), kind=kOutput, calls=%fused_computation.2 | convolution fusion | flops 273940480 | bytes 3407872 | tf_op jit(solution)/shard_map/ij,kj->ik/dot_general | solution.py:148
  35.8 0.7 %slice_add_fusion.4 = f32[8,256]{1,0:T(8,128)S(1)} fusion(f32[1032,256]{1,0:T(8,128)} %collective-permute-done.7, f32[1,256]{1,0:T(1,128)S(1)} %bitcast.120), kind=kLoop, calls=%fused_computation.60 | loop fusion | flops 2048 | bytes 17408 | tf_op jit(solution)/shard_map/add | solution.py:158
  36.7 1.6 %collective-permute-start.8 = (f32[520,256]{1,0:T(8,128)S(1)}, f32[520,256]{1,0:T(8,128)S(1)}, u32[]{:S(2)}, u32[]{:S(2)}) collective-permute-start(f32[520,256]{1,0:T(8,128)S(1)} %pad_maximum_fusion.3), channel_id=1, source_target_pairs={{0,2},{2,0},{1,3},{3,1},{4,6},{6,4},{5,7},{7,5},{8,10},{10,8},{9,1... | collective-permute-start | bytes 1597448 | tf_op jit(solution)/shard_map/ppermute | solution.py:9
  38.3 0.8 %fusion.22 = f32[256,256]{1,0:T(8,128)} fusion(f32[264,128]{1,0:T(8,128)S(1)} %get-tuple-element.44, f32[264,128]{1,0:T(8,128)S(1)} %get-tuple-element.43, bf16[256,256]{1,0:T(8,128)(2,1)S(1)} %copy-done.1, f32[256]{0:T(256)S(1)} %bitcast.123), kind=kLoop, calls=%fused_computation.47 | loop fusion | flops 262144 | bytes 664576 | tf_op jit(solution)/shard_map/div | solution.py:185
  39.1 12.1 %collective-permute-done.8 = f32[520,256]{1,0:T(8,128)S(1)} collective-permute-done((f32[520,256]{1,0:T(8,128)S(1)}, f32[520,256]{1,0:T(8,128)S(1)}, u32[]{:S(2)}, u32[]{:S(2)}) %collective-permute-start.8) | collective-permute-done | bytes 532512 | tf_op jit(solution)/shard_map/ppermute | solution.py:9
  51.2 0.9 %fusion.3 = f32[1,512,256]{2,1,0:T(8,128)} fusion(f32[520,256]{1,0:T(8,128)S(1)} %collective-permute-done.8, f32[2,512,256]{2,1,0:T(8,128)S(1)} %bitcast.118, s32[]{:T(128)S(6)} %select_n.205, f32[256]{0:T(256)S(1)} %bitcast.124, bf16[1,1024,256]{2,1,0:T(8,128)(2,1)S(1)} %copy-done, s32[]{:T(128)S(6)} %select_n.173), kind=kLoop, calls=%fused_computation.14 | loop fusion | flops 524288 | bytes 1836040 | tf_op jit(solution)/shard_map/broadcast_in_dim | solution.py:187
  (105 shorter events, 4.9 us)
Async XLA Ops:
  1.5 12.1 %collective-permute-start = (bf16[256,128]{1,0:T(8,128)(2,1)S(1)}, bf16[256,128]{1,0:T(8,128)(2,1)S(1)}, u32[]{:S(2)}, u32[]{:S(2)}) collective-permute-start(bf16[256,128]{1,0:T(8,128)(2,1)S(1)} %constant_dynamic-slice_fusion), channel_id=1, source_target_pairs={{0,4},{4,8},{8,12},{12,0},{1,5},{5,9},{9,13},{13,1},{2,6},{6,10},{... | collective-permute-start | bytes 196616 | tf_op jit(solution)/shard_map/ppermute | solution.py:9
  4.5 9.1 %collective-permute-start.1 = (bf16[256,128]{1,0:T(8,128)(2,1)S(1)}, bf16[256,128]{1,0:T(8,128)(2,1)S(1)}, u32[]{:S(2)}, u32[]{:S(2)}) collective-permute-start(bf16[256,128]{1,0:T(8,128)(2,1)S(1)} %constant_dynamic-slice_fusion), channel_id=1, source_target_pairs={{0,8},{4,12},{8,0},{12,4},{1,9},{5,13},{9,1},{13,5},{2,10},{6,14},... | collective-permute-start | bytes 196616 | tf_op jit(solution)/shard_map/ppermute | solution.py:9
  7.1 6.5 %collective-permute-start.2 = (bf16[256,128]{1,0:T(8,128)(2,1)S(1)}, bf16[256,128]{1,0:T(8,128)(2,1)S(1)}, u32[]{:S(2)}, u32[]{:S(2)}) collective-permute-start(bf16[256,128]{1,0:T(8,128)(2,1)S(1)} %constant_dynamic-slice_fusion), channel_id=1, source_target_pairs={{0,12},{4,0},{8,4},{12,8},{1,13},{5,1},{9,5},{13,9},{2,14},{6,2},{... | collective-permute-start | bytes 196616 | tf_op jit(solution)/shard_map/ppermute | solution.py:9
  8.4 3.6 %collective-permute-start.3 = (s32[4,2]{0,1:T(2,128)}, s32[4,2]{0,1:T(2,128)S(1)}, u32[]{:S(2)}, u32[]{:S(2)}) collective-permute-start(s32[4,2]{0,1:T(2,128)} %bitcast.125), channel_id=1, source_target_pairs={{0,1},{1,0},{2,3},{3,2},{4,5},{5,4},{6,7},{7,6},{8,9},{9,8},{10,11... | collective-permute-start | bytes 104 | tf_op jit(solution)/shard_map/ppermute | solution.py:9
  8.5 3.5 %collective-permute-start.4 = (s32[4]{0:T(128)}, s32[4]{0:T(128)S(1)}, u32[]{:S(2)}, u32[]{:S(2)}) collective-permute-start(s32[4]{0:T(128)} %bitcast.127), channel_id=1, source_target_pairs={{0,1},{1,0},{2,3},{3,2},{4,5},{5,4},{6,7},{7,6},{8,9},{9,8},{10,11... | collective-permute-start | bytes 56 | tf_op jit(solution)/shard_map/ppermute | solution.py:9
  9.0 1.7 %copy-start.5 = (s32[1,1,4,2]{2,3,1,0:T(2,128)S(1)}, s32[1,1,4,2]{2,3,1,0:T(2,128)}, u32[]{:S(2)}) copy-start(s32[1,1,4,2]{2,3,1,0:T(2,128)} %param.6) | copy-start | bytes 100
  9.0 1.7 %copy-start.6 = (s32[1,1,4]{2,1,0:T(1,128)S(1)}, s32[1,1,4]{2,1,0:T(1,128)}, u32[]{:S(2)}) copy-start(s32[1,1,4]{2,1,0:T(1,128)} %param.7) | copy-start | bytes 52
  9.0 2.8 %copy-start = (bf16[1,1024,256]{2,1,0:T(8,128)(2,1)S(1)}, bf16[1,1024,256]{2,1,0:T(8,128)(2,1)}, u32[]{:S(2)}) copy-start(bf16[1,1024,256]{2,1,0:T(8,128)(2,1)} %param.8) | copy-start | bytes 1572868
  11.9 4.1 %collective-permute-start.5 = (bf16[4,2,256,128]{3,2,1,0:T(8,128)(2,1)S(1)}, bf16[4,2,256,128]{3,2,1,0:T(8,128)(2,1)S(1)}, u32[]{:S(2)}, u32[]{:S(2)}) collective-permute-start(bf16[4,2,256,128]{3,2,1,0:T(8,128)(2,1)S(1)} %get-tuple-element.35), channel_id=1, source_target_pairs={{0,1},{1,0},{2,3},{3,2},{4,5},{5,4},{6,7},{7,6},{8,9},{9,8},{10,11... | collective-permute-start | bytes 1572872 | tf_op jit(solution)/shard_map/ppermute | solution.py:9
  12.0 4.4 %collective-permute-start.6 = (bf16[1024,256]{1,0:T(8,128)(2,1)S(1)}, bf16[1024,256]{1,0:T(8,128)(2,1)S(1)}, u32[]{:S(2)}, u32[]{:S(2)}) collective-permute-start(bf16[1024,256]{1,0:T(8,128)(2,1)S(1)} %bitcast.112), channel_id=1, source_target_pairs={{0,1},{1,0},{2,3},{3,2},{4,5},{5,4},{6,7},{7,6},{8,9},{9,8},{10,11... | collective-permute-start | bytes 1572872 | tf_op jit(solution)/shard_map/ppermute | solution.py:9
  14.6 1.5 %copy-start.2 = (bf16[1024,128]{0,1:T(8,128)(2,1)}, bf16[1024,128]{0,1:T(8,128)(2,1)S(1)}, u32[]{:S(2)}) copy-start(bf16[1024,128]{0,1:T(8,128)(2,1)S(1)} %get-tuple-element.28) | copy-start | bytes 786436
  14.6 1.5 %copy-start.3 = (bf16[1024,128]{0,1:T(8,128)(2,1)}, bf16[1024,128]{0,1:T(8,128)(2,1)S(1)}, u32[]{:S(2)}) copy-start(bf16[1024,128]{0,1:T(8,128)(2,1)S(1)} %get-tuple-element.29) | copy-start | bytes 786436
  16.6 1.6 %copy-start.4 = (f32[256]{0:T(256)}, f32[256]{0:T(256)S(1)}, u32[]{:S(2)}) copy-start(f32[256]{0:T(256)S(1)} %add.130) | copy-start | bytes 3076
  18.1 1.0 %copy-start.7 = (f32[512,256]{0,1:T(8,128)S(1)}, f32[512,256]{0,1:T(8,128)}, u32[]{:S(2)}) copy-start(f32[512,256]{0,1:T(8,128)} %fusion.24) | copy-start | bytes 1572868
  18.2 15.7 %collective-permute-start.7 = (f32[1032,256]{1,0:T(8,128)S(1)}, f32[1032,256]{1,0:T(8,128)}, u32[]{:S(2)}, u32[]{:S(2)}) collective-permute-start(f32[1032,256]{1,0:T(8,128)S(1)} %pad_maximum_fusion), channel_id=1, source_target_pairs={{0,1},{1,0},{2,3},{3,2},{4,5},{5,4},{6,7},{7,6},{8,9},{9,8},{10,11... | collective-permute-start | bytes 3170312 | tf_op jit(solution)/shard_map/ppermute | solution.py:9
  20.4 12.7 %collective-permute-start.10 = (f32[264,128]{1,0:T(8,128)}, f32[264,128]{1,0:T(8,128)S(1)}, u32[]{:S(2)}, u32[]{:S(2)}) collective-permute-start(f32[264,128]{1,0:T(8,128)} %get-tuple-element.46), channel_id=1, source_target_pairs={{0,8},{4,12},{8,0},{12,4},{1,9},{5,13},{9,1},{13,5},{2,10},{6,14},... | collective-permute-start | bytes 405512 | tf_op jit(solution)/shard_map/ppermute | solution.py:9
  20.5 12.6 %collective-permute-start.11 = (f32[264,128]{1,0:T(8,128)}, f32[264,128]{1,0:T(8,128)S(1)}, u32[]{:S(2)}, u32[]{:S(2)}) collective-permute-start(f32[264,128]{1,0:T(8,128)} %get-tuple-element.47), channel_id=1, source_target_pairs={{0,4},{4,8},{8,12},{12,0},{1,5},{5,9},{9,13},{13,1},{2,6},{6,10},{... | collective-permute-start | bytes 405512 | tf_op jit(solution)/shard_map/ppermute | solution.py:9
  22.1 11.0 %collective-permute-start.9 = (f32[264,128]{1,0:T(8,128)S(1)}, f32[264,128]{1,0:T(8,128)S(1)}, u32[]{:S(2)}, u32[]{:S(2)}) collective-permute-start(f32[264,128]{1,0:T(8,128)S(1)} %get-tuple-element.45), channel_id=1, source_target_pairs={{0,12},{4,0},{8,4},{12,8},{1,13},{5,1},{9,5},{13,9},{2,14},{6,2},{... | collective-permute-start | bytes 405512 | tf_op jit(solution)/shard_map/ppermute | solution.py:9
  33.8 4.4 %collective-permute-start.12 = (f32[264,128]{1,0:T(8,128)S(1)}, f32[264,128]{1,0:T(8,128)S(1)}, u32[]{:S(2)}, u32[]{:S(2)}) collective-permute-start(f32[264,128]{1,0:T(8,128)S(1)} %pad_maximum_fusion.12), channel_id=1, source_target_pairs={{0,1},{1,0},{2,3},{3,2},{4,5},{5,4},{6,7},{7,6},{8,9},{9,8},{10,11... | collective-permute-start | bytes 405512 | tf_op jit(solution)/shard_map/ppermute | solution.py:9
  35.8 2.4 %copy-start.1 = (bf16[256,256]{1,0:T(8,128)(2,1)S(1)}, bf16[256,256]{1,0:T(8,128)(2,1)}, u32[]{:S(2)}) copy-start(bf16[256,256]{1,0:T(8,128)(2,1)} %param.9) | copy-start | bytes 393220
  36.7 14.5 %collective-permute-start.8 = (f32[520,256]{1,0:T(8,128)S(1)}, f32[520,256]{1,0:T(8,128)S(1)}, u32[]{:S(2)}, u32[]{:S(2)}) collective-permute-start(f32[520,256]{1,0:T(8,128)S(1)} %pad_maximum_fusion.3), channel_id=1, source_target_pairs={{0,2},{2,0},{1,3},{3,1},{4,6},{6,4},{5,7},{7,5},{8,10},{10,8},{9,1... | collective-permute-start | bytes 1597448 | tf_op jit(solution)/shard_map/ppermute | solution.py:9

commit v14 on v13

--- a/solution.py
+++ b/solution.py
@@ -166,7 +166,6 @@
         message = shifted(jnp.concatenate([chunk, h_group]), "col", d)
         mine_w = mine_w + message[:share]
         got_h = got_h + message[share:]
-    h_total = from_rows(got_h, rank)
 
     w_rows_sum = lax.dynamic_slice_in_dim(as_rows(w_chip, width), sub_index * half, half, 1)
     mine_h = numer_h_piece[:, :half]
@@ -175,6 +174,8 @@
         d = (-e) % n_row
         message = jnp.concatenate([numer_h_piece[:, d * half:(d + 1) * half], w_rows_sum])
         message = shifted(message, "row", e)
+        if e == n_row - 1:
+            message, mine_w, got_h = lax.optimization_barrier((message, mine_w, got_h))
         mine_h = mine_h + message[:rank]
         got_w = got_w + message[rank:]
     final = jnp.concatenate([mine_h, got_w])
@@ -182,6 +183,7 @@
     numer_h = total[:rank]
     w_total = from_rows(total[rank:], rank)
 
+    h_total = from_rows(got_h, rank)
     h_new = h_factor.astype(jnp.float32) * numer_h / w_total[:, None]
     w_part = lax.dynamic_slice_in_dim(w_tile, col_index * share, share, 0).astype(jnp.float32)
     w_new = (w_part * mine_w / h_total[None, :])[None]

time: 52.6 us -> 41.7 us (0.79)
  waiting for transfers between devices: 20.9 us -> 16.3 us
  matrix products: 5.16 us -> 2.94 us
  other arithmetic: 5.48 us -> 3.42 us
  starting transfers between devices: 13.8 us -> 12 us
    ppermute x13, waiting for transfers between devices: 20.9 us -> 16.3 us  [shifted(): lax.ppermute(value, axis, [(i, (i + by) % length) for i in range(length)])]
    ppermute x13, starting transfers between devices: 13.8 us -> 12 us  [shifted(): lax.ppermute(value, axis, [(i, (i + by) % length) for i in range(length)])]
    dot_general x2, matrix products: 2.38 us -> 0.99 us  [piece_body(): jnp.einsum('ij,kj->ik', ratios, h_cols, preferred_element_type=jnp.float32)]
    unnamed x16 -> x8, local copies, waits for them, and re-layouts: 0.83 us -> 0.02 us
    dot_general x2, matrix products: 1.79 us -> 0.99 us  [piece_body(): jnp.einsum('ik,ij->kj', w_k, ratios, preferred_element_type=jnp.float32)]
    dynamic_slice x1, local copies, waits for them, and re-layouts: 1.33 us -> 2.09 us  [piece_body(): lax.dynamic_slice_in_dim(values, (sub_index + k) % n_sub * half, half, 3)]
    add x1, other arithmetic: 0.74 us -> 0.01 us  [piece_body(): h_group = h_group + back[tile_rows:]]
    concatenate x1, other arithmetic: 0.74 us -> 0.03 us  [piece_body(): jnp.concatenate([numer_h_piece[:, d * half:(d + 1) * half], w_rows_sum])]
  transfers between devices with their start and end apart: 13 -> 13, of which waited for: 2 -> 6; matrix products, arithmetic and copies ran while one was open for 23% -> 20% of each run, Pallas kernels for 0% -> 0%
where the time goes in v14:
time: 41.7 us; the launch traced here: 41.6 us
  waiting for transfers between devices  16.3 us (39%)
  starting transfers between devices  12 us (29%)
  local copies, waits for them, and re-layouts  5.83 us (14%)
  other arithmetic  3.42 us (8%)
  matrix products  2.94 us (7%)
  between operations  1.04 us (2%)
    ppermute x13, waiting for transfers between devices, shifted(): lax.ppermute(value, axis, [(i, (i + by) % length) for i in range(length)])  16.3 us
    ppermute x13, starting transfers between devices, shifted(): lax.ppermute(value, axis, [(i, (i + by) % length) for i in range(length)])  12 us
    dynamic_slice x1, local copies, waits for them, and re-layouts, piece_body(): lax.dynamic_slice_in_dim(values, (sub_index + k) % n_sub * half, half, 3)  2.09 us
    broadcast_in_dim x32, local copies, waits for them, and re-layouts, piece_body(): a_d = jnp.where(match[:, None, None], values_k[:, slot], a_d)  1.39 us
    dot_general x2, matrix products, piece_body(): jnp.einsum('ij,kj->ik', ratios, h_cols, preferred_element_type=jnp.float32)  0.99 us
    dot_general x2, matrix products, piece_body(): jnp.einsum('ik,ij->kj', w_k, ratios, preferred_element_type=jnp.float32)  0.99 us
    convert_element_type x2, other arithmetic, piece_body(): columns.append(r_d.astype(jnp.bfloat16).reshape(tile_rows, half))  0.98 us
    dot_general x2, matrix products, piece_body(): product = jnp.dot(w_k, h_cols, preferred_element_type=jnp.float32)  0.97 us
  transfers between devices with their start and end apart: 13, of which 6 were waited for; matrix products, arithmetic and copies ran while one was open for 20% of the time, Pallas kernels for 0%

profile of v14, /device:TPU:0, one launch (start us, length us, event | category | flops | bytes accessed | tf_op | source)
XLA Modules:
  0.0 41.6 jit_solution(12814027199367452933)
XLA Ops:
  0.7 0.9 %constant_dynamic-slice_fusion = bf16[256,128]{1,0:T(8,128)(2,1)S(1)} fusion(bf16[256,256]{1,0:T(8,128)(2,1)} %param.9, s32[]{:T(128)S(6)} %select_n.175), kind=kLoop, calls=%fused_computation.81 | loop fusion | bytes 131076 | tf_op jit(solution)/shard_map/dynamic_slice | solution.py:119
  1.6 5.0 %collective-permute-start.2 = (bf16[256,128]{1,0:T(8,128)(2,1)S(1)}, bf16[256,128]{1,0:T(8,128)(2,1)S(1)}, u32[]{:S(2)}, u32[]{:S(2)}) collective-permute-start(bf16[256,128]{1,0:T(8,128)(2,1)S(1)} %constant_dynamic-slice_fusion), channel_id=1, source_target_pairs={{0,12},{4,0},{8,4},{12,8},{1,13},{5,1},{9,5},{13,9},{2,14},{6,2},{... | collective-permute-start | bytes 196616 | tf_op jit(solution)/shard_map/ppermute | solution.py:9
  6.6 2.1 %dynamic-slice_bitcast_fusion.1 = (bf16[4,2,256,128]{3,2,1,0:T(8,128)(2,1)}, bf16[4,2,256,128]{3,2,1,0:T(8,128)(2,1)S(1)}) fusion(bf16[1,1,4,2,256,256]{5,4,3,2,1,0:T(8,128)(2,1)} %param.5, s32[]{:T(128)S(6)} %select_n.192, s32[]{:T(128)S(6)} %select_n.175), kind=kLoop, calls=%fused_computation.41 | loop fusion | bytes 2097160 | tf_op jit(solution)/shard_map/dynamic_slice | solution.py:125
  8.7 0.5 %collective-permute-start.5 = (bf16[4,2,256,128]{3,2,1,0:T(8,128)(2,1)}, bf16[4,2,256,128]{3,2,1,0:T(8,128)(2,1)S(1)}, u32[]{:S(2)}, u32[]{:S(2)}) collective-permute-start(bf16[4,2,256,128]{3,2,1,0:T(8,128)(2,1)} %get-tuple-element.40), channel_id=1, source_target_pairs={{0,1},{1,0},{2,3},{3,2},{4,5},{5,4},{6,7},{7,6},{8,9},{9,8},{10,11... | collective-permute-start | bytes 1572872 | tf_op jit(solution)/shard_map/ppermute | solution.py:9
  10.9 0.6 %collective-permute-start.3 = (s32[4,2]{0,1:T(2,128)S(1)}, s32[4,2]{0,1:T(2,128)S(1)}, u32[]{:S(2)}, u32[]{:S(2)}) collective-permute-start(s32[4,2]{0,1:T(2,128)S(1)} %bitcast.127), channel_id=1, source_target_pairs={{0,1},{1,0},{2,3},{3,2},{4,5},{5,4},{6,7},{7,6},{8,9},{9,8},{10,11... | collective-permute-start | bytes 104 | tf_op jit(solution)/shard_map/ppermute | solution.py:9
  11.5 0.8 %collective-permute-done.3 = s32[4,2]{0,1:T(2,128)S(1)} collective-permute-done((s32[4,2]{0,1:T(2,128)S(1)}, s32[4,2]{0,1:T(2,128)S(1)}, u32[]{:S(2)}, u32[]{:S(2)}) %collective-permute-start.3) | collective-permute-done | bytes 64 | tf_op jit(solution)/shard_map/ppermute | solution.py:9
  12.3 1.0 %collective-permute-start = (bf16[256,128]{1,0:T(8,128)(2,1)S(1)}, bf16[256,128]{1,0:T(8,128)(2,1)S(1)}, u32[]{:S(2)}, u32[]{:S(2)}) collective-permute-start(bf16[256,128]{1,0:T(8,128)(2,1)S(1)} %constant_dynamic-slice_fusion), channel_id=1, source_target_pairs={{0,4},{4,8},{8,12},{12,0},{1,5},{5,9},{9,13},{13,1},{2,6},{6,10},{... | collective-permute-start | bytes 196616 | tf_op jit(solution)/shard_map/ppermute | solution.py:9
  14.4 4.0 %collective-permute-done = bf16[256,128]{1,0:T(8,128)(2,1)S(1)} collective-permute-done((bf16[256,128]{1,0:T(8,128)(2,1)S(1)}, bf16[256,128]{1,0:T(8,128)(2,1)S(1)}, u32[]{:S(2)}, u32[]{:S(2)}) %collective-permute-start) | collective-permute-done | bytes 65568 | tf_op jit(solution)/shard_map/ppermute | solution.py:9
  19.4 0.5 %fusion.8 = (bf16[1024,128]{0,1:T(8,128)(2,1)S(1)}, bf16[1024,128]{0,1:T(8,128)(2,1)S(1)}, bf16[1024,128]{0,1:T(8,128)(2,1)S(1)}, bf16[1024,128]{0,1:T(8,128)(2,1)S(1)}) fusion(f32[1024,512]{0,1:T(8,128)S(1)} %convolution_bitcast_fusion, bf16[1024,128]{0,1:T(8,128)(2,1)S(1)} %copy.13, bf16[1024,128]{0,1:T(8,128)(2,1)S(1)} %copy.14, ...), kind=kLoop, calls=%fused_computation.23 | loop fusion | flops 3145728 | bytes 3682304 | tf_op jit(solution)/shard_map/convert_element_type | solution.py:144
  19.9 0.5 %fusion.22 = f32[1024,256]{1,0:T(8,128)S(1)} fusion(bf16[1024,128]{0,1:T(8,128)(2,1)S(1)} %get-tuple-element.33, bf16[1024,128]{0,1:T(8,128)(2,1)S(1)} %get-tuple-element.34, bf16[1024,128]{0,1:T(8,128)(2,1)S(1)} %get-tuple-element.35, bf16[1024,128]{0,1:T(8,128)(2,1)S(1)} %get-tuple-element.32, bf16[256,128]{1,0:T(8,128)(2,1)S(1)} %collective-permute-done.2, ...), kind=kOutput, calls=%fused_computation.52 | convolution fusion | flops 273678336 | bytes 2359296 | tf_op jit(solution)/shard_map/ij,kj->ik/dot_general | solution.py:148
  20.5 0.5 %convolution_bitcast_fusion.1 = f32[1024,512]{0,1:T(8,128)S(1)} fusion(bf16[1,1024,256]{2,1,0:T(8,128)(2,1)S(1)} %copy-done, bf16[256,128]{1,0:T(8,128)(2,1)S(1)} %collective-permute-done.2, bf16[256,128]{1,0:T(8,128)(2,1)S(1)} %collective-permute-done.1, bf16[256,128]{1,0:T(8,128)(2,1)S(1)} %collective-permute-done, ...), kind=kOutput, calls=%fused_computation.1 | convolution fusion | flops 269484032 | bytes 2883584 | tf_op jit(solution)/shard_map/dot_general | solution.py:132
  21.0 0.5 %fusion.16 = (bf16[1024,128]{0,1:T(8,128)(2,1)S(1)}, bf16[1024,128]{0,1:T(8,128)(2,1)S(1)}, bf16[1024,128]{0,1:T(8,128)(2,1)S(1)}, bf16[1024,128]{0,1:T(8,128)(2,1)S(1)}) fusion(f32[1024,512]{0,1:T(8,128)S(1)} %convolution_bitcast_fusion.1, bf16[1024,128]{0,1:T(8,128)(2,1)S(1)} %copy.11, bf16[1024,128]{0,1:T(8,128)(2,1)S(1)} %copy.12, ...), kind=kLoop, calls=%fused_computation.35 | loop fusion | flops 3145728 | bytes 3682304 | tf_op jit(solution)/shard_map/convert_element_type | solution.py:144
  21.5 0.5 %fusion.23 = f32[512,256]{0,1:T(8,128)S(1)} fusion(bf16[1024,128]{0,1:T(8,128)(2,1)S(1)} %get-tuple-element.37, bf16[1024,128]{0,1:T(8,128)(2,1)S(1)} %get-tuple-element.38, bf16[1024,128]{0,1:T(8,128)(2,1)S(1)} %get-tuple-element.39, bf16[1024,128]{0,1:T(8,128)(2,1)S(1)} %get-tuple-element.36, bf16[1,1024,256]{2,1,0:T(8,128)(2,1)S(1)} %copy-done), kind=kOutput, calls=%fused_computation.53 | convolution fusion | flops 272629760 | bytes 2097152 | tf_op jit(solution)/shard_map/ik,ij->kj/dot_general | solution.py:146
  22.0 0.5 %fusion = f32[256,512]{1,0:T(8,128)S(1)} fusion(f32[512,256]{0,1:T(8,128)S(1)} %fusion.23, bf16[1024,256]{1,0:T(8,128)(2,1)S(1)} %collective-permute-done.6, bf16[1024,128]{0,1:T(8,128)(2,1)S(1)} %get-tuple-element.33, bf16[1024,128]{0,1:T(8,128)(2,1)S(1)} %get-tuple-element.34, bf16[1024,128]{0,1:T(8,128)(2,1)S(1)} %get-tuple-element.35, ...), kind=kOutput, calls=%fused_computation.4 | convolution fusion | flops 272760832 | bytes 2621440 | tf_op jit(solution)/shard_map/ik,ij->kj/dot_general | solution.py:146
  22.5 0.7 %collective-permute-done.8 = f32[1032,256]{1,0:T(8,128)S(1)} collective-permute-done((f32[1032,256]{1,0:T(8,128)S(1)}, f32[1032,256]{1,0:T(8,128)S(1)}, u32[]{:S(2)}, u32[]{:S(2)}) %collective-permute-start.8) | collective-permute-done | bytes 1056800 | tf_op jit(solution)/shard_map/ppermute | solution.py:9
  23.2 0.5 %convolution_add_fusion = f32[1024,256]{1,0:T(8,128)S(1)} fusion(f32[1032,256]{1,0:T(8,128)S(1)} %collective-permute-done.8, bf16[1024,128]{0,1:T(8,128)(2,1)S(1)} %get-tuple-element.37, bf16[1024,128]{0,1:T(8,128)(2,1)S(1)} %get-tuple-element.38, bf16[1024,128]{0,1:T(8,128)(2,1)S(1)} %get-tuple-element.39, bf16[1024,128]{0,1:T(8,128)(2,1)S(1)} %get-tuple-element.36, ...), kind=kOutput, calls=%fused_computation.2 | convolution fusion | flops 273940480 | bytes 3407872 | tf_op jit(solution)/shard_map/ij,kj->ik/dot_general | solution.py:148
  23.8 1.5 %collective-permute-start.9 = (f32[520,256]{1,0:T(8,128)S(1)}, f32[520,256]{1,0:T(8,128)S(1)}, u32[]{:S(2)}, u32[]{:S(2)}) collective-permute-start(f32[520,256]{1,0:T(8,128)S(1)} %pad_maximum_fusion.3), channel_id=1, source_target_pairs={{0,2},{2,0},{1,3},{3,1},{4,6},{6,4},{5,7},{7,5},{8,10},{10,8},{9,1... | collective-permute-start | bytes 1597448 | tf_op jit(solution)/shard_map/ppermute | solution.py:9
  25.6 0.9 %collective-permute-start.7 = (f32[264,128]{1,0:T(8,128)S(1)}, f32[264,128]{1,0:T(8,128)S(1)}, u32[]{:S(2)}, u32[]{:S(2)}) collective-permute-start(f32[264,128]{1,0:T(8,128)S(1)} %get-tuple-element.53), channel_id=1, source_target_pairs={{0,12},{4,0},{8,4},{12,8},{1,13},{5,1},{9,5},{13,9},{2,14},{6,2},{... | collective-permute-start | bytes 405512 | tf_op jit(solution)/shard_map/ppermute | solution.py:9
  26.5 1.2 %collective-permute-start.11 = (f32[264,128]{1,0:T(8,128)S(1)}, f32[264,128]{1,0:T(8,128)S(1)}, u32[]{:S(2)}, u32[]{:S(2)}) collective-permute-start(f32[264,128]{1,0:T(8,128)S(1)} %get-tuple-element.52), channel_id=1, source_target_pairs={{0,4},{4,8},{8,12},{12,0},{1,5},{5,9},{9,13},{13,1},{2,6},{6,10},{... | collective-permute-start | bytes 405512 | tf_op jit(solution)/shard_map/ppermute | solution.py:9
  27.7 1.1 %collective-permute-start.10 = (f32[264,128]{1,0:T(8,128)S(1)}, f32[264,128]{1,0:T(8,128)S(1)}, u32[]{:S(2)}, u32[]{:S(2)}) collective-permute-start(f32[264,128]{1,0:T(8,128)S(1)} %get-tuple-element.51), channel_id=1, source_target_pairs={{0,8},{4,12},{8,0},{12,4},{1,9},{5,13},{9,1},{13,5},{2,10},{6,14},... | collective-permute-start | bytes 405512 | tf_op jit(solution)/shard_map/ppermute | solution.py:9
  28.8 9.2 %collective-permute-done.9 = f32[520,256]{1,0:T(8,128)S(1)} collective-permute-done((f32[520,256]{1,0:T(8,128)S(1)}, f32[520,256]{1,0:T(8,128)S(1)}, u32[]{:S(2)}, u32[]{:S(2)}) %collective-permute-start.9) | collective-permute-done | bytes 532512 | tf_op jit(solution)/shard_map/ppermute | solution.py:9
  38.1 1.1 %collective-permute-done.10 = f32[264,128]{1,0:T(8,128)S(1)} collective-permute-done((f32[264,128]{1,0:T(8,128)S(1)}, f32[264,128]{1,0:T(8,128)S(1)}, u32[]{:S(2)}, u32[]{:S(2)}) %collective-permute-start.10) | collective-permute-done | bytes 135200 | tf_op jit(solution)/shard_map/ppermute | solution.py:9
  39.4 0.9 %fusion.18 = f32[1,512,256]{2,1,0:T(8,128)} fusion(f32[512,256]{1,0:T(8,128)S(1)} %slice_add_fusion, f32[256]{0:T(256)S(1)} %bitcast.125, bf16[1,1024,256]{2,1,0:T(8,128)(2,1)S(1)} %copy-done, s32[]{:T(128)S(6)} %select_n.173), kind=kLoop, calls=%fused_computation.38 | loop fusion | flops 393216 | bytes 1311748 | tf_op jit(solution)/shard_map/broadcast_in_dim | solution.py:189
  40.8 0.8 %fusion.21 = f32[256,256]{1,0:T(8,128)} fusion(f32[264,128]{1,0:T(8,128)S(1)} %get-tuple-element.50, f32[264,128]{1,0:T(8,128)S(1)} %get-tuple-element.49, bf16[256,256]{1,0:T(8,128)(2,1)S(1)} %copy-done.1, f32[256]{0:T(256)S(1)} %bitcast.124), kind=kLoop, calls=%fused_computation.47 | loop fusion | flops 262144 | bytes 664576 | tf_op jit(solution)/shard_map/div | solution.py:187
  (98 shorter events, 4.7 us)
Async XLA Ops:
  0.6 8.7 %copy-start = (bf16[1,1024,256]{2,1,0:T(8,128)(2,1)S(1)}, bf16[1,1024,256]{2,1,0:T(8,128)(2,1)}, u32[]{:S(2)}) copy-start(bf16[1,1024,256]{2,1,0:T(8,128)(2,1)} %param.8) | copy-start | bytes 1572868
  0.6 8.6 %copy-start.3 = (s32[1,1,4]{2,1,0:T(1,128)S(1)}, s32[1,1,4]{2,1,0:T(1,128)}, u32[]{:S(2)}) copy-start(s32[1,1,4]{2,1,0:T(1,128)} %param.7) | copy-start | bytes 52
  0.7 8.7 %copy-start.2 = (s32[1,1,4,2]{2,3,1,0:T(2,128)S(1)}, s32[1,1,4,2]{2,3,1,0:T(2,128)}, u32[]{:S(2)}) copy-start(s32[1,1,4,2]{2,3,1,0:T(2,128)} %param.6) | copy-start | bytes 100
  1.6 12.8 %collective-permute-start.2 = (bf16[256,128]{1,0:T(8,128)(2,1)S(1)}, bf16[256,128]{1,0:T(8,128)(2,1)S(1)}, u32[]{:S(2)}, u32[]{:S(2)}) collective-permute-start(bf16[256,128]{1,0:T(8,128)(2,1)S(1)} %constant_dynamic-slice_fusion), channel_id=1, source_target_pairs={{0,12},{4,0},{8,4},{12,8},{1,13},{5,1},{9,5},{13,9},{2,14},{6,2},{... | collective-permute-start | bytes 196616 | tf_op jit(solution)/shard_map/ppermute | solution.py:9
  6.6 7.7 %collective-permute-start.1 = (bf16[256,128]{1,0:T(8,128)(2,1)S(1)}, bf16[256,128]{1,0:T(8,128)(2,1)S(1)}, u32[]{:S(2)}, u32[]{:S(2)}) collective-permute-start(bf16[256,128]{1,0:T(8,128)(2,1)S(1)} %constant_dynamic-slice_fusion), channel_id=1, source_target_pairs={{0,8},{4,12},{8,0},{12,4},{1,9},{5,13},{9,1},{13,5},{2,10},{6,14},... | collective-permute-start | bytes 196616 | tf_op jit(solution)/shard_map/ppermute | solution.py:9
  6.6 12.3 %collective-permute-start.6 = (bf16[1024,256]{1,0:T(8,128)(2,1)}, bf16[1024,256]{1,0:T(8,128)(2,1)S(1)}, u32[]{:S(2)}, u32[]{:S(2)}) collective-permute-start(bf16[1024,256]{1,0:T(8,128)(2,1)} %bitcast.112), channel_id=1, source_target_pairs={{0,1},{1,0},{2,3},{3,2},{4,5},{5,4},{6,7},{7,6},{8,9},{9,8},{10,11... | collective-permute-start | bytes 1572872 | tf_op jit(solution)/shard_map/ppermute | solution.py:9
  8.7 9.8 %collective-permute-start.5 = (bf16[4,2,256,128]{3,2,1,0:T(8,128)(2,1)}, bf16[4,2,256,128]{3,2,1,0:T(8,128)(2,1)S(1)}, u32[]{:S(2)}, u32[]{:S(2)}) collective-permute-start(bf16[4,2,256,128]{3,2,1,0:T(8,128)(2,1)} %get-tuple-element.40), channel_id=1, source_target_pairs={{0,1},{1,0},{2,3},{3,2},{4,5},{5,4},{6,7},{7,6},{8,9},{9,8},{10,11... | collective-permute-start | bytes 1572872 | tf_op jit(solution)/shard_map/ppermute | solution.py:9
  9.2 1.7 %collective-permute-start.4 = (s32[4]{0:T(128)S(1)}, s32[4]{0:T(128)S(1)}, u32[]{:S(2)}, u32[]{:S(2)}) collective-permute-start(s32[4]{0:T(128)S(1)} %bitcast.128), channel_id=1, source_target_pairs={{0,1},{1,0},{2,3},{3,2},{4,5},{5,4},{6,7},{7,6},{8,9},{9,8},{10,11... | collective-permute-start | bytes 56 | tf_op jit(solution)/shard_map/ppermute | solution.py:9
  10.9 1.4 %collective-permute-start.3 = (s32[4,2]{0,1:T(2,128)S(1)}, s32[4,2]{0,1:T(2,128)S(1)}, u32[]{:S(2)}, u32[]{:S(2)}) collective-permute-start(s32[4,2]{0,1:T(2,128)S(1)} %bitcast.127), channel_id=1, source_target_pairs={{0,1},{1,0},{2,3},{3,2},{4,5},{5,4},{6,7},{7,6},{8,9},{9,8},{10,11... | collective-permute-start | bytes 104 | tf_op jit(solution)/shard_map/ppermute | solution.py:9
  12.3 6.1 %collective-permute-start = (bf16[256,128]{1,0:T(8,128)(2,1)S(1)}, bf16[256,128]{1,0:T(8,128)(2,1)S(1)}, u32[]{:S(2)}, u32[]{:S(2)}) collective-permute-start(bf16[256,128]{1,0:T(8,128)(2,1)S(1)} %constant_dynamic-slice_fusion), channel_id=1, source_target_pairs={{0,4},{4,8},{8,12},{12,0},{1,5},{5,9},{9,13},{13,1},{2,6},{6,10},{... | collective-permute-start | bytes 196616 | tf_op jit(solution)/shard_map/ppermute | solution.py:9
  20.4 2.7 %collective-permute-start.8 = (f32[1032,256]{1,0:T(8,128)S(1)}, f32[1032,256]{1,0:T(8,128)S(1)}, u32[]{:S(2)}, u32[]{:S(2)}) collective-permute-start(f32[1032,256]{1,0:T(8,128)S(1)} %pad_maximum_fusion), channel_id=1, source_target_pairs={{0,1},{1,0},{2,3},{3,2},{4,5},{5,4},{6,7},{7,6},{8,9},{9,8},{10,11... | collective-permute-start | bytes 3170312 | tf_op jit(solution)/shard_map/ppermute | solution.py:9
  23.8 14.2 %collective-permute-start.9 = (f32[520,256]{1,0:T(8,128)S(1)}, f32[520,256]{1,0:T(8,128)S(1)}, u32[]{:S(2)}, u32[]{:S(2)}) collective-permute-start(f32[520,256]{1,0:T(8,128)S(1)} %pad_maximum_fusion.3), channel_id=1, source_target_pairs={{0,2},{2,0},{1,3},{3,1},{4,6},{6,4},{5,7},{7,5},{8,10},{10,8},{9,1... | collective-permute-start | bytes 1597448 | tf_op jit(solution)/shard_map/ppermute | solution.py:9
  25.6 12.5 %collective-permute-start.7 = (f32[264,128]{1,0:T(8,128)S(1)}, f32[264,128]{1,0:T(8,128)S(1)}, u32[]{:S(2)}, u32[]{:S(2)}) collective-permute-start(f32[264,128]{1,0:T(8,128)S(1)} %get-tuple-element.53), channel_id=1, source_target_pairs={{0,12},{4,0},{8,4},{12,8},{1,13},{5,1},{9,5},{13,9},{2,14},{6,2},{... | collective-permute-start | bytes 405512 | tf_op jit(solution)/shard_map/ppermute | solution.py:9
  26.5 11.6 %collective-permute-start.11 = (f32[264,128]{1,0:T(8,128)S(1)}, f32[264,128]{1,0:T(8,128)S(1)}, u32[]{:S(2)}, u32[]{:S(2)}) collective-permute-start(f32[264,128]{1,0:T(8,128)S(1)} %get-tuple-element.52), channel_id=1, source_target_pairs={{0,4},{4,8},{8,12},{12,0},{1,5},{5,9},{9,13},{13,1},{2,6},{6,10},{... | collective-permute-start | bytes 405512 | tf_op jit(solution)/shard_map/ppermute | solution.py:9
  27.7 13.1 %copy-start.1 = (bf16[256,256]{1,0:T(8,128)(2,1)S(1)}, bf16[256,256]{1,0:T(8,128)(2,1)}, u32[]{:S(2)}) copy-start(bf16[256,256]{1,0:T(8,128)(2,1)} %param.9) | copy-start | bytes 393220
  27.7 11.5 %collective-permute-start.10 = (f32[264,128]{1,0:T(8,128)S(1)}, f32[264,128]{1,0:T(8,128)S(1)}, u32[]{:S(2)}, u32[]{:S(2)}) collective-permute-start(f32[264,128]{1,0:T(8,128)S(1)} %get-tuple-element.51), channel_id=1, source_target_pairs={{0,8},{4,12},{8,0},{12,4},{1,9},{5,13},{9,1},{13,5},{2,10},{6,14},... | collective-permute-start | bytes 405512 | tf_op jit(solution)/shard_map/ppermute | solution.py:9
  39.3 1.4 %collective-permute-start.12 = (f32[264,128]{1,0:T(8,128)S(1)}, f32[264,128]{1,0:T(8,128)S(1)}, u32[]{:S(2)}, u32[]{:S(2)}) collective-permute-start(f32[264,128]{1,0:T(8,128)S(1)} %pad_maximum_fusion.12), channel_id=1, source_target_pairs={{0,1},{1,0},{2,3},{3,2},{4,5},{5,4},{6,7},{7,6},{8,9},{9,8},{10,11... | collective-permute-start | bytes 405512 | tf_op jit(solution)/shard_map/ppermute | solution.py:9

commit v15 on v11

--- a/solution.py
+++ b/solution.py
@@ -163,7 +163,7 @@
     extra = reduced[n_row * rank:]
     mine_h = reduced[:rank]
     got_w = extra
-    for d in reversed(range(1, n_row)):
+    for d in range(1, n_row):
         message = shifted(jnp.concatenate([reduced[d * rank:(d + 1) * rank], extra]), "row", d)
         mine_h = mine_h + message[:rank]
         got_w = got_w + message[rank:]

time: 36.4 us -> 36.8 us (1.011)
  waiting for transfers between devices: 10.1 us -> 11.1 us
    ppermute x10, waiting for transfers between devices: 10.1 us -> 11.1 us  [shifted(): lax.ppermute(value, axis, [(i, (i + by) % length) for i in range(length)])]
  transfers between devices with their start and end apart: 10 -> 10, of which waited for: 3 -> 4; matrix products, arithmetic and copies ran while one was open for 19% -> 18% of each run, Pallas kernels for 0% -> 0%
where the time goes in v15:
time: 36.8 us; the launch traced here: 36.5 us
  starting transfers between devices  12.8 us (35%)
  waiting for transfers between devices  11.1 us (30%)
  local copies, waits for them, and re-layouts  4.36 us (12%)
  matrix products  4 us (11%)
  other arithmetic  3.19 us (9%)
  between operations  1.07 us (3%)
    ppermute x10, starting transfers between devices, shifted(): lax.ppermute(value, axis, [(i, (i + by) % length) for i in range(length)])  12.8 us
    ppermute x10, waiting for transfers between devices, shifted(): lax.ppermute(value, axis, [(i, (i + by) % length) for i in range(length)])  11.1 us
    unnamed x15, local copies, waits for them, and re-layouts  2.08 us
    dot_general x1, matrix products, dense_terms(): jnp.einsum('ij,kj->ik', chunks[0], h_stack[0], preferred_element_type=jnp...  1.33 us
    dynamic_slice x1, local copies, waits for them, and re-layouts, body(): own_piece = lax.dynamic_slice_in_dim(h_factor, sub_index * half, half, 1)  0.92 us
    broadcast_in_dim x1, other arithmetic, body(): w_new = (w_part * mine_w / h_total[None, :])[None]  0.9 us
    div x1, other arithmetic, body(): h_new = h_factor.astype(jnp.float32) * numer_h / w_total[:, None]  0.82 us
    convert_element_type x1, other arithmetic, dense_terms(): chunks.append(r_d.astype(jnp.bfloat16).reshape(tile_rows, width))  0.74 us
  transfers between devices with their start and end apart: 10, of which 4 were waited for; matrix products, arithmetic and copies ran while one was open for 18% of the time, Pallas kernels for 0%

profile of v15, /device:TPU:0, one launch (start us, length us, event | category | flops | bytes accessed | tf_op | source)
XLA Modules:
  0.0 36.5 jit_solution(7006881706141143178)
XLA Ops:
  0.7 0.9 %constant_dynamic-slice_fusion = bf16[256,128]{1,0:T(8,128)(2,1)S(1)} fusion(bf16[256,256]{1,0:T(8,128)(2,1)} %param.9, s32[]{:T(128)S(6)} %select_n.153), kind=kLoop, calls=%fused_computation.86 | loop fusion | bytes 131076 | tf_op jit(solution)/shard_map/dynamic_slice | solution.py:123
  1.6 3.0 %collective-permute-start = (bf16[256,128]{1,0:T(8,128)(2,1)S(1)}, bf16[256,128]{1,0:T(8,128)(2,1)S(1)}, u32[]{:S(2)}, u32[]{:S(2)}) collective-permute-start(bf16[256,128]{1,0:T(8,128)(2,1)S(1)} %constant_dynamic-slice_fusion), channel_id=1, source_target_pairs={{0,4},{4,8},{8,12},{12,0},{1,5},{5,9},{9,13},{13,1},{2,6},{6,10},{... | collective-permute-start | bytes 196616 | tf_op jit(solution)/shard_map/ppermute | solution.py:9
  4.6 2.6 %collective-permute-start.1 = (bf16[256,128]{1,0:T(8,128)(2,1)S(1)}, bf16[256,128]{1,0:T(8,128)(2,1)S(1)}, u32[]{:S(2)}, u32[]{:S(2)}) collective-permute-start(bf16[256,128]{1,0:T(8,128)(2,1)S(1)} %constant_dynamic-slice_fusion), channel_id=1, source_target_pairs={{0,8},{4,12},{8,0},{12,4},{1,9},{5,13},{9,1},{13,5},{2,10},{6,14},... | collective-permute-start | bytes 196616 | tf_op jit(solution)/shard_map/ppermute | solution.py:9
  7.2 1.3 %collective-permute-start.2 = (bf16[256,128]{1,0:T(8,128)(2,1)S(1)}, bf16[256,128]{1,0:T(8,128)(2,1)S(1)}, u32[]{:S(2)}, u32[]{:S(2)}) collective-permute-start(bf16[256,128]{1,0:T(8,128)(2,1)S(1)} %constant_dynamic-slice_fusion), channel_id=1, source_target_pairs={{0,12},{4,0},{8,4},{12,8},{1,13},{5,1},{9,5},{13,9},{2,14},{6,2},{... | collective-permute-start | bytes 196616 | tf_op jit(solution)/shard_map/ppermute | solution.py:9
  8.6 1.3 %copy.15 = bf16[1,1,4,2,256,256]{5,4,2,3,1,0:T(8,128)(2,1)S(1)} copy(bf16[1,1,4,2,256,256]{5,4,3,2,1,0:T(8,128)(2,1)} %param.5) | data formatting | bytes 2097152 | tf_op args[0]
  10.0 0.4 %fusion.1 = bf16[4,256,256]{2,1,0:T(8,128)(2,1)S(1)} fusion(bf16[4,256,256]{2,1,0:T(8,128)(2,1)S(1)} %bitcast.103, pred[4]{0:T(512)(128)(4,1)S(1)} %get-tuple-element.46, pred[4]{0:T(512)(128)(4,1)S(1)} %get-tuple-element.45, pred[4]{0:T(512)(128)(4,1)S(1)} %get-tuple-element.44, bf16[256,256]{1,0:T(8,128)(2,1)S(1)} %copy-done.1, ...), kind=kOutput, calls=%fused_computation.5 | convolution fusion | flops 135790592 | bytes 2228236 | tf_op jit(solution)/shard_map/dot_general | solution.py:41
  10.4 0.4 convolution_bitcast_fusion.2
  10.8 1.3 %fusion.33 = f32[1024,256]{1,0:T(8,128)} fusion(bf16[1024,256]{1,0:T(8,128)(2,1)S(1)} %bitcast.107, bf16[256,256]{1,0:T(8,128)(2,1)S(1)} %copy-done.1), kind=kOutput, calls=%fused_computation.98 | convolution fusion | flops 134217728 | bytes 1703936 | tf_op jit(solution)/shard_map/ij,kj->ik/dot_general | solution.py:66
  13.3 0.2 copy.9
  13.7 1.4 %collective-permute-done.3 = bf16[3,256,128]{2,1,0:T(8,128)(2,1)S(1)} collective-permute-done((bf16[3,256,128]{2,1,0:T(8,128)(2,1)S(1)}, bf16[3,256,128]{2,1,0:T(8,128)(2,1)S(1)}, u32[]{:S(2)}, u32[]{:S(2)}) %collective-permute-start.3) | collective-permute-done | bytes 196640 | tf_op jit(solution)/shard_map/ppermute | solution.py:9
  15.2 0.6 %convolution_bitcast_fusion = f32[1024,768]{0,1:T(8,128)S(1)} fusion(bf16[1,1024,256]{2,1,0:T(8,128)(2,1)S(1)} %copy-done, bf16[256,256]{1,0:T(8,128)(2,1)S(1)} %get-tuple-element.28, bf16[256,256]{1,0:T(8,128)(2,1)S(1)} %get-tuple-element.29, bf16[256,256]{1,0:T(8,128)(2,1)S(1)} %get-tuple-element.27), kind=kOutput, calls=%fused_computation | convolution fusion | flops 403832832 | bytes 4063232 | tf_op jit(solution)/shard_map/dot_general | solution.py:42
  15.9 0.7 %fusion.7 = (bf16[1024,256]{0,1:T(8,128)(2,1)S(1)}, bf16[1024,256]{0,1:T(8,128)(2,1)S(1)}, bf16[1024,256]{0,1:T(8,128)(2,1)S(1)}) fusion(f32[1024,768]{0,1:T(8,128)S(1)} %convolution_bitcast_fusion, bf16[1024,256]{0,1:T(8,128)(2,1)S(1)} %copy.9, bf16[1024,256]{0,1:T(8,128)(2,1)S(1)} %copy.8, pred[1024]{0:T(1024)(128)(4,1)S(1)} %broadcast_in_dim.142, ...), kind=kLoop, calls=%fused_computation.16 | loop fusion | flops 4718592 | bytes 5776384 | tf_op jit(solution)/shard_map/convert_element_type | solution.py:57
  16.6 0.7 %convolution_bitcast_fusion.1 = f32[256,768]{1,0:T(8,128)S(1)} fusion(bf16[1024,256]{0,1:T(8,128)(2,1)S(1)} %get-tuple-element.15, bf16[1024,256]{0,1:T(8,128)(2,1)S(1)} %get-tuple-element.16, bf16[1024,256]{0,1:T(8,128)(2,1)S(1)} %get-tuple-element.14, bf16[1,1024,256]{2,1,0:T(8,128)(2,1)S(1)} %copy-done), kind=kOutput, calls=%fused_computation.6 | convolution fusion | flops 407371776 | bytes 2883584 | tf_op jit(solution)/shard_map/ik,ij->kj/dot_general | solution.py:62
  17.8 0.7 %copy-done.2 = f32[1024,256]{1,0:T(8,128)S(1)} copy-done((f32[1024,256]{1,0:T(8,128)S(1)}, f32[1024,256]{1,0:T(8,128)}, u32[]{:S(2)}) %copy-start.2) | copy-done | bytes 1048600
  18.5 0.6 %convolution_add_fusion = f32[1024,256]{1,0:T(8,128)S(1)} fusion(f32[1024,256]{1,0:T(8,128)S(1)} %copy-done.2, bf16[1024,256]{0,1:T(8,128)(2,1)S(1)} %get-tuple-element.15, bf16[1024,256]{0,1:T(8,128)(2,1)S(1)} %get-tuple-element.16, bf16[1024,256]{0,1:T(8,128)(2,1)S(1)} %get-tuple-element.14, bf16[256,256]{1,0:T(8,128)(2,1)S(1)} %get-tuple-element.28, ...), kind=kOutput, calls=%fused_computation.2 | convolution fusion | flops 408813568 | bytes 4063232 | tf_op jit(solution)/shard_map/ij,kj->ik/dot_general | solution.py:68
  19.2 1.6 %collective-permute-start.4 = (f32[520,256]{1,0:T(8,128)S(1)}, f32[520,256]{1,0:T(8,128)S(1)}, u32[]{:S(2)}, u32[]{:S(2)}) collective-permute-start(f32[520,256]{1,0:T(8,128)S(1)} %pad_maximum_fusion.3), channel_id=1, source_target_pairs={{0,2},{2,0},{1,3},{3,1},{4,6},{6,4},{5,7},{7,5},{8,10},{10,8},{9,1... | collective-permute-start | bytes 1597448 | tf_op jit(solution)/shard_map/ppermute | solution.py:9
  21.0 0.7 %collective-permute-start.6 = (f32[264,128]{1,0:T(8,128)S(1)}, f32[264,128]{1,0:T(8,128)S(1)}, u32[]{:S(2)}, u32[]{:S(2)}) collective-permute-start(f32[264,128]{1,0:T(8,128)S(1)} %get-tuple-element.36), channel_id=1, source_target_pairs={{0,4},{4,8},{8,12},{12,0},{1,5},{5,9},{9,13},{13,1},{2,6},{6,10},{... | collective-permute-start | bytes 405512 | tf_op jit(solution)/shard_map/ppermute | solution.py:9
  21.7 1.2 %collective-permute-start.7 = (f32[264,128]{1,0:T(8,128)S(1)}, f32[264,128]{1,0:T(8,128)S(1)}, u32[]{:S(2)}, u32[]{:S(2)}) collective-permute-start(f32[264,128]{1,0:T(8,128)S(1)} %get-tuple-element.37), channel_id=1, source_target_pairs={{0,8},{4,12},{8,0},{12,4},{1,9},{5,13},{9,1},{13,5},{2,10},{6,14},... | collective-permute-start | bytes 405512 | tf_op jit(solution)/shard_map/ppermute | solution.py:9
  22.9 2.0 %collective-permute-start.8 = (f32[264,128]{1,0:T(8,128)S(1)}, f32[264,128]{1,0:T(8,128)S(1)}, u32[]{:S(2)}, u32[]{:S(2)}) collective-permute-start(f32[264,128]{1,0:T(8,128)S(1)} %concatenate.48), channel_id=1, source_target_pairs={{0,12},{4,0},{8,4},{12,8},{1,13},{5,1},{9,5},{13,9},{2,14},{6,2},{... | collective-permute-start | bytes 405512 | tf_op jit(solution)/shard_map/ppermute | solution.py:9
  24.9 8.6 %collective-permute-done.4 = f32[520,256]{1,0:T(8,128)S(1)} collective-permute-done((f32[520,256]{1,0:T(8,128)S(1)}, f32[520,256]{1,0:T(8,128)S(1)}, u32[]{:S(2)}, u32[]{:S(2)}) %collective-permute-start.4) | collective-permute-done | bytes 532512 | tf_op jit(solution)/shard_map/ppermute | solution.py:9
  33.5 0.7 %collective-permute-done.7 = f32[264,128]{1,0:T(8,128)S(1)} collective-permute-done((f32[264,128]{1,0:T(8,128)S(1)}, f32[264,128]{1,0:T(8,128)S(1)}, u32[]{:S(2)}, u32[]{:S(2)}) %collective-permute-start.7) | collective-permute-done | bytes 135200 | tf_op jit(solution)/shard_map/ppermute | solution.py:9
  34.3 0.9 %fusion.10 = f32[1,512,256]{2,1,0:T(8,128)} fusion(f32[520,256]{1,0:T(8,128)S(1)} %collective-permute-done.4, f32[2,512,256]{2,1,0:T(8,128)S(1)} %bitcast.112, s32[]{:T(128)S(6)} %select_n.167, f32[256]{0:T(256)S(1)} %bitcast.123, bf16[1,1024,256]{2,1,0:T(8,128)(2,1)S(1)} %copy-done, s32[]{:T(128)S(6)} %select_n.143), kind=kLoop, calls=%fused_computation.25 | loop fusion | flops 524288 | bytes 1836040 | tf_op jit(solution)/shard_map/broadcast_in_dim | solution.py:177
  35.2 0.4 %collective-permute-done.9 = f32[264,128]{1,0:T(8,128)S(1)} collective-permute-done((f32[264,128]{1,0:T(8,128)S(1)}, f32[264,128]{1,0:T(8,128)S(1)}, u32[]{:S(2)}, u32[]{:S(2)}) %collective-permute-start.9) | collective-permute-done | bytes 135200 | tf_op jit(solution)/shard_map/ppermute | solution.py:9
  35.7 0.8 %fusion.17 = f32[256,256]{1,0:T(8,128)} fusion(f32[264,128]{1,0:T(8,128)S(1)} %get-tuple-element.33, f32[264,128]{1,0:T(8,128)S(1)} %get-tuple-element.32, bf16[256,256]{1,0:T(8,128)(2,1)S(1)} %copy-done.1, f32[256]{0:T(256)S(1)} %bitcast.121), kind=kLoop, calls=%fused_computation.42 | loop fusion | flops 262144 | bytes 664576 | tf_op jit(solution)/shard_map/div | solution.py:175
  (65 shorter events, 2.3 us)
Async XLA Ops:
  0.6 9.4 %copy-start.1 = (bf16[256,256]{1,0:T(8,128)(2,1)S(1)}, bf16[256,256]{1,0:T(8,128)(2,1)}, u32[]{:S(2)}) copy-start(bf16[256,256]{1,0:T(8,128)(2,1)} %param.9) | copy-start | bytes 393220
  0.6 9.3 %copy-start.3 = (s32[1,1,4,2]{2,3,1,0:T(2,128)S(1)}, s32[1,1,4,2]{2,3,1,0:T(2,128)}, u32[]{:S(2)}) copy-start(s32[1,1,4,2]{2,3,1,0:T(2,128)} %param.6) | copy-start | bytes 100
  0.7 9.3 %copy-start.4 = (s32[1,1,4]{2,1,0:T(1,128)S(1)}, s32[1,1,4]{2,1,0:T(1,128)}, u32[]{:S(2)}) copy-start(s32[1,1,4]{2,1,0:T(1,128)} %param.7) | copy-start | bytes 52
  0.7 9.4 %copy-start = (bf16[1,1024,256]{2,1,0:T(8,128)(2,1)S(1)}, bf16[1,1024,256]{2,1,0:T(8,128)(2,1)}, u32[]{:S(2)}) copy-start(bf16[1,1024,256]{2,1,0:T(8,128)(2,1)} %param.8) | copy-start | bytes 1572868
  1.6 12.0 %collective-permute-start = (bf16[256,128]{1,0:T(8,128)(2,1)S(1)}, bf16[256,128]{1,0:T(8,128)(2,1)S(1)}, u32[]{:S(2)}, u32[]{:S(2)}) collective-permute-start(bf16[256,128]{1,0:T(8,128)(2,1)S(1)} %constant_dynamic-slice_fusion), channel_id=1, source_target_pairs={{0,4},{4,8},{8,12},{12,0},{1,5},{5,9},{9,13},{13,1},{2,6},{6,10},{... | collective-permute-start | bytes 196616 | tf_op jit(solution)/shard_map/ppermute | solution.py:9
  4.6 8.9 %collective-permute-start.1 = (bf16[256,128]{1,0:T(8,128)(2,1)S(1)}, bf16[256,128]{1,0:T(8,128)(2,1)S(1)}, u32[]{:S(2)}, u32[]{:S(2)}) collective-permute-start(bf16[256,128]{1,0:T(8,128)(2,1)S(1)} %constant_dynamic-slice_fusion), channel_id=1, source_target_pairs={{0,8},{4,12},{8,0},{12,4},{1,9},{5,13},{9,1},{13,5},{2,10},{6,14},... | collective-permute-start | bytes 196616 | tf_op jit(solution)/shard_map/ppermute | solution.py:9
  7.2 6.4 %collective-permute-start.2 = (bf16[256,128]{1,0:T(8,128)(2,1)S(1)}, bf16[256,128]{1,0:T(8,128)(2,1)S(1)}, u32[]{:S(2)}, u32[]{:S(2)}) collective-permute-start(bf16[256,128]{1,0:T(8,128)(2,1)S(1)} %constant_dynamic-slice_fusion), channel_id=1, source_target_pairs={{0,12},{4,0},{8,4},{12,8},{1,13},{5,1},{9,5},{13,9},{2,14},{6,2},{... | collective-permute-start | bytes 196616 | tf_op jit(solution)/shard_map/ppermute | solution.py:9
  13.6 1.5 %collective-permute-start.3 = (bf16[3,256,128]{2,1,0:T(8,128)(2,1)S(1)}, bf16[3,256,128]{2,1,0:T(8,128)(2,1)S(1)}, u32[]{:S(2)}, u32[]{:S(2)}) collective-permute-start(bf16[3,256,128]{2,1,0:T(8,128)(2,1)S(1)} %pad_maximum_fusion.5), channel_id=1, source_target_pairs={{0,1},{1,0},{2,3},{3,2},{4,5},{5,4},{6,7},{7,6},{8,9},{9,8},{10,11... | collective-permute-start | bytes 589832 | tf_op jit(solution)/shard_map/ppermute | solution.py:9
  17.3 1.2 %copy-start.2 = (f32[1024,256]{1,0:T(8,128)S(1)}, f32[1024,256]{1,0:T(8,128)}, u32[]{:S(2)}) copy-start(f32[1024,256]{1,0:T(8,128)} %fusion.33) | copy-start | bytes 3145732
  17.4 3.4 %collective-permute-start.5 = (f32[1032,128]{1,0:T(8,128)S(1)}, f32[1032,128]{1,0:T(8,128)S(1)}, u32[]{:S(2)}, u32[]{:S(2)}) collective-permute-start(f32[1032,128]{1,0:T(8,128)S(1)} %broadcast_select_fusion), channel_id=1, source_target_pairs={{0,1},{1,0},{2,3},{3,2},{4,5},{5,4},{6,7},{7,6},{8,9},{9,8},{10,11... | collective-permute-start | bytes 1585160 | tf_op jit(solution)/shard_map/ppermute | solution.py:9
  19.2 14.2 %collective-permute-start.4 = (f32[520,256]{1,0:T(8,128)S(1)}, f32[520,256]{1,0:T(8,128)S(1)}, u32[]{:S(2)}, u32[]{:S(2)}) collective-permute-start(f32[520,256]{1,0:T(8,128)S(1)} %pad_maximum_fusion.3), channel_id=1, source_target_pairs={{0,2},{2,0},{1,3},{3,1},{4,6},{6,4},{5,7},{7,5},{8,10},{10,8},{9,1... | collective-permute-start | bytes 1597448 | tf_op jit(solution)/shard_map/ppermute | solution.py:9
  21.0 12.5 %collective-permute-start.6 = (f32[264,128]{1,0:T(8,128)S(1)}, f32[264,128]{1,0:T(8,128)S(1)}, u32[]{:S(2)}, u32[]{:S(2)}) collective-permute-start(f32[264,128]{1,0:T(8,128)S(1)} %get-tuple-element.36), channel_id=1, source_target_pairs={{0,4},{4,8},{8,12},{12,0},{1,5},{5,9},{9,13},{13,1},{2,6},{6,10},{... | collective-permute-start | bytes 405512 | tf_op jit(solution)/shard_map/ppermute | solution.py:9
  21.7 12.4 %collective-permute-start.7 = (f32[264,128]{1,0:T(8,128)S(1)}, f32[264,128]{1,0:T(8,128)S(1)}, u32[]{:S(2)}, u32[]{:S(2)}) collective-permute-start(f32[264,128]{1,0:T(8,128)S(1)} %get-tuple-element.37), channel_id=1, source_target_pairs={{0,8},{4,12},{8,0},{12,4},{1,9},{5,13},{9,1},{13,5},{2,10},{6,14},... | collective-permute-start | bytes 405512 | tf_op jit(solution)/shard_map/ppermute | solution.py:9
  22.9 11.2 %collective-permute-start.8 = (f32[264,128]{1,0:T(8,128)S(1)}, f32[264,128]{1,0:T(8,128)S(1)}, u32[]{:S(2)}, u32[]{:S(2)}) collective-permute-start(f32[264,128]{1,0:T(8,128)S(1)} %concatenate.48), channel_id=1, source_target_pairs={{0,12},{4,0},{8,4},{12,8},{1,13},{5,1},{9,5},{13,9},{2,14},{6,2},{... | collective-permute-start | bytes 405512 | tf_op jit(solution)/shard_map/ppermute | solution.py:9
  34.2 1.4 %collective-permute-start.9 = (f32[264,128]{1,0:T(8,128)S(1)}, f32[264,128]{1,0:T(8,128)S(1)}, u32[]{:S(2)}, u32[]{:S(2)}) collective-permute-start(f32[264,128]{1,0:T(8,128)S(1)} %pad_maximum_fusion.10), channel_id=1, source_target_pairs={{0,1},{1,0},{2,3},{3,2},{4,5},{5,4},{6,7},{7,6},{8,9},{9,8},{10,11... | collective-permute-start | bytes 405512 | tf_op jit(solution)/shard_map/ppermute | solution.py:9

commit v16 on v11

--- a/solution.py
+++ b/solution.py
@@ -120,7 +120,9 @@
 
     sub_index = lax.axis_index("sub")
     half = width // n_sub
-    own_piece = lax.dynamic_slice_in_dim(h_factor, sub_index * half, half, 1)
+    own_piece = h_factor[:, :half]
+    for p in range(1, n_sub):
+        own_piece = jnp.where(sub_index == p, h_factor[:, p * half:(p + 1) * half], own_piece)
     arrived = {d: shifted(own_piece, "row", d) for d in reversed(range(1, n_row))}
     fetched = jnp.stack([arrived[d] for d in range(1, n_row)])
     swapped = [fetched] + [shifted(fetched, "sub", k) for k in range(1, n_sub)]

time: 36.4 us -> 36.5 us (level)
  other arithmetic: 3.18 us -> 4.14 us
  local copies, waits for them, and re-layouts: 4.36 us -> 3.43 us
    select_n x0 -> x1, other arithmetic: none -> 0.96 us  [body(): jnp.where(sub_index == p, h_factor[:, p * half:(p + 1) * half], own_piece)]
    dynamic_slice x1 -> x0, local copies, waits for them, and re-layouts: 0.92 us -> none  [body(): own_piece = lax.dynamic_slice_in_dim(h_factor, sub_index * half, half, 1)]
where the time goes in v16:
time: 36.5 us; the launch traced here: 35.9 us
  starting transfers between devices  13.1 us (36%)
  waiting for transfers between devices  10.1 us (28%)
  other arithmetic  4.14 us (11%)
  matrix products  4.01 us (11%)
  local copies, waits for them, and re-layouts  3.43 us (9%)
  between operations  1.08 us (3%)
    ppermute x10, starting transfers between devices, shifted(): lax.ppermute(value, axis, [(i, (i + by) % length) for i in range(length)])  13.1 us
    ppermute x10, waiting for transfers between devices, shifted(): lax.ppermute(value, axis, [(i, (i + by) % length) for i in range(length)])  10.1 us
    unnamed x15, local copies, waits for them, and re-layouts  2.08 us
    dot_general x1, matrix products, dense_terms(): jnp.einsum('ij,kj->ik', chunks[0], h_stack[0], preferred_element_type=jnp...  1.34 us
    select_n x1, other arithmetic, body(): jnp.where(sub_index == p, h_factor[:, p * half:(p + 1) * half], own_piece)  0.96 us
    broadcast_in_dim x1, other arithmetic, body(): w_new = (w_part * mine_w / h_total[None, :])[None]  0.9 us
    div x1, other arithmetic, body(): h_new = h_factor.astype(jnp.float32) * numer_h / w_total[:, None]  0.82 us
    convert_element_type x1, other arithmetic, dense_terms(): chunks.append(r_d.astype(jnp.bfloat16).reshape(tile_rows, width))  0.74 us
  transfers between devices with their start and end apart: 10, of which 3 were waited for; matrix products, arithmetic and copies ran while one was open for 19% of the time, Pallas kernels for 0%

profile of v16, /device:TPU:0, one launch (start us, length us, event | category | flops | bytes accessed | tf_op | source)
XLA Modules:
  0.0 35.9 jit_solution(17308254355284613263)
XLA Ops:
  0.7 1.0 %slice_select_fusion = bf16[256,128]{1,0:T(8,128)(2,1)S(1)} fusion(bf16[256,256]{1,0:T(8,128)(2,1)} %param.9, pred[]{:T(512)S(6)} %eq.158), kind=kLoop, calls=%fused_computation.69 | loop fusion | flops 32768 | bytes 196609 | tf_op jit(solution)/shard_map/jit(_where)/select_n | solution.py:125
  1.6 3.1 %collective-permute-start = (bf16[256,128]{1,0:T(8,128)(2,1)S(1)}, bf16[256,128]{1,0:T(8,128)(2,1)S(1)}, u32[]{:S(2)}, u32[]{:S(2)}) collective-permute-start(bf16[256,128]{1,0:T(8,128)(2,1)S(1)} %slice_select_fusion), channel_id=1, source_target_pairs={{0,4},{4,8},{8,12},{12,0},{1,5},{5,9},{9,13},{13,1},{2,6},{6,10},{... | collective-permute-start | bytes 196616 | tf_op jit(solution)/shard_map/ppermute | solution.py:9
  4.7 2.6 %collective-permute-start.1 = (bf16[256,128]{1,0:T(8,128)(2,1)S(1)}, bf16[256,128]{1,0:T(8,128)(2,1)S(1)}, u32[]{:S(2)}, u32[]{:S(2)}) collective-permute-start(bf16[256,128]{1,0:T(8,128)(2,1)S(1)} %slice_select_fusion), channel_id=1, source_target_pairs={{0,8},{4,12},{8,0},{12,4},{1,9},{5,13},{9,1},{13,5},{2,10},{6,14},... | collective-permute-start | bytes 196616 | tf_op jit(solution)/shard_map/ppermute | solution.py:9
  7.3 1.3 %collective-permute-start.2 = (bf16[256,128]{1,0:T(8,128)(2,1)S(1)}, bf16[256,128]{1,0:T(8,128)(2,1)S(1)}, u32[]{:S(2)}, u32[]{:S(2)}) collective-permute-start(bf16[256,128]{1,0:T(8,128)(2,1)S(1)} %slice_select_fusion), channel_id=1, source_target_pairs={{0,12},{4,0},{8,4},{12,8},{1,13},{5,1},{9,5},{13,9},{2,14},{6,2},{... | collective-permute-start | bytes 196616 | tf_op jit(solution)/shard_map/ppermute | solution.py:9
  8.7 1.3 %copy.15 = bf16[1,1,4,2,256,256]{5,4,2,3,1,0:T(8,128)(2,1)S(1)} copy(bf16[1,1,4,2,256,256]{5,4,3,2,1,0:T(8,128)(2,1)} %param.5) | data formatting | bytes 2097152 | tf_op args[0]
  10.1 0.4 %fusion.1 = bf16[4,256,256]{2,1,0:T(8,128)(2,1)S(1)} fusion(bf16[4,256,256]{2,1,0:T(8,128)(2,1)S(1)} %bitcast.103, pred[4]{0:T(512)(128)(4,1)S(1)} %get-tuple-element.46, pred[4]{0:T(512)(128)(4,1)S(1)} %get-tuple-element.45, pred[4]{0:T(512)(128)(4,1)S(1)} %get-tuple-element.44, bf16[256,256]{1,0:T(8,128)(2,1)S(1)} %copy-done.1, ...), kind=kOutput, calls=%fused_computation.5 | convolution fusion | flops 135790592 | bytes 2228236 | tf_op jit(solution)/shard_map/dot_general | solution.py:41
  10.5 0.4 convolution_bitcast_fusion.2
  10.9 1.3 %fusion.33 = f32[1024,256]{1,0:T(8,128)} fusion(bf16[1024,256]{1,0:T(8,128)(2,1)S(1)} %bitcast.107, bf16[256,256]{1,0:T(8,128)(2,1)S(1)} %copy-done.1), kind=kOutput, calls=%fused_computation.98 | convolution fusion | flops 134217728 | bytes 1703936 | tf_op jit(solution)/shard_map/ij,kj->ik/dot_general | solution.py:66
  13.4 0.2 copy.9
  13.8 1.4 %collective-permute-done.3 = bf16[3,256,128]{2,1,0:T(8,128)(2,1)S(1)} collective-permute-done((bf16[3,256,128]{2,1,0:T(8,128)(2,1)S(1)}, bf16[3,256,128]{2,1,0:T(8,128)(2,1)S(1)}, u32[]{:S(2)}, u32[]{:S(2)}) %collective-permute-start.3) | collective-permute-done | bytes 196640 | tf_op jit(solution)/shard_map/ppermute | solution.py:9
  15.3 0.6 %convolution_bitcast_fusion = f32[1024,768]{0,1:T(8,128)S(1)} fusion(bf16[1,1024,256]{2,1,0:T(8,128)(2,1)S(1)} %copy-done, bf16[256,256]{1,0:T(8,128)(2,1)S(1)} %get-tuple-element.28, bf16[256,256]{1,0:T(8,128)(2,1)S(1)} %get-tuple-element.29, bf16[256,256]{1,0:T(8,128)(2,1)S(1)} %get-tuple-element.27), kind=kOutput, calls=%fused_computation | convolution fusion | flops 403832832 | bytes 4063232 | tf_op jit(solution)/shard_map/dot_general | solution.py:42
  15.9 0.7 %fusion.7 = (bf16[1024,256]{0,1:T(8,128)(2,1)S(1)}, bf16[1024,256]{0,1:T(8,128)(2,1)S(1)}, bf16[1024,256]{0,1:T(8,128)(2,1)S(1)}) fusion(f32[1024,768]{0,1:T(8,128)S(1)} %convolution_bitcast_fusion, bf16[1024,256]{0,1:T(8,128)(2,1)S(1)} %copy.9, bf16[1024,256]{0,1:T(8,128)(2,1)S(1)} %copy.8, pred[1024]{0:T(1024)(128)(4,1)S(1)} %broadcast_in_dim.142, ...), kind=kLoop, calls=%fused_computation.16 | loop fusion | flops 4718592 | bytes 5776384 | tf_op jit(solution)/shard_map/convert_element_type | solution.py:57
  16.7 0.7 %convolution_bitcast_fusion.1 = f32[256,768]{1,0:T(8,128)S(1)} fusion(bf16[1024,256]{0,1:T(8,128)(2,1)S(1)} %get-tuple-element.15, bf16[1024,256]{0,1:T(8,128)(2,1)S(1)} %get-tuple-element.16, bf16[1024,256]{0,1:T(8,128)(2,1)S(1)} %get-tuple-element.14, bf16[1,1024,256]{2,1,0:T(8,128)(2,1)S(1)} %copy-done), kind=kOutput, calls=%fused_computation.6 | convolution fusion | flops 407371776 | bytes 2883584 | tf_op jit(solution)/shard_map/ik,ij->kj/dot_general | solution.py:62
  17.5 0.2 collective-permute-start.5
  17.9 0.7 %copy-done.2 = f32[1024,256]{1,0:T(8,128)S(1)} copy-done((f32[1024,256]{1,0:T(8,128)S(1)}, f32[1024,256]{1,0:T(8,128)}, u32[]{:S(2)}) %copy-start.2) | copy-done | bytes 1048600
  18.6 0.7 %convolution_add_fusion = f32[1024,256]{1,0:T(8,128)S(1)} fusion(f32[1024,256]{1,0:T(8,128)S(1)} %copy-done.2, bf16[1024,256]{0,1:T(8,128)(2,1)S(1)} %get-tuple-element.15, bf16[1024,256]{0,1:T(8,128)(2,1)S(1)} %get-tuple-element.16, bf16[1024,256]{0,1:T(8,128)(2,1)S(1)} %get-tuple-element.14, bf16[256,256]{1,0:T(8,128)(2,1)S(1)} %get-tuple-element.28, ...), kind=kOutput, calls=%fused_computation.2 | convolution fusion | flops 408813568 | bytes 4063232 | tf_op jit(solution)/shard_map/ij,kj->ik/dot_general | solution.py:68
  19.3 1.5 %collective-permute-start.4 = (f32[520,256]{1,0:T(8,128)S(1)}, f32[520,256]{1,0:T(8,128)S(1)}, u32[]{:S(2)}, u32[]{:S(2)}) collective-permute-start(f32[520,256]{1,0:T(8,128)S(1)} %pad_maximum_fusion.3), channel_id=1, source_target_pairs={{0,2},{2,0},{1,3},{3,1},{4,6},{6,4},{5,7},{7,5},{8,10},{10,8},{9,1... | collective-permute-start | bytes 1597448 | tf_op jit(solution)/shard_map/ppermute | solution.py:9
  21.0 0.4 %collective-permute-start.7 = (f32[264,128]{1,0:T(8,128)S(1)}, f32[264,128]{1,0:T(8,128)S(1)}, u32[]{:S(2)}, u32[]{:S(2)}) collective-permute-start(f32[264,128]{1,0:T(8,128)S(1)} %get-tuple-element.36), channel_id=1, source_target_pairs={{0,8},{4,12},{8,0},{12,4},{1,9},{5,13},{9,1},{13,5},{2,10},{6,14},... | collective-permute-start | bytes 405512 | tf_op jit(solution)/shard_map/ppermute | solution.py:9
  21.5 1.6 %collective-permute-start.8 = (f32[264,128]{1,0:T(8,128)S(1)}, f32[264,128]{1,0:T(8,128)S(1)}, u32[]{:S(2)}, u32[]{:S(2)}) collective-permute-start(f32[264,128]{1,0:T(8,128)S(1)} %get-tuple-element.37), channel_id=1, source_target_pairs={{0,4},{4,8},{8,12},{12,0},{1,5},{5,9},{9,13},{13,1},{2,6},{6,10},{... | collective-permute-start | bytes 405512 | tf_op jit(solution)/shard_map/ppermute | solution.py:9
  23.1 2.2 %collective-permute-start.6 = (f32[264,128]{1,0:T(8,128)S(1)}, f32[264,128]{1,0:T(8,128)S(1)}, u32[]{:S(2)}, u32[]{:S(2)}) collective-permute-start(f32[264,128]{1,0:T(8,128)S(1)} %concatenate.48), channel_id=1, source_target_pairs={{0,12},{4,0},{8,4},{12,8},{1,13},{5,1},{9,5},{13,9},{2,14},{6,2},{... | collective-permute-start | bytes 405512 | tf_op jit(solution)/shard_map/ppermute | solution.py:9
  25.3 8.2 %collective-permute-done.4 = f32[520,256]{1,0:T(8,128)S(1)} collective-permute-done((f32[520,256]{1,0:T(8,128)S(1)}, f32[520,256]{1,0:T(8,128)S(1)}, u32[]{:S(2)}, u32[]{:S(2)}) %collective-permute-start.4) | collective-permute-done | bytes 532512 | tf_op jit(solution)/shard_map/ppermute | solution.py:9
  33.7 0.9 %fusion.10 = f32[1,512,256]{2,1,0:T(8,128)} fusion(f32[520,256]{1,0:T(8,128)S(1)} %collective-permute-done.4, f32[2,512,256]{2,1,0:T(8,128)S(1)} %bitcast.112, s32[]{:T(128)S(6)} %select_n.173, f32[256]{0:T(256)S(1)} %bitcast.123, bf16[1,1024,256]{2,1,0:T(8,128)(2,1)S(1)} %copy-done, s32[]{:T(128)S(6)} %select_n.148), kind=kLoop, calls=%fused_computation.25 | loop fusion | flops 524288 | bytes 1836040 | tf_op jit(solution)/shard_map/broadcast_in_dim | solution.py:179
  34.6 0.4 %collective-permute-done.9 = f32[264,128]{1,0:T(8,128)S(1)} collective-permute-done((f32[264,128]{1,0:T(8,128)S(1)}, f32[264,128]{1,0:T(8,128)S(1)}, u32[]{:S(2)}, u32[]{:S(2)}) %collective-permute-start.9) | collective-permute-done | bytes 135200 | tf_op jit(solution)/shard_map/ppermute | solution.py:9
  35.1 0.8 %fusion.17 = f32[256,256]{1,0:T(8,128)} fusion(f32[264,128]{1,0:T(8,128)S(1)} %get-tuple-element.33, f32[264,128]{1,0:T(8,128)S(1)} %get-tuple-element.32, bf16[256,256]{1,0:T(8,128)(2,1)S(1)} %copy-done.1, f32[256]{0:T(256)S(1)} %bitcast.121), kind=kLoop, calls=%fused_computation.42 | loop fusion | flops 262144 | bytes 664576 | tf_op jit(solution)/shard_map/div | solution.py:177
  (65 shorter events, 2.2 us)
Async XLA Ops:
  0.6 9.5 %copy-start.1 = (bf16[256,256]{1,0:T(8,128)(2,1)S(1)}, bf16[256,256]{1,0:T(8,128)(2,1)}, u32[]{:S(2)}) copy-start(bf16[256,256]{1,0:T(8,128)(2,1)} %param.9) | copy-start | bytes 393220
  0.6 9.4 %copy-start.3 = (s32[1,1,4,2]{2,3,1,0:T(2,128)S(1)}, s32[1,1,4,2]{2,3,1,0:T(2,128)}, u32[]{:S(2)}) copy-start(s32[1,1,4,2]{2,3,1,0:T(2,128)} %param.6) | copy-start | bytes 100
  0.7 9.4 %copy-start.4 = (s32[1,1,4]{2,1,0:T(1,128)S(1)}, s32[1,1,4]{2,1,0:T(1,128)}, u32[]{:S(2)}) copy-start(s32[1,1,4]{2,1,0:T(1,128)} %param.7) | copy-start | bytes 52
  0.7 9.5 %copy-start = (bf16[1,1024,256]{2,1,0:T(8,128)(2,1)S(1)}, bf16[1,1024,256]{2,1,0:T(8,128)(2,1)}, u32[]{:S(2)}) copy-start(bf16[1,1024,256]{2,1,0:T(8,128)(2,1)} %param.8) | copy-start | bytes 1572868
  1.6 12.0 %collective-permute-start = (bf16[256,128]{1,0:T(8,128)(2,1)S(1)}, bf16[256,128]{1,0:T(8,128)(2,1)S(1)}, u32[]{:S(2)}, u32[]{:S(2)}) collective-permute-start(bf16[256,128]{1,0:T(8,128)(2,1)S(1)} %slice_select_fusion), channel_id=1, source_target_pairs={{0,4},{4,8},{8,12},{12,0},{1,5},{5,9},{9,13},{13,1},{2,6},{6,10},{... | collective-permute-start | bytes 196616 | tf_op jit(solution)/shard_map/ppermute | solution.py:9
  4.7 8.9 %collective-permute-start.1 = (bf16[256,128]{1,0:T(8,128)(2,1)S(1)}, bf16[256,128]{1,0:T(8,128)(2,1)S(1)}, u32[]{:S(2)}, u32[]{:S(2)}) collective-permute-start(bf16[256,128]{1,0:T(8,128)(2,1)S(1)} %slice_select_fusion), channel_id=1, source_target_pairs={{0,8},{4,12},{8,0},{12,4},{1,9},{5,13},{9,1},{13,5},{2,10},{6,14},... | collective-permute-start | bytes 196616 | tf_op jit(solution)/shard_map/ppermute | solution.py:9
  7.3 6.4 %collective-permute-start.2 = (bf16[256,128]{1,0:T(8,128)(2,1)S(1)}, bf16[256,128]{1,0:T(8,128)(2,1)S(1)}, u32[]{:S(2)}, u32[]{:S(2)}) collective-permute-start(bf16[256,128]{1,0:T(8,128)(2,1)S(1)} %slice_select_fusion), channel_id=1, source_target_pairs={{0,12},{4,0},{8,4},{12,8},{1,13},{5,1},{9,5},{13,9},{2,14},{6,2},{... | collective-permute-start | bytes 196616 | tf_op jit(solution)/shard_map/ppermute | solution.py:9
  13.7 1.5 %collective-permute-start.3 = (bf16[3,256,128]{2,1,0:T(8,128)(2,1)S(1)}, bf16[3,256,128]{2,1,0:T(8,128)(2,1)S(1)}, u32[]{:S(2)}, u32[]{:S(2)}) collective-permute-start(bf16[3,256,128]{2,1,0:T(8,128)(2,1)S(1)} %pad_maximum_fusion.5), channel_id=1, source_target_pairs={{0,1},{1,0},{2,3},{3,2},{4,5},{5,4},{6,7},{7,6},{8,9},{9,8},{10,11... | collective-permute-start | bytes 589832 | tf_op jit(solution)/shard_map/ppermute | solution.py:9
  17.3 1.2 %copy-start.2 = (f32[1024,256]{1,0:T(8,128)S(1)}, f32[1024,256]{1,0:T(8,128)}, u32[]{:S(2)}) copy-start(f32[1024,256]{1,0:T(8,128)} %fusion.33) | copy-start | bytes 3145732
  17.5 3.3 %collective-permute-start.5 = (f32[1032,128]{1,0:T(8,128)S(1)}, f32[1032,128]{1,0:T(8,128)S(1)}, u32[]{:S(2)}, u32[]{:S(2)}) collective-permute-start(f32[1032,128]{1,0:T(8,128)S(1)} %broadcast_select_fusion), channel_id=1, source_target_pairs={{0,1},{1,0},{2,3},{3,2},{4,5},{5,4},{6,7},{7,6},{8,9},{9,8},{10,11... | collective-permute-start | bytes 1585160 | tf_op jit(solution)/shard_map/ppermute | solution.py:9
  19.3 14.2 %collective-permute-start.4 = (f32[520,256]{1,0:T(8,128)S(1)}, f32[520,256]{1,0:T(8,128)S(1)}, u32[]{:S(2)}, u32[]{:S(2)}) collective-permute-start(f32[520,256]{1,0:T(8,128)S(1)} %pad_maximum_fusion.3), channel_id=1, source_target_pairs={{0,2},{2,0},{1,3},{3,1},{4,6},{6,4},{5,7},{7,5},{8,10},{10,8},{9,1... | collective-permute-start | bytes 1597448 | tf_op jit(solution)/shard_map/ppermute | solution.py:9
  21.0 12.5 %collective-permute-start.7 = (f32[264,128]{1,0:T(8,128)S(1)}, f32[264,128]{1,0:T(8,128)S(1)}, u32[]{:S(2)}, u32[]{:S(2)}) collective-permute-start(f32[264,128]{1,0:T(8,128)S(1)} %get-tuple-element.36), channel_id=1, source_target_pairs={{0,8},{4,12},{8,0},{12,4},{1,9},{5,13},{9,1},{13,5},{2,10},{6,14},... | collective-permute-start | bytes 405512 | tf_op jit(solution)/shard_map/ppermute | solution.py:9
  21.5 12.1 %collective-permute-start.8 = (f32[264,128]{1,0:T(8,128)S(1)}, f32[264,128]{1,0:T(8,128)S(1)}, u32[]{:S(2)}, u32[]{:S(2)}) collective-permute-start(f32[264,128]{1,0:T(8,128)S(1)} %get-tuple-element.37), channel_id=1, source_target_pairs={{0,4},{4,8},{8,12},{12,0},{1,5},{5,9},{9,13},{13,1},{2,6},{6,10},{... | collective-permute-start | bytes 405512 | tf_op jit(solution)/shard_map/ppermute | solution.py:9
  23.1 10.5 %collective-permute-start.6 = (f32[264,128]{1,0:T(8,128)S(1)}, f32[264,128]{1,0:T(8,128)S(1)}, u32[]{:S(2)}, u32[]{:S(2)}) collective-permute-start(f32[264,128]{1,0:T(8,128)S(1)} %concatenate.48), channel_id=1, source_target_pairs={{0,12},{4,0},{8,4},{12,8},{1,13},{5,1},{9,5},{13,9},{2,14},{6,2},{... | collective-permute-start | bytes 405512 | tf_op jit(solution)/shard_map/ppermute | solution.py:9
  33.7 1.4 %collective-permute-start.9 = (f32[264,128]{1,0:T(8,128)S(1)}, f32[264,128]{1,0:T(8,128)S(1)}, u32[]{:S(2)}, u32[]{:S(2)}) collective-permute-start(f32[264,128]{1,0:T(8,128)S(1)} %pad_maximum_fusion.10), channel_id=1, source_target_pairs={{0,1},{1,0},{2,3},{3,2},{4,5},{5,4},{6,7},{7,6},{8,9},{9,8},{10,11... | collective-permute-start | bytes 405512 | tf_op jit(solution)/shard_map/ppermute | solution.py:9

commit v17 on v16

--- a/solution.py
+++ b/solution.py
@@ -63,9 +63,7 @@
         ],
         axis=1,
     )
-    numer_w = jnp.einsum(
-        "ij,kj->ik", chunks[0], h_stack[0], preferred_element_type=jnp.float32
-    ) + jnp.einsum("ij,kj->ik", ratios_rest, h_rest, preferred_element_type=jnp.float32)
+    numer_w = (chunks[0], h_stack[0], ratios_rest, h_rest)
     starts = [((-e) % n_row) * width for e in range(n_row)]
     return [numer_h_all[:, s:s + width] for s in starts], numer_w
 
@@ -131,10 +129,23 @@
     h_sum = jnp.sum(h_stack.astype(jnp.float32), axis=(0, 2))
     w_sum = jnp.sum(w_tile.astype(jnp.float32), axis=0)
 
-    if tile_rows * n_row * width * 4 <= (8 << 20):
-        numer_h_stack, numer_w = dense_terms(values, lists, counts, w_tile, h_stack, row_index)
+    dense = tile_rows * n_row * width * 4 <= (8 << 20)
+    if dense:
+        numer_h_stack, w_inputs = dense_terms(values, lists, counts, w_tile, h_stack, row_index)
     else:
         numer_h_stack, numer_w = slot_terms(values, lists, counts, w_tile, h_stack, row_index)
+
+    w_rows_sum = as_rows(w_sum, width)
+    messages = [
+        jnp.concatenate([x[:, p * half:(p + 1) * half] for x in numer_h_stack + [w_rows_sum]])
+        for p in range(n_sub)
+    ]
+    if dense:
+        messages, w_inputs = lax.optimization_barrier((messages, w_inputs))
+        own_r, own_h, rest_r, rest_h = w_inputs
+        numer_w = jnp.einsum(
+            "ij,kj->ik", own_r, own_h, preferred_element_type=jnp.float32
+        ) + jnp.einsum("ij,kj->ik", rest_r, rest_h, preferred_element_type=jnp.float32)
 
     share = tile_rows // n_col
     chunks = numer_w.reshape(n_col, share, rank)
@@ -148,11 +159,6 @@
         got_h = got_h + message[share:]
     h_total = from_rows(got_h, rank)
 
-    w_rows_sum = as_rows(w_sum, width)
-    messages = [
-        jnp.concatenate([x[:, p * half:(p + 1) * half] for x in numer_h_stack + [w_rows_sum]])
-        for p in range(n_sub)
-    ]
     def piece_message(k):
         want = (sub_index + k) % n_sub
         chosen = messages[0]

time: 36.5 us -> 45.5 us (1.25)
  local copies, waits for them, and re-layouts: 3.43 us -> 9.83 us
  other arithmetic: 4.14 us -> 7.3 us
  matrix products: 4.01 us -> 3.02 us
    broadcast_in_dim x12, local copies, waits for them, and re-layouts: 0.52 us -> 5.22 us  [dense_terms(): a_d = jnp.where(match[:, None, None], values[:, slot], a_d)]
    broadcast_in_dim x6, local copies, waits for them, and re-layouts: 0.26 us -> 2.62 us  [dense_terms(): r_d = jnp.where(covered[:, None, None], a_d.astype(jnp.float32) / p_d, 0.0)]
    dot_general x2, matrix products: 1.99 us -> 0.98 us  [the longest x1 0.66 us: body(): jnp.einsum('ij,kj->ik', rest_r, rest_h, preferred_element_type=jnp.float32)]
    select_n x2, other arithmetic: 0.06 us -> 0.96 us  [assemble(): chosen = jnp.where(want == k, pieces[k], chosen)]
    another operation x1, other arithmetic: 0.03 us -> 0.93 us  [body(): fetched = jnp.stack([arrived[d] for d in range(1, n_row)])]
    unnamed x15 -> x25, local copies, waits for them, and re-layouts: 2.08 us -> 1.42 us
    select_n x1, other arithmetic: 0.96 us -> 1.59 us  [body(): jnp.where(sub_index == p, h_factor[:, p * half:(p + 1) * half], own_piece)]
    or x1, other arithmetic: 0.02 us -> 0.6 us  [dense_terms(): covered = covered | match]
  transfers between devices with their start and end apart: 10 -> 10, of which waited for: 3 -> 3; matrix products, arithmetic and copies ran while one was open for 19% -> 30% of each run, Pallas kernels for 0% -> 0%
where the time goes in v17:
time: 45.5 us; the launch traced here: 44.8 us
  starting transfers between devices  13.1 us (29%)
  waiting for transfers between devices  10.3 us (23%)
  local copies, waits for them, and re-layouts  9.83 us (22%)
  other arithmetic  7.3 us (16%)
  matrix products  3.02 us (7%)
  between operations  1.18 us (3%)
    ppermute x10, starting transfers between devices, shifted(): lax.ppermute(value, axis, [(i, (i + by) % length) for i in range(length)])  13.1 us
    ppermute x10, waiting for transfers between devices, shifted(): lax.ppermute(value, axis, [(i, (i + by) % length) for i in range(length)])  10.3 us
    broadcast_in_dim x12, local copies, waits for them, and re-layouts, dense_terms(): a_d = jnp.where(match[:, None, None], values[:, slot], a_d)  5.22 us
    broadcast_in_dim x6, local copies, waits for them, and re-layouts, dense_terms(): r_d = jnp.where(covered[:, None, None], a_d.astype(jnp.float32) / p_d, 0.0)  2.62 us
    select_n x1, other arithmetic, body(): jnp.where(sub_index == p, h_factor[:, p * half:(p + 1) * half], own_piece)  1.59 us
    unnamed x25, local copies, waits for them, and re-layouts  1.42 us
    select_n x2, other arithmetic, assemble(): chosen = jnp.where(want == k, pieces[k], chosen)  0.96 us
    another operation x1, other arithmetic, body(): fetched = jnp.stack([arrived[d] for d in range(1, n_row)])  0.93 us
  transfers between devices with their start and end apart: 10, of which 3 were waited for; matrix products, arithmetic and copies ran while one was open for 30% of the time, Pallas kernels for 0%

profile of v17, /device:TPU:0, one launch (start us, length us, event | category | flops | bytes accessed | tf_op | source)
XLA Modules:
  0.0 44.8 jit_solution(4391444781352020858)
XLA Ops:
  0.7 1.6 %slice_select_fusion = bf16[256,128]{1,0:T(8,128)(2,1)} fusion(bf16[256,256]{1,0:T(8,128)(2,1)} %param.9, pred[]{:T(512)S(6)} %eq.158), kind=kLoop, calls=%fused_computation.69 | loop fusion | flops 32768 | bytes 196609 | tf_op jit(solution)/shard_map/jit(_where)/select_n | solution.py:123
  2.3 3.0 %collective-permute-start = (bf16[256,128]{1,0:T(8,128)(2,1)}, bf16[256,128]{1,0:T(8,128)(2,1)}, u32[]{:S(2)}, u32[]{:S(2)}) collective-permute-start(bf16[256,128]{1,0:T(8,128)(2,1)} %slice_select_fusion), channel_id=1, source_target_pairs={{0,4},{4,8},{8,12},{12,0},{1,5},{5,9},{9,13},{13,1},{2,6},{6,10},{... | collective-permute-start | bytes 196616 | tf_op jit(solution)/shard_map/ppermute | solution.py:9
  5.3 2.6 %collective-permute-start.1 = (bf16[256,128]{1,0:T(8,128)(2,1)}, bf16[256,128]{1,0:T(8,128)(2,1)}, u32[]{:S(2)}, u32[]{:S(2)}) collective-permute-start(bf16[256,128]{1,0:T(8,128)(2,1)} %slice_select_fusion), channel_id=1, source_target_pairs={{0,8},{4,12},{8,0},{12,4},{1,9},{5,13},{9,1},{13,5},{2,10},{6,14},... | collective-permute-start | bytes 196616 | tf_op jit(solution)/shard_map/ppermute | solution.py:9
  7.9 1.3 %collective-permute-start.2 = (bf16[256,128]{1,0:T(8,128)(2,1)}, bf16[256,128]{1,0:T(8,128)(2,1)}, u32[]{:S(2)}, u32[]{:S(2)}) collective-permute-start(bf16[256,128]{1,0:T(8,128)(2,1)} %slice_select_fusion), channel_id=1, source_target_pairs={{0,12},{4,0},{8,4},{12,8},{1,13},{5,1},{9,5},{13,9},{2,14},{6,2},{... | collective-permute-start | bytes 196616 | tf_op jit(solution)/shard_map/ppermute | solution.py:9
  9.2 1.3 %copy.15 = bf16[1,1,4,2,256,256]{5,4,2,3,1,0:T(8,128)(2,1)S(1)} copy(bf16[1,1,4,2,256,256]{5,4,3,2,1,0:T(8,128)(2,1)} %param.5) | data formatting | bytes 2097152 | tf_op args[0]
  12.2 0.7 %broadcast_in_dim.135 = pred[4,256]{1,0:T(4,128)(4,1)S(1)} broadcast(pred[4]{0:T(512)(128)(4,1)} %get-tuple-element.14), dimensions={0} | broadcast | bytes 1028 | tf_op jit(solution)/shard_map/jit(_where)/broadcast_in_dim | solution.py:56
  13.0 0.7 %broadcast_in_dim.138 = pred[4,256]{1,0:T(4,128)(4,1)S(1)} broadcast(pred[4]{0:T(512)(128)(4,1)} %get-tuple-element.15), dimensions={0} | broadcast | bytes 1028 | tf_op jit(solution)/shard_map/jit(_where)/broadcast_in_dim | solution.py:53
  13.6 0.7 %broadcast_in_dim.141 = pred[4,256]{1,0:T(4,128)(4,1)S(1)} broadcast(pred[4]{0:T(512)(128)(4,1)} %get-tuple-element.16), dimensions={0} | broadcast | bytes 1028 | tf_op jit(solution)/shard_map/jit(_where)/broadcast_in_dim | solution.py:53
  14.3 0.7 %broadcast_in_dim.145 = pred[4,256]{1,0:T(4,128)(4,1)S(1)} broadcast(pred[4]{0:T(512)(128)(4,1)} %get-tuple-element.50), dimensions={0} | broadcast | bytes 1028 | tf_op jit(solution)/shard_map/jit(_where)/broadcast_in_dim | solution.py:56
  15.6 0.7 %broadcast_in_dim.148 = pred[4,256]{1,0:T(4,128)(4,1)S(1)} broadcast(pred[4]{0:T(512)(128)(4,1)} %get-tuple-element.51), dimensions={0} | broadcast | bytes 1028 | tf_op jit(solution)/shard_map/jit(_where)/broadcast_in_dim | solution.py:53
  16.9 0.7 %broadcast_in_dim.151 = pred[4,256]{1,0:T(4,128)(4,1)S(1)} broadcast(pred[4]{0:T(512)(128)(4,1)} %get-tuple-element.52), dimensions={0} | broadcast | bytes 1028 | tf_op jit(solution)/shard_map/jit(_where)/broadcast_in_dim | solution.py:53
  20.5 0.9 %pad_maximum_fusion.3 = bf16[3,256,128]{2,1,0:T(8,128)(2,1)S(1)} fusion(bf16[1,256,128]{2,1,0:T(8,128)(2,1)} %bitcast.20, bf16[1,256,128]{2,1,0:T(8,128)(2,1)} %bitcast.19, bf16[1,256,128]{2,1,0:T(8,128)(2,1)} %bitcast.18), kind=kLoop, calls=%fused_computation.43 | loop fusion | flops 196608 | bytes 393216 | tf_op jit(solution)/shard_map/stack | solution.py:125
  21.6 1.4 %collective-permute-done.3 = bf16[3,256,128]{2,1,0:T(8,128)(2,1)S(1)} collective-permute-done((bf16[3,256,128]{2,1,0:T(8,128)(2,1)S(1)}, bf16[3,256,128]{2,1,0:T(8,128)(2,1)S(1)}, u32[]{:S(2)}, u32[]{:S(2)}) %collective-permute-start.3) | collective-permute-done | bytes 196640 | tf_op jit(solution)/shard_map/ppermute | solution.py:9
  23.0 0.9 %broadcast_select_fusion.2 = (bf16[3,256,128]{2,1,0:T(8,128)(2,1)S(1)}, bf16[3,256,128]{2,1,0:T(8,128)(2,1)S(1)}) fusion(bf16[3,256,128]{2,1,0:T(8,128)(2,1)S(1)} %collective-permute-done.3, pred[]{:T(512)S(6)} %eq.157, bf16[1,256,128]{2,1,0:T(8,128)(2,1)} %bitcast.20, bf16[1,256,128]{2,1,0:T(8,128)(2,1)} %bitcast.19, bf16[1,256,128]{2,1,0:T(8,128)(2,1)} %bitcast.18, ...), kind=kLoop, calls=%fused_computation.45 | loop fusion | flops 393216 | bytes 786434 | tf_op jit(solution)/shard_map/jit(_where)/select_n | solution.py:29
  24.0 0.6 %convolution_bitcast_fusion = f32[1024,768]{0,1:T(8,128)S(1)} fusion(bf16[1,1024,256]{2,1,0:T(8,128)(2,1)S(1)} %copy-done, bf16[256,256]{1,0:T(8,128)(2,1)S(1)} %get-tuple-element.40, bf16[256,256]{1,0:T(8,128)(2,1)S(1)} %get-tuple-element.41, bf16[256,256]{1,0:T(8,128)(2,1)S(1)} %get-tuple-element.39), kind=kOutput, calls=%fused_computation | convolution fusion | flops 403832832 | bytes 4063232 | tf_op jit(solution)/shard_map/dot_general | solution.py:42
  24.7 0.7 %fusion.7 = (bf16[1024,256]{0,1:T(8,128)(2,1)S(1)}, bf16[1024,256]{0,1:T(8,128)(2,1)S(1)}, bf16[1024,256]{0,1:T(8,128)(2,1)S(1)}) fusion(f32[1024,768]{0,1:T(8,128)S(1)} %convolution_bitcast_fusion, bf16[1024,256]{0,1:T(8,128)(2,1)S(1)} %copy.9, bf16[1024,256]{0,1:T(8,128)(2,1)S(1)} %copy.8, pred[1024]{0:T(1024)(128)(4,1)S(1)} %broadcast_in_dim.142, ...), kind=kLoop, calls=%fused_computation.16 | loop fusion | flops 4718592 | bytes 5776384 | tf_op jit(solution)/shard_map/convert_element_type | solution.py:57
  25.6 0.7 %convolution_bitcast_fusion.1 = f32[256,768]{1,0:T(8,128)S(1)} fusion(bf16[1,1024,256]{2,1,0:T(8,128)(2,1)S(1)} %copy-done, bf16[1024,256]{0,1:T(8,128)(2,1)S(1)} %get-tuple-element.27, bf16[1024,256]{0,1:T(8,128)(2,1)S(1)} %get-tuple-element.28, bf16[1024,256]{0,1:T(8,128)(2,1)S(1)} %get-tuple-element.26), kind=kOutput, calls=%fused_computation.6 | convolution fusion | flops 407371776 | bytes 2883584 | tf_op jit(solution)/shard_map/ik,ij->kj/dot_general | solution.py:62
  27.2 0.7 %convolution_add_fusion = f32[1024,256]{1,0:T(8,128)S(1)} fusion(f32[1024,256]{1,0:T(8,128)S(1)} %fusion.30, bf16[1024,768]{0,1:T(8,128)(2,1)S(1)} %pad_maximum_fusion, bf16[256,768]{1,0:T(8,128)(2,1)S(1)} %pad_maximum_fusion.2), kind=kOutput, calls=%fused_computation.2 | convolution fusion | flops 402915328 | bytes 4063232 | tf_op jit(solution)/shard_map/ij,kj->ik/dot_general | solution.py:148
  27.9 1.6 %collective-permute-start.4 = (f32[520,256]{1,0:T(8,128)S(1)}, f32[520,256]{1,0:T(8,128)S(1)}, u32[]{:S(2)}, u32[]{:S(2)}) collective-permute-start(f32[520,256]{1,0:T(8,128)S(1)} %pad_maximum_fusion.1), channel_id=1, source_target_pairs={{0,2},{2,0},{1,3},{3,1},{4,6},{6,4},{5,7},{7,5},{8,10},{10,8},{9,1... | collective-permute-start | bytes 1597448 | tf_op jit(solution)/shard_map/ppermute | solution.py:9
  30.1 0.7 %collective-permute-start.8 = (f32[264,128]{1,0:T(8,128)S(1)}, f32[264,128]{1,0:T(8,128)S(1)}, u32[]{:S(2)}, u32[]{:S(2)}) collective-permute-start(f32[264,128]{1,0:T(8,128)S(1)} %get-tuple-element.49), channel_id=1, source_target_pairs={{0,4},{4,8},{8,12},{12,0},{1,5},{5,9},{9,13},{13,1},{2,6},{6,10},{... | collective-permute-start | bytes 405512 | tf_op jit(solution)/shard_map/ppermute | solution.py:9
  30.8 3.1 %collective-permute-start.6 = (f32[264,128]{1,0:T(8,128)S(1)}, f32[264,128]{1,0:T(8,128)S(1)}, u32[]{:S(2)}, u32[]{:S(2)}) collective-permute-start(f32[264,128]{1,0:T(8,128)S(1)} %concatenate.48), channel_id=1, source_target_pairs={{0,12},{4,0},{8,4},{12,8},{1,13},{5,1},{9,5},{13,9},{2,14},{6,2},{... | collective-permute-start | bytes 405512 | tf_op jit(solution)/shard_map/ppermute | solution.py:9
  33.9 8.5 %collective-permute-done.4 = f32[520,256]{1,0:T(8,128)S(1)} collective-permute-done((f32[520,256]{1,0:T(8,128)S(1)}, f32[520,256]{1,0:T(8,128)S(1)}, u32[]{:S(2)}, u32[]{:S(2)}) %collective-permute-start.4) | collective-permute-done | bytes 532512 | tf_op jit(solution)/shard_map/ppermute | solution.py:9
  42.6 0.9 %fusion.10 = f32[1,512,256]{2,1,0:T(8,128)} fusion(f32[520,256]{1,0:T(8,128)S(1)} %collective-permute-done.4, f32[2,512,256]{2,1,0:T(8,128)S(1)} %bitcast.109, s32[]{:T(128)S(6)} %select_n.173, f32[256]{0:T(256)S(1)} %bitcast.119, bf16[1,1024,256]{2,1,0:T(8,128)(2,1)S(1)} %copy-done, s32[]{:T(128)S(6)} %select_n.148), kind=kLoop, calls=%fused_computation.25 | loop fusion | flops 524288 | bytes 1836040 | tf_op jit(solution)/shard_map/broadcast_in_dim | solution.py:185
  44.0 0.8 %fusion.17 = f32[256,256]{1,0:T(8,128)} fusion(f32[264,128]{1,0:T(8,128)S(1)} %get-tuple-element.45, f32[264,128]{1,0:T(8,128)S(1)} %get-tuple-element.44, bf16[256,256]{1,0:T(8,128)(2,1)S(1)} %copy-done.1, f32[256]{0:T(256)S(1)} %bitcast.117), kind=kLoop, calls=%fused_computation.42 | loop fusion | flops 262144 | bytes 664576 | tf_op jit(solution)/shard_map/div | solution.py:183
  (77 shorter events, 8.0 us)
Async XLA Ops:
  0.6 10.6 %copy-start.1 = (bf16[256,256]{1,0:T(8,128)(2,1)S(1)}, bf16[256,256]{1,0:T(8,128)(2,1)}, u32[]{:S(2)}) copy-start(bf16[256,256]{1,0:T(8,128)(2,1)} %param.9) | copy-start | bytes 393220
  0.6 10.0 %copy-start.8 = (s32[1,1,4,2]{2,3,1,0:T(2,128)S(1)}, s32[1,1,4,2]{2,3,1,0:T(2,128)}, u32[]{:S(2)}) copy-start(s32[1,1,4,2]{2,3,1,0:T(2,128)} %param.6) | copy-start | bytes 100
  0.7 10.0 %copy-start.9 = (s32[1,1,4]{2,1,0:T(1,128)S(1)}, s32[1,1,4]{2,1,0:T(1,128)}, u32[]{:S(2)}) copy-start(s32[1,1,4]{2,1,0:T(1,128)} %param.7) | copy-start | bytes 52
  0.7 10.6 %copy-start = (bf16[1,1024,256]{2,1,0:T(8,128)(2,1)S(1)}, bf16[1,1024,256]{2,1,0:T(8,128)(2,1)}, u32[]{:S(2)}) copy-start(bf16[1,1024,256]{2,1,0:T(8,128)(2,1)} %param.8) | copy-start | bytes 1572868
  2.3 18.2 %collective-permute-start = (bf16[256,128]{1,0:T(8,128)(2,1)}, bf16[256,128]{1,0:T(8,128)(2,1)}, u32[]{:S(2)}, u32[]{:S(2)}) collective-permute-start(bf16[256,128]{1,0:T(8,128)(2,1)} %slice_select_fusion), channel_id=1, source_target_pairs={{0,4},{4,8},{8,12},{12,0},{1,5},{5,9},{9,13},{13,1},{2,6},{6,10},{... | collective-permute-start | bytes 196616 | tf_op jit(solution)/shard_map/ppermute | solution.py:9
  5.3 15.2 %collective-permute-start.1 = (bf16[256,128]{1,0:T(8,128)(2,1)}, bf16[256,128]{1,0:T(8,128)(2,1)}, u32[]{:S(2)}, u32[]{:S(2)}) collective-permute-start(bf16[256,128]{1,0:T(8,128)(2,1)} %slice_select_fusion), channel_id=1, source_target_pairs={{0,8},{4,12},{8,0},{12,4},{1,9},{5,13},{9,1},{13,5},{2,10},{6,14},... | collective-permute-start | bytes 196616 | tf_op jit(solution)/shard_map/ppermute | solution.py:9
  7.9 12.7 %collective-permute-start.2 = (bf16[256,128]{1,0:T(8,128)(2,1)}, bf16[256,128]{1,0:T(8,128)(2,1)}, u32[]{:S(2)}, u32[]{:S(2)}) collective-permute-start(bf16[256,128]{1,0:T(8,128)(2,1)} %slice_select_fusion), channel_id=1, source_target_pairs={{0,12},{4,0},{8,4},{12,8},{1,13},{5,1},{9,5},{13,9},{2,14},{6,2},{... | collective-permute-start | bytes 196616 | tf_op jit(solution)/shard_map/ppermute | solution.py:9
  21.5 3.2 %copy-start.2 = (pred[1024]{0:T(1024)(128)(4,1)S(1)}, pred[1024]{0:T(1024)(128)(4,1)}, u32[]{:S(2)}) copy-start(pred[1024]{0:T(1024)(128)(4,1)} %broadcast_in_dim.146) | copy-start | bytes 3076
  21.5 3.2 %copy-start.3 = (pred[1024]{0:T(1024)(128)(4,1)S(1)}, pred[1024]{0:T(1024)(128)(4,1)}, u32[]{:S(2)}) copy-start(pred[1024]{0:T(1024)(128)(4,1)} %broadcast_in_dim.149) | copy-start | bytes 3076
  21.5 3.2 %copy-start.4 = (pred[1024]{0:T(1024)(128)(4,1)S(1)}, pred[1024]{0:T(1024)(128)(4,1)}, u32[]{:S(2)}) copy-start(pred[1024]{0:T(1024)(128)(4,1)} %broadcast_in_dim.152) | copy-start | bytes 3076
  21.5 3.2 %copy-start.5 = (pred[1024]{0:T(1024)(128)(4,1)S(1)}, pred[1024]{0:T(1024)(128)(4,1)}, u32[]{:S(2)}) copy-start(pred[1024]{0:T(1024)(128)(4,1)} %broadcast_in_dim.155) | copy-start | bytes 3076
  21.5 3.2 %copy-start.6 = (pred[1024]{0:T(1024)(128)(4,1)S(1)}, pred[1024]{0:T(1024)(128)(4,1)}, u32[]{:S(2)}) copy-start(pred[1024]{0:T(1024)(128)(4,1)} %broadcast_in_dim.158) | copy-start | bytes 3076
  21.5 3.2 %copy-start.7 = (pred[1024]{0:T(1024)(128)(4,1)S(1)}, pred[1024]{0:T(1024)(128)(4,1)}, u32[]{:S(2)}) copy-start(pred[1024]{0:T(1024)(128)(4,1)} %broadcast_in_dim.161) | copy-start | bytes 3076
  21.5 1.5 %collective-permute-start.3 = (bf16[3,256,128]{2,1,0:T(8,128)(2,1)S(1)}, bf16[3,256,128]{2,1,0:T(8,128)(2,1)S(1)}, u32[]{:S(2)}, u32[]{:S(2)}) collective-permute-start(bf16[3,256,128]{2,1,0:T(8,128)(2,1)S(1)} %pad_maximum_fusion.3), channel_id=1, source_target_pairs={{0,1},{1,0},{2,3},{3,2},{4,5},{5,4},{6,7},{7,6},{8,9},{9,8},{10,11... | collective-permute-start | bytes 589832 | tf_op jit(solution)/shard_map/ppermute | solution.py:9
  26.5 3.0 %collective-permute-start.5 = (f32[1032,128]{1,0:T(8,128)S(1)}, f32[1032,128]{1,0:T(8,128)S(1)}, u32[]{:S(2)}, u32[]{:S(2)}) collective-permute-start(f32[1032,128]{1,0:T(8,128)S(1)} %broadcast_select_fusion), channel_id=1, source_target_pairs={{0,1},{1,0},{2,3},{3,2},{4,5},{5,4},{6,7},{7,6},{8,9},{9,8},{10,11... | collective-permute-start | bytes 1585160 | tf_op jit(solution)/shard_map/ppermute | solution.py:9
  27.9 14.4 %collective-permute-start.4 = (f32[520,256]{1,0:T(8,128)S(1)}, f32[520,256]{1,0:T(8,128)S(1)}, u32[]{:S(2)}, u32[]{:S(2)}) collective-permute-start(f32[520,256]{1,0:T(8,128)S(1)} %pad_maximum_fusion.1), channel_id=1, source_target_pairs={{0,2},{2,0},{1,3},{3,1},{4,6},{6,4},{5,7},{7,5},{8,10},{10,8},{9,1... | collective-permute-start | bytes 1597448 | tf_op jit(solution)/shard_map/ppermute | solution.py:9
  29.7 12.7 %collective-permute-start.7 = (f32[264,128]{1,0:T(8,128)S(1)}, f32[264,128]{1,0:T(8,128)S(1)}, u32[]{:S(2)}, u32[]{:S(2)}) collective-permute-start(f32[264,128]{1,0:T(8,128)S(1)} %get-tuple-element.48), channel_id=1, source_target_pairs={{0,8},{4,12},{8,0},{12,4},{1,9},{5,13},{9,1},{13,5},{2,10},{6,14},... | collective-permute-start | bytes 405512 | tf_op jit(solution)/shard_map/ppermute | solution.py:9
  30.1 12.3 %collective-permute-start.8 = (f32[264,128]{1,0:T(8,128)S(1)}, f32[264,128]{1,0:T(8,128)S(1)}, u32[]{:S(2)}, u32[]{:S(2)}) collective-permute-start(f32[264,128]{1,0:T(8,128)S(1)} %get-tuple-element.49), channel_id=1, source_target_pairs={{0,4},{4,8},{8,12},{12,0},{1,5},{5,9},{9,13},{13,1},{2,6},{6,10},{... | collective-permute-start | bytes 405512 | tf_op jit(solution)/shard_map/ppermute | solution.py:9
  30.8 11.6 %collective-permute-start.6 = (f32[264,128]{1,0:T(8,128)S(1)}, f32[264,128]{1,0:T(8,128)S(1)}, u32[]{:S(2)}, u32[]{:S(2)}) collective-permute-start(f32[264,128]{1,0:T(8,128)S(1)} %concatenate.48), channel_id=1, source_target_pairs={{0,12},{4,0},{8,4},{12,8},{1,13},{5,1},{9,5},{13,9},{2,14},{6,2},{... | collective-permute-start | bytes 405512 | tf_op jit(solution)/shard_map/ppermute | solution.py:9
  42.5 1.4 %collective-permute-start.9 = (f32[264,128]{1,0:T(8,128)S(1)}, f32[264,128]{1,0:T(8,128)S(1)}, u32[]{:S(2)}, u32[]{:S(2)}) collective-permute-start(f32[264,128]{1,0:T(8,128)S(1)} %pad_maximum_fusion.6), channel_id=1, source_target_pairs={{0,1},{1,0},{2,3},{3,2},{4,5},{5,4},{6,7},{7,6},{8,9},{9,8},{10,11... | collective-permute-start | bytes 405512 | tf_op jit(solution)/shard_map/ppermute | solution.py:9

commit v18 on v16

--- a/solution.py
+++ b/solution.py
@@ -104,6 +104,56 @@
     return [numer_h_stack[e] for e in range(n_row)], numer_w
 
 
+def split_terms(values, lists, counts, w_tile, h_own, fetched, swapped, row_index, sub_index):
+    row_blocks, stored, width = values.shape[0], values.shape[1], values.shape[2]
+    n_row, rank = fetched.shape[0] + 1, h_own.shape[0]
+    tile_rows = w_tile.shape[0]
+    half = fetched.shape[2]
+
+    def placed(d):
+        block = (row_index - d) % n_row
+        a_d = jnp.zeros((row_blocks, width, width), values.dtype)
+        covered = jnp.zeros((row_blocks,), jnp.bool_)
+        for slot in range(stored):
+            match = (lists[:, slot] == block) & (slot < counts)
+            a_d = jnp.where(match[:, None, None], values[:, slot], a_d)
+            covered = covered | match
+        return a_d, covered
+
+    def ratios_of(a_d, covered, p_d, cols):
+        p_d = p_d.reshape(row_blocks, width, cols)
+        r_d = jnp.where(covered[:, None, None], a_d.astype(jnp.float32) / p_d, 0.0)
+        return r_d.astype(jnp.bfloat16).reshape(tile_rows, cols)
+
+    def piece_of(a_d, first):
+        lo, hi = a_d[:, :, :half], a_d[:, :, half:]
+        return jnp.where(sub_index == 0, lo, hi) if first else jnp.where(sub_index == 0, hi, lo)
+
+    a_own, c_own = placed(0)
+    r_own = ratios_of(a_own, c_own, jnp.dot(w_tile, h_own, preferred_element_type=jnp.float32), width)
+    nh_own = jnp.einsum("ik,ij->kj", w_tile, r_own, preferred_element_type=jnp.float32)
+    nw = jnp.einsum("ij,kj->ik", r_own, h_own, preferred_element_type=jnp.float32)
+
+    remote = [placed(d) for d in range(1, n_row)]
+    halves = []
+    for first, h_half in ((True, fetched), (False, swapped)):
+        h_cols = jnp.concatenate([h_half[d] for d in range(n_row - 1)], axis=1)
+        product = jnp.dot(w_tile, h_cols, preferred_element_type=jnp.float32)
+        cols = [
+            ratios_of(piece_of(a_d, first), cov, product[:, i * half:(i + 1) * half], half)
+            for i, (a_d, cov) in enumerate(remote)
+        ]
+        ratios = jnp.concatenate(cols, axis=1)
+        halves.append(jnp.einsum("ik,ij->kj", w_tile, ratios, preferred_element_type=jnp.float32))
+        nw = nw + jnp.einsum("ij,kj->ik", ratios, h_cols, preferred_element_type=jnp.float32)
+    chunks_h = [nh_own]
+    for i in range(n_row - 1):
+        a_part = halves[0][:, i * half:(i + 1) * half]
+        b_part = halves[1][:, i * half:(i + 1) * half]
+        chunks_h.append(assemble([a_part, b_part], sub_index, 2, 1))
+    return [chunks_h[(-e) % n_row] for e in range(n_row)], nw
+
+
 def body(a_blocks, block_list, block_count, w_factor, h_factor):
     values = a_blocks[0, 0]
     lists = block_list[0, 0]
@@ -131,7 +181,11 @@
     h_sum = jnp.sum(h_stack.astype(jnp.float32), axis=(0, 2))
     w_sum = jnp.sum(w_tile.astype(jnp.float32), axis=0)
 
-    if tile_rows * n_row * width * 4 <= (8 << 20):
+    if tile_rows * n_row * width * 4 <= (8 << 20) and n_sub == 2:
+        numer_h_stack, numer_w = split_terms(
+            values, lists, counts, w_tile, h_factor, fetched, swapped[1], row_index, sub_index
+        )
+    elif tile_rows * n_row * width * 4 <= (8 << 20):
         numer_h_stack, numer_w = dense_terms(values, lists, counts, w_tile, h_stack, row_index)
     else:
         numer_h_stack, numer_w = slot_terms(values, lists, counts, w_tile, h_stack, row_index)

time: 36.5 us -> 54.2 us (1.48)
  local copies, waits for them, and re-layouts: 3.43 us -> 16.8 us
  other arithmetic: 4.14 us -> 9.09 us
  waiting for transfers between devices: 10.1 us -> 8.81 us
    slice x1 -> x8, local copies, waits for them, and re-layouts: 0.07 us -> 10.7 us  [split_terms(): product[:, i * half:(i + 1) * half]]
    unnamed x15 -> x42, local copies, waits for them, and re-layouts: 2.08 us -> 4.28 us
    convert_element_type x1 -> x2, other arithmetic: 0.74 us -> 2.2 us  [ratios_of(): return r_d.astype(jnp.bfloat16).reshape(tile_rows, cols)]
    ppermute x10, waiting for transfers between devices: 10.1 us -> 8.81 us  [shifted(): lax.ppermute(value, axis, [(i, (i + by) % length) for i in range(length)])]
    select_n x0 -> x1, other arithmetic: none -> 1.32 us  [placed(): a_d = jnp.where(match[:, None, None], values[:, slot], a_d)]
    select_n x2, other arithmetic: 0.06 us -> 1 us  [assemble(): chosen = jnp.where(want == k, pieces[k], chosen)]
    concatenate x0 -> x1, local copies, waits for them, and re-layouts: none -> 0.86 us  [split_terms(): h_cols = jnp.concatenate([h_half[d] for d in range(n_row - 1)], axis=1)]
    broadcast_in_dim x18 -> x0, local copies, waits for them, and re-layouts: 0.78 us -> none  [the longest x12 0.52 us: dense_terms(): a_d = jnp.where(match[:, None, None], values[:, slot], a_d)]
  transfers between devices with their start and end apart: 10 -> 10, of which waited for: 3 -> 2; matrix products, arithmetic and copies ran while one was open for 19% -> 26% of each run, Pallas kernels for 0% -> 0%
where the time goes in v18:
time: 54.2 us; the launch traced here: 53.2 us
  local copies, waits for them, and re-layouts  16.8 us (31%)
  starting transfers between devices  13.4 us (25%)
  other arithmetic  9.09 us (17%)
  waiting for transfers between devices  8.81 us (16%)
  matrix products  3.81 us (7%)
  between operations  1.22 us (2%)
    ppermute x10, starting transfers between devices, shifted(): lax.ppermute(value, axis, [(i, (i + by) % length) for i in range(length)])  13.4 us
    slice x8, local copies, waits for them, and re-layouts, split_terms(): product[:, i * half:(i + 1) * half]  10.7 us
    ppermute x10, waiting for transfers between devices, shifted(): lax.ppermute(value, axis, [(i, (i + by) % length) for i in range(length)])  8.81 us
    unnamed x42, local copies, waits for them, and re-layouts  4.28 us
    convert_element_type x2, other arithmetic, ratios_of(): return r_d.astype(jnp.bfloat16).reshape(tile_rows, cols)  2.2 us
    select_n x1, other arithmetic, placed(): a_d = jnp.where(match[:, None, None], values[:, slot], a_d)  1.32 us
  transfers between devices with their start and end apart: 10, of which 2 were waited for; matrix products, arithmetic and copies ran while one was open for 26% of the time, Pallas kernels for 0%

profile of v18, /device:TPU:0, one launch (start us, length us, event | category | flops | bytes accessed | tf_op | source)
XLA Modules:
  0.0 53.2 jit_solution(6287500082177649506)
XLA Ops:
  0.7 1.0 %slice_select_fusion = bf16[256,128]{1,0:T(8,128)(2,1)S(1)} fusion(bf16[256,256]{1,0:T(8,128)(2,1)} %param.9, pred[]{:T(512)S(6)} %eq.178), kind=kLoop, calls=%fused_computation.68 | loop fusion | flops 32768 | bytes 196609 | tf_op jit(solution)/shard_map/jit(_where)/select_n | solution.py:175
  1.6 3.1 %collective-permute-start = (bf16[256,128]{1,0:T(8,128)(2,1)S(1)}, bf16[256,128]{1,0:T(8,128)(2,1)S(1)}, u32[]{:S(2)}, u32[]{:S(2)}) collective-permute-start(bf16[256,128]{1,0:T(8,128)(2,1)S(1)} %slice_select_fusion), channel_id=1, source_target_pairs={{0,4},{4,8},{8,12},{12,0},{1,5},{5,9},{9,13},{13,1},{2,6},{6,10},{... | collective-permute-start | bytes 196616 | tf_op jit(solution)/shard_map/ppermute | solution.py:9
  4.7 2.6 %collective-permute-start.1 = (bf16[256,128]{1,0:T(8,128)(2,1)S(1)}, bf16[256,128]{1,0:T(8,128)(2,1)S(1)}, u32[]{:S(2)}, u32[]{:S(2)}) collective-permute-start(bf16[256,128]{1,0:T(8,128)(2,1)S(1)} %slice_select_fusion), channel_id=1, source_target_pairs={{0,8},{4,12},{8,0},{12,4},{1,9},{5,13},{9,1},{13,5},{2,10},{6,14},... | collective-permute-start | bytes 196616 | tf_op jit(solution)/shard_map/ppermute | solution.py:9
  7.3 1.3 %collective-permute-start.2 = (bf16[256,128]{1,0:T(8,128)(2,1)S(1)}, bf16[256,128]{1,0:T(8,128)(2,1)S(1)}, u32[]{:S(2)}, u32[]{:S(2)}) collective-permute-start(bf16[256,128]{1,0:T(8,128)(2,1)S(1)} %slice_select_fusion), channel_id=1, source_target_pairs={{0,12},{4,0},{8,4},{12,8},{1,13},{5,1},{9,5},{13,9},{2,14},{6,2},{... | collective-permute-start | bytes 196616 | tf_op jit(solution)/shard_map/ppermute | solution.py:9
  8.7 1.3 %copy.15 = bf16[1,1,4,2,256,256]{5,4,2,3,1,0:T(8,128)(2,1)S(1)} copy(bf16[1,1,4,2,256,256]{5,4,3,2,1,0:T(8,128)(2,1)} %param.5) | data formatting | bytes 2097152 | tf_op args[0]
  12.3 1.3 %select_select_fusion.2 = (bf16[4,256,256]{2,1,0:T(8,128)(2,1)}, bf16[4,256,256]{2,1,0:T(8,128)(2,1)}, bf16[4,256,256]{2,1,0:T(8,128)(2,1)}) fusion(pred[4]{0:T(512)(128)(4,1)S(1)} %get-tuple-element.4, pred[4]{0:T(512)(128)(4,1)S(1)} %get-tuple-element.3, bf16[4,2,256,256]{3,2,0,1:T(8,128)(2,1)S(1)} %bitcast.137, pred[4]{0:T(512)(128)(4,1)S(1)} %get-tuple-element.50, ...), kind=kLoop, calls=%fused_computation.37 | loop fusion | flops 1572864 | bytes 2621464 | tf_op jit(solution)/shard_map/jit(_where)/select_n | solution.py:119
  14.6 0.9 %constant_dynamic-update-slice_fusion.1 = bf16[256,384]{1,0:T(8,128)(2,1)S(1)} fusion(bf16[256,384]{1,0:T(8,128)(2,1)S(1)} %constant_dynamic-update-slice_fusion.2, bf16[256,128]{1,0:T(8,128)(2,1)} %copy-done.7), kind=kLoop, calls=%fused_computation.70 | loop fusion | bytes 131072
  15.5 0.9 %constant_dynamic-update-slice_fusion = bf16[256,384]{1,0:T(8,128)(2,1)S(1)} fusion(bf16[256,384]{1,0:T(8,128)(2,1)S(1)} %constant_dynamic-update-slice_fusion.1, bf16[256,128]{1,0:T(8,128)(2,1)} %copy-done.9), kind=kLoop, calls=%fused_computation.69 | loop fusion | bytes 131072 | tf_op jit(solution)/shard_map/concatenate | solution.py:140
  16.8 0.9 %fusion.24 = (f32[1024,128]{0,1:T(8,128)S(1)}, f32[1024,128]{0,1:T(8,128)}, f32[1024,128]{0,1:T(8,128)S(1)}) fusion(f32[1024,384]{0,1:T(8,128)S(1)} %convolution_bitcast_fusion.1), kind=kLoop, calls=%fused_computation.101 | loop fusion | bytes 3145728 | tf_op jit(solution)/shard_map/slice | solution.py:143
  17.7 1.0 %copy.8 = f32[1024,128]{1,0:T(8,128)} copy(f32[1024,128]{0,1:T(8,128)S(1)} %get-tuple-element.17) | data formatting | bytes 1048576 | tf_op jit(solution)/shard_map/slice | solution.py:143
  18.9 1.2 %copy.10 = f32[1024,128]{1,0:T(8,128)S(1)} copy(f32[1024,128]{0,1:T(8,128)} %get-tuple-element.18) | data formatting | bytes 1048576 | tf_op jit(solution)/shard_map/slice | solution.py:143
  20.2 0.9 %slice_bitcast_fusion.4 = (bf16[256,128]{1,0:T(8,128)(2,1)S(1)}, bf16[256,128]{1,0:T(8,128)(2,1)S(1)}, bf16[256,128]{1,0:T(8,128)(2,1)S(1)}) fusion(bf16[3,256,128]{2,1,0:T(8,128)(2,1)} %collective-permute-done.3), kind=kLoop, calls=%fused_computation.67 | loop fusion | bytes 393216 | tf_op jit(solution)/shard_map/squeeze | solution.py:140
  22.2 1.2 %fusion.23 = (f32[1024,128]{0,1:T(8,128)}, f32[1024,128]{0,1:T(8,128)}, f32[1024,128]{0,1:T(8,128)}) fusion(f32[1024,384]{0,1:T(8,128)S(1)} %convolution_bitcast_fusion), kind=kLoop, calls=%fused_computation.100 | loop fusion | bytes 3145728 | tf_op jit(solution)/shard_map/slice | solution.py:143
  23.3 2.0 %copy.11 = f32[1024,128]{1,0:T(8,128)} copy(f32[1024,128]{0,1:T(8,128)} %get-tuple-element.14) | data formatting | bytes 1048576 | tf_op jit(solution)/shard_map/slice | solution.py:143
  25.4 2.0 %copy.12 = f32[1024,128]{1,0:T(8,128)} copy(f32[1024,128]{0,1:T(8,128)} %get-tuple-element.16) | data formatting | bytes 1048576 | tf_op jit(solution)/shard_map/slice | solution.py:143
  27.4 2.0 %copy.13 = f32[1024,128]{1,0:T(8,128)} copy(f32[1024,128]{0,1:T(8,128)} %get-tuple-element.15) | data formatting | bytes 1048576 | tf_op jit(solution)/shard_map/slice | solution.py:143
  29.5 1.7 %select_convert_fusion.2 = (bf16[4,256,128]{2,1,0:T(8,128)(2,1)S(1)}, bf16[4,256,128]{2,1,0:T(8,128)(2,1)S(1)}) fusion(f32[4,256,128]{2,1,0:T(8,128)} %bitcast.145, pred[4]{0:T(512)(128)(4,1)} %get-tuple-element.2, pred[]{:T(512)S(6)} %eq.177, bf16[4,256,256]{2,1,0:T(8,128)(2,1)} %get-tuple-element.20, f32[4,256,128]{2,1,0:T(8,128)} %bitcast.144), kind=kLoop, calls=%fused_computation.31 | loop fusion | flops 1310720 | bytes 2097157 | tf_op jit(solution)/shard_map/convert_element_type | solution.py:126
  34.7 1.0 %broadcast_select_fusion.2 = (bf16[3,256,128]{2,1,0:T(8,128)(2,1)S(1)}, bf16[3,256,128]{2,1,0:T(8,128)(2,1)S(1)}) fusion(bf16[3,256,128]{2,1,0:T(8,128)(2,1)} %collective-permute-done.3, pred[]{:T(512)S(6)} %eq.189, bf16[1,256,128]{2,1,0:T(8,128)(2,1)S(1)} %bitcast.160, bf16[1,256,128]{2,1,0:T(8,128)(2,1)S(1)} %bitcast.158, ...), kind=kLoop, calls=%fused_computation.47 | loop fusion | flops 393216 | bytes 786434 | tf_op jit(solution)/shard_map/jit(_where)/select_n | solution.py:29
  36.5 1.6 %collective-permute-start.4 = (f32[520,256]{1,0:T(8,128)S(1)}, f32[520,256]{1,0:T(8,128)S(1)}, u32[]{:S(2)}, u32[]{:S(2)}) collective-permute-start(f32[520,256]{1,0:T(8,128)S(1)} %pad_maximum_fusion.2), channel_id=1, source_target_pairs={{0,2},{2,0},{1,3},{3,1},{4,6},{6,4},{5,7},{7,5},{8,10},{10,8},{9,1... | collective-permute-start | bytes 1597448 | tf_op jit(solution)/shard_map/ppermute | solution.py:9
  38.6 1.4 %collective-permute-start.8 = (f32[264,128]{1,0:T(8,128)S(1)}, f32[264,128]{1,0:T(8,128)S(1)}, u32[]{:S(2)}, u32[]{:S(2)}) collective-permute-start(f32[264,128]{1,0:T(8,128)S(1)} %get-tuple-element.47), channel_id=1, source_target_pairs={{0,4},{4,8},{8,12},{12,0},{1,5},{5,9},{9,13},{13,1},{2,6},{6,10},{... | collective-permute-start | bytes 405512 | tf_op jit(solution)/shard_map/ppermute | solution.py:9
  40.0 2.4 %collective-permute-start.6 = (f32[264,128]{1,0:T(8,128)S(1)}, f32[264,128]{1,0:T(8,128)S(1)}, u32[]{:S(2)}, u32[]{:S(2)}) collective-permute-start(f32[264,128]{1,0:T(8,128)S(1)} %concatenate.56), channel_id=1, source_target_pairs={{0,12},{4,0},{8,4},{12,8},{1,13},{5,1},{9,5},{13,9},{2,14},{6,2},{... | collective-permute-start | bytes 405512 | tf_op jit(solution)/shard_map/ppermute | solution.py:9
  42.4 8.4 %collective-permute-done.4 = f32[520,256]{1,0:T(8,128)S(1)} collective-permute-done((f32[520,256]{1,0:T(8,128)S(1)}, f32[520,256]{1,0:T(8,128)S(1)}, u32[]{:S(2)}, u32[]{:S(2)}) %collective-permute-start.4) | collective-permute-done | bytes 532512 | tf_op jit(solution)/shard_map/ppermute | solution.py:9
  51.0 0.9 %fusion.4 = f32[1,512,256]{2,1,0:T(8,128)} fusion(f32[520,256]{1,0:T(8,128)S(1)} %collective-permute-done.4, f32[2,512,256]{2,1,0:T(8,128)S(1)} %bitcast.152, s32[]{:T(128)S(6)} %select_n.248, f32[256]{0:T(256)S(1)} %bitcast.171, bf16[1,1024,256]{2,1,0:T(8,128)(2,1)S(1)} %copy-done, s32[]{:T(128)S(6)} %select_n.219), kind=kLoop, calls=%fused_computation.20 | loop fusion | flops 524288 | bytes 1836040 | tf_op jit(solution)/shard_map/broadcast_in_dim | solution.py:233
  52.4 0.8 %fusion.12 = f32[256,256]{1,0:T(8,128)} fusion(f32[264,128]{1,0:T(8,128)S(1)} %get-tuple-element.40, f32[264,128]{1,0:T(8,128)S(1)} %get-tuple-element.39, bf16[256,256]{1,0:T(8,128)(2,1)S(1)} %copy-done.6, f32[256]{0:T(256)S(1)} %bitcast.169), kind=kLoop, calls=%fused_computation.43 | loop fusion | flops 262144 | bytes 664576 | tf_op jit(solution)/shard_map/div | solution.py:231
  (88 shorter events, 10.1 us)
Async XLA Ops:
  0.6 9.9 %copy-start.6 = (bf16[256,256]{1,0:T(8,128)(2,1)S(1)}, bf16[256,256]{1,0:T(8,128)(2,1)}, u32[]{:S(2)}) copy-start(bf16[256,256]{1,0:T(8,128)(2,1)} %param.9) | copy-start | bytes 393220
  0.6 9.3 %copy-start.17 = (s32[1,1,4,2]{2,3,1,0:T(2,128)S(1)}, s32[1,1,4,2]{2,3,1,0:T(2,128)}, u32[]{:S(2)}) copy-start(s32[1,1,4,2]{2,3,1,0:T(2,128)} %param.6) | copy-start | bytes 100
  0.7 9.3 %copy-start.18 = (s32[1,1,4]{2,1,0:T(1,128)S(1)}, s32[1,1,4]{2,1,0:T(1,128)}, u32[]{:S(2)}) copy-start(s32[1,1,4]{2,1,0:T(1,128)} %param.7) | copy-start | bytes 52
  0.7 9.9 %copy-start = (bf16[1,1024,256]{2,1,0:T(8,128)(2,1)S(1)}, bf16[1,1024,256]{2,1,0:T(8,128)(2,1)}, u32[]{:S(2)}) copy-start(bf16[1,1024,256]{2,1,0:T(8,128)(2,1)} %param.8) | copy-start | bytes 1572868
  1.6 12.2 %collective-permute-start = (bf16[256,128]{1,0:T(8,128)(2,1)S(1)}, bf16[256,128]{1,0:T(8,128)(2,1)S(1)}, u32[]{:S(2)}, u32[]{:S(2)}) collective-permute-start(bf16[256,128]{1,0:T(8,128)(2,1)S(1)} %slice_select_fusion), channel_id=1, source_target_pairs={{0,4},{4,8},{8,12},{12,0},{1,5},{5,9},{9,13},{13,1},{2,6},{6,10},{... | collective-permute-start | bytes 196616 | tf_op jit(solution)/shard_map/ppermute | solution.py:9
  4.7 9.1 %collective-permute-start.1 = (bf16[256,128]{1,0:T(8,128)(2,1)S(1)}, bf16[256,128]{1,0:T(8,128)(2,1)S(1)}, u32[]{:S(2)}, u32[]{:S(2)}) collective-permute-start(bf16[256,128]{1,0:T(8,128)(2,1)S(1)} %slice_select_fusion), channel_id=1, source_target_pairs={{0,8},{4,12},{8,0},{12,4},{1,9},{5,13},{9,1},{13,5},{2,10},{6,14},... | collective-permute-start | bytes 196616 | tf_op jit(solution)/shard_map/ppermute | solution.py:9
  7.3 6.6 %collective-permute-start.2 = (bf16[256,128]{1,0:T(8,128)(2,1)S(1)}, bf16[256,128]{1,0:T(8,128)(2,1)S(1)}, u32[]{:S(2)}, u32[]{:S(2)}) collective-permute-start(bf16[256,128]{1,0:T(8,128)(2,1)S(1)} %slice_select_fusion), channel_id=1, source_target_pairs={{0,12},{4,0},{8,4},{12,8},{1,13},{5,1},{9,5},{13,9},{2,14},{6,2},{... | collective-permute-start | bytes 196616 | tf_op jit(solution)/shard_map/ppermute | solution.py:9
  14.6 5.6 %collective-permute-start.3 = (bf16[3,256,128]{2,1,0:T(8,128)(2,1)}, bf16[3,256,128]{2,1,0:T(8,128)(2,1)}, u32[]{:S(2)}, u32[]{:S(2)}) collective-permute-start(bf16[3,256,128]{2,1,0:T(8,128)(2,1)} %pad_maximum_fusion.7), channel_id=1, source_target_pairs={{0,1},{1,0},{2,3},{3,2},{4,5},{5,4},{6,7},{7,6},{8,9},{9,8},{10,11... | collective-permute-start | bytes 589832 | tf_op jit(solution)/shard_map/ppermute | solution.py:9
  29.5 1.8 %copy-start.2 = (f32[1024,128]{1,0:T(8,128)S(1)}, f32[1024,128]{1,0:T(8,128)}, u32[]{:S(2)}) copy-start(f32[1024,128]{1,0:T(8,128)} %copy.12) | copy-start | bytes 1572868
  29.5 1.8 %copy-start.3 = (f32[1024,128]{1,0:T(8,128)S(1)}, f32[1024,128]{1,0:T(8,128)}, u32[]{:S(2)}) copy-start(f32[1024,128]{1,0:T(8,128)} %copy.13) | copy-start | bytes 1572868
  29.5 1.8 %copy-start.4 = (bf16[4,256,256]{2,1,0:T(8,128)(2,1)S(1)}, bf16[4,256,256]{2,1,0:T(8,128)(2,1)}, u32[]{:S(2)}) copy-start(bf16[4,256,256]{2,1,0:T(8,128)(2,1)} %get-tuple-element.21) | copy-start | bytes 1572868
  29.5 2.0 %copy-start.5 = (bf16[4,256,256]{2,1,0:T(8,128)(2,1)S(1)}, bf16[4,256,256]{2,1,0:T(8,128)(2,1)}, u32[]{:S(2)}) copy-start(bf16[4,256,256]{2,1,0:T(8,128)(2,1)} %get-tuple-element.22) | copy-start | bytes 1572868
  32.4 1.0 %copy-start.1 = (f32[1032,128]{1,0:T(8,128)S(1)}, f32[1032,128]{1,0:T(8,128)}, u32[]{:S(2)}) copy-start(f32[1032,128]{1,0:T(8,128)} %get-tuple-element.42) | copy-start | bytes 1585156
  33.6 1.1 %copy-start.8 = (bf16[256,128]{1,0:T(8,128)(2,1)S(1)}, bf16[256,128]{1,0:T(8,128)(2,1)}, u32[]{:S(2)}) copy-start(bf16[256,128]{1,0:T(8,128)(2,1)} %copy-done.7) | copy-start | bytes 196612
  33.6 1.1 %copy-start.10 = (bf16[256,128]{1,0:T(8,128)(2,1)S(1)}, bf16[256,128]{1,0:T(8,128)(2,1)}, u32[]{:S(2)}) copy-start(bf16[256,128]{1,0:T(8,128)(2,1)} %copy-done.9) | copy-start | bytes 196612
  33.6 2.2 %copy-start.12 = (bf16[256,128]{1,0:T(8,128)(2,1)S(1)}, bf16[256,128]{1,0:T(8,128)(2,1)}, u32[]{:S(2)}) copy-start(bf16[256,128]{1,0:T(8,128)(2,1)} %copy-done.11) | copy-start | bytes 196612
  33.6 2.2 %copy-start.14 = (bf16[256,128]{1,0:T(8,128)(2,1)S(1)}, bf16[256,128]{1,0:T(8,128)(2,1)}, u32[]{:S(2)}) copy-start(bf16[256,128]{1,0:T(8,128)(2,1)} %copy-done.13) | copy-start | bytes 196612
  33.7 2.2 %copy-start.16 = (bf16[256,128]{1,0:T(8,128)(2,1)S(1)}, bf16[256,128]{1,0:T(8,128)(2,1)}, u32[]{:S(2)}) copy-start(bf16[256,128]{1,0:T(8,128)(2,1)} %copy-done.15) | copy-start | bytes 196612
  33.7 4.4 %collective-permute-start.5 = (f32[1032,128]{1,0:T(8,128)S(1)}, f32[1032,128]{1,0:T(8,128)S(1)}, u32[]{:S(2)}, u32[]{:S(2)}) collective-permute-start(f32[1032,128]{1,0:T(8,128)S(1)} %broadcast_select_fusion), channel_id=1, source_target_pairs={{0,1},{1,0},{2,3},{3,2},{4,5},{5,4},{6,7},{7,6},{8,9},{9,8},{10,11... | collective-permute-start | bytes 1585160 | tf_op jit(solution)/shard_map/ppermute | solution.py:9
  36.5 14.3 %collective-permute-start.4 = (f32[520,256]{1,0:T(8,128)S(1)}, f32[520,256]{1,0:T(8,128)S(1)}, u32[]{:S(2)}, u32[]{:S(2)}) collective-permute-start(f32[520,256]{1,0:T(8,128)S(1)} %pad_maximum_fusion.2), channel_id=1, source_target_pairs={{0,2},{2,0},{1,3},{3,1},{4,6},{6,4},{5,7},{7,5},{8,10},{10,8},{9,1... | collective-permute-start | bytes 1597448 | tf_op jit(solution)/shard_map/ppermute | solution.py:9
  38.2 12.6 %collective-permute-start.7 = (f32[264,128]{1,0:T(8,128)S(1)}, f32[264,128]{1,0:T(8,128)S(1)}, u32[]{:S(2)}, u32[]{:S(2)}) collective-permute-start(f32[264,128]{1,0:T(8,128)S(1)} %get-tuple-element.46), channel_id=1, source_target_pairs={{0,8},{4,12},{8,0},{12,4},{1,9},{5,13},{9,1},{13,5},{2,10},{6,14},... | collective-permute-start | bytes 405512 | tf_op jit(solution)/shard_map/ppermute | solution.py:9
  38.6 12.2 %collective-permute-start.8 = (f32[264,128]{1,0:T(8,128)S(1)}, f32[264,128]{1,0:T(8,128)S(1)}, u32[]{:S(2)}, u32[]{:S(2)}) collective-permute-start(f32[264,128]{1,0:T(8,128)S(1)} %get-tuple-element.47), channel_id=1, source_target_pairs={{0,4},{4,8},{8,12},{12,0},{1,5},{5,9},{9,13},{13,1},{2,6},{6,10},{... | collective-permute-start | bytes 405512 | tf_op jit(solution)/shard_map/ppermute | solution.py:9
  40.0 10.8 %collective-permute-start.6 = (f32[264,128]{1,0:T(8,128)S(1)}, f32[264,128]{1,0:T(8,128)S(1)}, u32[]{:S(2)}, u32[]{:S(2)}) collective-permute-start(f32[264,128]{1,0:T(8,128)S(1)} %concatenate.56), channel_id=1, source_target_pairs={{0,12},{4,0},{8,4},{12,8},{1,13},{5,1},{9,5},{13,9},{2,14},{6,2},{... | collective-permute-start | bytes 405512 | tf_op jit(solution)/shard_map/ppermute | solution.py:9
  50.9 1.4 %collective-permute-start.9 = (f32[264,128]{1,0:T(8,128)S(1)}, f32[264,128]{1,0:T(8,128)S(1)}, u32[]{:S(2)}, u32[]{:S(2)}) collective-permute-start(f32[264,128]{1,0:T(8,128)S(1)} %pad_maximum_fusion.11), channel_id=1, source_target_pairs={{0,1},{1,0},{2,3},{3,2},{4,5},{5,4},{6,7},{7,6},{8,9},{9,8},{10,11... | collective-permute-start | bytes 405512 | tf_op jit(solution)/shard_map/ppermute | solution.py:9
  (5 other events, 3.4 us)

commit v19 on v16

--- a/solution.py
+++ b/solution.py
@@ -148,9 +148,9 @@
         got_h = got_h + message[share:]
     h_total = from_rows(got_h, rank)
 
-    w_rows_sum = as_rows(w_sum, width)
+    w_rows_sum = as_rows(w_sum, half)
     messages = [
-        jnp.concatenate([x[:, p * half:(p + 1) * half] for x in numer_h_stack + [w_rows_sum]])
+        jnp.concatenate([x[:, p * half:(p + 1) * half] for x in numer_h_stack] + [w_rows_sum])
         for p in range(n_sub)
     ]
     def piece_message(k):
@@ -169,12 +169,11 @@
         message = shifted(jnp.concatenate([reduced[d * rank:(d + 1) * rank], extra]), "row", d)
         mine_h = mine_h + message[:rank]
         got_w = got_w + message[rank:]
-    final = jnp.concatenate([mine_h, got_w])
-    total = assemble([final] + [shifted(final, "sub", k) for k in range(1, n_sub)], sub_index, n_sub, 1)
-    numer_h = total[:rank]
-    w_total = from_rows(total[rank:], rank)
-
-    h_new = h_factor.astype(jnp.float32) * numer_h / w_total[:, None]
+    w_total = from_rows(got_w, rank)
+    h_piece = own_piece.astype(jnp.float32) * mine_h / w_total[:, None]
+    h_new = assemble(
+        [h_piece] + [shifted(h_piece, "sub", k) for k in range(1, n_sub)], sub_index, n_sub, 1
+    )
     w_part = lax.dynamic_slice_in_dim(w_tile, col_index * share, share, 0).astype(jnp.float32)
     w_new = (w_part * mine_w / h_total[None, :])[None]
     return (w_new, h_new)

time: 36.5 us -> 36.5 us (level)
    concatenate x1, other arithmetic: 0.01 us -> 0.72 us  [assemble(): return jnp.concatenate(out, axis=axis)]
    div x1, other arithmetic: 0.82 us -> 0.13 us  [body(): h_piece = own_piece.astype(jnp.float32) * mine_h / w_total[:, None]]
where the time goes in v19:
time: 36.5 us; the launch traced here: 35.9 us
  starting transfers between devices  13.1 us (36%)
  waiting for transfers between devices  10.1 us (28%)
  other arithmetic  4.1 us (11%)
  matrix products  4.01 us (11%)
  local copies, waits for them, and re-layouts  3.43 us (9%)
  between operations  1.07 us (3%)
    ppermute x10, starting transfers between devices, shifted(): lax.ppermute(value, axis, [(i, (i + by) % length) for i in range(length)])  13.1 us
    ppermute x10, waiting for transfers between devices, shifted(): lax.ppermute(value, axis, [(i, (i + by) % length) for i in range(length)])  10.1 us
    unnamed x15, local copies, waits for them, and re-layouts  2.08 us
    dot_general x1, matrix products, dense_terms(): jnp.einsum('ij,kj->ik', chunks[0], h_stack[0], preferred_element_type=jnp...  1.34 us
    select_n x1, other arithmetic, body(): jnp.where(sub_index == p, h_factor[:, p * half:(p + 1) * half], own_piece)  0.96 us
    broadcast_in_dim x1, other arithmetic, body(): w_new = (w_part * mine_w / h_total[None, :])[None]  0.9 us
    convert_element_type x1, other arithmetic, dense_terms(): chunks.append(r_d.astype(jnp.bfloat16).reshape(tile_rows, width))  0.74 us
  transfers between devices with their start and end apart: 10, of which 3 were waited for; matrix products, arithmetic and copies ran while one was open for 19% of the time, Pallas kernels for 0%

profile of v19, /device:TPU:0, one launch (start us, length us, event | category | flops | bytes accessed | tf_op | source)
XLA Modules:
  0.0 35.9 jit_solution(14148896253917655980)
XLA Ops:
  0.7 1.0 %slice_select_fusion = bf16[256,128]{1,0:T(8,128)(2,1)S(1)} fusion(bf16[256,256]{1,0:T(8,128)(2,1)} %param.9, pred[]{:T(512)S(6)} %eq.158), kind=kLoop, calls=%fused_computation.64 | loop fusion | flops 32768 | bytes 196609 | tf_op jit(solution)/shard_map/jit(_where)/select_n | solution.py:125
  1.6 3.1 %collective-permute-start = (bf16[256,128]{1,0:T(8,128)(2,1)S(1)}, bf16[256,128]{1,0:T(8,128)(2,1)S(1)}, u32[]{:S(2)}, u32[]{:S(2)}) collective-permute-start(bf16[256,128]{1,0:T(8,128)(2,1)S(1)} %slice_select_fusion), channel_id=1, source_target_pairs={{0,4},{4,8},{8,12},{12,0},{1,5},{5,9},{9,13},{13,1},{2,6},{6,10},{... | collective-permute-start | bytes 196616 | tf_op jit(solution)/shard_map/ppermute | solution.py:9
  4.7 2.6 %collective-permute-start.1 = (bf16[256,128]{1,0:T(8,128)(2,1)S(1)}, bf16[256,128]{1,0:T(8,128)(2,1)S(1)}, u32[]{:S(2)}, u32[]{:S(2)}) collective-permute-start(bf16[256,128]{1,0:T(8,128)(2,1)S(1)} %slice_select_fusion), channel_id=1, source_target_pairs={{0,8},{4,12},{8,0},{12,4},{1,9},{5,13},{9,1},{13,5},{2,10},{6,14},... | collective-permute-start | bytes 196616 | tf_op jit(solution)/shard_map/ppermute | solution.py:9
  7.3 1.3 %collective-permute-start.2 = (bf16[256,128]{1,0:T(8,128)(2,1)S(1)}, bf16[256,128]{1,0:T(8,128)(2,1)S(1)}, u32[]{:S(2)}, u32[]{:S(2)}) collective-permute-start(bf16[256,128]{1,0:T(8,128)(2,1)S(1)} %slice_select_fusion), channel_id=1, source_target_pairs={{0,12},{4,0},{8,4},{12,8},{1,13},{5,1},{9,5},{13,9},{2,14},{6,2},{... | collective-permute-start | bytes 196616 | tf_op jit(solution)/shard_map/ppermute | solution.py:9
  8.7 1.3 %copy.15 = bf16[1,1,4,2,256,256]{5,4,2,3,1,0:T(8,128)(2,1)S(1)} copy(bf16[1,1,4,2,256,256]{5,4,3,2,1,0:T(8,128)(2,1)} %param.5) | data formatting | bytes 2097152 | tf_op args[0]
  10.1 0.4 %fusion.1 = bf16[4,256,256]{2,1,0:T(8,128)(2,1)S(1)} fusion(bf16[4,256,256]{2,1,0:T(8,128)(2,1)S(1)} %bitcast.104, pred[4]{0:T(512)(128)(4,1)S(1)} %get-tuple-element.46, pred[4]{0:T(512)(128)(4,1)S(1)} %get-tuple-element.45, pred[4]{0:T(512)(128)(4,1)S(1)} %get-tuple-element.44, bf16[256,256]{1,0:T(8,128)(2,1)S(1)} %copy-done.1, ...), kind=kOutput, calls=%fused_computation.5 | convolution fusion | flops 135790592 | bytes 2228236 | tf_op jit(solution)/shard_map/dot_general | solution.py:41
  10.5 0.4 convolution_bitcast_fusion.2
  10.9 1.3 %fusion.32 = f32[1024,256]{1,0:T(8,128)} fusion(bf16[1024,256]{1,0:T(8,128)(2,1)S(1)} %bitcast.108, bf16[256,256]{1,0:T(8,128)(2,1)S(1)} %copy-done.1), kind=kOutput, calls=%fused_computation.93 | convolution fusion | flops 134217728 | bytes 1703936 | tf_op jit(solution)/shard_map/ij,kj->ik/dot_general | solution.py:66
  13.4 0.2 copy.9
  13.8 1.4 %collective-permute-done.3 = bf16[3,256,128]{2,1,0:T(8,128)(2,1)S(1)} collective-permute-done((bf16[3,256,128]{2,1,0:T(8,128)(2,1)S(1)}, bf16[3,256,128]{2,1,0:T(8,128)(2,1)S(1)}, u32[]{:S(2)}, u32[]{:S(2)}) %collective-permute-start.3) | collective-permute-done | bytes 196640 | tf_op jit(solution)/shard_map/ppermute | solution.py:9
  15.3 0.6 %convolution_bitcast_fusion = f32[1024,768]{0,1:T(8,128)S(1)} fusion(bf16[1,1024,256]{2,1,0:T(8,128)(2,1)S(1)} %copy-done, bf16[256,256]{1,0:T(8,128)(2,1)S(1)} %get-tuple-element.28, bf16[256,256]{1,0:T(8,128)(2,1)S(1)} %get-tuple-element.29, bf16[256,256]{1,0:T(8,128)(2,1)S(1)} %get-tuple-element.27), kind=kOutput, calls=%fused_computation | convolution fusion | flops 403832832 | bytes 4063232 | tf_op jit(solution)/shard_map/dot_general | solution.py:42
  15.9 0.7 %fusion.7 = (bf16[1024,256]{0,1:T(8,128)(2,1)S(1)}, bf16[1024,256]{0,1:T(8,128)(2,1)S(1)}, bf16[1024,256]{0,1:T(8,128)(2,1)S(1)}) fusion(f32[1024,768]{0,1:T(8,128)S(1)} %convolution_bitcast_fusion, bf16[1024,256]{0,1:T(8,128)(2,1)S(1)} %copy.9, bf16[1024,256]{0,1:T(8,128)(2,1)S(1)} %copy.8, pred[1024]{0:T(1024)(128)(4,1)S(1)} %broadcast_in_dim.142, ...), kind=kLoop, calls=%fused_computation.16 | loop fusion | flops 4718592 | bytes 5776384 | tf_op jit(solution)/shard_map/convert_element_type | solution.py:57
  16.7 0.7 %convolution_bitcast_fusion.1 = f32[256,768]{1,0:T(8,128)S(1)} fusion(bf16[1024,256]{0,1:T(8,128)(2,1)S(1)} %get-tuple-element.15, bf16[1024,256]{0,1:T(8,128)(2,1)S(1)} %get-tuple-element.16, bf16[1024,256]{0,1:T(8,128)(2,1)S(1)} %get-tuple-element.14, bf16[1,1024,256]{2,1,0:T(8,128)(2,1)S(1)} %copy-done), kind=kOutput, calls=%fused_computation.6 | convolution fusion | flops 407371776 | bytes 2883584 | tf_op jit(solution)/shard_map/ik,ij->kj/dot_general | solution.py:62
  17.5 0.2 collective-permute-start.5
  17.9 0.7 %copy-done.2 = f32[1024,256]{1,0:T(8,128)S(1)} copy-done((f32[1024,256]{1,0:T(8,128)S(1)}, f32[1024,256]{1,0:T(8,128)}, u32[]{:S(2)}) %copy-start.2) | copy-done | bytes 1048600
  18.6 0.7 %convolution_add_fusion = f32[1024,256]{1,0:T(8,128)S(1)} fusion(f32[1024,256]{1,0:T(8,128)S(1)} %copy-done.2, bf16[1024,256]{0,1:T(8,128)(2,1)S(1)} %get-tuple-element.15, bf16[1024,256]{0,1:T(8,128)(2,1)S(1)} %get-tuple-element.16, bf16[1024,256]{0,1:T(8,128)(2,1)S(1)} %get-tuple-element.14, bf16[256,256]{1,0:T(8,128)(2,1)S(1)} %get-tuple-element.28, ...), kind=kOutput, calls=%fused_computation.2 | convolution fusion | flops 408813568 | bytes 4063232 | tf_op jit(solution)/shard_map/ij,kj->ik/dot_general | solution.py:68
  19.3 1.5 %collective-permute-start.4 = (f32[520,256]{1,0:T(8,128)S(1)}, f32[520,256]{1,0:T(8,128)S(1)}, u32[]{:S(2)}, u32[]{:S(2)}) collective-permute-start(f32[520,256]{1,0:T(8,128)S(1)} %pad_maximum_fusion.3), channel_id=1, source_target_pairs={{0,2},{2,0},{1,3},{3,1},{4,6},{6,4},{5,7},{7,5},{8,10},{10,8},{9,1... | collective-permute-start | bytes 1597448 | tf_op jit(solution)/shard_map/ppermute | solution.py:9
  21.0 0.4 %collective-permute-start.7 = (f32[264,128]{1,0:T(8,128)S(1)}, f32[264,128]{1,0:T(8,128)S(1)}, u32[]{:S(2)}, u32[]{:S(2)}) collective-permute-start(f32[264,128]{1,0:T(8,128)S(1)} %get-tuple-element.36), channel_id=1, source_target_pairs={{0,8},{4,12},{8,0},{12,4},{1,9},{5,13},{9,1},{13,5},{2,10},{6,14},... | collective-permute-start | bytes 405512 | tf_op jit(solution)/shard_map/ppermute | solution.py:9
  21.5 1.6 %collective-permute-start.8 = (f32[264,128]{1,0:T(8,128)S(1)}, f32[264,128]{1,0:T(8,128)S(1)}, u32[]{:S(2)}, u32[]{:S(2)}) collective-permute-start(f32[264,128]{1,0:T(8,128)S(1)} %get-tuple-element.37), channel_id=1, source_target_pairs={{0,4},{4,8},{8,12},{12,0},{1,5},{5,9},{9,13},{13,1},{2,6},{6,10},{... | collective-permute-start | bytes 405512 | tf_op jit(solution)/shard_map/ppermute | solution.py:9
  23.1 2.2 %collective-permute-start.6 = (f32[264,128]{1,0:T(8,128)S(1)}, f32[264,128]{1,0:T(8,128)S(1)}, u32[]{:S(2)}, u32[]{:S(2)}) collective-permute-start(f32[264,128]{1,0:T(8,128)S(1)} %concatenate.44), channel_id=1, source_target_pairs={{0,12},{4,0},{8,4},{12,8},{1,13},{5,1},{9,5},{13,9},{2,14},{6,2},{... | collective-permute-start | bytes 405512 | tf_op jit(solution)/shard_map/ppermute | solution.py:9
  25.3 8.2 %collective-permute-done.4 = f32[520,256]{1,0:T(8,128)S(1)} collective-permute-done((f32[520,256]{1,0:T(8,128)S(1)}, f32[520,256]{1,0:T(8,128)S(1)}, u32[]{:S(2)}, u32[]{:S(2)}) %collective-permute-start.4) | collective-permute-done | bytes 532512 | tf_op jit(solution)/shard_map/ppermute | solution.py:9
  33.8 0.9 %fusion.10 = f32[1,512,256]{2,1,0:T(8,128)} fusion(f32[520,256]{1,0:T(8,128)S(1)} %collective-permute-done.4, f32[2,512,256]{2,1,0:T(8,128)S(1)} %bitcast.113, s32[]{:T(128)S(6)} %select_n.173, f32[256]{0:T(256)S(1)} %bitcast.123, bf16[1,1024,256]{2,1,0:T(8,128)(2,1)S(1)} %copy-done, s32[]{:T(128)S(6)} %select_n.148), kind=kLoop, calls=%fused_computation.25 | loop fusion | flops 524288 | bytes 1836040 | tf_op jit(solution)/shard_map/broadcast_in_dim | solution.py:178
  34.7 0.4 %collective-permute-done.9 = f32[256,128]{1,0:T(8,128)S(1)} collective-permute-done((f32[256,128]{1,0:T(8,128)S(1)}, f32[256,128]{1,0:T(8,128)S(1)}, u32[]{:S(2)}, u32[]{:S(2)}) %collective-permute-start.9) | collective-permute-done | bytes 131104 | tf_op jit(solution)/shard_map/ppermute | solution.py:9
  35.2 0.7 %pad_maximum_fusion.5 = f32[256,256]{1,0:T(8,128)} fusion(f32[256,128]{1,0:T(8,128)S(1)} %get-tuple-element.33, f32[256,128]{1,0:T(8,128)S(1)} %get-tuple-element.32), kind=kLoop, calls=%fused_computation.38 | loop fusion | flops 65536 | bytes 524288 | tf_op jit(solution)/shard_map/concatenate | solution.py:31
  (64 shorter events, 2.2 us)
Async XLA Ops:
  0.6 9.5 %copy-start.1 = (bf16[256,256]{1,0:T(8,128)(2,1)S(1)}, bf16[256,256]{1,0:T(8,128)(2,1)}, u32[]{:S(2)}) copy-start(bf16[256,256]{1,0:T(8,128)(2,1)} %param.9) | copy-start | bytes 393220
  0.6 9.4 %copy-start.3 = (s32[1,1,4,2]{2,3,1,0:T(2,128)S(1)}, s32[1,1,4,2]{2,3,1,0:T(2,128)}, u32[]{:S(2)}) copy-start(s32[1,1,4,2]{2,3,1,0:T(2,128)} %param.6) | copy-start | bytes 100
  0.7 9.4 %copy-start.4 = (s32[1,1,4]{2,1,0:T(1,128)S(1)}, s32[1,1,4]{2,1,0:T(1,128)}, u32[]{:S(2)}) copy-start(s32[1,1,4]{2,1,0:T(1,128)} %param.7) | copy-start | bytes 52
  0.7 9.5 %copy-start = (bf16[1,1024,256]{2,1,0:T(8,128)(2,1)S(1)}, bf16[1,1024,256]{2,1,0:T(8,128)(2,1)}, u32[]{:S(2)}) copy-start(bf16[1,1024,256]{2,1,0:T(8,128)(2,1)} %param.8) | copy-start | bytes 1572868
  1.6 12.0 %collective-permute-start = (bf16[256,128]{1,0:T(8,128)(2,1)S(1)}, bf16[256,128]{1,0:T(8,128)(2,1)S(1)}, u32[]{:S(2)}, u32[]{:S(2)}) collective-permute-start(bf16[256,128]{1,0:T(8,128)(2,1)S(1)} %slice_select_fusion), channel_id=1, source_target_pairs={{0,4},{4,8},{8,12},{12,0},{1,5},{5,9},{9,13},{13,1},{2,6},{6,10},{... | collective-permute-start | bytes 196616 | tf_op jit(solution)/shard_map/ppermute | solution.py:9
  4.7 8.9 %collective-permute-start.1 = (bf16[256,128]{1,0:T(8,128)(2,1)S(1)}, bf16[256,128]{1,0:T(8,128)(2,1)S(1)}, u32[]{:S(2)}, u32[]{:S(2)}) collective-permute-start(bf16[256,128]{1,0:T(8,128)(2,1)S(1)} %slice_select_fusion), channel_id=1, source_target_pairs={{0,8},{4,12},{8,0},{12,4},{1,9},{5,13},{9,1},{13,5},{2,10},{6,14},... | collective-permute-start | bytes 196616 | tf_op jit(solution)/shard_map/ppermute | solution.py:9
  7.3 6.4 %collective-permute-start.2 = (bf16[256,128]{1,0:T(8,128)(2,1)S(1)}, bf16[256,128]{1,0:T(8,128)(2,1)S(1)}, u32[]{:S(2)}, u32[]{:S(2)}) collective-permute-start(bf16[256,128]{1,0:T(8,128)(2,1)S(1)} %slice_select_fusion), channel_id=1, source_target_pairs={{0,12},{4,0},{8,4},{12,8},{1,13},{5,1},{9,5},{13,9},{2,14},{6,2},{... | collective-permute-start | bytes 196616 | tf_op jit(solution)/shard_map/ppermute | solution.py:9
  13.7 1.5 %collective-permute-start.3 = (bf16[3,256,128]{2,1,0:T(8,128)(2,1)S(1)}, bf16[3,256,128]{2,1,0:T(8,128)(2,1)S(1)}, u32[]{:S(2)}, u32[]{:S(2)}) collective-permute-start(bf16[3,256,128]{2,1,0:T(8,128)(2,1)S(1)} %pad_maximum_fusion.6), channel_id=1, source_target_pairs={{0,1},{1,0},{2,3},{3,2},{4,5},{5,4},{6,7},{7,6},{8,9},{9,8},{10,11... | collective-permute-start | bytes 589832 | tf_op jit(solution)/shard_map/ppermute | solution.py:9
  17.3 1.2 %copy-start.2 = (f32[1024,256]{1,0:T(8,128)S(1)}, f32[1024,256]{1,0:T(8,128)}, u32[]{:S(2)}) copy-start(f32[1024,256]{1,0:T(8,128)} %fusion.32) | copy-start | bytes 3145732
  17.5 3.3 %collective-permute-start.5 = (f32[1032,128]{1,0:T(8,128)S(1)}, f32[1032,128]{1,0:T(8,128)S(1)}, u32[]{:S(2)}, u32[]{:S(2)}) collective-permute-start(f32[1032,128]{1,0:T(8,128)S(1)} %broadcast_select_fusion), channel_id=1, source_target_pairs={{0,1},{1,0},{2,3},{3,2},{4,5},{5,4},{6,7},{7,6},{8,9},{9,8},{10,11... | collective-permute-start | bytes 1585160 | tf_op jit(solution)/shard_map/ppermute | solution.py:9
  19.3 14.2 %collective-permute-start.4 = (f32[520,256]{1,0:T(8,128)S(1)}, f32[520,256]{1,0:T(8,128)S(1)}, u32[]{:S(2)}, u32[]{:S(2)}) collective-permute-start(f32[520,256]{1,0:T(8,128)S(1)} %pad_maximum_fusion.3), channel_id=1, source_target_pairs={{0,2},{2,0},{1,3},{3,1},{4,6},{6,4},{5,7},{7,5},{8,10},{10,8},{9,1... | collective-permute-start | bytes 1597448 | tf_op jit(solution)/shard_map/ppermute | solution.py:9
  21.0 12.5 %collective-permute-start.7 = (f32[264,128]{1,0:T(8,128)S(1)}, f32[264,128]{1,0:T(8,128)S(1)}, u32[]{:S(2)}, u32[]{:S(2)}) collective-permute-start(f32[264,128]{1,0:T(8,128)S(1)} %get-tuple-element.36), channel_id=1, source_target_pairs={{0,8},{4,12},{8,0},{12,4},{1,9},{5,13},{9,1},{13,5},{2,10},{6,14},... | collective-permute-start | bytes 405512 | tf_op jit(solution)/shard_map/ppermute | solution.py:9
  21.5 12.1 %collective-permute-start.8 = (f32[264,128]{1,0:T(8,128)S(1)}, f32[264,128]{1,0:T(8,128)S(1)}, u32[]{:S(2)}, u32[]{:S(2)}) collective-permute-start(f32[264,128]{1,0:T(8,128)S(1)} %get-tuple-element.37), channel_id=1, source_target_pairs={{0,4},{4,8},{8,12},{12,0},{1,5},{5,9},{9,13},{13,1},{2,6},{6,10},{... | collective-permute-start | bytes 405512 | tf_op jit(solution)/shard_map/ppermute | solution.py:9
  23.1 10.5 %collective-permute-start.6 = (f32[264,128]{1,0:T(8,128)S(1)}, f32[264,128]{1,0:T(8,128)S(1)}, u32[]{:S(2)}, u32[]{:S(2)}) collective-permute-start(f32[264,128]{1,0:T(8,128)S(1)} %concatenate.44), channel_id=1, source_target_pairs={{0,12},{4,0},{8,4},{12,8},{1,13},{5,1},{9,5},{13,9},{2,14},{6,2},{... | collective-permute-start | bytes 405512 | tf_op jit(solution)/shard_map/ppermute | solution.py:9
  33.7 1.4 %collective-permute-start.9 = (f32[256,128]{1,0:T(8,128)S(1)}, f32[256,128]{1,0:T(8,128)S(1)}, u32[]{:S(2)}, u32[]{:S(2)}) collective-permute-start(f32[256,128]{1,0:T(8,128)S(1)} %fusion.20), channel_id=1, source_target_pairs={{0,1},{1,0},{2,3},{3,2},{4,5},{5,4},{6,7},{7,6},{8,9},{9,8},{10,11... | collective-permute-start | bytes 393224 | tf_op jit(solution)/shard_map/ppermute | solution.py:9

commit v20 on v16

--- a/solution.py
+++ b/solution.py
@@ -174,9 +174,9 @@
     numer_h = total[:rank]
     w_total = from_rows(total[rank:], rank)
 
-    h_new = h_factor.astype(jnp.float32) * numer_h / w_total[:, None]
+    h_new = h_factor.astype(jnp.float32) * numer_h * (1.0 / w_total)[:, None]
     w_part = lax.dynamic_slice_in_dim(w_tile, col_index * share, share, 0).astype(jnp.float32)
-    w_new = (w_part * mine_w / h_total[None, :])[None]
+    w_new = (w_part * mine_w * (1.0 / h_total)[None, :])[None]
     return (w_new, h_new)
 
 

time: 36.5 us -> 36.5 us (level)
    mul x0 -> x1, other arithmetic: none -> 0.81 us  [body(): h_new = h_factor.astype(jnp.float32) * numer_h * (1.0 / w_total)[:, None]]
    div x1 -> x2, other arithmetic: 0.82 us -> 0.02 us  [the longest x1 0.01 us: body(): w_new = (w_part * mine_w * (1.0 / h_total)[None, :])[None]]
where the time goes in v20:
time: 36.5 us; the launch traced here: 35.9 us
  starting transfers between devices  13.1 us (36%)
  waiting for transfers between devices  10.1 us (28%)
  other arithmetic  4.14 us (11%)
  matrix products  4.01 us (11%)
  local copies, waits for them, and re-layouts  3.43 us (9%)
  between operations  1.08 us (3%)
    ppermute x10, starting transfers between devices, shifted(): lax.ppermute(value, axis, [(i, (i + by) % length) for i in range(length)])  13.1 us
    ppermute x10, waiting for transfers between devices, shifted(): lax.ppermute(value, axis, [(i, (i + by) % length) for i in range(length)])  10.1 us
    unnamed x15, local copies, waits for them, and re-layouts  2.08 us
    dot_general x1, matrix products, dense_terms(): jnp.einsum('ij,kj->ik', chunks[0], h_stack[0], preferred_element_type=jnp...  1.34 us
    select_n x1, other arithmetic, body(): jnp.where(sub_index == p, h_factor[:, p * half:(p + 1) * half], own_piece)  0.96 us
    broadcast_in_dim x1, other arithmetic, body(): w_new = (w_part * mine_w * (1.0 / h_total)[None, :])[None]  0.9 us
    mul x1, other arithmetic, body(): h_new = h_factor.astype(jnp.float32) * numer_h * (1.0 / w_total)[:, None]  0.81 us
    convert_element_type x1, other arithmetic, dense_terms(): chunks.append(r_d.astype(jnp.bfloat16).reshape(tile_rows, width))  0.74 us
  transfers between devices with their start and end apart: 10, of which 3 were waited for; matrix products, arithmetic and copies ran while one was open for 19% of the time, Pallas kernels for 0%

profile of v20, /device:TPU:0, one launch (start us, length us, event | category | flops | bytes accessed | tf_op | source)
XLA Modules:
  0.0 35.9 jit_solution(13349821575126004955)
XLA Ops:
  0.7 1.0 %slice_select_fusion = bf16[256,128]{1,0:T(8,128)(2,1)S(1)} fusion(bf16[256,256]{1,0:T(8,128)(2,1)} %param.9, pred[]{:T(512)S(6)} %eq.158), kind=kLoop, calls=%fused_computation.69 | loop fusion | flops 32768 | bytes 196609 | tf_op jit(solution)/shard_map/jit(_where)/select_n | solution.py:125
  1.6 3.1 %collective-permute-start = (bf16[256,128]{1,0:T(8,128)(2,1)S(1)}, bf16[256,128]{1,0:T(8,128)(2,1)S(1)}, u32[]{:S(2)}, u32[]{:S(2)}) collective-permute-start(bf16[256,128]{1,0:T(8,128)(2,1)S(1)} %slice_select_fusion), channel_id=1, source_target_pairs={{0,4},{4,8},{8,12},{12,0},{1,5},{5,9},{9,13},{13,1},{2,6},{6,10},{... | collective-permute-start | bytes 196616 | tf_op jit(solution)/shard_map/ppermute | solution.py:9
  4.7 2.6 %collective-permute-start.1 = (bf16[256,128]{1,0:T(8,128)(2,1)S(1)}, bf16[256,128]{1,0:T(8,128)(2,1)S(1)}, u32[]{:S(2)}, u32[]{:S(2)}) collective-permute-start(bf16[256,128]{1,0:T(8,128)(2,1)S(1)} %slice_select_fusion), channel_id=1, source_target_pairs={{0,8},{4,12},{8,0},{12,4},{1,9},{5,13},{9,1},{13,5},{2,10},{6,14},... | collective-permute-start | bytes 196616 | tf_op jit(solution)/shard_map/ppermute | solution.py:9
  7.3 1.3 %collective-permute-start.2 = (bf16[256,128]{1,0:T(8,128)(2,1)S(1)}, bf16[256,128]{1,0:T(8,128)(2,1)S(1)}, u32[]{:S(2)}, u32[]{:S(2)}) collective-permute-start(bf16[256,128]{1,0:T(8,128)(2,1)S(1)} %slice_select_fusion), channel_id=1, source_target_pairs={{0,12},{4,0},{8,4},{12,8},{1,13},{5,1},{9,5},{13,9},{2,14},{6,2},{... | collective-permute-start | bytes 196616 | tf_op jit(solution)/shard_map/ppermute | solution.py:9
  8.7 1.3 %copy.15 = bf16[1,1,4,2,256,256]{5,4,2,3,1,0:T(8,128)(2,1)S(1)} copy(bf16[1,1,4,2,256,256]{5,4,3,2,1,0:T(8,128)(2,1)} %param.5) | data formatting | bytes 2097152 | tf_op args[0]
  10.1 0.4 %fusion.1 = bf16[4,256,256]{2,1,0:T(8,128)(2,1)S(1)} fusion(bf16[4,256,256]{2,1,0:T(8,128)(2,1)S(1)} %bitcast.103, pred[4]{0:T(512)(128)(4,1)S(1)} %get-tuple-element.46, pred[4]{0:T(512)(128)(4,1)S(1)} %get-tuple-element.45, pred[4]{0:T(512)(128)(4,1)S(1)} %get-tuple-element.44, bf16[256,256]{1,0:T(8,128)(2,1)S(1)} %copy-done.1, ...), kind=kOutput, calls=%fused_computation.5 | convolution fusion | flops 135790592 | bytes 2228236 | tf_op jit(solution)/shard_map/dot_general | solution.py:41
  10.5 0.4 convolution_bitcast_fusion.2
  10.9 1.3 %fusion.35 = f32[1024,256]{1,0:T(8,128)} fusion(bf16[1024,256]{1,0:T(8,128)(2,1)S(1)} %bitcast.107, bf16[256,256]{1,0:T(8,128)(2,1)S(1)} %copy-done.1), kind=kOutput, calls=%fused_computation.100 | convolution fusion | flops 134217728 | bytes 1703936 | tf_op jit(solution)/shard_map/ij,kj->ik/dot_general | solution.py:66
  13.4 0.2 copy.9
  13.8 1.4 %collective-permute-done.3 = bf16[3,256,128]{2,1,0:T(8,128)(2,1)S(1)} collective-permute-done((bf16[3,256,128]{2,1,0:T(8,128)(2,1)S(1)}, bf16[3,256,128]{2,1,0:T(8,128)(2,1)S(1)}, u32[]{:S(2)}, u32[]{:S(2)}) %collective-permute-start.3) | collective-permute-done | bytes 196640 | tf_op jit(solution)/shard_map/ppermute | solution.py:9
  15.3 0.6 %convolution_bitcast_fusion = f32[1024,768]{0,1:T(8,128)S(1)} fusion(bf16[1,1024,256]{2,1,0:T(8,128)(2,1)S(1)} %copy-done, bf16[256,256]{1,0:T(8,128)(2,1)S(1)} %get-tuple-element.28, bf16[256,256]{1,0:T(8,128)(2,1)S(1)} %get-tuple-element.29, bf16[256,256]{1,0:T(8,128)(2,1)S(1)} %get-tuple-element.27), kind=kOutput, calls=%fused_computation | convolution fusion | flops 403832832 | bytes 4063232 | tf_op jit(solution)/shard_map/dot_general | solution.py:42
  15.9 0.7 %fusion.7 = (bf16[1024,256]{0,1:T(8,128)(2,1)S(1)}, bf16[1024,256]{0,1:T(8,128)(2,1)S(1)}, bf16[1024,256]{0,1:T(8,128)(2,1)S(1)}) fusion(f32[1024,768]{0,1:T(8,128)S(1)} %convolution_bitcast_fusion, bf16[1024,256]{0,1:T(8,128)(2,1)S(1)} %copy.9, bf16[1024,256]{0,1:T(8,128)(2,1)S(1)} %copy.8, pred[1024]{0:T(1024)(128)(4,1)S(1)} %broadcast_in_dim.142, ...), kind=kLoop, calls=%fused_computation.16 | loop fusion | flops 4718592 | bytes 5776384 | tf_op jit(solution)/shard_map/convert_element_type | solution.py:57
  16.7 0.7 %convolution_bitcast_fusion.1 = f32[256,768]{1,0:T(8,128)S(1)} fusion(bf16[1024,256]{0,1:T(8,128)(2,1)S(1)} %get-tuple-element.15, bf16[1024,256]{0,1:T(8,128)(2,1)S(1)} %get-tuple-element.16, bf16[1024,256]{0,1:T(8,128)(2,1)S(1)} %get-tuple-element.14, bf16[1,1024,256]{2,1,0:T(8,128)(2,1)S(1)} %copy-done), kind=kOutput, calls=%fused_computation.6 | convolution fusion | flops 407371776 | bytes 2883584 | tf_op jit(solution)/shard_map/ik,ij->kj/dot_general | solution.py:62
  17.5 0.2 collective-permute-start.5
  17.9 0.7 %copy-done.2 = f32[1024,256]{1,0:T(8,128)S(1)} copy-done((f32[1024,256]{1,0:T(8,128)S(1)}, f32[1024,256]{1,0:T(8,128)}, u32[]{:S(2)}) %copy-start.2) | copy-done | bytes 1048600
  18.6 0.7 %convolution_add_fusion = f32[1024,256]{1,0:T(8,128)S(1)} fusion(f32[1024,256]{1,0:T(8,128)S(1)} %copy-done.2, bf16[1024,256]{0,1:T(8,128)(2,1)S(1)} %get-tuple-element.15, bf16[1024,256]{0,1:T(8,128)(2,1)S(1)} %get-tuple-element.16, bf16[1024,256]{0,1:T(8,128)(2,1)S(1)} %get-tuple-element.14, bf16[256,256]{1,0:T(8,128)(2,1)S(1)} %get-tuple-element.28, ...), kind=kOutput, calls=%fused_computation.2 | convolution fusion | flops 408813568 | bytes 4063232 | tf_op jit(solution)/shard_map/ij,kj->ik/dot_general | solution.py:68
  19.3 1.5 %collective-permute-start.4 = (f32[520,256]{1,0:T(8,128)S(1)}, f32[520,256]{1,0:T(8,128)S(1)}, u32[]{:S(2)}, u32[]{:S(2)}) collective-permute-start(f32[520,256]{1,0:T(8,128)S(1)} %pad_maximum_fusion.3), channel_id=1, source_target_pairs={{0,2},{2,0},{1,3},{3,1},{4,6},{6,4},{5,7},{7,5},{8,10},{10,8},{9,1... | collective-permute-start | bytes 1597448 | tf_op jit(solution)/shard_map/ppermute | solution.py:9
  21.0 0.4 %collective-permute-start.7 = (f32[264,128]{1,0:T(8,128)S(1)}, f32[264,128]{1,0:T(8,128)S(1)}, u32[]{:S(2)}, u32[]{:S(2)}) collective-permute-start(f32[264,128]{1,0:T(8,128)S(1)} %get-tuple-element.36), channel_id=1, source_target_pairs={{0,8},{4,12},{8,0},{12,4},{1,9},{5,13},{9,1},{13,5},{2,10},{6,14},... | collective-permute-start | bytes 405512 | tf_op jit(solution)/shard_map/ppermute | solution.py:9
  21.5 1.6 %collective-permute-start.8 = (f32[264,128]{1,0:T(8,128)S(1)}, f32[264,128]{1,0:T(8,128)S(1)}, u32[]{:S(2)}, u32[]{:S(2)}) collective-permute-start(f32[264,128]{1,0:T(8,128)S(1)} %get-tuple-element.37), channel_id=1, source_target_pairs={{0,4},{4,8},{8,12},{12,0},{1,5},{5,9},{9,13},{13,1},{2,6},{6,10},{... | collective-permute-start | bytes 405512 | tf_op jit(solution)/shard_map/ppermute | solution.py:9
  23.1 2.2 %collective-permute-start.6 = (f32[264,128]{1,0:T(8,128)S(1)}, f32[264,128]{1,0:T(8,128)S(1)}, u32[]{:S(2)}, u32[]{:S(2)}) collective-permute-start(f32[264,128]{1,0:T(8,128)S(1)} %concatenate.48), channel_id=1, source_target_pairs={{0,12},{4,0},{8,4},{12,8},{1,13},{5,1},{9,5},{13,9},{2,14},{6,2},{... | collective-permute-start | bytes 405512 | tf_op jit(solution)/shard_map/ppermute | solution.py:9
  25.3 8.2 %collective-permute-done.4 = f32[520,256]{1,0:T(8,128)S(1)} collective-permute-done((f32[520,256]{1,0:T(8,128)S(1)}, f32[520,256]{1,0:T(8,128)S(1)}, u32[]{:S(2)}, u32[]{:S(2)}) %collective-permute-start.4) | collective-permute-done | bytes 532512 | tf_op jit(solution)/shard_map/ppermute | solution.py:9
  33.7 0.9 %fusion.10 = f32[1,512,256]{2,1,0:T(8,128)} fusion(f32[520,256]{1,0:T(8,128)S(1)} %collective-permute-done.4, f32[2,512,256]{2,1,0:T(8,128)S(1)} %bitcast.112, s32[]{:T(128)S(6)} %select_n.173, f32[256]{0:T(256)S(1)} %bitcast.123, bf16[1,1024,256]{2,1,0:T(8,128)(2,1)S(1)} %copy-done, s32[]{:T(128)S(6)} %select_n.148), kind=kLoop, calls=%fused_computation.25 | loop fusion | flops 524288 | bytes 1836040 | tf_op jit(solution)/shard_map/broadcast_in_dim | solution.py:179
  34.6 0.4 %collective-permute-done.9 = f32[264,128]{1,0:T(8,128)S(1)} collective-permute-done((f32[264,128]{1,0:T(8,128)S(1)}, f32[264,128]{1,0:T(8,128)S(1)}, u32[]{:S(2)}, u32[]{:S(2)}) %collective-permute-start.9) | collective-permute-done | bytes 135200 | tf_op jit(solution)/shard_map/ppermute | solution.py:9
  35.1 0.8 %fusion.17 = f32[256,256]{1,0:T(8,128)} fusion(f32[264,128]{1,0:T(8,128)S(1)} %get-tuple-element.33, f32[264,128]{1,0:T(8,128)S(1)} %get-tuple-element.32, bf16[256,256]{1,0:T(8,128)(2,1)S(1)} %copy-done.1, f32[256]{0:T(256)S(1)} %bitcast.121), kind=kLoop, calls=%fused_computation.42 | loop fusion | flops 262144 | bytes 664576 | tf_op jit(solution)/shard_map/mul | solution.py:177
  (65 shorter events, 2.2 us)
Async XLA Ops:
  0.6 9.5 %copy-start.1 = (bf16[256,256]{1,0:T(8,128)(2,1)S(1)}, bf16[256,256]{1,0:T(8,128)(2,1)}, u32[]{:S(2)}) copy-start(bf16[256,256]{1,0:T(8,128)(2,1)} %param.9) | copy-start | bytes 393220
  0.6 9.4 %copy-start.3 = (s32[1,1,4,2]{2,3,1,0:T(2,128)S(1)}, s32[1,1,4,2]{2,3,1,0:T(2,128)}, u32[]{:S(2)}) copy-start(s32[1,1,4,2]{2,3,1,0:T(2,128)} %param.6) | copy-start | bytes 100
  0.7 9.4 %copy-start.4 = (s32[1,1,4]{2,1,0:T(1,128)S(1)}, s32[1,1,4]{2,1,0:T(1,128)}, u32[]{:S(2)}) copy-start(s32[1,1,4]{2,1,0:T(1,128)} %param.7) | copy-start | bytes 52
  0.7 9.5 %copy-start = (bf16[1,1024,256]{2,1,0:T(8,128)(2,1)S(1)}, bf16[1,1024,256]{2,1,0:T(8,128)(2,1)}, u32[]{:S(2)}) copy-start(bf16[1,1024,256]{2,1,0:T(8,128)(2,1)} %param.8) | copy-start | bytes 1572868
  1.6 12.0 %collective-permute-start = (bf16[256,128]{1,0:T(8,128)(2,1)S(1)}, bf16[256,128]{1,0:T(8,128)(2,1)S(1)}, u32[]{:S(2)}, u32[]{:S(2)}) collective-permute-start(bf16[256,128]{1,0:T(8,128)(2,1)S(1)} %slice_select_fusion), channel_id=1, source_target_pairs={{0,4},{4,8},{8,12},{12,0},{1,5},{5,9},{9,13},{13,1},{2,6},{6,10},{... | collective-permute-start | bytes 196616 | tf_op jit(solution)/shard_map/ppermute | solution.py:9
  4.7 8.9 %collective-permute-start.1 = (bf16[256,128]{1,0:T(8,128)(2,1)S(1)}, bf16[256,128]{1,0:T(8,128)(2,1)S(1)}, u32[]{:S(2)}, u32[]{:S(2)}) collective-permute-start(bf16[256,128]{1,0:T(8,128)(2,1)S(1)} %slice_select_fusion), channel_id=1, source_target_pairs={{0,8},{4,12},{8,0},{12,4},{1,9},{5,13},{9,1},{13,5},{2,10},{6,14},... | collective-permute-start | bytes 196616 | tf_op jit(solution)/shard_map/ppermute | solution.py:9
  7.3 6.4 %collective-permute-start.2 = (bf16[256,128]{1,0:T(8,128)(2,1)S(1)}, bf16[256,128]{1,0:T(8,128)(2,1)S(1)}, u32[]{:S(2)}, u32[]{:S(2)}) collective-permute-start(bf16[256,128]{1,0:T(8,128)(2,1)S(1)} %slice_select_fusion), channel_id=1, source_target_pairs={{0,12},{4,0},{8,4},{12,8},{1,13},{5,1},{9,5},{13,9},{2,14},{6,2},{... | collective-permute-start | bytes 196616 | tf_op jit(solution)/shard_map/ppermute | solution.py:9
  13.7 1.5 %collective-permute-start.3 = (bf16[3,256,128]{2,1,0:T(8,128)(2,1)S(1)}, bf16[3,256,128]{2,1,0:T(8,128)(2,1)S(1)}, u32[]{:S(2)}, u32[]{:S(2)}) collective-permute-start(bf16[3,256,128]{2,1,0:T(8,128)(2,1)S(1)} %pad_maximum_fusion.5), channel_id=1, source_target_pairs={{0,1},{1,0},{2,3},{3,2},{4,5},{5,4},{6,7},{7,6},{8,9},{9,8},{10,11... | collective-permute-start | bytes 589832 | tf_op jit(solution)/shard_map/ppermute | solution.py:9
  17.3 1.2 %copy-start.2 = (f32[1024,256]{1,0:T(8,128)S(1)}, f32[1024,256]{1,0:T(8,128)}, u32[]{:S(2)}) copy-start(f32[1024,256]{1,0:T(8,128)} %fusion.35) | copy-start | bytes 3145732
  17.5 3.3 %collective-permute-start.5 = (f32[1032,128]{1,0:T(8,128)S(1)}, f32[1032,128]{1,0:T(8,128)S(1)}, u32[]{:S(2)}, u32[]{:S(2)}) collective-permute-start(f32[1032,128]{1,0:T(8,128)S(1)} %broadcast_select_fusion), channel_id=1, source_target_pairs={{0,1},{1,0},{2,3},{3,2},{4,5},{5,4},{6,7},{7,6},{8,9},{9,8},{10,11... | collective-permute-start | bytes 1585160 | tf_op jit(solution)/shard_map/ppermute | solution.py:9
  19.3 14.2 %collective-permute-start.4 = (f32[520,256]{1,0:T(8,128)S(1)}, f32[520,256]{1,0:T(8,128)S(1)}, u32[]{:S(2)}, u32[]{:S(2)}) collective-permute-start(f32[520,256]{1,0:T(8,128)S(1)} %pad_maximum_fusion.3), channel_id=1, source_target_pairs={{0,2},{2,0},{1,3},{3,1},{4,6},{6,4},{5,7},{7,5},{8,10},{10,8},{9,1... | collective-permute-start | bytes 1597448 | tf_op jit(solution)/shard_map/ppermute | solution.py:9
  21.0 12.5 %collective-permute-start.7 = (f32[264,128]{1,0:T(8,128)S(1)}, f32[264,128]{1,0:T(8,128)S(1)}, u32[]{:S(2)}, u32[]{:S(2)}) collective-permute-start(f32[264,128]{1,0:T(8,128)S(1)} %get-tuple-element.36), channel_id=1, source_target_pairs={{0,8},{4,12},{8,0},{12,4},{1,9},{5,13},{9,1},{13,5},{2,10},{6,14},... | collective-permute-start | bytes 405512 | tf_op jit(solution)/shard_map/ppermute | solution.py:9
  21.5 12.1 %collective-permute-start.8 = (f32[264,128]{1,0:T(8,128)S(1)}, f32[264,128]{1,0:T(8,128)S(1)}, u32[]{:S(2)}, u32[]{:S(2)}) collective-permute-start(f32[264,128]{1,0:T(8,128)S(1)} %get-tuple-element.37), channel_id=1, source_target_pairs={{0,4},{4,8},{8,12},{12,0},{1,5},{5,9},{9,13},{13,1},{2,6},{6,10},{... | collective-permute-start | bytes 405512 | tf_op jit(solution)/shard_map/ppermute | solution.py:9
  23.1 10.5 %collective-permute-start.6 = (f32[264,128]{1,0:T(8,128)S(1)}, f32[264,128]{1,0:T(8,128)S(1)}, u32[]{:S(2)}, u32[]{:S(2)}) collective-permute-start(f32[264,128]{1,0:T(8,128)S(1)} %concatenate.48), channel_id=1, source_target_pairs={{0,12},{4,0},{8,4},{12,8},{1,13},{5,1},{9,5},{13,9},{2,14},{6,2},{... | collective-permute-start | bytes 405512 | tf_op jit(solution)/shard_map/ppermute | solution.py:9
  33.7 1.4 %collective-permute-start.9 = (f32[264,128]{1,0:T(8,128)S(1)}, f32[264,128]{1,0:T(8,128)S(1)}, u32[]{:S(2)}, u32[]{:S(2)}) collective-permute-start(f32[264,128]{1,0:T(8,128)S(1)} %pad_maximum_fusion.10), channel_id=1, source_target_pairs={{0,1},{1,0},{2,3},{3,2},{4,5},{5,4},{6,7},{7,6},{8,9},{9,8},{10,11... | collective-permute-start | bytes 405512 | tf_op jit(solution)/shard_map/ppermute | solution.py:9

commit v21 on v16

--- a/solution.py
+++ b/solution.py
@@ -104,6 +104,33 @@
     return [numer_h_stack[e] for e in range(n_row)], numer_w
 
 
+def pair_exchange(numer_h_stack, w_rows_sum, sub_index, rank, half):
+    n_row = len(numer_h_stack)
+
+    def halves(x):
+        lo, hi = x[:, :half], x[:, half:]
+        return jnp.where(sub_index == 0, lo, hi), jnp.where(sub_index == 0, hi, lo)
+
+    kept, sent = zip(*[halves(x) for x in numer_h_stack[1:] + [w_rows_sum]])
+    reduced = jnp.concatenate(kept) + shifted(jnp.concatenate(sent), "sub", 1)
+    extra = reduced[(n_row - 1) * rank:]
+    own_mine, own_theirs = halves(numer_h_stack[0])
+    mine_h = own_mine
+    got_w = extra
+    for d in reversed(range(1, n_row)):
+        message = jnp.concatenate([reduced[(d - 1) * rank:d * rank], extra])
+        message = shifted(message, "row", d)
+        mine_h = mine_h + message[:rank]
+        got_w = got_w + message[rank:]
+    final = jnp.concatenate([mine_h, got_w])
+    got = shifted(jnp.concatenate([final, own_theirs]), "sub", 1)
+    extra_rows = final.shape[0] - rank
+    mine = jnp.concatenate([final[:rank] + got[final.shape[0]:], final[rank:]])
+    theirs = jnp.concatenate([got[:rank] + own_theirs, got[rank:final.shape[0]]])
+    total = assemble([mine, theirs], sub_index, 2, 1)
+    return total[:rank], from_rows(total[rank:rank + extra_rows], rank)
+
+
 def body(a_blocks, block_list, block_count, w_factor, h_factor):
     values = a_blocks[0, 0]
     lists = block_list[0, 0]
@@ -149,30 +176,34 @@
     h_total = from_rows(got_h, rank)
 
     w_rows_sum = as_rows(w_sum, width)
-    messages = [
-        jnp.concatenate([x[:, p * half:(p + 1) * half] for x in numer_h_stack + [w_rows_sum]])
-        for p in range(n_sub)
-    ]
-    def piece_message(k):
-        want = (sub_index + k) % n_sub
-        chosen = messages[0]
-        for p in range(1, n_sub):
-            chosen = jnp.where(want == p, messages[p], chosen)
-        return chosen
-    reduced = piece_message(0)
-    for k in range(1, n_sub):
-        reduced = reduced + shifted(piece_message(k), "sub", k)
-    extra = reduced[n_row * rank:]
-    mine_h = reduced[:rank]
-    got_w = extra
-    for d in reversed(range(1, n_row)):
-        message = shifted(jnp.concatenate([reduced[d * rank:(d + 1) * rank], extra]), "row", d)
-        mine_h = mine_h + message[:rank]
-        got_w = got_w + message[rank:]
-    final = jnp.concatenate([mine_h, got_w])
-    total = assemble([final] + [shifted(final, "sub", k) for k in range(1, n_sub)], sub_index, n_sub, 1)
-    numer_h = total[:rank]
-    w_total = from_rows(total[rank:], rank)
+    if n_sub == 2:
+        numer_h, w_total = pair_exchange(numer_h_stack, w_rows_sum, sub_index, rank, half)
+    else:
+        messages = [
+            jnp.concatenate([x[:, p * half:(p + 1) * half] for x in numer_h_stack + [w_rows_sum]])
+            for p in range(n_sub)
+        ]
+        def piece_message(k):
+            want = (sub_index + k) % n_sub
+            chosen = messages[0]
+            for p in range(1, n_sub):
+                chosen = jnp.where(want == p, messages[p], chosen)
+            return chosen
+        reduced = piece_message(0)
+        for k in range(1, n_sub):
+            reduced = reduced + shifted(piece_message(k), "sub", k)
+        extra = reduced[n_row * rank:]
+        mine_h = reduced[:rank]
+        got_w = extra
+        for d in reversed(range(1, n_row)):
+            message = shifted(jnp.concatenate([reduced[d * rank:(d + 1) * rank], extra]), "row", d)
+            mine_h = mine_h + message[:rank]
+            got_w = got_w + message[rank:]
+        final = jnp.concatenate([mine_h, got_w])
+        total = assemble([final] + [shifted(final, "sub", k) for k in range(1, n_sub)], sub_index, n_sub, 1)
+        numer_h = total[:rank]
+        w_total = from_rows(total[rank:], rank)
+
 
     h_new = h_factor.astype(jnp.float32) * numer_h / w_total[:, None]
     w_part = lax.dynamic_slice_in_dim(w_tile, col_index * share, share, 0).astype(jnp.float32)

time: 36.5 us -> 43.2 us (1.18)
  waiting for transfers between devices: 10.1 us -> 13.4 us
  local copies, waits for them, and re-layouts: 3.43 us -> 6.15 us
  other arithmetic: 4.14 us -> 6.52 us
  starting transfers between devices: 13.1 us -> 12.1 us
    ppermute x10, waiting for transfers between devices: 10.1 us -> 13.4 us  [shifted(): lax.ppermute(value, axis, [(i, (i + by) % length) for i in range(length)])]
    broadcast_in_dim x12, local copies, waits for them, and re-layouts: 0.52 us -> 2.81 us  [dense_terms(): a_d = jnp.where(match[:, None, None], values[:, slot], a_d)]
    or x1, other arithmetic: 0.02 us -> 1.37 us  [dense_terms(): covered = covered | match]
    broadcast_in_dim x6, local copies, waits for them, and re-layouts: 0.26 us -> 1.38 us  [dense_terms(): r_d = jnp.where(covered[:, None, None], a_d.astype(jnp.float32) / p_d, 0.0)]
    ppermute x10, starting transfers between devices: 13.1 us -> 12.1 us  [shifted(): lax.ppermute(value, axis, [(i, (i + by) % length) for i in range(length)])]
    reduce_sum x1, other arithmetic: 0.15 us -> 1.19 us  [body(): w_sum = jnp.sum(w_tile.astype(jnp.float32), axis=0)]
    dot_general x1, matrix products: 1.34 us -> 0.33 us  [dense_terms(): jnp.einsum('ij,kj->ik', chunks[0], h_stack[0], preferred_element_type=jnp...]
    dot_general x1, matrix products: 0.39 us -> 1.08 us  [dense_terms(): jnp.dot(w_tile, h_stack[0], preferred_element_type=jnp.float32)]
  transfers between devices with their start and end apart: 10 -> 10, of which waited for: 3 -> 4; matrix products, arithmetic and copies ran while one was open for 19% -> 28% of each run, Pallas kernels for 0% -> 0%
where the time goes in v21:
time: 43.2 us; the launch traced here: 42.9 us
  waiting for transfers between devices  13.4 us (31%)
  starting transfers between devices  12.1 us (28%)
  other arithmetic  6.52 us (15%)
  local copies, waits for them, and re-layouts  6.15 us (14%)
  matrix products  3.67 us (8%)
  between operations  1.04 us (2%)
    ppermute x10, waiting for transfers between devices, shifted(): lax.ppermute(value, axis, [(i, (i + by) % length) for i in range(length)])  13.4 us
    ppermute x10, starting transfers between devices, shifted(): lax.ppermute(value, axis, [(i, (i + by) % length) for i in range(length)])  12.1 us
    broadcast_in_dim x12, local copies, waits for them, and re-layouts, dense_terms(): a_d = jnp.where(match[:, None, None], values[:, slot], a_d)  2.81 us
    unnamed x17, local copies, waits for them, and re-layouts  1.39 us
    broadcast_in_dim x6, local copies, waits for them, and re-layouts, dense_terms(): r_d = jnp.where(covered[:, None, None], a_d.astype(jnp.float32) / p_d, 0.0)  1.38 us
    or x1, other arithmetic, dense_terms(): covered = covered | match  1.37 us
    reduce_sum x1, other arithmetic, body(): w_sum = jnp.sum(w_tile.astype(jnp.float32), axis=0)  1.19 us
    dot_general x1, matrix products, dense_terms(): jnp.dot(w_tile, h_stack[0], preferred_element_type=jnp.float32)  1.08 us
  transfers between devices with their start and end apart: 10, of which 4 were waited for; matrix products, arithmetic and copies ran while one was open for 28% of the time, Pallas kernels for 0%

profile of v21, /device:TPU:0, one launch (start us, length us, event | category | flops | bytes accessed | tf_op | source)
XLA Modules:
  0.0 42.9 jit_solution(4380124119740519009)
XLA Ops:
  0.6 0.9 %slice_select_fusion.7 = bf16[256,128]{1,0:T(8,128)(2,1)S(1)} fusion(bf16[256,256]{1,0:T(8,128)(2,1)} %param.9, pred[]{:T(512)S(6)} %eq.164), kind=kLoop, calls=%fused_computation.72 | loop fusion | flops 32768 | bytes 196609 | tf_op jit(solution)/shard_map/jit(_where)/select_n | solution.py:152
  1.5 5.1 %collective-permute-start.2 = (bf16[256,128]{1,0:T(8,128)(2,1)S(1)}, bf16[256,128]{1,0:T(8,128)(2,1)S(1)}, u32[]{:S(2)}, u32[]{:S(2)}) collective-permute-start(bf16[256,128]{1,0:T(8,128)(2,1)S(1)} %slice_select_fusion.7), channel_id=1, source_target_pairs={{0,12},{4,0},{8,4},{12,8},{1,13},{5,1},{9,5},{13,9},{2,14},{6,2},{... | collective-permute-start | bytes 196616 | tf_op jit(solution)/shard_map/ppermute | solution.py:9
  6.6 1.0 %collective-permute-start = (bf16[256,128]{1,0:T(8,128)(2,1)S(1)}, bf16[256,128]{1,0:T(8,128)(2,1)S(1)}, u32[]{:S(2)}, u32[]{:S(2)}) collective-permute-start(bf16[256,128]{1,0:T(8,128)(2,1)S(1)} %slice_select_fusion.7), channel_id=1, source_target_pairs={{0,4},{4,8},{8,12},{12,0},{1,5},{5,9},{9,13},{13,1},{2,6},{6,10},{... | collective-permute-start | bytes 196616 | tf_op jit(solution)/shard_map/ppermute | solution.py:9
  7.6 1.2 %convert_reduce_fusion = f32[256]{0:T(256)S(1)} fusion(bf16[1,1024,256]{2,1,0:T(8,128)(2,1)} %param.8), kind=kLoop, calls=%fused_computation.18 | loop fusion | flops 524032 | bytes 525312 | tf_op jit(solution)/shard_map/reduce_sum | solution.py:159
  8.9 1.4 %fusion.31 = (pred[4]{0:T(512)(128)(4,1)S(1)}, pred[4]{0:T(512)(128)(4,1)S(1)}, pred[4]{0:T(512)(128)(4,1)S(1)}, pred[4]{0:T(512)(128)(4,1)S(1)}, pred[4]{0:T(51...) fusion(s32[1,1,4]{2,1,0:T(1,128)} %param.7, ...), kind=kLoop, calls=%fused_computation.95 | loop fusion | flops 88 | bytes 112 | tf_op jit(solution)/shard_map/or | solution.py:54
  10.6 0.6 %broadcast_in_dim.146 = pred[1024]{0:T(1024)(128)(4,1)} reshape(pred[4,256]{1,0:T(4,128)(4,1)S(1)} %broadcast_in_dim.145) | data formatting | bytes 2048 | tf_op jit(solution)/shard_map/jit(_where)/broadcast_in_dim | solution.py:56
  11.2 0.6 %broadcast_in_dim.149 = pred[1024]{0:T(1024)(128)(4,1)} reshape(pred[4,256]{1,0:T(4,128)(4,1)S(1)} %broadcast_in_dim.148) | data formatting | bytes 2048 | tf_op jit(solution)/shard_map/jit(_where)/broadcast_in_dim | solution.py:53
  11.9 0.6 %broadcast_in_dim.152 = pred[1024]{0:T(1024)(128)(4,1)} reshape(pred[4,256]{1,0:T(4,128)(4,1)S(1)} %broadcast_in_dim.151) | data formatting | bytes 2048 | tf_op jit(solution)/shard_map/jit(_where)/broadcast_in_dim | solution.py:53
  13.2 0.6 %broadcast_in_dim.158 = pred[1024]{0:T(1024)(128)(4,1)} reshape(pred[4,256]{1,0:T(4,128)(4,1)S(1)} %broadcast_in_dim.157) | data formatting | bytes 2048 | tf_op jit(solution)/shard_map/jit(_where)/broadcast_in_dim | solution.py:53
  14.4 1.4 %copy.15 = bf16[1,1,4,2,256,256]{5,4,2,3,1,0:T(8,128)(2,1)S(1)} copy(bf16[1,1,4,2,256,256]{5,4,3,2,1,0:T(8,128)(2,1)} %param.5) | data formatting | bytes 2097152 | tf_op args[0]
  16.3 1.1 %fusion.1 = bf16[4,256,256]{2,1,0:T(8,128)(2,1)S(1)} fusion(bf16[4,256,256]{2,1,0:T(8,128)(2,1)S(1)} %bitcast.103, pred[4]{0:T(512)(128)(4,1)} %get-tuple-element.48, pred[4]{0:T(512)(128)(4,1)} %get-tuple-element.47, pred[4]{0:T(512)(128)(4,1)} %get-tuple-element.46, bf16[256,256]{1,0:T(8,128)(2,1)S(1)} %copy-done.1, bf16[4,2,256,256]{3,2,0,1:T(8,128)(2,1)S(1)} %bitcast.105), kind=kOutput, calls=%fused_computation.5 | convolution fusion | flops 135790592 | bytes 2228236 | tf_op jit(solution)/shard_map/dot_general | solution.py:41
  18.0 1.0 %collective-permute-done.3 = bf16[3,256,128]{2,1,0:T(8,128)(2,1)S(1)} collective-permute-done((bf16[3,256,128]{2,1,0:T(8,128)(2,1)S(1)}, bf16[3,256,128]{2,1,0:T(8,128)(2,1)S(1)}, u32[]{:S(2)}, u32[]{:S(2)}) %collective-permute-start.3) | collective-permute-done | bytes 196640 | tf_op jit(solution)/shard_map/ppermute | solution.py:9
  19.1 0.6 %convolution_bitcast_fusion = f32[1024,768]{0,1:T(8,128)S(1)} fusion(bf16[1,1024,256]{2,1,0:T(8,128)(2,1)S(1)} %copy-done, bf16[256,256]{1,0:T(8,128)(2,1)S(1)} %get-tuple-element.28, bf16[256,256]{1,0:T(8,128)(2,1)S(1)} %get-tuple-element.29, bf16[256,256]{1,0:T(8,128)(2,1)S(1)} %get-tuple-element.27), kind=kOutput, calls=%fused_computation | convolution fusion | flops 403832832 | bytes 4063232 | tf_op jit(solution)/shard_map/dot_general | solution.py:42
  19.8 0.7 %fusion.7 = (bf16[1024,256]{0,1:T(8,128)(2,1)S(1)}, bf16[1024,256]{0,1:T(8,128)(2,1)S(1)}, bf16[1024,256]{0,1:T(8,128)(2,1)S(1)}) fusion(f32[1024,768]{0,1:T(8,128)S(1)} %convolution_bitcast_fusion, bf16[1024,256]{0,1:T(8,128)(2,1)S(1)} %copy.9, bf16[1024,256]{0,1:T(8,128)(2,1)S(1)} %copy.8, pred[1024]{0:T(1024)(128)(4,1)S(1)} %broadcast_in_dim.142, ...), kind=kLoop, calls=%fused_computation.16 | loop fusion | flops 4718592 | bytes 5776384 | tf_op jit(solution)/shard_map/convert_element_type | solution.py:57
  20.5 0.7 %convolution_bitcast_fusion.1 = f32[256,768]{1,0:T(8,128)S(1)} fusion(bf16[1024,256]{0,1:T(8,128)(2,1)S(1)} %get-tuple-element.15, bf16[1024,256]{0,1:T(8,128)(2,1)S(1)} %get-tuple-element.16, bf16[1024,256]{0,1:T(8,128)(2,1)S(1)} %get-tuple-element.14, bf16[1,1024,256]{2,1,0:T(8,128)(2,1)S(1)} %copy-done), kind=kOutput, calls=%fused_computation.6 | convolution fusion | flops 407371776 | bytes 2883584 | tf_op jit(solution)/shard_map/ik,ij->kj/dot_general | solution.py:62
  21.5 0.6 %convolution_add_fusion = f32[1024,256]{1,0:T(8,128)S(1)} fusion(f32[1024,256]{1,0:T(8,128)S(1)} %fusion.37, bf16[1024,256]{0,1:T(8,128)(2,1)S(1)} %get-tuple-element.15, bf16[1024,256]{0,1:T(8,128)(2,1)S(1)} %get-tuple-element.16, bf16[1024,256]{0,1:T(8,128)(2,1)S(1)} %get-tuple-element.14, bf16[256,256]{1,0:T(8,128)(2,1)S(1)} %get-tuple-element.28, ...), kind=kOutput, calls=%fused_computation.2 | convolution fusion | flops 408813568 | bytes 4063232 | tf_op jit(solution)/shard_map/ij,kj->ik/dot_general | solution.py:68
  22.4 1.6 %collective-permute-start.4 = (f32[520,256]{1,0:T(8,128)S(1)}, f32[520,256]{1,0:T(8,128)S(1)}, u32[]{:S(2)}, u32[]{:S(2)}) collective-permute-start(f32[520,256]{1,0:T(8,128)S(1)} %pad_maximum_fusion.3), channel_id=1, source_target_pairs={{0,2},{2,0},{1,3},{3,1},{4,6},{6,4},{5,7},{7,5},{8,10},{10,8},{9,1... | collective-permute-start | bytes 1597448 | tf_op jit(solution)/shard_map/ppermute | solution.py:9
  24.0 2.9 %collective-permute-start.6 = (f32[264,128]{1,0:T(8,128)S(1)}, f32[264,128]{1,0:T(8,128)S(1)}, u32[]{:S(2)}, u32[]{:S(2)}) collective-permute-start(f32[264,128]{1,0:T(8,128)S(1)} %concatenate.56), channel_id=1, source_target_pairs={{0,12},{4,0},{8,4},{12,8},{1,13},{5,1},{9,5},{13,9},{2,14},{6,2},{... | collective-permute-start | bytes 405512 | tf_op jit(solution)/shard_map/ppermute | solution.py:9
  27.0 1.2 %collective-permute-start.7 = (f32[264,128]{1,0:T(8,128)S(1)}, f32[264,128]{1,0:T(8,128)S(1)}, u32[]{:S(2)}, u32[]{:S(2)}) collective-permute-start(f32[264,128]{1,0:T(8,128)S(1)} %get-tuple-element.38), channel_id=1, source_target_pairs={{0,8},{4,12},{8,0},{12,4},{1,9},{5,13},{9,1},{13,5},{2,10},{6,14},... | collective-permute-start | bytes 405512 | tf_op jit(solution)/shard_map/ppermute | solution.py:9
  28.5 8.3 %collective-permute-done.4 = f32[520,256]{1,0:T(8,128)S(1)} collective-permute-done((f32[520,256]{1,0:T(8,128)S(1)}, f32[520,256]{1,0:T(8,128)S(1)}, u32[]{:S(2)}, u32[]{:S(2)}) %collective-permute-start.4) | collective-permute-done | bytes 532512 | tf_op jit(solution)/shard_map/ppermute | solution.py:9
  36.9 3.4 %collective-permute-done.7 = f32[264,128]{1,0:T(8,128)S(1)} collective-permute-done((f32[264,128]{1,0:T(8,128)S(1)}, f32[264,128]{1,0:T(8,128)S(1)}, u32[]{:S(2)}, u32[]{:S(2)}) %collective-permute-start.7) | collective-permute-done | bytes 135200 | tf_op jit(solution)/shard_map/ppermute | solution.py:9
  40.5 0.9 %fusion.10 = f32[1,512,256]{2,1,0:T(8,128)} fusion(f32[520,256]{1,0:T(8,128)S(1)} %collective-permute-done.4, f32[2,512,256]{2,1,0:T(8,128)S(1)} %bitcast.112, s32[]{:T(128)S(6)} %select_n.201, f32[256]{0:T(256)S(1)} %bitcast.123, bf16[1,1024,256]{2,1,0:T(8,128)(2,1)S(1)} %copy-done, s32[]{:T(128)S(6)} %select_n.176), kind=kLoop, calls=%fused_computation.24 | loop fusion | flops 524288 | bytes 1836040 | tf_op jit(solution)/shard_map/broadcast_in_dim | solution.py:210
  41.4 0.6 %collective-permute-done.9 = f32[520,128]{1,0:T(8,128)S(1)} collective-permute-done((f32[520,128]{1,0:T(8,128)S(1)}, f32[520,128]{1,0:T(8,128)S(1)}, u32[]{:S(2)}, u32[]{:S(2)}) %collective-permute-start.9) | collective-permute-done | bytes 266272 | tf_op jit(solution)/shard_map/ppermute | solution.py:9
  42.1 0.8 %fusion.17 = f32[256,256]{1,0:T(8,128)} fusion(f32[264,128]{1,0:T(8,128)S(1)} %get-tuple-element.33, f32[264,128]{1,0:T(8,128)S(1)} %get-tuple-element.32, bf16[256,256]{1,0:T(8,128)(2,1)S(1)} %copy-done.1, f32[256]{0:T(256)S(1)} %bitcast.121), kind=kLoop, calls=%fused_computation.43 | loop fusion | flops 262144 | bytes 664576 | tf_op jit(solution)/shard_map/div | solution.py:208
  (70 shorter events, 4.1 us)
Async XLA Ops:
  1.5 15.9 %collective-permute-start.2 = (bf16[256,128]{1,0:T(8,128)(2,1)S(1)}, bf16[256,128]{1,0:T(8,128)(2,1)S(1)}, u32[]{:S(2)}, u32[]{:S(2)}) collective-permute-start(bf16[256,128]{1,0:T(8,128)(2,1)S(1)} %slice_select_fusion.7), channel_id=1, source_target_pairs={{0,12},{4,0},{8,4},{12,8},{1,13},{5,1},{9,5},{13,9},{2,14},{6,2},{... | collective-permute-start | bytes 196616 | tf_op jit(solution)/shard_map/ppermute | solution.py:9
  6.6 10.8 %collective-permute-start.1 = (bf16[256,128]{1,0:T(8,128)(2,1)S(1)}, bf16[256,128]{1,0:T(8,128)(2,1)S(1)}, u32[]{:S(2)}, u32[]{:S(2)}) collective-permute-start(bf16[256,128]{1,0:T(8,128)(2,1)S(1)} %slice_select_fusion.7), channel_id=1, source_target_pairs={{0,8},{4,12},{8,0},{12,4},{1,9},{5,13},{9,1},{13,5},{2,10},{6,14},... | collective-permute-start | bytes 196616 | tf_op jit(solution)/shard_map/ppermute | solution.py:9
  6.6 10.8 %collective-permute-start = (bf16[256,128]{1,0:T(8,128)(2,1)S(1)}, bf16[256,128]{1,0:T(8,128)(2,1)S(1)}, u32[]{:S(2)}, u32[]{:S(2)}) collective-permute-start(bf16[256,128]{1,0:T(8,128)(2,1)S(1)} %slice_select_fusion.7), channel_id=1, source_target_pairs={{0,4},{4,8},{8,12},{12,0},{1,5},{5,9},{9,13},{13,1},{2,6},{6,10},{... | collective-permute-start | bytes 196616 | tf_op jit(solution)/shard_map/ppermute | solution.py:9
  14.4 1.9 %copy-start = (bf16[1,1024,256]{2,1,0:T(8,128)(2,1)S(1)}, bf16[1,1024,256]{2,1,0:T(8,128)(2,1)}, u32[]{:S(2)}) copy-start(bf16[1,1024,256]{2,1,0:T(8,128)(2,1)} %param.8) | copy-start | bytes 1572868
  14.4 1.9 %copy-start.1 = (bf16[256,256]{1,0:T(8,128)(2,1)S(1)}, bf16[256,256]{1,0:T(8,128)(2,1)}, u32[]{:S(2)}) copy-start(bf16[256,256]{1,0:T(8,128)(2,1)} %param.9) | copy-start | bytes 393220
  17.5 1.5 %collective-permute-start.3 = (bf16[3,256,128]{2,1,0:T(8,128)(2,1)S(1)}, bf16[3,256,128]{2,1,0:T(8,128)(2,1)S(1)}, u32[]{:S(2)}, u32[]{:S(2)}) collective-permute-start(bf16[3,256,128]{2,1,0:T(8,128)(2,1)S(1)} %pad_maximum_fusion.7), channel_id=1, source_target_pairs={{0,1},{1,0},{2,3},{3,2},{4,5},{5,4},{6,7},{7,6},{8,9},{9,8},{10,11... | collective-permute-start | bytes 589832 | tf_op jit(solution)/shard_map/ppermute | solution.py:9
  17.9 1.8 %copy-start.2 = (pred[1024]{0:T(1024)(128)(4,1)S(1)}, pred[1024]{0:T(1024)(128)(4,1)}, u32[]{:S(2)}) copy-start(pred[1024]{0:T(1024)(128)(4,1)} %broadcast_in_dim.146) | copy-start | bytes 3076
  17.9 1.8 %copy-start.3 = (pred[1024]{0:T(1024)(128)(4,1)S(1)}, pred[1024]{0:T(1024)(128)(4,1)}, u32[]{:S(2)}) copy-start(pred[1024]{0:T(1024)(128)(4,1)} %broadcast_in_dim.149) | copy-start | bytes 3076
  17.9 1.8 %copy-start.4 = (pred[1024]{0:T(1024)(128)(4,1)S(1)}, pred[1024]{0:T(1024)(128)(4,1)}, u32[]{:S(2)}) copy-start(pred[1024]{0:T(1024)(128)(4,1)} %broadcast_in_dim.152) | copy-start | bytes 3076
  17.9 1.8 %copy-start.5 = (pred[1024]{0:T(1024)(128)(4,1)S(1)}, pred[1024]{0:T(1024)(128)(4,1)}, u32[]{:S(2)}) copy-start(pred[1024]{0:T(1024)(128)(4,1)} %broadcast_in_dim.155) | copy-start | bytes 3076
  17.9 1.8 %copy-start.6 = (pred[1024]{0:T(1024)(128)(4,1)S(1)}, pred[1024]{0:T(1024)(128)(4,1)}, u32[]{:S(2)}) copy-start(pred[1024]{0:T(1024)(128)(4,1)} %broadcast_in_dim.158) | copy-start | bytes 3076
  18.0 1.8 %copy-start.7 = (pred[1024]{0:T(1024)(128)(4,1)S(1)}, pred[1024]{0:T(1024)(128)(4,1)}, u32[]{:S(2)}) copy-start(pred[1024]{0:T(1024)(128)(4,1)} %broadcast_in_dim.161) | copy-start | bytes 3076
  21.3 2.7 %collective-permute-start.5 = (f32[776,128]{1,0:T(8,128)S(1)}, f32[776,128]{1,0:T(8,128)S(1)}, u32[]{:S(2)}, u32[]{:S(2)}) collective-permute-start(f32[776,128]{1,0:T(8,128)S(1)} %pad_maximum_fusion.4), channel_id=1, source_target_pairs={{0,1},{1,0},{2,3},{3,2},{4,5},{5,4},{6,7},{7,6},{8,9},{9,8},{10,11... | collective-permute-start | bytes 1191944 | tf_op jit(solution)/shard_map/ppermute | solution.py:9
  22.4 14.4 %collective-permute-start.4 = (f32[520,256]{1,0:T(8,128)S(1)}, f32[520,256]{1,0:T(8,128)S(1)}, u32[]{:S(2)}, u32[]{:S(2)}) collective-permute-start(f32[520,256]{1,0:T(8,128)S(1)} %pad_maximum_fusion.3), channel_id=1, source_target_pairs={{0,2},{2,0},{1,3},{3,1},{4,6},{6,4},{5,7},{7,5},{8,10},{10,8},{9,1... | collective-permute-start | bytes 1597448 | tf_op jit(solution)/shard_map/ppermute | solution.py:9
  24.0 12.8 %collective-permute-start.6 = (f32[264,128]{1,0:T(8,128)S(1)}, f32[264,128]{1,0:T(8,128)S(1)}, u32[]{:S(2)}, u32[]{:S(2)}) collective-permute-start(f32[264,128]{1,0:T(8,128)S(1)} %concatenate.56), channel_id=1, source_target_pairs={{0,12},{4,0},{8,4},{12,8},{1,13},{5,1},{9,5},{13,9},{2,14},{6,2},{... | collective-permute-start | bytes 405512 | tf_op jit(solution)/shard_map/ppermute | solution.py:9
  27.0 13.3 %collective-permute-start.7 = (f32[264,128]{1,0:T(8,128)S(1)}, f32[264,128]{1,0:T(8,128)S(1)}, u32[]{:S(2)}, u32[]{:S(2)}) collective-permute-start(f32[264,128]{1,0:T(8,128)S(1)} %get-tuple-element.38), channel_id=1, source_target_pairs={{0,8},{4,12},{8,0},{12,4},{1,9},{5,13},{9,1},{13,5},{2,10},{6,14},... | collective-permute-start | bytes 405512 | tf_op jit(solution)/shard_map/ppermute | solution.py:9
  28.2 12.1 %collective-permute-start.8 = (f32[264,128]{1,0:T(8,128)S(1)}, f32[264,128]{1,0:T(8,128)S(1)}, u32[]{:S(2)}, u32[]{:S(2)}) collective-permute-start(f32[264,128]{1,0:T(8,128)S(1)} %get-tuple-element.39), channel_id=1, source_target_pairs={{0,4},{4,8},{8,12},{12,0},{1,5},{5,9},{9,13},{13,1},{2,6},{6,10},{... | collective-permute-start | bytes 405512 | tf_op jit(solution)/shard_map/ppermute | solution.py:9
  40.4 1.6 %collective-permute-start.9 = (f32[520,128]{1,0:T(8,128)S(1)}, f32[520,128]{1,0:T(8,128)S(1)}, u32[]{:S(2)}, u32[]{:S(2)}) collective-permute-start(f32[520,128]{1,0:T(8,128)S(1)} %pad_maximum_fusion.6), channel_id=1, source_target_pairs={{0,1},{1,0},{2,3},{3,2},{4,5},{5,4},{6,7},{7,6},{8,9},{9,8},{10,11... | collective-permute-start | bytes 798728 | tf_op jit(solution)/shard_map/ppermute | solution.py:9
